TPU v7x, 32 devices: a whole 2x2x4 slice. The times are simulated.
32 devices in a mesh: exp: 4 (over z), row: 4 (over y, core), col: 2 (over x).
Axes of the slice: x: 2, y: 2, z: 4, core: 2. Of those that a mesh axis runs over, the one named last changes fastest.
Arguments:
- exposures: float32 [64, 128, 1024], P('exp', 'row', 'col'), may hold values from -6 to 6
- bad_pixels: int32 [64, 128, 1024], P('exp', 'row', 'col'), may hold values 0 or 1
- offsets: int32 [64, 2], P('exp'), may hold values from -8 to 8, as said below
- warp_index: int32 [64, 2], P('exp'), may hold values from 0 to 15
- blur_index: int32 [64], P('exp'), may hold values from 0 to 7
Outputs:
- residual: float32 [64, 128, 1024], P('exp', 'row', 'col')
- median_sky: float32 [128, 1024], P('row', 'col')
Inputs may be any that keep to these rules, and one draw needn't show every extreme that they name: `offsets`: in each component some exposure has the offset -8 and some has 8.
All inputs are finite; a program needn't handle non-finite values. No bound on the sum of `bad_pixels` on one device may be relied on, other than what follows from the above.
Results may differ from a plain program's by a relative error of at most 0.0003.
Values sent between devices are 32-bit elements; how exact they have to be, the bound alone decides.
No kernel may reach another device: no remote copies, remote signals or barrier semaphores. Data moves between devices by JAX's collectives and lax.ppermute only.
A program may use at most 64 MiB of HBM per device.

v0:
```python
import jax
import jax.numpy as jnp
from jax import lax
from jax.sharding import PartitionSpec as P

NFRAC = 16
NPSF = 8
PSF_RADIUS = 4
PASSES = 16
HALO = 11


sentinel = 1000000.0
half_sentinel = 500000.0
pivot_span = 16.0


def extended(block, sides, width):
    for axis, dim in sides:
        count = lax.axis_size(axis)
        forward = [(i, i + 1) for i in range(count - 1)]
        backward = [(target, source) for source, target in forward]
        low = lax.ppermute(
            lax.slice_in_dim(block, block.shape[dim] - width, None, axis=dim), axis, forward
        )
        high = lax.ppermute(lax.slice_in_dim(block, 0, width, axis=dim), axis, backward)
        block = jnp.concatenate([low, block, high], axis=dim)
    return block


def lanczos_table():
    fraction = jnp.arange(NFRAC, dtype=jnp.float32) / NFRAC
    offset_grid = jnp.arange(-2, 4, dtype=jnp.float32)
    spread = offset_grid[None, :] - fraction[:, None]
    kernel = jnp.sinc(spread) * jnp.sinc(spread / 3.0)
    return kernel / jnp.sum(kernel, axis=1, keepdims=True)


def blur_table():
    offset_grid = jnp.arange(-PSF_RADIUS, PSF_RADIUS + 1, dtype=jnp.float32)
    widths = 0.7 + 0.2 * jnp.arange(NPSF, dtype=jnp.float32)
    kernel = jnp.exp(-0.5 * (offset_grid[None, :] / widths[:, None]) ** 2)
    return kernel / jnp.sum(kernel, axis=1, keepdims=True)


def lookup(indices, entries, kernel_table):
    chooser = (indices[:, None] == lax.broadcasted_iota(jnp.int32, (1, entries), 1)).astype(
        jnp.float32
    )
    return jnp.dot(chooser, kernel_table, precision=lax.Precision.HIGHEST)


def placed_taps(weights, shifts):
    reach = 2 * HALO + 1
    positions = lax.broadcasted_iota(jnp.int32, (1, 1, reach), 2)
    tap_slot = HALO + shifts[:, None, None] + lax.broadcasted_iota(jnp.int32, (1, 6, 1), 1) - 2
    spread = (tap_slot == positions).astype(jnp.float32)
    return jnp.sum(weights[:, :, None] * spread, axis=1)


def resample_axis(stack, coefficients, out_len, which_axis):
    out_shape = list(stack.shape)
    out_shape[which_axis] = out_len
    total = jnp.zeros(tuple(out_shape), jnp.float32)
    for position in range(2 * HALO + 1):
        window = lax.slice_in_dim(stack, position, position + out_len, 1, which_axis)
        total = total + coefficients[:, position, None, None] * window
    return total


def bisect_lower(valid_count, count_below):

    def one_pass(sweep_no, bounds):
        lower_edge, upper_edge = bounds
        middle = 0.5 * (lower_edge + upper_edge)
        enough = 2.0 * count_below(middle) >= valid_count
        return (jnp.where(enough, lower_edge, middle), jnp.where(enough, middle, upper_edge))

    initial = (
        jnp.full(valid_count.shape, -pivot_span, jnp.float32),
        jnp.full(valid_count.shape, pivot_span, jnp.float32),
    )
    return lax.fori_loop(0, PASSES, one_pass, initial)[0]


def stack_median(pixel_stack):
    valid_count = jnp.sum(pixel_stack < half_sentinel, axis=0, dtype=jnp.float32)

    def count_below(middle):
        return jnp.sum(pixel_stack <= middle[None], axis=0, dtype=jnp.float32)

    lower_edge = bisect_lower(valid_count, count_below)
    return jnp.min(jnp.where(pixel_stack > lower_edge[None], pixel_stack, sentinel), axis=0)


def body(exposures, bad_pixels, offsets, warp_index, blur_index):
    group_size, row_count, col_count = exposures.shape
    kernel_table = lanczos_table()
    coef_down = placed_taps(lookup(warp_index[:, 0], NFRAC, kernel_table), offsets[:, 0])
    coef_across = placed_taps(lookup(warp_index[:, 1], NFRAC, kernel_table), offsets[:, 1])
    padded = extended(exposures, (("row", 1), ("col", 2)), HALO)
    across = resample_axis(padded, coef_down, row_count, 1)
    warped = resample_axis(across, coef_across, col_count, 2)
    flagged = jnp.where(bad_pixels == 1, sentinel, warped)
    band = stack_median(lax.all_to_all(flagged, "exp", split_axis=1, concat_axis=0, tiled=True))
    median_sky = lax.all_gather(band, "exp", axis=0, tiled=True)
    bordered = extended(median_sky, (("row", 0), ("col", 1)), PSF_RADIUS)
    blur = blur_table()
    taps = 2 * PSF_RADIUS + 1
    blurred_rows = jnp.zeros((NPSF, row_count, col_count + 2 * PSF_RADIUS), jnp.float32)
    for tap_no in range(taps):
        blurred_rows = (
            blurred_rows
            + blur[:, tap_no, None, None] * bordered[None, tap_no : tap_no + row_count, :]
        )
    smoothed = jnp.zeros((NPSF, row_count, col_count), jnp.float32)
    for tap_no in range(taps):
        smoothed = (
            smoothed + blur[:, tap_no, None, None] * blurred_rows[:, :, tap_no : tap_no + col_count]
        )
    chooser = (blur_index[:, None] == lax.broadcasted_iota(jnp.int32, (1, NPSF), 1)).astype(
        jnp.float32
    )
    sky_model = jnp.zeros((group_size, row_count, col_count), jnp.float32)
    for kernel_no in range(NPSF):
        sky_model = sky_model + chooser[:, kernel_no, None, None] * smoothed[kernel_no][None]
    residual = jnp.where(bad_pixels == 1, 0.0, warped - sky_model)
    return (residual, median_sky)


def solution(mesh):
    return jax.shard_map(
        body,
        mesh=mesh,
        in_specs=(
            P("exp", "row", "col"),
            P("exp", "row", "col"),
            P("exp", None),
            P("exp", None),
            P("exp"),
        ),
        out_specs=(P("exp", "row", "col"), P("row", "col")),
        check_vma=False,
    )
```

profile of v0, /device:TPU:1, one launch (start us, length us, event | category | flops | bytes accessed | tf_op | source)
XLA Modules:
  0.0 98.5 jit_solution(2107724615975199273)
XLA Ops:
  0.6 1.3 %fusion.132 = (f32[16,11,512]{2,1,0:T(8,128)S(1)}, f32[16,11,512]{2,1,0:T(8,128)S(1)}) fusion(f32[16,32,512]{2,1,0:T(8,128)} %param.8), kind=kLoop, calls=%fused_computation.309 | loop fusion | bytes 1441792 | tf_op jit(solution)/shard_map/slice | solution.py:26
  2.2 4.7 %collective-permute-start = (f32[16,11,512]{2,0,1:T(8,128)S(1)}, f32[16,11,512]{2,0,1:T(8,128)S(1)}, u32[]{:S(2)}, u32[]{:S(2)}) collective-permute-start(f32[16,11,512]{2,0,1:T(8,128)S(1)} %copy.32), channel_id=1, source_target_pairs={{0,2},{2,4},{4,6},{1,3},{3,5},{5,7},{8,10},{10,12},{12,14},{9,11},... | collective-permute-start | bytes 1081352 | tf_op jit(solution)/shard_map/ppermute | solution.py:23
  7.1 1.9 %collective-permute-start.1 = (f32[16,11,512]{2,0,1:T(8,128)S(1)}, f32[16,11,512]{2,0,1:T(8,128)S(1)}, u32[]{:S(2)}, u32[]{:S(2)}) collective-permute-start(f32[16,11,512]{2,0,1:T(8,128)S(1)} %copy.33), channel_id=1, source_target_pairs={{2,0},{4,2},{6,4},{3,1},{5,3},{7,5},{10,8},{12,10},{14,12},{11,9},... | collective-permute-start | bytes 1081352 | tf_op jit(solution)/shard_map/ppermute | solution.py:26
  9.4 0.2 fusion.63
  9.8 0.2 slice_reduce_fusion.43
  10.0 0.5 slice_reduce_fusion.44
  10.6 0.5 slice_reduce_fusion.45
  11.3 0.6 constant_dynamic-update-slice_fusion.1
  11.9 4.3 %collective-permute-done.1 = f32[16,11,512]{2,0,1:T(8,128)S(1)} collective-permute-done((f32[16,11,512]{2,0,1:T(8,128)S(1)}, f32[16,11,512]{2,0,1:T(8,128)S(1)}, u32[]{:S(2)}, u32[]{:S(2)}) %collective-permute-start.1) | collective-permute-done | bytes 360480 | tf_op jit(solution)/shard_map/ppermute | solution.py:26
  16.4 1.3 %collective-permute-start.3 = (f32[16,54,11]{2,0,1:T(8,128)S(1)}, f32[16,54,11]{2,0,1:T(8,128)S(1)}, u32[]{:S(2)}, u32[]{:S(2)}) collective-permute-start(f32[16,54,11]{2,0,1:T(8,128)S(1)} %get-tuple-element.117), channel_id=1, source_target_pairs={{1,0},{3,2},{5,4},{7,6},{9,8},{11,10},{13,12},{15,14},{17,16},{19,... | collective-permute-start | bytes 114056 | tf_op jit(solution)/shard_map/ppermute | solution.py:26
  17.7 4.0 %collective-permute-start.2 = (f32[16,54,11]{2,0,1:T(8,128)S(1)}, f32[16,54,11]{2,0,1:T(8,128)S(1)}, u32[]{:S(2)}, u32[]{:S(2)}) collective-permute-start(f32[16,54,11]{2,0,1:T(8,128)S(1)} %get-tuple-element.116), channel_id=1, source_target_pairs={{0,1},{2,3},{4,5},{6,7},{8,9},{10,11},{12,13},{14,15},{16,17},{18,... | collective-permute-start | bytes 114056 | tf_op jit(solution)/shard_map/ppermute | solution.py:23
  21.9 3.5 %collective-permute-done.3 = f32[16,54,11]{2,0,1:T(8,128)S(1)} collective-permute-done((f32[16,54,11]{2,0,1:T(8,128)S(1)}, f32[16,54,11]{2,0,1:T(8,128)S(1)}, u32[]{:S(2)}, u32[]{:S(2)}) %collective-permute-start.3) | collective-permute-done | bytes 38048 | tf_op jit(solution)/shard_map/ppermute | solution.py:26
  25.4 1.5 %collective-permute-done.2 = f32[16,54,11]{2,0,1:T(8,128)S(1)} collective-permute-done((f32[16,54,11]{2,0,1:T(8,128)S(1)}, f32[16,54,11]{2,0,1:T(8,128)S(1)}, u32[]{:S(2)}, u32[]{:S(2)}) %collective-permute-start.2) | collective-permute-done | bytes 38048 | tf_op jit(solution)/shard_map/ppermute | solution.py:23
  26.9 0.8 pad_maximum_fusion
  27.7 3.1 %fusion = f32[16,32,534]{2,0,1:T(8,128)S(1)} fusion(f32[16,54,534]{2,0,1:T(8,128)S(1)} %pad_maximum_fusion, f32[16]{0:T(128)S(1)} %get-tuple-element.79, f32[16]{0:T(128)S(1)} %get-tuple-element.80, f32[16]{0:T(128)S(1)} %get-tuple-element.81, f32[16]{0:T(128)S(1)} %get-tuple-element.82, f32[16]{0:T(128)S(1)} %get-tuple-element.83, ...), kind=kLoop, calls=%fused_computation.8 | loop fusion | flops 12303360 | bytes 26248640 | tf_op jit(solution)/shard_map/add | solution.py:67
  30.8 7.0 %broadcast_select_fusion = (f32[16,32,512]{2,0,1:T(8,128)}, f32[16,32,512]{2,0,1:T(8,128)S(1)}, pred[16,32,512]{2,0,1:T(8,128)(4,1)S(1)}) fusion(f32[16,32,534]{2,0,1:T(8,128)S(1)} %fusion, f32[16]{0:T(128)S(1)} %get-tuple-element.56, f32[16]{0:T(128)S(1)} %get-tuple-element.57, f32[16]{0:T(128)S(1)} %get-tuple-element.58, f32[16]{0:T(128)S(1)} %get-tuple-element.59, ...), kind=kLoop, calls=%fused_computation.119 | loop fusion | flops 12320768 | bytes 27526592 | tf_op jit(solution)/shard_map/jit(_where)/select_n | solution.py:104
  37.8 4.6 %all-to-all-start = ((f32[16,32,512]{2,0,1:T(8,128)}), f32[16,32,512]{2,0,1:T(8,128)S(1)}, u32[]{:S(2)}, u32[]{:S(2)}) async-start(f32[16,32,512]{2,0,1:T(8,128)} %get-tuple-element.113), calls=%async_computation | async-start | bytes 2097152 | tf_op jit(solution)/shard_map/all_to_all | solution.py:105
  42.6 22.2 %all-to-all-done = f32[16,32,512]{2,0,1:T(8,128)S(1)} async-done(((f32[16,32,512]{2,0,1:T(8,128)}), f32[16,32,512]{2,0,1:T(8,128)S(1)}, u32[]{:S(2)}, u32[]{:S(2)}) %all-to-all-start) | async-done | bytes 1048608 | tf_op jit(solution)/shard_map/all_to_all | solution.py:105
  64.8 0.6 copy.28
  65.5 3.6 %while.13 = (s32[]{:T(128)}, f32[8,512]{1,0:T(8,128)S(1)}, f32[8,512]{1,0:T(8,128)S(1)}, f32[64,8,512]{2,1,0:T(8,128)S(1)}, f32[8,512]{1,0:T(8,128)S(1)}, /*index=5*/s32[]{:T(128)}, s32[]{:T(128)}) while((s32[]{:T(128)}, f32[8,512]{1,0:T(8,128)S(1)}, f32[8,512]{1,0:T(8,128)S(1)}, f32[64,8,512]{2,1,0:T(8,128)S(1)}, ...), condition=%wide.region_7.9_spmd.clone, body=%wide.region_5.8_spmd.clone.sunk | while | flops 1110019 | bytes 1302625 | solution.py:83
  69.3 10.2 %all_gather.3 = f32[32,512]{1,0:T(8,128)S(1)} all-gather(f32[8,512]{1,0:T(8,128)S(1)} %fusion.22), channel_id=1, replica_groups=mesh['exp'=4,'row'=4,'col'=2] {'exp'}, dimensions={0}, use_global_device_ids=true | all-gather | bytes 81920 | tf_op jit(solution)/shard_map/all_gather | solution.py:106
  79.6 4.5 %collective-permute-start.5 = (f32[4,512]{1,0:T(4,128)S(1)}, f32[4,512]{1,0:T(4,128)S(1)}, u32[]{:S(2)}, u32[]{:S(2)}) collective-permute-start(f32[4,512]{1,0:T(4,128)S(1)} %get-tuple-element.140), channel_id=1, source_target_pairs={{2,0},{4,2},{6,4},{3,1},{5,3},{7,5},{10,8},{12,10},{14,12},{11,9},... | collective-permute-start | bytes 24584 | tf_op jit(solution)/shard_map/ppermute | solution.py:26
  84.1 2.1 %collective-permute-start.4 = (f32[4,512]{1,0:T(4,128)S(1)}, f32[4,512]{1,0:T(4,128)S(1)}, u32[]{:S(2)}, u32[]{:S(2)}) collective-permute-start(f32[4,512]{1,0:T(4,128)S(1)} %get-tuple-element.139), channel_id=1, source_target_pairs={{0,2},{2,4},{4,6},{1,3},{3,5},{5,7},{8,10},{10,12},{12,14},{9,11},... | collective-permute-start | bytes 24584 | tf_op jit(solution)/shard_map/ppermute | solution.py:23
  86.2 0.9 collective-permute-done.4
  87.2 1.3 %collective-permute-start.7 = (f32[40,4]{1,0:T(8,128)S(1)}, f32[40,4]{1,0:T(8,128)S(1)}, u32[]{:S(2)}, u32[]{:S(2)}) collective-permute-start(f32[40,4]{1,0:T(8,128)S(1)} %get-tuple-element.138), channel_id=1, source_target_pairs={{1,0},{3,2},{5,4},{7,6},{9,8},{11,10},{13,12},{15,14},{17,16},{19,... | collective-permute-start | bytes 1928 | tf_op jit(solution)/shard_map/ppermute | solution.py:26
  88.5 4.3 %collective-permute-start.6 = (f32[40,4]{1,0:T(8,128)S(1)}, f32[40,4]{1,0:T(8,128)S(1)}, u32[]{:S(2)}, u32[]{:S(2)}) collective-permute-start(f32[40,4]{1,0:T(8,128)S(1)} %get-tuple-element.137), channel_id=1, source_target_pairs={{0,1},{2,3},{4,5},{6,7},{8,9},{10,11},{12,13},{14,15},{16,17},{18,... | collective-permute-start | bytes 1928 | tf_op jit(solution)/shard_map/ppermute | solution.py:23
  92.9 0.7 collective-permute-done.6
  93.7 0.6 multiply_add_fusion
  94.3 1.3 %fusion.45 = f32[8,32,512]{2,1,0:T(8,128)S(1)} fusion(f32[8,32,520]{2,1,0:T(8,128)S(1)} %multiply_add_fusion, f32[8]{0:T(128)S(1)} %get-tuple-element.142, f32[8]{0:T(128)S(1)} %get-tuple-element.143, f32[8]{0:T(128)S(1)} %get-tuple-element.144, f32[8]{0:T(128)S(1)} %get-tuple-element.145, f32[8]{0:T(128)S(1)} %get-tuple-element.146, ...), kind=kLoop, calls=%fused_computation.103 | loop fusion | flops 2228224 | bytes 5243168 | tf_op jit(solution)/shard_map/add | solution.py:119
  95.6 0.7 subtract_select_fusion
  96.3 1.6 %copy.29 = f32[16,32,512]{2,1,0:T(8,128)} copy(f32[16,32,512]{2,0,1:T(8,128)S(1)} %subtract_select_fusion) | data formatting | bytes 2097152
  97.9 0.6 copy.47
  (124 shorter events, 5.3 us)
Async XLA Ops:
  2.0 7.1 %copy-start.2 = (s32[16,2]{0,1:T(2,128)S(1)}, s32[16,2]{0,1:T(2,128)}, u32[]{:S(2)}) copy-start(s32[16,2]{0,1:T(2,128)} %param.11) | copy-start | bytes 388
  2.0 7.1 %copy-start.3 = (s32[16,2]{0,1:T(2,128)S(1)}, s32[16,2]{0,1:T(2,128)}, u32[]{:S(2)}) copy-start(s32[16,2]{0,1:T(2,128)} %param.10) | copy-start | bytes 388
  2.2 9.1 %copy-start = (f32[16,32,512]{2,1,0:T(8,128)S(1)}, f32[16,32,512]{2,1,0:T(8,128)}, u32[]{:S(2)}) copy-start(f32[16,32,512]{2,1,0:T(8,128)} %param.8) | copy-start | bytes 3145732
  2.2 9.0 %collective-permute-start = (f32[16,11,512]{2,0,1:T(8,128)S(1)}, f32[16,11,512]{2,0,1:T(8,128)S(1)}, u32[]{:S(2)}, u32[]{:S(2)}) collective-permute-start(f32[16,11,512]{2,0,1:T(8,128)S(1)} %copy.32), channel_id=1, source_target_pairs={{0,2},{2,4},{4,6},{1,3},{3,5},{5,7},{8,10},{10,12},{12,14},{9,11},... | collective-permute-start | bytes 1081352 | tf_op jit(solution)/shard_map/ppermute | solution.py:23
  7.1 9.0 %collective-permute-start.1 = (f32[16,11,512]{2,0,1:T(8,128)S(1)}, f32[16,11,512]{2,0,1:T(8,128)S(1)}, u32[]{:S(2)}, u32[]{:S(2)}) collective-permute-start(f32[16,11,512]{2,0,1:T(8,128)S(1)} %copy.33), channel_id=1, source_target_pairs={{2,0},{4,2},{6,4},{3,1},{5,3},{7,5},{10,8},{12,10},{14,12},{11,9},... | collective-permute-start | bytes 1081352 | tf_op jit(solution)/shard_map/ppermute | solution.py:26
  16.4 9.0 %collective-permute-start.3 = (f32[16,54,11]{2,0,1:T(8,128)S(1)}, f32[16,54,11]{2,0,1:T(8,128)S(1)}, u32[]{:S(2)}, u32[]{:S(2)}) collective-permute-start(f32[16,54,11]{2,0,1:T(8,128)S(1)} %get-tuple-element.117), channel_id=1, source_target_pairs={{1,0},{3,2},{5,4},{7,6},{9,8},{11,10},{13,12},{15,14},{17,16},{19,... | collective-permute-start | bytes 114056 | tf_op jit(solution)/shard_map/ppermute | solution.py:26
  17.7 9.3 %collective-permute-start.2 = (f32[16,54,11]{2,0,1:T(8,128)S(1)}, f32[16,54,11]{2,0,1:T(8,128)S(1)}, u32[]{:S(2)}, u32[]{:S(2)}) collective-permute-start(f32[16,54,11]{2,0,1:T(8,128)S(1)} %get-tuple-element.116), channel_id=1, source_target_pairs={{0,1},{2,3},{4,5},{6,7},{8,9},{10,11},{12,13},{14,15},{16,17},{18,... | collective-permute-start | bytes 114056 | tf_op jit(solution)/shard_map/ppermute | solution.py:23
  27.7 3.1 %copy-start.1 = (s32[16,32,512]{2,1,0:T(8,128)S(1)}, s32[16,32,512]{2,1,0:T(8,128)}, u32[]{:S(2)}) copy-start(s32[16,32,512]{2,1,0:T(8,128)} %param.9) | copy-start | bytes 3145732
  37.8 27.0 %all-to-all-start = ((f32[16,32,512]{2,0,1:T(8,128)}), f32[16,32,512]{2,0,1:T(8,128)S(1)}, u32[]{:S(2)}, u32[]{:S(2)}) async-start(f32[16,32,512]{2,0,1:T(8,128)} %get-tuple-element.113), calls=%async_computation | async-start | bytes 2097152 | tf_op jit(solution)/shard_map/all_to_all | solution.py:105
  65.5 20.7 %copy-start.4 = (s32[16]{0:T(128)S(1)}, s32[16]{0:T(128)}, u32[]{:S(2)}) copy-start(s32[16]{0:T(128)} %param.12) | copy-start | bytes 196
  79.6 6.6 %collective-permute-start.5 = (f32[4,512]{1,0:T(4,128)S(1)}, f32[4,512]{1,0:T(4,128)S(1)}, u32[]{:S(2)}, u32[]{:S(2)}) collective-permute-start(f32[4,512]{1,0:T(4,128)S(1)} %get-tuple-element.140), channel_id=1, source_target_pairs={{2,0},{4,2},{6,4},{3,1},{5,3},{7,5},{10,8},{12,10},{14,12},{11,9},... | collective-permute-start | bytes 24584 | tf_op jit(solution)/shard_map/ppermute | solution.py:26
  84.1 3.1 %collective-permute-start.4 = (f32[4,512]{1,0:T(4,128)S(1)}, f32[4,512]{1,0:T(4,128)S(1)}, u32[]{:S(2)}, u32[]{:S(2)}) collective-permute-start(f32[4,512]{1,0:T(4,128)S(1)} %get-tuple-element.139), channel_id=1, source_target_pairs={{0,2},{2,4},{4,6},{1,3},{3,5},{5,7},{8,10},{10,12},{12,14},{9,11},... | collective-permute-start | bytes 24584 | tf_op jit(solution)/shard_map/ppermute | solution.py:23
  87.2 5.6 %collective-permute-start.7 = (f32[40,4]{1,0:T(8,128)S(1)}, f32[40,4]{1,0:T(8,128)S(1)}, u32[]{:S(2)}, u32[]{:S(2)}) collective-permute-start(f32[40,4]{1,0:T(8,128)S(1)} %get-tuple-element.138), channel_id=1, source_target_pairs={{1,0},{3,2},{5,4},{7,6},{9,8},{11,10},{13,12},{15,14},{17,16},{19,... | collective-permute-start | bytes 1928 | tf_op jit(solution)/shard_map/ppermute | solution.py:26
  88.5 5.0 %collective-permute-start.6 = (f32[40,4]{1,0:T(8,128)S(1)}, f32[40,4]{1,0:T(8,128)S(1)}, u32[]{:S(2)}, u32[]{:S(2)}) collective-permute-start(f32[40,4]{1,0:T(8,128)S(1)} %get-tuple-element.137), channel_id=1, source_target_pairs={{0,1},{2,3},{4,5},{6,7},{8,9},{10,11},{12,13},{14,15},{16,17},{18,... | collective-permute-start | bytes 1928 | tf_op jit(solution)/shard_map/ppermute | solution.py:23
where the time goes:
time: 100 us; the launch traced here: 98.5 us
  waiting for transfers between devices  33.2 us (33%)
  starting transfers between devices  28.7 us (29%)
  other arithmetic  17.3 us (17%)
  blocking collectives  10.2 us (10%)
  local copies, waits for them, and re-layouts  7.03 us (7%)
    all_to_all x1, waiting for transfers between devices, body(): lax.all_to_all(flagged, 'exp', split_axis=1, concat_axis=0, tiled=True)  22.2 us
    ppermute x4, starting transfers between devices, extended(): lax.ppermute(lax.slice_in_dim(block, block.shape[dim] - width, None, axis...  15.1 us
    all_gather x1, blocking collectives, body(): median_sky = lax.all_gather(band, 'exp', axis=0, tiled=True)  10.2 us
    ppermute x4, starting transfers between devices, extended(): lax.ppermute(lax.slice_in_dim(block, 0, width, axis=dim), axis, backward)  8.99 us
    ppermute x4, waiting for transfers between devices, extended(): lax.ppermute(lax.slice_in_dim(block, 0, width, axis=dim), axis, backward)  7.75 us
    select_n x1, other arithmetic, body(): flagged = jnp.where(bad_pixels == 1, sentinel, warped)  6.99 us
    all_to_all x1, starting transfers between devices, body(): lax.all_to_all(flagged, 'exp', split_axis=1, concat_axis=0, tiled=True)  4.59 us
    unnamed x16, local copies, waits for them, and re-layouts  3.31 us
  transfers between devices with their start and end apart: 9, of which 7 were waited for; matrix products, arithmetic and copies ran while one was open for 3% of the time, Pallas kernels for 0%

commit v1 on v0

--- a/solution.py
+++ b/solution.py
@@ -15,17 +15,46 @@
 pivot_span = 16.0
 
 
-def extended(block, sides, width):
-    for axis, dim in sides:
-        count = lax.axis_size(axis)
-        forward = [(i, i + 1) for i in range(count - 1)]
-        backward = [(target, source) for source, target in forward]
-        low = lax.ppermute(
-            lax.slice_in_dim(block, block.shape[dim] - width, None, axis=dim), axis, forward
-        )
-        high = lax.ppermute(lax.slice_in_dim(block, 0, width, axis=dim), axis, backward)
-        block = jnp.concatenate([low, block, high], axis=dim)
-    return block
+def _grid_pairs(nrow, ncol, dr, dc, flat):
+    pairs = []
+    for r in range(nrow):
+        for c in range(ncol):
+            tr, tc = r - dr, c - dc
+            if 0 <= tr < nrow and 0 <= tc < ncol:
+                pairs.append((flat(r, c), flat(tr, tc)))
+    return pairs
+
+
+def extended(block, row_dim, col_dim, width):
+    nrow = lax.axis_size("row")
+    ncol = lax.axis_size("col")
+    rows = block.shape[row_dim]
+    cols = block.shape[col_dim]
+
+    def piece(dr, dc):
+        part = block
+        if dr == -1:
+            part = lax.slice_in_dim(part, rows - width, rows, axis=row_dim)
+        elif dr == 1:
+            part = lax.slice_in_dim(part, 0, width, axis=row_dim)
+        if dc == -1:
+            part = lax.slice_in_dim(part, cols - width, cols, axis=col_dim)
+        elif dc == 1:
+            part = lax.slice_in_dim(part, 0, width, axis=col_dim)
+        if dr == 0:
+            pairs = _grid_pairs(1, ncol, 0, dc, lambda r, c: c)
+            return lax.ppermute(part, "col", pairs)
+        if dc == 0:
+            pairs = _grid_pairs(nrow, 1, dr, 0, lambda r, c: r)
+            return lax.ppermute(part, "row", pairs)
+        pairs = _grid_pairs(nrow, ncol, dr, dc, lambda r, c: r * ncol + c)
+        return lax.ppermute(part, ("row", "col"), pairs)
+
+    bands = []
+    for dr in (-1, 0, 1):
+        line = [block if (dr, dc) == (0, 0) else piece(dr, dc) for dc in (-1, 0, 1)]
+        bands.append(jnp.concatenate(line, axis=col_dim))
+    return jnp.concatenate(bands, axis=row_dim)
 
 
 def lanczos_table():
@@ -98,13 +127,16 @@
     kernel_table = lanczos_table()
     coef_down = placed_taps(lookup(warp_index[:, 0], NFRAC, kernel_table), offsets[:, 0])
     coef_across = placed_taps(lookup(warp_index[:, 1], NFRAC, kernel_table), offsets[:, 1])
-    padded = extended(exposures, (("row", 1), ("col", 2)), HALO)
+    padded = extended(exposures, 1, 2, HALO)
     across = resample_axis(padded, coef_down, row_count, 1)
     warped = resample_axis(across, coef_across, col_count, 2)
     flagged = jnp.where(bad_pixels == 1, sentinel, warped)
     band = stack_median(lax.all_to_all(flagged, "exp", split_axis=1, concat_axis=0, tiled=True))
-    median_sky = lax.all_gather(band, "exp", axis=0, tiled=True)
-    bordered = extended(median_sky, (("row", 0), ("col", 1)), PSF_RADIUS)
+    groups = lax.axis_size("exp")
+    median_sky = lax.all_to_all(
+        jnp.tile(band, (groups, 1)), "exp", split_axis=0, concat_axis=0, tiled=True
+    )
+    bordered = extended(median_sky, 0, 1, PSF_RADIUS)
     blur = blur_table()
     taps = 2 * PSF_RADIUS + 1
     blurred_rows = jnp.zeros((NPSF, row_count, col_count + 2 * PSF_RADIUS), jnp.float32)

time: 100 us -> 120 us (1.20)
  starting transfers between devices: 28.7 us -> 55.2 us
  blocking collectives: 10.2 us -> 0 us
  waiting for transfers between devices: 33.2 us -> 36.5 us
    ppermute x8 -> x16, starting transfers between devices: 24.1 us -> 47.2 us  [the longest x8 24.6 us: piece(): return lax.ppermute(part, ('row', 'col'), pairs)]
    all_gather x1 -> x0, blocking collectives: 10.2 us -> none  [body(): median_sky = lax.all_gather(band, 'exp', axis=0, tiled=True)]
    all_to_all x0 -> x1, waiting for transfers between devices: none -> 4.55 us  [body(): lax.all_to_all(jnp.tile(band, (groups, 1)), 'exp', split_axis=0, concat_a...]
    ppermute x8 -> x16, waiting for transfers between devices: 11 us -> 6.83 us  [the longest x4 4.33 us: piece(): return lax.ppermute(part, 'col', pairs)]
    all_to_all x0 -> x1, starting transfers between devices: none -> 3.28 us  [body(): lax.all_to_all(jnp.tile(band, (groups, 1)), 'exp', split_axis=0, concat_a...]
    all_to_all x1, waiting for transfers between devices: 22.2 us -> 25.1 us  [body(): lax.all_to_all(flagged, 'exp', split_axis=1, concat_axis=0, tiled=True)]
    unnamed x16 -> x11, local copies, waits for them, and re-layouts: 3.31 us -> 4.07 us
  transfers between devices with their start and end apart: 9 -> 18, of which waited for: 7 -> 6; matrix products, arithmetic and copies ran while one was open for 3% -> 2% of each run, Pallas kernels for 0% -> 0%
where the time goes in v1:
time: 120 us; the launch traced here: 119 us
  starting transfers between devices  55.2 us (46%)
  waiting for transfers between devices  36.5 us (30%)
  other arithmetic  17.9 us (15%)
  local copies, waits for them, and re-layouts  7.33 us (6%)
    all_to_all x1, waiting for transfers between devices, body(): lax.all_to_all(flagged, 'exp', split_axis=1, concat_axis=0, tiled=True)  25.1 us
    ppermute x8, starting transfers between devices, piece(): return lax.ppermute(part, ('row', 'col'), pairs)  24.6 us
    ppermute x4, starting transfers between devices, piece(): return lax.ppermute(part, 'row', pairs)  15.6 us
    select_n x1, other arithmetic, body(): flagged = jnp.where(bad_pixels == 1, sentinel, warped)  6.99 us
    ppermute x4, starting transfers between devices, piece(): return lax.ppermute(part, 'col', pairs)  6.92 us
    all_to_all x1, starting transfers between devices, body(): lax.all_to_all(flagged, 'exp', split_axis=1, concat_axis=0, tiled=True)  4.72 us
    all_to_all x1, waiting for transfers between devices, body(): lax.all_to_all(jnp.tile(band, (groups, 1)), 'exp', split_axis=0, concat_a...  4.55 us
    ppermute x4, waiting for transfers between devices, piece(): return lax.ppermute(part, 'col', pairs)  4.33 us
  transfers between devices with their start and end apart: 18, of which 6 were waited for; matrix products, arithmetic and copies ran while one was open for 2% of the time, Pallas kernels for 0%

profile of v1, /device:TPU:1, one launch (start us, length us, event | category | flops | bytes accessed | tf_op | source)
XLA Modules:
  0.0 119.1 jit_solution(8014442783377771152)
XLA Ops:
  0.6 1.8 %copy.37 = f32[16,32,512]{2,0,1:T(8,128)S(1)} copy(f32[16,32,512]{2,1,0:T(8,128)} %param.8) | data formatting | bytes 2097152 | tf_op args[0]
  2.6 5.6 %collective-permute-start = (f32[16,11,11]{2,0,1:T(8,128)S(1)}, f32[16,11,11]{2,0,1:T(8,128)S(1)}, u32[]{:S(2)}, u32[]{:S(2)}) collective-permute-start(f32[16,11,11]{2,0,1:T(8,128)S(1)} %get-tuple-element.118), channel_id=1, source_target_pairs={{0,3},{2,5},{4,7},{8,11},{10,13},{12,15},{16,19},{18,21},{20,23},{... | collective-permute-start | bytes 23240 | tf_op jit(solution)/shard_map/ppermute | solution.py:51
  8.2 1.3 %collective-permute-start.2 = (f32[16,11,11]{2,0,1:T(8,128)S(1)}, f32[16,11,11]{2,0,1:T(8,128)S(1)}, u32[]{:S(2)}, u32[]{:S(2)}) collective-permute-start(f32[16,11,11]{2,0,1:T(8,128)S(1)} %get-tuple-element.121), channel_id=1, source_target_pairs={{1,2},{3,4},{5,6},{9,10},{11,12},{13,14},{17,18},{19,20},{21,22},{... | collective-permute-start | bytes 23240 | tf_op jit(solution)/shard_map/ppermute | solution.py:51
  9.5 4.3 %collective-permute-start.5 = (f32[16,11,11]{2,0,1:T(8,128)S(1)}, f32[16,11,11]{2,0,1:T(8,128)S(1)}, u32[]{:S(2)}, u32[]{:S(2)}) collective-permute-start(f32[16,11,11]{2,0,1:T(8,128)S(1)} %get-tuple-element.120), channel_id=1, source_target_pairs={{2,1},{4,3},{6,5},{10,9},{12,11},{14,13},{18,17},{20,19},{22,21},{... | collective-permute-start | bytes 23240 | tf_op jit(solution)/shard_map/ppermute | solution.py:51
  13.8 2.8 %collective-permute-start.1 = (f32[16,11,512]{2,0,1:T(8,128)S(1)}, f32[16,11,512]{2,0,1:T(8,128)S(1)}, u32[]{:S(2)}, u32[]{:S(2)}) collective-permute-start(f32[16,11,512]{2,0,1:T(8,128)S(1)} %get-tuple-element.122), channel_id=1, source_target_pairs={{0,2},{2,4},{4,6},{1,3},{3,5},{5,7},{8,10},{10,12},{12,14},{9,11},... | collective-permute-start | bytes 1081352 | tf_op jit(solution)/shard_map/ppermute | solution.py:49
  16.7 1.9 %collective-permute-start.6 = (f32[16,11,512]{2,0,1:T(8,128)S(1)}, f32[16,11,512]{2,0,1:T(8,128)S(1)}, u32[]{:S(2)}, u32[]{:S(2)}) collective-permute-start(f32[16,11,512]{2,0,1:T(8,128)S(1)} %get-tuple-element.123), channel_id=1, source_target_pairs={{2,0},{4,2},{6,4},{3,1},{5,3},{7,5},{10,8},{12,10},{14,12},{11,9},... | collective-permute-start | bytes 1081352 | tf_op jit(solution)/shard_map/ppermute | solution.py:49
  20.8 1.3 %collective-permute-start.7 = (f32[16,11,11]{2,0,1:T(8,128)S(1)}, f32[16,11,11]{2,0,1:T(8,128)S(1)}, u32[]{:S(2)}, u32[]{:S(2)}) collective-permute-start(f32[16,11,11]{2,0,1:T(8,128)S(1)} %get-tuple-element.119), channel_id=1, source_target_pairs={{3,0},{5,2},{7,4},{11,8},{13,10},{15,12},{19,16},{21,18},{23,20},{... | collective-permute-start | bytes 23240 | tf_op jit(solution)/shard_map/ppermute | solution.py:51
  22.1 2.9 %collective-permute-start.3 = (f32[16,32,11]{2,0,1:T(8,128)S(1)}, f32[16,32,11]{2,0,1:T(8,128)S(1)}, u32[]{:S(2)}, u32[]{:S(2)}) collective-permute-start(f32[16,32,11]{2,0,1:T(8,128)S(1)} %get-tuple-element.124), channel_id=1, source_target_pairs={{0,1},{2,3},{4,5},{6,7},{8,9},{10,11},{12,13},{14,15},{16,17},{18,... | collective-permute-start | bytes 67592 | tf_op jit(solution)/shard_map/ppermute | solution.py:46
  25.0 1.3 %collective-permute-start.4 = (f32[16,32,11]{2,0,1:T(8,128)S(1)}, f32[16,32,11]{2,0,1:T(8,128)S(1)}, u32[]{:S(2)}, u32[]{:S(2)}) collective-permute-start(f32[16,32,11]{2,0,1:T(8,128)S(1)} %get-tuple-element.125), channel_id=1, source_target_pairs={{1,0},{3,2},{5,4},{7,6},{9,8},{11,10},{13,12},{15,14},{17,16},{19,... | collective-permute-start | bytes 67592 | tf_op jit(solution)/shard_map/ppermute | solution.py:46
  26.5 2.0 %collective-permute-done.7 = f32[16,11,11]{2,0,1:T(8,128)S(1)} collective-permute-done((f32[16,11,11]{2,0,1:T(8,128)S(1)}, f32[16,11,11]{2,0,1:T(8,128)S(1)}, u32[]{:S(2)}, u32[]{:S(2)}) %collective-permute-start.7) | collective-permute-done | bytes 7776 | tf_op jit(solution)/shard_map/ppermute | solution.py:51
  28.7 4.1 %collective-permute-done.4 = f32[16,32,11]{2,0,1:T(8,128)S(1)} collective-permute-done((f32[16,32,11]{2,0,1:T(8,128)S(1)}, f32[16,32,11]{2,0,1:T(8,128)S(1)}, u32[]{:S(2)}, u32[]{:S(2)}) %collective-permute-start.4) | collective-permute-done | bytes 22560 | tf_op jit(solution)/shard_map/ppermute | solution.py:46
  32.8 1.2 maximum_maximum_fusion
  34.0 3.3 %fusion = f32[16,32,534]{2,0,1:T(8,128)S(1)} fusion(f32[16,43,534]{2,0,1:T(8,128)S(1)} %get-tuple-element.117, f32[16,43,534]{2,0,1:T(8,128)S(1)} %get-tuple-element.116, f32[16,32,11]{2,0,1:T(8,128)S(1)} %collective-permute-done.4, f32[16,32,512]{2,0,1:T(8,128)S(1)} %copy.37, f32[16,32,11]{2,0,1:T(8,128)S(1)} %collective-permute-done.3, ...), kind=kLoop, calls=%fused_computation.9 | loop fusion | flops 12850176 | bytes 26248640 | tf_op jit(solution)/shard_map/add | solution.py:96
  37.3 7.0 %broadcast_select_fusion = (f32[16,32,512]{2,0,1:T(8,128)}, f32[16,32,512]{2,0,1:T(8,128)S(1)}, pred[16,32,512]{2,0,1:T(8,128)(4,1)S(1)}) fusion(f32[16,32,534]{2,0,1:T(8,128)S(1)} %fusion, f32[16]{0:T(128)S(1)} %get-tuple-element.56, f32[16]{0:T(128)S(1)} %get-tuple-element.57, f32[16]{0:T(128)S(1)} %get-tuple-element.58, f32[16]{0:T(128)S(1)} %get-tuple-element.59, ...), kind=kLoop, calls=%fused_computation.120 | loop fusion | flops 12320768 | bytes 27526592 | tf_op jit(solution)/shard_map/jit(_where)/select_n | solution.py:133
  44.3 4.7 %all-to-all-start = ((f32[16,32,512]{2,0,1:T(8,128)}), f32[16,32,512]{2,0,1:T(8,128)S(1)}, u32[]{:S(2)}, u32[]{:S(2)}) async-start(f32[16,32,512]{2,0,1:T(8,128)} %get-tuple-element.113), calls=%async_computation | async-start | bytes 2097152 | tf_op jit(solution)/shard_map/all_to_all | solution.py:134
  49.2 25.1 %all-to-all-done = f32[16,32,512]{2,0,1:T(8,128)S(1)} async-done(((f32[16,32,512]{2,0,1:T(8,128)}), f32[16,32,512]{2,0,1:T(8,128)S(1)}, u32[]{:S(2)}, u32[]{:S(2)}) %all-to-all-start) | async-done | bytes 1048608 | tf_op jit(solution)/shard_map/all_to_all | solution.py:134
  75.1 3.6 %while.13 = (s32[]{:T(128)}, f32[8,512]{1,0:T(8,128)S(1)}, f32[8,512]{1,0:T(8,128)S(1)}, f32[64,8,512]{2,1,0:T(8,128)S(1)}, f32[8,512]{1,0:T(8,128)S(1)}, /*index=5*/s32[]{:T(128)}, s32[]{:T(128)}) while((s32[]{:T(128)}, f32[8,512]{1,0:T(8,128)S(1)}, f32[8,512]{1,0:T(8,128)S(1)}, f32[64,8,512]{2,1,0:T(8,128)S(1)}, ...), condition=%wide.region_7.9_spmd.clone, body=%wide.region_5.8_spmd.clone.sunk | while | flops 1110019 | bytes 1302617 | solution.py:112
  78.9 0.6 tile.2
  79.5 3.3 %all-to-all-start.1 = ((f32[4,8,512]{2,1,0:T(8,128)}), f32[4,8,512]{2,1,0:T(8,128)S(1)}, u32[]{:S(2)}, u32[]{:S(2)}) async-start(f32[4,8,512]{2,1,0:T(8,128)} %tile.2), calls=%async_computation.1 | async-start | bytes 131072 | tf_op jit(solution)/shard_map/all_to_all | solution.py:136
  82.8 4.5 %all-to-all-done.1 = f32[4,8,512]{2,1,0:T(8,128)S(1)} async-done(((f32[4,8,512]{2,1,0:T(8,128)}), f32[4,8,512]{2,1,0:T(8,128)S(1)}, u32[]{:S(2)}, u32[]{:S(2)}) %all-to-all-start.1) | async-done | bytes 65568 | tf_op jit(solution)/shard_map/all_to_all | solution.py:136
  87.4 1.5 %collective-permute-start.11 = (f32[32,4]{1,0:T(8,128)S(1)}, f32[32,4]{1,0:T(8,128)S(1)}, u32[]{:S(2)}, u32[]{:S(2)}) collective-permute-start(f32[32,4]{1,0:T(8,128)S(1)} %get-tuple-element.150), channel_id=1, source_target_pairs={{0,1},{2,3},{4,5},{6,7},{8,9},{10,11},{12,13},{14,15},{16,17},{18,... | collective-permute-start | bytes 1544 | tf_op jit(solution)/shard_map/ppermute | solution.py:46
  89.0 1.3 %collective-permute-start.12 = (f32[32,4]{1,0:T(8,128)S(1)}, f32[32,4]{1,0:T(8,128)S(1)}, u32[]{:S(2)}, u32[]{:S(2)}) collective-permute-start(f32[32,4]{1,0:T(8,128)S(1)} %get-tuple-element.151), channel_id=1, source_target_pairs={{1,0},{3,2},{5,4},{7,6},{9,8},{11,10},{13,12},{15,14},{17,16},{19,... | collective-permute-start | bytes 1544 | tf_op jit(solution)/shard_map/ppermute | solution.py:46
  90.3 2.9 %collective-permute-start.14 = (f32[4,512]{1,0:T(4,128)S(1)}, f32[4,512]{1,0:T(4,128)S(1)}, u32[]{:S(2)}, u32[]{:S(2)}) collective-permute-start(f32[4,512]{1,0:T(4,128)S(1)} %get-tuple-element.149), channel_id=1, source_target_pairs={{2,0},{4,2},{6,4},{3,1},{5,3},{7,5},{10,8},{12,10},{14,12},{11,9},... | collective-permute-start | bytes 24584 | tf_op jit(solution)/shard_map/ppermute | solution.py:49
  93.2 8.0 %collective-permute-start.9 = (f32[4,512]{1,0:T(4,128)S(1)}, f32[4,512]{1,0:T(4,128)S(1)}, u32[]{:S(2)}, u32[]{:S(2)}) collective-permute-start(f32[4,512]{1,0:T(4,128)S(1)} %get-tuple-element.148), channel_id=1, source_target_pairs={{0,2},{2,4},{4,6},{1,3},{3,5},{5,7},{8,10},{10,12},{12,14},{9,11},... | collective-permute-start | bytes 24584 | tf_op jit(solution)/shard_map/ppermute | solution.py:49
  101.2 1.3 %collective-permute-start.10 = (f32[4,4]{1,0:T(4,128)S(1)}, f32[4,4]{1,0:T(4,128)S(1)}, u32[]{:S(2)}, u32[]{:S(2)}) collective-permute-start(f32[4,4]{1,0:T(4,128)S(1)} %get-tuple-element.147), channel_id=1, source_target_pairs={{1,2},{3,4},{5,6},{9,10},{11,12},{13,14},{17,18},{19,20},{21,22},{... | collective-permute-start | bytes 200 | tf_op jit(solution)/shard_map/ppermute | solution.py:51
  102.5 4.3 %collective-permute-start.13 = (f32[4,4]{1,0:T(4,128)S(1)}, f32[4,4]{1,0:T(4,128)S(1)}, u32[]{:S(2)}, u32[]{:S(2)}) collective-permute-start(f32[4,4]{1,0:T(4,128)S(1)} %get-tuple-element.146), channel_id=1, source_target_pairs={{2,1},{4,3},{6,5},{10,9},{12,11},{14,13},{18,17},{20,19},{22,21},{... | collective-permute-start | bytes 200 | tf_op jit(solution)/shard_map/ppermute | solution.py:51
  106.8 1.3 %collective-permute-start.15 = (f32[4,4]{1,0:T(4,128)S(1)}, f32[4,4]{1,0:T(4,128)S(1)}, u32[]{:S(2)}, u32[]{:S(2)}) collective-permute-start(f32[4,4]{1,0:T(4,128)S(1)} %get-tuple-element.145), channel_id=1, source_target_pairs={{3,0},{5,2},{7,4},{11,8},{13,10},{15,12},{19,16},{21,18},{23,20},{... | collective-permute-start | bytes 200 | tf_op jit(solution)/shard_map/ppermute | solution.py:51
  108.2 5.3 %collective-permute-start.8 = (f32[4,4]{1,0:T(4,128)S(1)}, f32[4,4]{1,0:T(4,128)S(1)}, u32[]{:S(2)}, u32[]{:S(2)}) collective-permute-start(f32[4,4]{1,0:T(4,128)S(1)} %get-tuple-element.144), channel_id=1, source_target_pairs={{0,3},{2,5},{4,7},{8,11},{10,13},{12,15},{16,19},{18,21},{20,23},{... | collective-permute-start | bytes 200 | tf_op jit(solution)/shard_map/ppermute | solution.py:51
  114.9 1.3 %fusion.45 = f32[8,32,512]{2,1,0:T(8,128)S(1)} fusion(f32[8,32,520]{2,1,0:T(8,128)S(1)} %multiply_add_fusion, f32[8]{0:T(128)S(1)} %get-tuple-element.153, f32[8]{0:T(128)S(1)} %get-tuple-element.154, f32[8]{0:T(128)S(1)} %get-tuple-element.155, f32[8]{0:T(128)S(1)} %get-tuple-element.156, f32[8]{0:T(128)S(1)} %get-tuple-element.157, ...), kind=kLoop, calls=%fused_computation.104 | loop fusion | flops 2228224 | bytes 5243168 | tf_op jit(solution)/shard_map/add | solution.py:151
  116.2 0.7 subtract_select_fusion
  116.9 1.6 %copy.47 = f32[16,32,512]{2,1,0:T(8,128)} copy(f32[16,32,512]{2,0,1:T(8,128)S(1)} %subtract_select_fusion) | data formatting | bytes 2097152
  118.5 0.6 copy.60
  (140 shorter events, 8.3 us)
Async XLA Ops:
  2.6 16.2 %copy-start.1 = (s32[16,2]{0,1:T(2,128)S(1)}, s32[16,2]{0,1:T(2,128)}, u32[]{:S(2)}) copy-start(s32[16,2]{0,1:T(2,128)} %param.11) | copy-start | bytes 388
  2.6 16.2 %copy-start.2 = (s32[16,2]{0,1:T(2,128)S(1)}, s32[16,2]{0,1:T(2,128)}, u32[]{:S(2)}) copy-start(s32[16,2]{0,1:T(2,128)} %param.10) | copy-start | bytes 388
  2.6 18.2 %collective-permute-start = (f32[16,11,11]{2,0,1:T(8,128)S(1)}, f32[16,11,11]{2,0,1:T(8,128)S(1)}, u32[]{:S(2)}, u32[]{:S(2)}) collective-permute-start(f32[16,11,11]{2,0,1:T(8,128)S(1)} %get-tuple-element.118), channel_id=1, source_target_pairs={{0,3},{2,5},{4,7},{8,11},{10,13},{12,15},{16,19},{18,21},{20,23},{... | collective-permute-start | bytes 23240 | tf_op jit(solution)/shard_map/ppermute | solution.py:51
  8.2 13.9 %collective-permute-start.2 = (f32[16,11,11]{2,0,1:T(8,128)S(1)}, f32[16,11,11]{2,0,1:T(8,128)S(1)}, u32[]{:S(2)}, u32[]{:S(2)}) collective-permute-start(f32[16,11,11]{2,0,1:T(8,128)S(1)} %get-tuple-element.121), channel_id=1, source_target_pairs={{1,2},{3,4},{5,6},{9,10},{11,12},{13,14},{17,18},{19,20},{21,22},{... | collective-permute-start | bytes 23240 | tf_op jit(solution)/shard_map/ppermute | solution.py:51
  9.5 15.5 %collective-permute-start.5 = (f32[16,11,11]{2,0,1:T(8,128)S(1)}, f32[16,11,11]{2,0,1:T(8,128)S(1)}, u32[]{:S(2)}, u32[]{:S(2)}) collective-permute-start(f32[16,11,11]{2,0,1:T(8,128)S(1)} %get-tuple-element.120), channel_id=1, source_target_pairs={{2,1},{4,3},{6,5},{10,9},{12,11},{14,13},{18,17},{20,19},{22,21},{... | collective-permute-start | bytes 23240 | tf_op jit(solution)/shard_map/ppermute | solution.py:51
  13.8 18.9 %collective-permute-start.1 = (f32[16,11,512]{2,0,1:T(8,128)S(1)}, f32[16,11,512]{2,0,1:T(8,128)S(1)}, u32[]{:S(2)}, u32[]{:S(2)}) collective-permute-start(f32[16,11,512]{2,0,1:T(8,128)S(1)} %get-tuple-element.122), channel_id=1, source_target_pairs={{0,2},{2,4},{4,6},{1,3},{3,5},{5,7},{8,10},{10,12},{12,14},{9,11},... | collective-permute-start | bytes 1081352 | tf_op jit(solution)/shard_map/ppermute | solution.py:49
  16.7 16.1 %collective-permute-start.6 = (f32[16,11,512]{2,0,1:T(8,128)S(1)}, f32[16,11,512]{2,0,1:T(8,128)S(1)}, u32[]{:S(2)}, u32[]{:S(2)}) collective-permute-start(f32[16,11,512]{2,0,1:T(8,128)S(1)} %get-tuple-element.123), channel_id=1, source_target_pairs={{2,0},{4,2},{6,4},{3,1},{5,3},{7,5},{10,8},{12,10},{14,12},{11,9},... | collective-permute-start | bytes 1081352 | tf_op jit(solution)/shard_map/ppermute | solution.py:49
  20.8 7.7 %collective-permute-start.7 = (f32[16,11,11]{2,0,1:T(8,128)S(1)}, f32[16,11,11]{2,0,1:T(8,128)S(1)}, u32[]{:S(2)}, u32[]{:S(2)}) collective-permute-start(f32[16,11,11]{2,0,1:T(8,128)S(1)} %get-tuple-element.119), channel_id=1, source_target_pairs={{3,0},{5,2},{7,4},{11,8},{13,10},{15,12},{19,16},{21,18},{23,20},{... | collective-permute-start | bytes 23240 | tf_op jit(solution)/shard_map/ppermute | solution.py:51
  22.1 6.6 %collective-permute-start.3 = (f32[16,32,11]{2,0,1:T(8,128)S(1)}, f32[16,32,11]{2,0,1:T(8,128)S(1)}, u32[]{:S(2)}, u32[]{:S(2)}) collective-permute-start(f32[16,32,11]{2,0,1:T(8,128)S(1)} %get-tuple-element.124), channel_id=1, source_target_pairs={{0,1},{2,3},{4,5},{6,7},{8,9},{10,11},{12,13},{14,15},{16,17},{18,... | collective-permute-start | bytes 67592 | tf_op jit(solution)/shard_map/ppermute | solution.py:46
  25.0 7.8 %collective-permute-start.4 = (f32[16,32,11]{2,0,1:T(8,128)S(1)}, f32[16,32,11]{2,0,1:T(8,128)S(1)}, u32[]{:S(2)}, u32[]{:S(2)}) collective-permute-start(f32[16,32,11]{2,0,1:T(8,128)S(1)} %get-tuple-element.125), channel_id=1, source_target_pairs={{1,0},{3,2},{5,4},{7,6},{9,8},{11,10},{13,12},{15,14},{17,16},{19,... | collective-permute-start | bytes 67592 | tf_op jit(solution)/shard_map/ppermute | solution.py:46
  33.9 3.3 %copy-start = (s32[16,32,512]{2,1,0:T(8,128)S(1)}, s32[16,32,512]{2,1,0:T(8,128)}, u32[]{:S(2)}) copy-start(s32[16,32,512]{2,1,0:T(8,128)} %param.9) | copy-start | bytes 3145732
  44.3 4.8 %copy-start.3 = (s32[16]{0:T(128)S(1)}, s32[16]{0:T(128)}, u32[]{:S(2)}) copy-start(s32[16]{0:T(128)} %param.12) | copy-start | bytes 196
  44.3 30.0 %all-to-all-start = ((f32[16,32,512]{2,0,1:T(8,128)}), f32[16,32,512]{2,0,1:T(8,128)S(1)}, u32[]{:S(2)}, u32[]{:S(2)}) async-start(f32[16,32,512]{2,0,1:T(8,128)} %get-tuple-element.113), calls=%async_computation | async-start | bytes 2097152 | tf_op jit(solution)/shard_map/all_to_all | solution.py:134
  79.5 7.9 %all-to-all-start.1 = ((f32[4,8,512]{2,1,0:T(8,128)}), f32[4,8,512]{2,1,0:T(8,128)S(1)}, u32[]{:S(2)}, u32[]{:S(2)}) async-start(f32[4,8,512]{2,1,0:T(8,128)} %tile.2), calls=%async_computation.1 | async-start | bytes 131072 | tf_op jit(solution)/shard_map/all_to_all | solution.py:136
  87.4 15.1 %collective-permute-start.11 = (f32[32,4]{1,0:T(8,128)S(1)}, f32[32,4]{1,0:T(8,128)S(1)}, u32[]{:S(2)}, u32[]{:S(2)}) collective-permute-start(f32[32,4]{1,0:T(8,128)S(1)} %get-tuple-element.150), channel_id=1, source_target_pairs={{0,1},{2,3},{4,5},{6,7},{8,9},{10,11},{12,13},{14,15},{16,17},{18,... | collective-permute-start | bytes 1544 | tf_op jit(solution)/shard_map/ppermute | solution.py:46
  89.0 17.8 %collective-permute-start.12 = (f32[32,4]{1,0:T(8,128)S(1)}, f32[32,4]{1,0:T(8,128)S(1)}, u32[]{:S(2)}, u32[]{:S(2)}) collective-permute-start(f32[32,4]{1,0:T(8,128)S(1)} %get-tuple-element.151), channel_id=1, source_target_pairs={{1,0},{3,2},{5,4},{7,6},{9,8},{11,10},{13,12},{15,14},{17,16},{19,... | collective-permute-start | bytes 1544 | tf_op jit(solution)/shard_map/ppermute | solution.py:46
  90.3 23.8 %collective-permute-start.14 = (f32[4,512]{1,0:T(4,128)S(1)}, f32[4,512]{1,0:T(4,128)S(1)}, u32[]{:S(2)}, u32[]{:S(2)}) collective-permute-start(f32[4,512]{1,0:T(4,128)S(1)} %get-tuple-element.149), channel_id=1, source_target_pairs={{2,0},{4,2},{6,4},{3,1},{5,3},{7,5},{10,8},{12,10},{14,12},{11,9},... | collective-permute-start | bytes 24584 | tf_op jit(solution)/shard_map/ppermute | solution.py:49
  93.2 20.9 %collective-permute-start.9 = (f32[4,512]{1,0:T(4,128)S(1)}, f32[4,512]{1,0:T(4,128)S(1)}, u32[]{:S(2)}, u32[]{:S(2)}) collective-permute-start(f32[4,512]{1,0:T(4,128)S(1)} %get-tuple-element.148), channel_id=1, source_target_pairs={{0,2},{2,4},{4,6},{1,3},{3,5},{5,7},{8,10},{10,12},{12,14},{9,11},... | collective-permute-start | bytes 24584 | tf_op jit(solution)/shard_map/ppermute | solution.py:49
  101.2 7.0 %collective-permute-start.10 = (f32[4,4]{1,0:T(4,128)S(1)}, f32[4,4]{1,0:T(4,128)S(1)}, u32[]{:S(2)}, u32[]{:S(2)}) collective-permute-start(f32[4,4]{1,0:T(4,128)S(1)} %get-tuple-element.147), channel_id=1, source_target_pairs={{1,2},{3,4},{5,6},{9,10},{11,12},{13,14},{17,18},{19,20},{21,22},{... | collective-permute-start | bytes 200 | tf_op jit(solution)/shard_map/ppermute | solution.py:51
  102.5 11.0 %collective-permute-start.13 = (f32[4,4]{1,0:T(4,128)S(1)}, f32[4,4]{1,0:T(4,128)S(1)}, u32[]{:S(2)}, u32[]{:S(2)}) collective-permute-start(f32[4,4]{1,0:T(4,128)S(1)} %get-tuple-element.146), channel_id=1, source_target_pairs={{2,1},{4,3},{6,5},{10,9},{12,11},{14,13},{18,17},{20,19},{22,21},{... | collective-permute-start | bytes 200 | tf_op jit(solution)/shard_map/ppermute | solution.py:51
  106.8 6.8 %collective-permute-start.15 = (f32[4,4]{1,0:T(4,128)S(1)}, f32[4,4]{1,0:T(4,128)S(1)}, u32[]{:S(2)}, u32[]{:S(2)}) collective-permute-start(f32[4,4]{1,0:T(4,128)S(1)} %get-tuple-element.145), channel_id=1, source_target_pairs={{3,0},{5,2},{7,4},{11,8},{13,10},{15,12},{19,16},{21,18},{23,20},{... | collective-permute-start | bytes 200 | tf_op jit(solution)/shard_map/ppermute | solution.py:51
  108.2 5.9 %collective-permute-start.8 = (f32[4,4]{1,0:T(4,128)S(1)}, f32[4,4]{1,0:T(4,128)S(1)}, u32[]{:S(2)}, u32[]{:S(2)}) collective-permute-start(f32[4,4]{1,0:T(4,128)S(1)} %get-tuple-element.144), channel_id=1, source_target_pairs={{0,3},{2,5},{4,7},{8,11},{10,13},{12,15},{16,19},{18,21},{20,23},{... | collective-permute-start | bytes 200 | tf_op jit(solution)/shard_map/ppermute | solution.py:51

commit v2 on v0

--- a/solution.py
+++ b/solution.py
@@ -15,17 +15,41 @@
 pivot_span = 16.0
 
 
-def extended(block, sides, width):
-    for axis, dim in sides:
-        count = lax.axis_size(axis)
+def _row_halo(block, dim, width):
+    count = lax.axis_size("row")
+    forward = [(i, i + 1) for i in range(count - 1)]
+    backward = [(target, source) for source, target in forward]
+    size = block.shape[dim]
+    low = lax.ppermute(lax.slice_in_dim(block, size - width, None, axis=dim), "row", forward)
+    high = lax.ppermute(lax.slice_in_dim(block, 0, width, axis=dim), "row", backward)
+    return jnp.concatenate([low, block, high], axis=dim)
+
+
+def _col_halo(block, dim, width):
+    count = lax.axis_size("col")
+    size = block.shape[dim]
+    right_edge = lax.slice_in_dim(block, size - width, None, axis=dim)
+    left_edge = lax.slice_in_dim(block, 0, width, axis=dim)
+    if count != 2:
         forward = [(i, i + 1) for i in range(count - 1)]
         backward = [(target, source) for source, target in forward]
-        low = lax.ppermute(
-            lax.slice_in_dim(block, block.shape[dim] - width, None, axis=dim), axis, forward
-        )
-        high = lax.ppermute(lax.slice_in_dim(block, 0, width, axis=dim), axis, backward)
-        block = jnp.concatenate([low, block, high], axis=dim)
-    return block
+        low = lax.ppermute(right_edge, "col", forward)
+        high = lax.ppermute(left_edge, "col", backward)
+        return jnp.concatenate([low, block, high], axis=dim)
+    first = lax.axis_index("col") == 0
+    outgoing = jnp.moveaxis(jnp.where(first, right_edge, left_edge), dim, 0)
+    packed_shape = outgoing.shape
+    packed = outgoing.reshape(width, -1)
+    arrived = lax.ppermute(packed, "col", [(0, 1), (1, 0)])
+    arrived = jnp.moveaxis(arrived.reshape(packed_shape), 0, dim)
+    zeros = jnp.zeros_like(arrived)
+    low = jnp.where(first, zeros, arrived)
+    high = jnp.where(first, arrived, zeros)
+    return jnp.concatenate([low, block, high], axis=dim)
+
+
+def extended(block, row_dim, col_dim, width):
+    return _col_halo(_row_halo(block, row_dim, width), col_dim, width)
 
 
 def lanczos_table():
@@ -98,13 +122,16 @@
     kernel_table = lanczos_table()
     coef_down = placed_taps(lookup(warp_index[:, 0], NFRAC, kernel_table), offsets[:, 0])
     coef_across = placed_taps(lookup(warp_index[:, 1], NFRAC, kernel_table), offsets[:, 1])
-    padded = extended(exposures, (("row", 1), ("col", 2)), HALO)
+    padded = extended(exposures, 1, 2, HALO)
     across = resample_axis(padded, coef_down, row_count, 1)
     warped = resample_axis(across, coef_across, col_count, 2)
     flagged = jnp.where(bad_pixels == 1, sentinel, warped)
     band = stack_median(lax.all_to_all(flagged, "exp", split_axis=1, concat_axis=0, tiled=True))
-    median_sky = lax.all_gather(band, "exp", axis=0, tiled=True)
-    bordered = extended(median_sky, (("row", 0), ("col", 1)), PSF_RADIUS)
+    groups = lax.axis_size("exp")
+    median_sky = lax.all_to_all(
+        jnp.tile(band, (groups, 1)), "exp", split_axis=0, concat_axis=0, tiled=True
+    )
+    bordered = extended(median_sky, 0, 1, PSF_RADIUS)
     blur = blur_table()
     taps = 2 * PSF_RADIUS + 1
     blurred_rows = jnp.zeros((NPSF, row_count, col_count + 2 * PSF_RADIUS), jnp.float32)

time: 100 us -> 91.4 us (0.914)
  blocking collectives: 10.2 us -> 0 us
  starting transfers between devices: 28.7 us -> 22.7 us
  local copies, waits for them, and re-layouts: 7.03 us -> 11.5 us
  waiting for transfers between devices: 33.2 us -> 34.6 us
    all_gather x1 -> x0, blocking collectives: 10.2 us -> none  [body(): median_sky = lax.all_gather(band, 'exp', axis=0, tiled=True)]
    ppermute x8 -> x6, starting transfers between devices: 24.1 us -> 14.8 us  [the longest x2 7.28 us: _row_halo(): lax.ppermute(lax.slice_in_dim(block, size - width, None, axis=dim), 'row'...]
    ppermute x8 -> x6, waiting for transfers between devices: 11 us -> 5.01 us  [the longest x2 3.02 us: _col_halo(): arrived = lax.ppermute(packed, 'col', [(0, 1), (1, 0)])]
    all_to_all x0 -> x1, waiting for transfers between devices: none -> 4.55 us  [body(): lax.all_to_all(jnp.tile(band, (groups, 1)), 'exp', split_axis=0, concat_a...]
    all_to_all x0 -> x1, starting transfers between devices: none -> 3.28 us  [body(): lax.all_to_all(jnp.tile(band, (groups, 1)), 'exp', split_axis=0, concat_a...]
    all_to_all x1, waiting for transfers between devices: 22.2 us -> 25.1 us  [body(): lax.all_to_all(flagged, 'exp', split_axis=1, concat_axis=0, tiled=True)]
    slice x4, local copies, waits for them, and re-layouts: 1.42 us -> 3.13 us  [resample_axis(): total = total + coefficients[:, position, None, None] * window]
    unnamed x16 -> x94, local copies, waits for them, and re-layouts: 3.31 us -> 4.46 us
  transfers between devices with their start and end apart: 9 -> 8, of which waited for: 7 -> 6; matrix products, arithmetic and copies ran while one was open for 3% -> 7% of each run, Pallas kernels for 0% -> 0%
where the time goes in v2:
time: 91.4 us; the launch traced here: 89.8 us
  waiting for transfers between devices  34.6 us (38%)
  starting transfers between devices  22.7 us (25%)
  other arithmetic  18.2 us (20%)
  local copies, waits for them, and re-layouts  11.5 us (13%)
  between operations  1.6 us (2%)
    all_to_all x1, waiting for transfers between devices, body(): lax.all_to_all(flagged, 'exp', split_axis=1, concat_axis=0, tiled=True)  25.1 us
    ppermute x2, starting transfers between devices, _row_halo(): lax.ppermute(lax.slice_in_dim(block, size - width, None, axis=dim), 'row'...  7.28 us
    select_n x1, other arithmetic, body(): flagged = jnp.where(bad_pixels == 1, sentinel, warped)  6.99 us
    ppermute x2, starting transfers between devices, _row_halo(): lax.ppermute(lax.slice_in_dim(block, 0, width, axis=dim), 'row', backward)  5.03 us
    all_to_all x1, starting transfers between devices, body(): lax.all_to_all(flagged, 'exp', split_axis=1, concat_axis=0, tiled=True)  4.59 us
    all_to_all x1, waiting for transfers between devices, body(): lax.all_to_all(jnp.tile(band, (groups, 1)), 'exp', split_axis=0, concat_a...  4.55 us
    unnamed x94, local copies, waits for them, and re-layouts  4.46 us
    add x1, other arithmetic, resample_axis(): total = total + coefficients[:, position, None, None] * window  3.86 us
  transfers between devices with their start and end apart: 8, of which 6 were waited for; matrix products, arithmetic and copies ran while one was open for 7% of the time, Pallas kernels for 0%

profile of v2, /device:TPU:1, one launch (start us, length us, event | category | flops | bytes accessed | tf_op | source)
XLA Modules:
  0.0 89.8 jit_solution(72379477720639308)
XLA Ops:
  0.6 1.3 %fusion.134 = (f32[16,11,512]{2,1,0:T(8,128)S(1)}, f32[16,11,512]{2,1,0:T(8,128)S(1)}) fusion(f32[16,32,512]{2,1,0:T(8,128)} %param.8), kind=kLoop, calls=%fused_computation.315 | loop fusion | bytes 1441792 | tf_op jit(solution)/shard_map/slice | solution.py:24
  2.2 4.7 %collective-permute-start = (f32[16,11,512]{2,0,1:T(8,128)S(1)}, f32[16,11,512]{2,0,1:T(8,128)}, u32[]{:S(2)}, u32[]{:S(2)}) collective-permute-start(f32[16,11,512]{2,0,1:T(8,128)S(1)} %copy.47), channel_id=1, source_target_pairs={{0,2},{2,4},{4,6},{1,3},{3,5},{5,7},{8,10},{10,12},{12,14},{9,11},... | collective-permute-start | bytes 1081352 | tf_op jit(solution)/shard_map/ppermute | solution.py:23
  7.1 1.9 %collective-permute-start.1 = (f32[16,11,512]{2,0,1:T(8,128)S(1)}, f32[16,11,512]{2,0,1:T(8,128)S(1)}, u32[]{:S(2)}, u32[]{:S(2)}) collective-permute-start(f32[16,11,512]{2,0,1:T(8,128)S(1)} %copy.48), channel_id=1, source_target_pairs={{2,0},{4,2},{6,4},{3,1},{5,3},{7,5},{10,8},{12,10},{14,12},{11,9},... | collective-permute-start | bytes 1081352 | tf_op jit(solution)/shard_map/ppermute | solution.py:24
  9.8 0.8 slice_reduce_fusion.43
  10.5 1.1 %slice_reduce_fusion.44 = (f32[16]{0:T(128)}, f32[16]{0:T(128)}, f32[16]{0:T(128)}, f32[16]{0:T(128)}, f32[16]{0:T(128)}, /*index=5*/f32[16]{0:T(128)}, f32[16]{...) fusion(f32[16,23]{1,0:T(8,128)S(1)} %select_reduce_fusion), kind=kLoop, calls=%fused_computation.204 | loop fusion | bytes 2432 | tf_op jit(solution)/shard_map/slice | solution.py:91
  11.7 1.1 %slice_reduce_fusion.45 = (f32[16]{0:T(128)S(1)}, f32[16]{0:T(128)S(1)}, f32[16]{0:T(128)}, f32[16]{0:T(128)}, f32[16]{0:T(128)}, /*index=5*/f32[16]{0:T(128)}, ...) fusion(f32[16,23]{1,0:T(8,128)S(1)} %select_reduce_fusion.1), kind=kLoop, calls=%fused_computation.205 | loop fusion | bytes 2432 | tf_op jit(solution)/shard_map/slice | solution.py:91
  12.8 1.0 %constant_dynamic-update-slice_fusion.2 = f32[16,54,512]{2,0,1:T(8,128)S(1)} fusion(f32[16,11,512]{2,0,1:T(8,128)} %collective-permute-done), kind=kLoop, calls=%fused_computation.208 | loop fusion | bytes 720896
  13.8 0.6 constant_dynamic-update-slice_fusion.1
  14.4 1.4 %collective-permute-done.1 = f32[16,11,512]{2,0,1:T(8,128)S(1)} collective-permute-done((f32[16,11,512]{2,0,1:T(8,128)S(1)}, f32[16,11,512]{2,0,1:T(8,128)S(1)}, u32[]{:S(2)}, u32[]{:S(2)}) %collective-permute-start.1) | collective-permute-done | bytes 360480 | tf_op jit(solution)/shard_map/ppermute | solution.py:24
  16.4 1.3 %collective-permute-start.2 = (f32[11,864]{1,0:T(8,128)S(1)}, f32[11,864]{1,0:T(8,128)S(1)}, u32[]{:S(2)}, u32[]{:S(2)}) collective-permute-start(f32[11,864]{1,0:T(8,128)S(1)} %reshape.187), channel_id=1, source_target_pairs={{0,1},{1,0},{2,3},{3,2},{4,5},{5,4},{6,7},{7,6},{8,9},{9,8},{10,11... | collective-permute-start | bytes 114056 | tf_op jit(solution)/shard_map/ppermute | solution.py:43
  17.9 1.6 %collective-permute-done.2 = f32[11,864]{1,0:T(8,128)S(1)} collective-permute-done((f32[11,864]{1,0:T(8,128)S(1)}, f32[11,864]{1,0:T(8,128)S(1)}, u32[]{:S(2)}, u32[]{:S(2)}) %collective-permute-start.2) | collective-permute-done | bytes 38048 | tf_op jit(solution)/shard_map/ppermute | solution.py:43
  20.1 0.3 copy.41
  20.6 0.7 pad_maximum_fusion
  21.8 3.9 %fusion = f32[16,32,534]{2,0,1:T(8,128)S(1)} fusion(f32[16,54,534]{2,0,1:T(8,128)S(1)} %pad_maximum_fusion, f32[16]{0:T(128)S(1)} %copy-done.24, f32[16]{0:T(128)S(1)} %copy-done.25, f32[16]{0:T(128)S(1)} %copy-done.26, f32[16]{0:T(128)S(1)} %copy-done.27, f32[16]{0:T(128)S(1)} %copy-done.28, f32[16]{0:T(128)S(1)} %copy-done.29, f32[16]{0:T(128)S(1)} %copy-done.30, ...), kind=kLoop, calls=%fused_computation.8 | loop fusion | flops 12303360 | bytes 26248640 | tf_op jit(solution)/shard_map/add | solution.py:91
  25.8 7.0 %broadcast_select_fusion = (f32[16,32,512]{2,0,1:T(8,128)}, f32[16,32,512]{2,0,1:T(8,128)S(1)}, pred[16,32,512]{2,0,1:T(8,128)(4,1)S(1)}) fusion(f32[16,32,534]{2,0,1:T(8,128)S(1)} %fusion, f32[16]{0:T(128)S(1)} %get-tuple-element.56, f32[16]{0:T(128)S(1)} %copy-done.2, f32[16]{0:T(128)S(1)} %copy-done.3, f32[16]{0:T(128)S(1)} %copy-done.4, ...), kind=kLoop, calls=%fused_computation.119 | loop fusion | flops 12320768 | bytes 27526592 | tf_op jit(solution)/shard_map/jit(_where)/select_n | solution.py:128
  32.8 4.6 %all-to-all-start = ((f32[16,32,512]{2,0,1:T(8,128)}), f32[16,32,512]{2,0,1:T(8,128)S(1)}, u32[]{:S(2)}, u32[]{:S(2)}) async-start(f32[16,32,512]{2,0,1:T(8,128)} %get-tuple-element.113), calls=%async_computation | async-start | bytes 2097152 | tf_op jit(solution)/shard_map/all_to_all | solution.py:129
  37.6 25.1 %all-to-all-done = f32[16,32,512]{2,0,1:T(8,128)S(1)} async-done(((f32[16,32,512]{2,0,1:T(8,128)}), f32[16,32,512]{2,0,1:T(8,128)S(1)}, u32[]{:S(2)}, u32[]{:S(2)}) %all-to-all-start) | async-done | bytes 1048608 | tf_op jit(solution)/shard_map/all_to_all | solution.py:129
  62.7 0.6 copy.43
  63.4 3.6 %while.13 = (s32[]{:T(128)}, f32[8,512]{1,0:T(8,128)S(1)}, f32[8,512]{1,0:T(8,128)S(1)}, f32[64,8,512]{2,1,0:T(8,128)S(1)}, f32[8,512]{1,0:T(8,128)S(1)}, /*index=5*/s32[]{:T(128)}, s32[]{:T(128)}) while((s32[]{:T(128)}, f32[8,512]{1,0:T(8,128)S(1)}, f32[8,512]{1,0:T(8,128)S(1)}, f32[64,8,512]{2,1,0:T(8,128)S(1)}, ...), condition=%wide.region_7.9_spmd.clone, body=%wide.region_5.8_spmd.clone.sunk | while | flops 1110019 | bytes 1302625 | solution.py:107
  67.2 0.6 tile.2
  67.9 3.3 %all-to-all-start.1 = ((f32[4,8,512]{2,1,0:T(8,128)}), f32[4,8,512]{2,1,0:T(8,128)S(1)}, u32[]{:S(2)}, u32[]{:S(2)}) async-start(f32[4,8,512]{2,1,0:T(8,128)} %tile.2), calls=%async_computation.1 | async-start | bytes 131072 | tf_op jit(solution)/shard_map/all_to_all | solution.py:131
  71.2 4.5 %all-to-all-done.1 = f32[4,8,512]{2,1,0:T(8,128)S(1)} async-done(((f32[4,8,512]{2,1,0:T(8,128)}), f32[4,8,512]{2,1,0:T(8,128)S(1)}, u32[]{:S(2)}, u32[]{:S(2)}) %all-to-all-start.1) | async-done | bytes 65568 | tf_op jit(solution)/shard_map/all_to_all | solution.py:131
  75.7 3.1 %collective-permute-start.4 = (f32[4,512]{1,0:T(4,128)S(1)}, f32[4,512]{1,0:T(4,128)S(1)}, u32[]{:S(2)}, u32[]{:S(2)}) collective-permute-start(f32[4,512]{1,0:T(4,128)S(1)} %get-tuple-element.136), channel_id=1, source_target_pairs={{2,0},{4,2},{6,4},{3,1},{5,3},{7,5},{10,8},{12,10},{14,12},{11,9},... | collective-permute-start | bytes 24584 | tf_op jit(solution)/shard_map/ppermute | solution.py:24
  78.9 2.6 %collective-permute-start.3 = (f32[4,512]{1,0:T(4,128)S(1)}, f32[4,512]{1,0:T(4,128)S(1)}, u32[]{:S(2)}, u32[]{:S(2)}) collective-permute-start(f32[4,512]{1,0:T(4,128)S(1)} %get-tuple-element.135), channel_id=1, source_target_pairs={{0,2},{2,4},{4,6},{1,3},{3,5},{5,7},{8,10},{10,12},{12,14},{9,11},... | collective-permute-start | bytes 24584 | tf_op jit(solution)/shard_map/ppermute | solution.py:23
  81.5 0.6 collective-permute-done.3
  82.1 1.2 %collective-permute-start.5 = (f32[4,40]{0,1:T(8,128)S(1)}, f32[4,40]{0,1:T(8,128)S(1)}, u32[]{:S(2)}, u32[]{:S(2)}) collective-permute-start(f32[4,40]{0,1:T(8,128)S(1)} %fusion.55), channel_id=1, source_target_pairs={{0,1},{1,0},{2,3},{3,2},{4,5},{5,4},{6,7},{7,6},{8,9},{9,8},{10,11... | collective-permute-start | bytes 1928 | tf_op jit(solution)/shard_map/ppermute | solution.py:43
  83.4 1.4 %collective-permute-done.5 = f32[4,40]{0,1:T(8,128)S(1)} collective-permute-done((f32[4,40]{0,1:T(8,128)S(1)}, f32[4,40]{0,1:T(8,128)S(1)}, u32[]{:S(2)}, u32[]{:S(2)}) %collective-permute-start.5) | collective-permute-done | bytes 672 | tf_op jit(solution)/shard_map/ppermute | solution.py:43
  85.0 0.6 multiply_add_fusion
  85.5 1.3 %fusion.45 = f32[8,32,512]{2,1,0:T(8,128)S(1)} fusion(f32[8,32,520]{2,1,0:T(8,128)S(1)} %multiply_add_fusion, f32[8]{0:T(128)S(1)} %get-tuple-element.142, f32[8]{0:T(128)S(1)} %get-tuple-element.143, f32[8]{0:T(128)S(1)} %get-tuple-element.144, f32[8]{0:T(128)S(1)} %get-tuple-element.145, f32[8]{0:T(128)S(1)} %get-tuple-element.146, ...), kind=kLoop, calls=%fused_computation.103 | loop fusion | flops 2228224 | bytes 5243168 | tf_op jit(solution)/shard_map/add | solution.py:146
  86.8 0.7 subtract_select_fusion
  87.6 1.6 %copy.44 = f32[16,32,512]{2,1,0:T(8,128)} copy(f32[16,32,512]{2,0,1:T(8,128)S(1)} %subtract_select_fusion) | data formatting | bytes 2097152
  89.1 0.6 copy.62
  (208 shorter events, 6.4 us)
Async XLA Ops:
  2.0 7.1 %copy-start.41 = (s32[16,2]{0,1:T(2,128)S(1)}, s32[16,2]{0,1:T(2,128)}, u32[]{:S(2)}) copy-start(s32[16,2]{0,1:T(2,128)} %param.11) | copy-start | bytes 388
  2.0 7.1 %copy-start.42 = (s32[16,2]{0,1:T(2,128)S(1)}, s32[16,2]{0,1:T(2,128)}, u32[]{:S(2)}) copy-start(s32[16,2]{0,1:T(2,128)} %param.10) | copy-start | bytes 388
  2.2 11.6 %copy-start = (f32[16,32,512]{2,1,0:T(8,128)S(1)}, f32[16,32,512]{2,1,0:T(8,128)}, u32[]{:S(2)}) copy-start(f32[16,32,512]{2,1,0:T(8,128)} %param.8) | copy-start | bytes 3145732
  2.2 10.6 %collective-permute-start = (f32[16,11,512]{2,0,1:T(8,128)S(1)}, f32[16,11,512]{2,0,1:T(8,128)}, u32[]{:S(2)}, u32[]{:S(2)}) collective-permute-start(f32[16,11,512]{2,0,1:T(8,128)S(1)} %copy.47), channel_id=1, source_target_pairs={{0,2},{2,4},{4,6},{1,3},{3,5},{5,7},{8,10},{10,12},{12,14},{9,11},... | collective-permute-start | bytes 1081352 | tf_op jit(solution)/shard_map/ppermute | solution.py:23
  7.1 8.7 %collective-permute-start.1 = (f32[16,11,512]{2,0,1:T(8,128)S(1)}, f32[16,11,512]{2,0,1:T(8,128)S(1)}, u32[]{:S(2)}, u32[]{:S(2)}) collective-permute-start(f32[16,11,512]{2,0,1:T(8,128)S(1)} %copy.48), channel_id=1, source_target_pairs={{2,0},{4,2},{6,4},{3,1},{5,3},{7,5},{10,8},{12,10},{14,12},{11,9},... | collective-permute-start | bytes 1081352 | tf_op jit(solution)/shard_map/ppermute | solution.py:24
  16.4 3.1 %collective-permute-start.2 = (f32[11,864]{1,0:T(8,128)S(1)}, f32[11,864]{1,0:T(8,128)S(1)}, u32[]{:S(2)}, u32[]{:S(2)}) collective-permute-start(f32[11,864]{1,0:T(8,128)S(1)} %reshape.187), channel_id=1, source_target_pairs={{0,1},{1,0},{2,3},{3,2},{4,5},{5,4},{6,7},{7,6},{8,9},{9,8},{10,11... | collective-permute-start | bytes 114056 | tf_op jit(solution)/shard_map/ppermute | solution.py:43
  20.4 1.0 %copy-start.19 = (f32[16]{0:T(128)S(1)}, f32[16]{0:T(128)}, u32[]{:S(2)}) copy-start(f32[16]{0:T(128)} %get-tuple-element.97) | copy-start | bytes 196
  20.4 1.0 %copy-start.20 = (f32[16]{0:T(128)S(1)}, f32[16]{0:T(128)}, u32[]{:S(2)}) copy-start(f32[16]{0:T(128)} %get-tuple-element.98) | copy-start | bytes 196
  21.6 4.0 %copy-start.1 = (s32[16,32,512]{2,1,0:T(8,128)S(1)}, s32[16,32,512]{2,1,0:T(8,128)}, u32[]{:S(2)}) copy-start(s32[16,32,512]{2,1,0:T(8,128)} %param.9) | copy-start | bytes 3145732
  21.6 4.0 %copy-start.2 = (f32[16]{0:T(128)S(1)}, f32[16]{0:T(128)}, u32[]{:S(2)}) copy-start(f32[16]{0:T(128)} %get-tuple-element.57) | copy-start | bytes 196
  21.6 4.0 %copy-start.3 = (f32[16]{0:T(128)S(1)}, f32[16]{0:T(128)}, u32[]{:S(2)}) copy-start(f32[16]{0:T(128)} %get-tuple-element.58) | copy-start | bytes 196
  21.6 4.0 %copy-start.4 = (f32[16]{0:T(128)S(1)}, f32[16]{0:T(128)}, u32[]{:S(2)}) copy-start(f32[16]{0:T(128)} %get-tuple-element.59) | copy-start | bytes 196
  21.6 4.0 %copy-start.5 = (f32[16]{0:T(128)S(1)}, f32[16]{0:T(128)}, u32[]{:S(2)}) copy-start(f32[16]{0:T(128)} %get-tuple-element.60) | copy-start | bytes 196
  21.6 4.0 %copy-start.6 = (f32[16]{0:T(128)S(1)}, f32[16]{0:T(128)}, u32[]{:S(2)}) copy-start(f32[16]{0:T(128)} %get-tuple-element.61) | copy-start | bytes 196
  21.7 4.0 %copy-start.7 = (f32[16]{0:T(128)S(1)}, f32[16]{0:T(128)}, u32[]{:S(2)}) copy-start(f32[16]{0:T(128)} %get-tuple-element.62) | copy-start | bytes 196
  21.7 4.0 %copy-start.8 = (f32[16]{0:T(128)S(1)}, f32[16]{0:T(128)}, u32[]{:S(2)}) copy-start(f32[16]{0:T(128)} %get-tuple-element.63) | copy-start | bytes 196
  21.7 4.0 %copy-start.9 = (f32[16]{0:T(128)S(1)}, f32[16]{0:T(128)}, u32[]{:S(2)}) copy-start(f32[16]{0:T(128)} %get-tuple-element.64) | copy-start | bytes 196
  21.7 4.0 %copy-start.10 = (f32[16]{0:T(128)S(1)}, f32[16]{0:T(128)}, u32[]{:S(2)}) copy-start(f32[16]{0:T(128)} %get-tuple-element.65) | copy-start | bytes 196
  21.7 4.0 %copy-start.11 = (f32[16]{0:T(128)S(1)}, f32[16]{0:T(128)}, u32[]{:S(2)}) copy-start(f32[16]{0:T(128)} %get-tuple-element.66) | copy-start | bytes 196
  21.7 4.0 %copy-start.12 = (f32[16]{0:T(128)S(1)}, f32[16]{0:T(128)}, u32[]{:S(2)}) copy-start(f32[16]{0:T(128)} %get-tuple-element.67) | copy-start | bytes 196
  21.7 4.0 %copy-start.13 = (f32[16]{0:T(128)S(1)}, f32[16]{0:T(128)}, u32[]{:S(2)}) copy-start(f32[16]{0:T(128)} %get-tuple-element.68) | copy-start | bytes 196
  21.7 4.0 %copy-start.14 = (f32[16]{0:T(128)S(1)}, f32[16]{0:T(128)}, u32[]{:S(2)}) copy-start(f32[16]{0:T(128)} %get-tuple-element.69) | copy-start | bytes 196
  21.7 4.0 %copy-start.15 = (f32[16]{0:T(128)S(1)}, f32[16]{0:T(128)}, u32[]{:S(2)}) copy-start(f32[16]{0:T(128)} %get-tuple-element.70) | copy-start | bytes 196
  21.7 4.0 %copy-start.16 = (f32[16]{0:T(128)S(1)}, f32[16]{0:T(128)}, u32[]{:S(2)}) copy-start(f32[16]{0:T(128)} %get-tuple-element.71) | copy-start | bytes 196
  21.8 4.0 %copy-start.17 = (f32[16]{0:T(128)S(1)}, f32[16]{0:T(128)}, u32[]{:S(2)}) copy-start(f32[16]{0:T(128)} %get-tuple-element.72) | copy-start | bytes 196
  21.8 4.0 %copy-start.18 = (f32[16]{0:T(128)S(1)}, f32[16]{0:T(128)}, u32[]{:S(2)}) copy-start(f32[16]{0:T(128)} %get-tuple-element.73) | copy-start | bytes 196
  32.8 29.9 %all-to-all-start = ((f32[16,32,512]{2,0,1:T(8,128)}), f32[16,32,512]{2,0,1:T(8,128)S(1)}, u32[]{:S(2)}, u32[]{:S(2)}) async-start(f32[16,32,512]{2,0,1:T(8,128)} %get-tuple-element.113), calls=%async_computation | async-start | bytes 2097152 | tf_op jit(solution)/shard_map/all_to_all | solution.py:129
  67.1 14.4 %copy-start.43 = (s32[16]{0:T(128)S(1)}, s32[16]{0:T(128)}, u32[]{:S(2)}) copy-start(s32[16]{0:T(128)} %param.12) | copy-start | bytes 196
  67.9 7.9 %all-to-all-start.1 = ((f32[4,8,512]{2,1,0:T(8,128)}), f32[4,8,512]{2,1,0:T(8,128)S(1)}, u32[]{:S(2)}, u32[]{:S(2)}) async-start(f32[4,8,512]{2,1,0:T(8,128)} %tile.2), calls=%async_computation.1 | async-start | bytes 131072 | tf_op jit(solution)/shard_map/all_to_all | solution.py:131
  75.7 5.8 %collective-permute-start.4 = (f32[4,512]{1,0:T(4,128)S(1)}, f32[4,512]{1,0:T(4,128)S(1)}, u32[]{:S(2)}, u32[]{:S(2)}) collective-permute-start(f32[4,512]{1,0:T(4,128)S(1)} %get-tuple-element.136), channel_id=1, source_target_pairs={{2,0},{4,2},{6,4},{3,1},{5,3},{7,5},{10,8},{12,10},{14,12},{11,9},... | collective-permute-start | bytes 24584 | tf_op jit(solution)/shard_map/ppermute | solution.py:24
  78.9 3.2 %collective-permute-start.3 = (f32[4,512]{1,0:T(4,128)S(1)}, f32[4,512]{1,0:T(4,128)S(1)}, u32[]{:S(2)}, u32[]{:S(2)}) collective-permute-start(f32[4,512]{1,0:T(4,128)S(1)} %get-tuple-element.135), channel_id=1, source_target_pairs={{0,2},{2,4},{4,6},{1,3},{3,5},{5,7},{8,10},{10,12},{12,14},{9,11},... | collective-permute-start | bytes 24584 | tf_op jit(solution)/shard_map/ppermute | solution.py:23
  82.1 2.6 %collective-permute-start.5 = (f32[4,40]{0,1:T(8,128)S(1)}, f32[4,40]{0,1:T(8,128)S(1)}, u32[]{:S(2)}, u32[]{:S(2)}) collective-permute-start(f32[4,40]{0,1:T(8,128)S(1)} %fusion.55), channel_id=1, source_target_pairs={{0,1},{1,0},{2,3},{3,2},{4,5},{5,4},{6,7},{7,6},{8,9},{9,8},{10,11... | collective-permute-start | bytes 1928 | tf_op jit(solution)/shard_map/ppermute | solution.py:43
  (20 other events, 19.5 us)

commit v3 on v2

--- a/solution.py
+++ b/solution.py
@@ -2,6 +2,8 @@
 import jax.numpy as jnp
 from jax import lax
 from jax.sharding import PartitionSpec as P
+from jax.experimental import pallas as pl
+from jax.experimental.pallas import tpu as pltpu
 
 NFRAC = 16
 NPSF = 8
@@ -117,15 +119,62 @@
     return jnp.min(jnp.where(pixel_stack > lower_edge[None], pixel_stack, sentinel), axis=0)
 
 
+TAPS = 6
+
+
+def _warp_kernel(
+    row_shift, col_shift, row_weight, col_weight, padded, bad, warped_out, flagged_out
+):
+    group_size, row_count, col_count = warped_out.shape
+    width = padded.shape[2]
+
+    height = padded.shape[1]
+
+    def one_exposure(e, carry):
+        block = pltpu.roll(padded[e], height - row_shift[e], 0)
+        across = None
+        for tap in range(TAPS):
+            term = row_weight[e * TAPS + tap] * block[tap : tap + row_count, :]
+            across = term if across is None else across + term
+        across = pltpu.roll(across, width - col_shift[e], 1)
+        total = None
+        for tap in range(TAPS):
+            term = col_weight[e * TAPS + tap] * across[:, tap : tap + col_count]
+            total = term if total is None else total + term
+        warped_out[e] = total
+        flagged_out[e] = jnp.where(bad[e] == 1, sentinel, total)
+        return carry
+
+    lax.fori_loop(0, group_size, one_exposure, 0)
+
+
+def warp_and_flag(padded, bad_pixels, offsets, warp_index):
+    group_size, row_count, col_count = bad_pixels.shape
+    kernel_table = lanczos_table()
+    row_weight = lookup(warp_index[:, 0], NFRAC, kernel_table).reshape(-1)
+    col_weight = lookup(warp_index[:, 1], NFRAC, kernel_table).reshape(-1)
+    row_shift = offsets[:, 0] + (HALO - 2)
+    col_shift = offsets[:, 1] + (HALO - 2)
+    lanes = -(-padded.shape[2] // 128) * 128
+    rows = -(-padded.shape[1] // 8) * 8
+    padded = jnp.pad(
+        padded, ((0, 0), (0, rows - padded.shape[1]), (0, lanes - padded.shape[2]))
+    )
+    smem = pl.BlockSpec(memory_space=pltpu.SMEM)
+    vmem = pl.BlockSpec(memory_space=pltpu.VMEM)
+    shape = jax.ShapeDtypeStruct((group_size, row_count, col_count), jnp.float32)
+    return pl.pallas_call(
+        _warp_kernel,
+        out_shape=(shape, shape),
+        in_specs=[smem, smem, smem, smem, vmem, vmem],
+        out_specs=(vmem, vmem),
+    )(row_shift, col_shift, row_weight, col_weight, padded, bad_pixels)
+
+
 def body(exposures, bad_pixels, offsets, warp_index, blur_index):
     group_size, row_count, col_count = exposures.shape
-    kernel_table = lanczos_table()
-    coef_down = placed_taps(lookup(warp_index[:, 0], NFRAC, kernel_table), offsets[:, 0])
-    coef_across = placed_taps(lookup(warp_index[:, 1], NFRAC, kernel_table), offsets[:, 1])
     padded = extended(exposures, 1, 2, HALO)
-    across = resample_axis(padded, coef_down, row_count, 1)
-    warped = resample_axis(across, coef_across, col_count, 2)
-    flagged = jnp.where(bad_pixels == 1, sentinel, warped)
+    warped, flagged = warp_and_flag(padded, bad_pixels, offsets, warp_index)
     band = stack_median(lax.all_to_all(flagged, "exp", split_axis=1, concat_axis=0, tiled=True))
     groups = lax.axis_size("exp")
     median_sky = lax.all_to_all(

time: 91.4 us -> 89.1 us (0.975); the launches traced: 89.8 us -> 88.6 us
  Pallas kernels: 0 us -> 8.6 us
  other arithmetic: 18.2 us -> 10.5 us
  waiting for transfers between devices: 34.6 us -> 36.8 us
  local copies, waits for them, and re-layouts: 11.5 us -> 9.55 us
  starting transfers between devices: 22.7 us -> 21.1 us
    pallas_call x0 -> x1, Pallas kernels: none -> 8.6 us  [warp_and_flag(): pl.pallas_call(_warp_kernel, out_shape=(shape, shape), in_specs=[smem, sm...]
    select_n x1 -> x0, other arithmetic: 6.99 us -> none  [body(): flagged = jnp.where(bad_pixels == 1, sentinel, warped)]
    ppermute x2, waiting for transfers between devices: 1.43 us -> 6.92 us  [_row_halo(): lax.ppermute(lax.slice_in_dim(block, 0, width, axis=dim), 'row', backward)]
    slice x5 -> x0, local copies, waits for them, and re-layouts: 4.46 us -> none  [the longest x4 3.13 us: resample_axis(): total = total + coefficients[:, position, None, None] * window]
    all_to_all x1, waiting for transfers between devices: 25.1 us -> 21 us  [body(): lax.all_to_all(flagged, 'exp', split_axis=1, concat_axis=0, tiled=True)]
    unnamed x94 -> x11, local copies, waits for them, and re-layouts: 4.46 us -> 0.85 us
    add x2 -> x1, other arithmetic: 3.86 us -> 0.52 us  [warp_and_flag(): col_shift = offsets[:, 1] + (HALO - 2)]
    pallas_call x0 -> x1, local copies, waits for them, and re-layouts: none -> 2.81 us  [warp_and_flag(): pl.pallas_call(_warp_kernel, out_shape=(shape, shape), in_specs=[smem, sm...]
  transfers between devices with their start and end apart: 8 -> 8, of which waited for: 6 -> 7; matrix products, arithmetic and copies ran while one was open for 7% -> 4% of each run, Pallas kernels for 0% -> 0%
where the time goes in v3:
time: 89.1 us; the launch traced here: 88.6 us
  waiting for transfers between devices  36.8 us (41%)
  starting transfers between devices  21.1 us (24%)
  other arithmetic  10.5 us (12%)
  local copies, waits for them, and re-layouts  9.55 us (11%)
  Pallas kernels  8.6 us (10%)
    all_to_all x1, waiting for transfers between devices, body(): lax.all_to_all(flagged, 'exp', split_axis=1, concat_axis=0, tiled=True)  21 us
    pallas_call x1, Pallas kernels, warp_and_flag(): pl.pallas_call(_warp_kernel, out_shape=(shape, shape), in_specs=[smem, sm...  8.6 us
    ppermute x2, waiting for transfers between devices, _row_halo(): lax.ppermute(lax.slice_in_dim(block, 0, width, axis=dim), 'row', backward)  6.92 us
    ppermute x2, starting transfers between devices, _row_halo(): lax.ppermute(lax.slice_in_dim(block, size - width, None, axis=dim), 'row'...  6.44 us
    all_to_all x1, starting transfers between devices, body(): lax.all_to_all(flagged, 'exp', split_axis=1, concat_axis=0, tiled=True)  4.59 us
    all_to_all x1, waiting for transfers between devices, body(): lax.all_to_all(jnp.tile(band, (groups, 1)), 'exp', split_axis=0, concat_a...  4.55 us
    ppermute x2, starting transfers between devices, _row_halo(): lax.ppermute(lax.slice_in_dim(block, 0, width, axis=dim), 'row', backward)  4.32 us
    all_to_all x1, starting transfers between devices, body(): lax.all_to_all(jnp.tile(band, (groups, 1)), 'exp', split_axis=0, concat_a...  3.28 us
  transfers between devices with their start and end apart: 8, of which 7 were waited for; matrix products, arithmetic and copies ran while one was open for 4% of the time, Pallas kernels for 0%

profile of v3, /device:TPU:1, one launch (start us, length us, event | category | flops | bytes accessed | tf_op | source)
XLA Modules:
  0.0 88.6 jit_solution(9401628531169867253)
XLA Ops:
  0.6 1.4 %fusion.99 = (f32[16,11,512]{2,1,0:T(8,128)S(1)}, f32[16,11,512]{2,1,0:T(8,128)S(1)}) fusion(f32[16,32,512]{2,1,0:T(8,128)} %param.8), kind=kLoop, calls=%fused_computation.182 | loop fusion | bytes 1441792 | tf_op jit(solution)/shard_map/slice | solution.py:25
  2.1 4.5 %collective-permute-start = (f32[16,11,512]{2,1,0:T(8,128)S(1)}, f32[16,11,512]{2,1,0:T(8,128)S(1)}, u32[]{:S(2)}, u32[]{:S(2)}) collective-permute-start(f32[16,11,512]{2,1,0:T(8,128)S(1)} %get-tuple-element.65), channel_id=1, source_target_pairs={{0,2},{2,4},{4,6},{1,3},{3,5},{5,7},{8,10},{10,12},{12,14},{9,11},... | collective-permute-start | bytes 1081352 | tf_op jit(solution)/shard_map/ppermute | solution.py:25
  6.6 1.9 %collective-permute-start.1 = (f32[16,11,512]{2,1,0:T(8,128)S(1)}, f32[16,11,512]{2,1,0:T(8,128)S(1)}, u32[]{:S(2)}, u32[]{:S(2)}) collective-permute-start(f32[16,11,512]{2,1,0:T(8,128)S(1)} %get-tuple-element.66), channel_id=1, source_target_pairs={{2,0},{4,2},{6,4},{3,1},{5,3},{7,5},{10,8},{12,10},{14,12},{11,9},... | collective-permute-start | bytes 1081352 | tf_op jit(solution)/shard_map/ppermute | solution.py:26
  8.6 0.8 slice_bitcast_fusion.25
  9.8 2.9 %collective-permute-done = f32[16,11,512]{2,1,0:T(8,128)S(1)} collective-permute-done((f32[16,11,512]{2,1,0:T(8,128)S(1)}, f32[16,11,512]{2,1,0:T(8,128)S(1)}, u32[]{:S(2)}, u32[]{:S(2)}) %collective-permute-start) | collective-permute-done | bytes 360480 | tf_op jit(solution)/shard_map/ppermute | solution.py:25
  12.7 4.4 %collective-permute-done.1 = f32[16,11,512]{2,1,0:T(8,128)S(1)} collective-permute-done((f32[16,11,512]{2,1,0:T(8,128)S(1)}, f32[16,11,512]{2,1,0:T(8,128)S(1)}, u32[]{:S(2)}, u32[]{:S(2)}) %collective-permute-start.1) | collective-permute-done | bytes 360480 | tf_op jit(solution)/shard_map/ppermute | solution.py:26
  17.3 0.2 copy.25
  17.7 1.3 %collective-permute-start.2 = (f32[11,864]{1,0:T(8,128)S(1)}, f32[11,864]{1,0:T(8,128)S(1)}, u32[]{:S(2)}, u32[]{:S(2)}) collective-permute-start(f32[11,864]{1,0:T(8,128)S(1)} %reshape.81), channel_id=1, source_target_pairs={{0,1},{1,0},{2,3},{3,2},{4,5},{5,4},{6,7},{7,6},{8,9},{9,8},{10,11... | collective-permute-start | bytes 114056 | tf_op jit(solution)/shard_map/ppermute | solution.py:45
  19.0 0.5 add_bitcast_fusion
  19.5 0.6 reshape.79.row_weight
  20.1 0.6 reshape.80.col_weight
  20.9 0.3 copy.26
  21.3 0.3 copy.27
  21.5 2.4 %select_maximum_fusion.padded = f32[16,56,640]{2,1,0:T(8,128)} fusion(f32[16,54,11]{2,1,0:T(8,128)S(1)} %bitcast.78, f32[16,54,11]{2,1,0:T(8,128)S(1)} %bitcast.77, f32[16,11,512]{2,1,0:T(8,128)S(1)} %collective-permute-done.1, f32[16,32,512]{2,1,0:T(8,128)S(1)} %copy-done, f32[16,11,512]{2,1,0:T(8,128)S(1)} %collective-permute-done), kind=kLoop, calls=%fused_computation.6 | loop fusion | flops 9748480 | bytes 4139264 | tf_op jit(solution)/shard_map/concatenate | solution.py:50
  24.0 8.6 %shard_map.68 = (f32[16,32,512]{2,1,0:T(8,128)}, f32[16,32,512]{2,1,0:T(8,128)}) custom-call(s32[16]{0:T(128)} %get-tuple-element.110.row_shift, s32[16]{0:T(128)} %get-tuple-element.109.col_shift, f32[96]{0:T(128)} %reshape.79.row_weight, f32[96]{0:T(128)} %reshape.80.col_weight, f32[16,56,640]{2,1,0:T(8,128)} %select_maximum_fusion.padded, s32[16,32,512]{2,1,0:T(8,128)} %bad.1), custom_call_target="tpu_custom_call" | custom-call | tf_op jit(solution)/shard_map/pallas_call | solution.py:166
  32.6 2.8 %copy.28 = f32[16,32,512]{2,0,1:T(8,128)} copy(f32[16,32,512]{2,1,0:T(8,128)} %get-tuple-element.33) | data formatting | bytes 2097152 | tf_op jit(solution)/shard_map/pallas_call | solution.py:166
  35.4 4.6 %all-to-all-start = ((f32[16,32,512]{2,0,1:T(8,128)}), f32[16,32,512]{2,0,1:T(8,128)S(1)}, u32[]{:S(2)}, u32[]{:S(2)}) async-start(f32[16,32,512]{2,0,1:T(8,128)} %copy.28), calls=%async_computation | async-start | bytes 2097152 | tf_op jit(solution)/shard_map/all_to_all | solution.py:178
  40.2 21.0 %all-to-all-done = f32[16,32,512]{2,0,1:T(8,128)S(1)} async-done(((f32[16,32,512]{2,0,1:T(8,128)}), f32[16,32,512]{2,0,1:T(8,128)S(1)}, u32[]{:S(2)}, u32[]{:S(2)}) %all-to-all-start) | async-done | bytes 1048608 | tf_op jit(solution)/shard_map/all_to_all | solution.py:178
  61.2 0.6 copy.29
  61.9 3.6 %while.13 = (s32[]{:T(128)}, f32[8,512]{1,0:T(8,128)S(1)}, f32[8,512]{1,0:T(8,128)S(1)}, f32[64,8,512]{2,1,0:T(8,128)S(1)}, f32[8,512]{1,0:T(8,128)S(1)}, /*index=5*/s32[]{:T(128)}, s32[]{:T(128)}) while((s32[]{:T(128)}, f32[8,512]{1,0:T(8,128)S(1)}, f32[8,512]{1,0:T(8,128)S(1)}, f32[64,8,512]{2,1,0:T(8,128)S(1)}, ...), condition=%wide.region_5.7_spmd.clone, body=%wide.region_3.6_spmd.clone.sunk | while | flops 1110019 | bytes 1302617 | solution.py:109
  65.7 0.6 tile.2
  66.4 3.3 %all-to-all-start.1 = ((f32[4,8,512]{2,1,0:T(8,128)}), f32[4,8,512]{2,1,0:T(8,128)S(1)}, u32[]{:S(2)}, u32[]{:S(2)}) async-start(f32[4,8,512]{2,1,0:T(8,128)} %tile.2), calls=%async_computation.1 | async-start | bytes 131072 | tf_op jit(solution)/shard_map/all_to_all | solution.py:180
  69.7 4.5 %all-to-all-done.1 = f32[4,8,512]{2,1,0:T(8,128)S(1)} async-done(((f32[4,8,512]{2,1,0:T(8,128)}), f32[4,8,512]{2,1,0:T(8,128)S(1)}, u32[]{:S(2)}, u32[]{:S(2)}) %all-to-all-start.1) | async-done | bytes 65568 | tf_op jit(solution)/shard_map/all_to_all | solution.py:180
  74.2 1.9 %collective-permute-start.3 = (f32[4,512]{1,0:T(4,128)S(1)}, f32[4,512]{1,0:T(4,128)S(1)}, u32[]{:S(2)}, u32[]{:S(2)}) collective-permute-start(f32[4,512]{1,0:T(4,128)S(1)} %get-tuple-element.84), channel_id=1, source_target_pairs={{0,2},{2,4},{4,6},{1,3},{3,5},{5,7},{8,10},{10,12},{12,14},{9,11},... | collective-permute-start | bytes 24584 | tf_op jit(solution)/shard_map/ppermute | solution.py:25
  76.1 2.4 %collective-permute-start.4 = (f32[4,512]{1,0:T(4,128)S(1)}, f32[4,512]{1,0:T(4,128)S(1)}, u32[]{:S(2)}, u32[]{:S(2)}) collective-permute-start(f32[4,512]{1,0:T(4,128)S(1)} %get-tuple-element.85), channel_id=1, source_target_pairs={{2,0},{4,2},{6,4},{3,1},{5,3},{7,5},{10,8},{12,10},{14,12},{11,9},... | collective-permute-start | bytes 24584 | tf_op jit(solution)/shard_map/ppermute | solution.py:26
  78.6 2.5 %collective-permute-done.4 = f32[4,512]{1,0:T(4,128)S(1)} collective-permute-done((f32[4,512]{1,0:T(4,128)S(1)}, f32[4,512]{1,0:T(4,128)S(1)}, u32[]{:S(2)}, u32[]{:S(2)}) %collective-permute-start.4) | collective-permute-done | bytes 8224 | tf_op jit(solution)/shard_map/ppermute | solution.py:26
  81.2 1.2 %collective-permute-start.5 = (f32[4,40]{0,1:T(8,128)S(1)}, f32[4,40]{0,1:T(8,128)S(1)}, u32[]{:S(2)}, u32[]{:S(2)}) collective-permute-start(f32[4,40]{0,1:T(8,128)S(1)} %fusion.21), channel_id=1, source_target_pairs={{0,1},{1,0},{2,3},{3,2},{4,5},{5,4},{6,7},{7,6},{8,9},{9,8},{10,11... | collective-permute-start | bytes 1928 | tf_op jit(solution)/shard_map/ppermute | solution.py:45
  82.4 1.4 %collective-permute-done.5 = f32[4,40]{0,1:T(8,128)S(1)} collective-permute-done((f32[4,40]{0,1:T(8,128)S(1)}, f32[4,40]{0,1:T(8,128)S(1)}, u32[]{:S(2)}, u32[]{:S(2)}) %collective-permute-start.5) | collective-permute-done | bytes 672 | tf_op jit(solution)/shard_map/ppermute | solution.py:45
  84.0 0.6 multiply_add_fusion
  84.6 1.3 %fusion.10 = f32[8,32,512]{2,1,0:T(8,128)S(1)} fusion(f32[8,32,520]{2,1,0:T(8,128)S(1)} %multiply_add_fusion, f32[8]{0:T(128)S(1)} %get-tuple-element.91, f32[8]{0:T(128)S(1)} %get-tuple-element.92, f32[8]{0:T(128)S(1)} %get-tuple-element.93, f32[8]{0:T(128)S(1)} %get-tuple-element.94, f32[8]{0:T(128)S(1)} %get-tuple-element.95, f32[8]{0:T(128)S(1)} %get-tuple-element.96, ...), kind=kLoop, calls=%fused_computation.24 | loop fusion | flops 2228224 | bytes 5243168 | tf_op jit(solution)/shard_map/add | solution.py:195
  86.2 1.8 %subtract_select_fusion = f32[16,32,512]{2,1,0:T(8,128)} fusion(f32[16,32,512]{2,1,0:T(8,128)S(1)} %copy-done.2, s32[16,32,512]{2,1,0:T(8,128)S(1)} %copy-done.1, f32[32,512]{1,0:T(8,128)S(1)} %get-tuple-element.68, f32[16]{0:T(128)S(1)} %get-tuple-element.100, f32[32,512]{1,0:T(8,128)S(1)} %get-tuple-element.69, f32[16]{0:T(128)S(1)} %get-tuple-element.101, ...), kind=kLoop, calls=%fused_computation.20 | loop fusion | flops 4718592 | bytes 3670528 | tf_op jit(solution)/shard_map/jit(_where)/select_n | solution.py:203
  88.0 0.6 copy.42
  (119 shorter events, 5.1 us)
Async XLA Ops:
  0.6 16.5 %copy-start = (f32[16,32,512]{2,1,0:T(8,128)S(1)}, f32[16,32,512]{2,1,0:T(8,128)}, u32[]{:S(2)}) copy-start(f32[16,32,512]{2,1,0:T(8,128)} %param.8) | copy-start | bytes 3145732
  2.1 16.9 %copy-start.3 = (s32[16,2]{0,1:T(2,128)S(1)}, s32[16,2]{0,1:T(2,128)}, u32[]{:S(2)}) copy-start(s32[16,2]{0,1:T(2,128)} %param.10) | copy-start | bytes 388
  2.1 10.6 %collective-permute-start = (f32[16,11,512]{2,1,0:T(8,128)S(1)}, f32[16,11,512]{2,1,0:T(8,128)S(1)}, u32[]{:S(2)}, u32[]{:S(2)}) collective-permute-start(f32[16,11,512]{2,1,0:T(8,128)S(1)} %get-tuple-element.65), channel_id=1, source_target_pairs={{0,2},{2,4},{4,6},{1,3},{3,5},{5,7},{8,10},{10,12},{12,14},{9,11},... | collective-permute-start | bytes 1081352 | tf_op jit(solution)/shard_map/ppermute | solution.py:25
  6.6 10.5 %collective-permute-start.1 = (f32[16,11,512]{2,1,0:T(8,128)S(1)}, f32[16,11,512]{2,1,0:T(8,128)S(1)}, u32[]{:S(2)}, u32[]{:S(2)}) collective-permute-start(f32[16,11,512]{2,1,0:T(8,128)S(1)} %get-tuple-element.66), channel_id=1, source_target_pairs={{2,0},{4,2},{6,4},{3,1},{5,3},{7,5},{10,8},{12,10},{14,12},{11,9},... | collective-permute-start | bytes 1081352 | tf_op jit(solution)/shard_map/ppermute | solution.py:26
  17.7 3.1 %collective-permute-start.2 = (f32[11,864]{1,0:T(8,128)S(1)}, f32[11,864]{1,0:T(8,128)S(1)}, u32[]{:S(2)}, u32[]{:S(2)}) collective-permute-start(f32[11,864]{1,0:T(8,128)S(1)} %reshape.81), channel_id=1, source_target_pairs={{0,1},{1,0},{2,3},{3,2},{4,5},{5,4},{6,7},{7,6},{8,9},{9,8},{10,11... | collective-permute-start | bytes 114056 | tf_op jit(solution)/shard_map/ppermute | solution.py:45
  35.4 25.8 %all-to-all-start = ((f32[16,32,512]{2,0,1:T(8,128)}), f32[16,32,512]{2,0,1:T(8,128)S(1)}, u32[]{:S(2)}, u32[]{:S(2)}) async-start(f32[16,32,512]{2,0,1:T(8,128)} %copy.28), calls=%async_computation | async-start | bytes 2097152 | tf_op jit(solution)/shard_map/all_to_all | solution.py:178
  61.9 16.6 %copy-start.4 = (s32[16]{0:T(128)S(1)}, s32[16]{0:T(128)}, u32[]{:S(2)}) copy-start(s32[16]{0:T(128)} %param.12) | copy-start | bytes 196
  66.4 7.9 %all-to-all-start.1 = ((f32[4,8,512]{2,1,0:T(8,128)}), f32[4,8,512]{2,1,0:T(8,128)S(1)}, u32[]{:S(2)}, u32[]{:S(2)}) async-start(f32[4,8,512]{2,1,0:T(8,128)} %tile.2), calls=%async_computation.1 | async-start | bytes 131072 | tf_op jit(solution)/shard_map/all_to_all | solution.py:180
  74.2 4.4 %collective-permute-start.3 = (f32[4,512]{1,0:T(4,128)S(1)}, f32[4,512]{1,0:T(4,128)S(1)}, u32[]{:S(2)}, u32[]{:S(2)}) collective-permute-start(f32[4,512]{1,0:T(4,128)S(1)} %get-tuple-element.84), channel_id=1, source_target_pairs={{0,2},{2,4},{4,6},{1,3},{3,5},{5,7},{8,10},{10,12},{12,14},{9,11},... | collective-permute-start | bytes 24584 | tf_op jit(solution)/shard_map/ppermute | solution.py:25
  76.1 5.0 %collective-permute-start.4 = (f32[4,512]{1,0:T(4,128)S(1)}, f32[4,512]{1,0:T(4,128)S(1)}, u32[]{:S(2)}, u32[]{:S(2)}) collective-permute-start(f32[4,512]{1,0:T(4,128)S(1)} %get-tuple-element.85), channel_id=1, source_target_pairs={{2,0},{4,2},{6,4},{3,1},{5,3},{7,5},{10,8},{12,10},{14,12},{11,9},... | collective-permute-start | bytes 24584 | tf_op jit(solution)/shard_map/ppermute | solution.py:26
  81.2 2.6 %collective-permute-start.5 = (f32[4,40]{0,1:T(8,128)S(1)}, f32[4,40]{0,1:T(8,128)S(1)}, u32[]{:S(2)}, u32[]{:S(2)}) collective-permute-start(f32[4,40]{0,1:T(8,128)S(1)} %fusion.21), channel_id=1, source_target_pairs={{0,1},{1,0},{2,3},{3,2},{4,5},{5,4},{6,7},{7,6},{8,9},{9,8},{10,11... | collective-permute-start | bytes 1928 | tf_op jit(solution)/shard_map/ppermute | solution.py:45
  84.6 1.3 %copy-start.1 = (s32[16,32,512]{2,1,0:T(8,128)S(1)}, s32[16,32,512]{2,1,0:T(8,128)}, u32[]{:S(2)}) copy-start(s32[16,32,512]{2,1,0:T(8,128)} %bad.1) | copy-start | bytes 3145732
  84.6 1.5 %copy-start.2 = (f32[16,32,512]{2,1,0:T(8,128)S(1)}, f32[16,32,512]{2,1,0:T(8,128)}, u32[]{:S(2)}) copy-start(f32[16,32,512]{2,1,0:T(8,128)} %get-tuple-element.32) | copy-start | bytes 3145732

commit v4 on v3

--- a/solution.py
+++ b/solution.py
@@ -122,27 +122,45 @@
 TAPS = 6
 
 
+def _banded(shape, shift, weight, base, first):
+    down = lax.broadcasted_iota(jnp.int32, shape, 0)
+    across = lax.broadcasted_iota(jnp.int32, shape, 1)
+    gap = (across - down if first else down - across) + (base - shift)
+    matrix = jnp.zeros(shape, jnp.float32)
+    for tap in range(TAPS):
+        matrix = jnp.where(gap == tap, weight[tap], matrix)
+    return matrix
+
+
 def _warp_kernel(
     row_shift, col_shift, row_weight, col_weight, padded, bad, warped_out, flagged_out
 ):
     group_size, row_count, col_count = warped_out.shape
-    width = padded.shape[2]
-
     height = padded.shape[1]
+    bands, _, band_rows, _ = flagged_out.shape
+    lane = 128
+    exact = lax.Precision.HIGHEST
 
     def one_exposure(e, carry):
-        block = pltpu.roll(padded[e], height - row_shift[e], 0)
-        across = None
-        for tap in range(TAPS):
-            term = row_weight[e * TAPS + tap] * block[tap : tap + row_count, :]
-            across = term if across is None else across + term
-        across = pltpu.roll(across, width - col_shift[e], 1)
-        total = None
-        for tap in range(TAPS):
-            term = col_weight[e * TAPS + tap] * across[:, tap : tap + col_count]
-            total = term if total is None else total + term
+        rw = [row_weight[e * TAPS + tap] for tap in range(TAPS)]
+        cw = [col_weight[e * TAPS + tap] for tap in range(TAPS)]
+        down = _banded((row_count, height), row_shift[e], rw, 0, True)
+        across = jnp.dot(down, padded[e], precision=exact, preferred_element_type=jnp.float32)
+        same = _banded((lane, lane), col_shift[e], cw, 0, False)
+        after = _banded((lane, lane), col_shift[e], cw, lane, False)
+        pieces = []
+        for block in range(col_count // lane):
+            here = across[:, block * lane : (block + 1) * lane]
+            ahead = across[:, (block + 1) * lane : (block + 2) * lane]
+            pieces.append(
+                jnp.dot(here, same, precision=exact, preferred_element_type=jnp.float32)
+                + jnp.dot(ahead, after, precision=exact, preferred_element_type=jnp.float32)
+            )
+        total = jnp.concatenate(pieces, axis=1)
         warped_out[e] = total
-        flagged_out[e] = jnp.where(bad[e] == 1, sentinel, total)
+        flagged = jnp.where(bad[e] == 1, sentinel, total)
+        for band in range(bands):
+            flagged_out[band, e] = flagged[band * band_rows : (band + 1) * band_rows]
         return carry
 
     lax.fori_loop(0, group_size, one_exposure, 0)
@@ -163,9 +181,13 @@
     smem = pl.BlockSpec(memory_space=pltpu.SMEM)
     vmem = pl.BlockSpec(memory_space=pltpu.VMEM)
     shape = jax.ShapeDtypeStruct((group_size, row_count, col_count), jnp.float32)
+    bands = lax.axis_size("exp")
+    banded = jax.ShapeDtypeStruct(
+        (bands, group_size, row_count // bands, col_count), jnp.float32
+    )
     return pl.pallas_call(
         _warp_kernel,
-        out_shape=(shape, shape),
+        out_shape=(shape, banded),
         in_specs=[smem, smem, smem, smem, vmem, vmem],
         out_specs=(vmem, vmem),
     )(row_shift, col_shift, row_weight, col_weight, padded, bad_pixels)
@@ -175,7 +197,8 @@
     group_size, row_count, col_count = exposures.shape
     padded = extended(exposures, 1, 2, HALO)
     warped, flagged = warp_and_flag(padded, bad_pixels, offsets, warp_index)
-    band = stack_median(lax.all_to_all(flagged, "exp", split_axis=1, concat_axis=0, tiled=True))
+    gathered = lax.all_to_all(flagged, "exp", split_axis=0, concat_axis=0, tiled=True)
+    band = stack_median(gathered.reshape((-1,) + gathered.shape[2:]))
     groups = lax.axis_size("exp")
     median_sky = lax.all_to_all(
         jnp.tile(band, (groups, 1)), "exp", split_axis=0, concat_axis=0, tiled=True

time: 89.1 us -> 92.5 us (1.038)
  Pallas kernels: 8.6 us -> 15.5 us
  local copies, waits for them, and re-layouts: 9.55 us -> 6.13 us
    pallas_call x1, Pallas kernels: 8.6 us -> 15.5 us  [warp_and_flag(): pl.pallas_call(_warp_kernel, out_shape=(shape, banded), in_specs=[smem, s...]
    pallas_call x1 -> x0, local copies, waits for them, and re-layouts: 2.81 us -> none  [warp_and_flag(): pl.pallas_call(_warp_kernel, out_shape=(shape, shape), in_specs=[smem, sm...]
where the time goes in v4:
time: 92.5 us; the launch traced here: 92 us
  waiting for transfers between devices  36.8 us (40%)
  starting transfers between devices  21.1 us (23%)
  Pallas kernels  15.5 us (17%)
  other arithmetic  10.5 us (11%)
  local copies, waits for them, and re-layouts  6.13 us (7%)
    all_to_all x1, waiting for transfers between devices, body(): lax.all_to_all(flagged, 'exp', split_axis=0, concat_axis=0, tiled=True)  21 us
    pallas_call x1, Pallas kernels, warp_and_flag(): pl.pallas_call(_warp_kernel, out_shape=(shape, banded), in_specs=[smem, s...  15.5 us
    ppermute x2, waiting for transfers between devices, _row_halo(): lax.ppermute(lax.slice_in_dim(block, 0, width, axis=dim), 'row', backward)  6.92 us
    ppermute x2, starting transfers between devices, _row_halo(): lax.ppermute(lax.slice_in_dim(block, size - width, None, axis=dim), 'row'...  6.44 us
    all_to_all x1, starting transfers between devices, body(): lax.all_to_all(flagged, 'exp', split_axis=0, concat_axis=0, tiled=True)  4.59 us
    all_to_all x1, waiting for transfers between devices, body(): lax.all_to_all(jnp.tile(band, (groups, 1)), 'exp', split_axis=0, concat_a...  4.55 us
    ppermute x2, starting transfers between devices, _row_halo(): lax.ppermute(lax.slice_in_dim(block, 0, width, axis=dim), 'row', backward)  4.32 us
    all_to_all x1, starting transfers between devices, body(): lax.all_to_all(jnp.tile(band, (groups, 1)), 'exp', split_axis=0, concat_a...  3.28 us
  transfers between devices with their start and end apart: 8, of which 7 were waited for; matrix products, arithmetic and copies ran while one was open for 4% of the time, Pallas kernels for 0%

profile of v4, /device:TPU:1, one launch (start us, length us, event | category | flops | bytes accessed | tf_op | source)
XLA Modules:
  0.0 92.0 jit_solution(18300952135316531831)
XLA Ops:
  0.6 1.4 %fusion.99 = (f32[16,11,512]{2,1,0:T(8,128)S(1)}, f32[16,11,512]{2,1,0:T(8,128)S(1)}) fusion(f32[16,32,512]{2,1,0:T(8,128)} %param.8), kind=kLoop, calls=%fused_computation.182 | loop fusion | bytes 1441792 | tf_op jit(solution)/shard_map/slice | solution.py:25
  2.1 4.5 %collective-permute-start = (f32[16,11,512]{2,1,0:T(8,128)S(1)}, f32[16,11,512]{2,1,0:T(8,128)S(1)}, u32[]{:S(2)}, u32[]{:S(2)}) collective-permute-start(f32[16,11,512]{2,1,0:T(8,128)S(1)} %get-tuple-element.65), channel_id=1, source_target_pairs={{0,2},{2,4},{4,6},{1,3},{3,5},{5,7},{8,10},{10,12},{12,14},{9,11},... | collective-permute-start | bytes 1081352 | tf_op jit(solution)/shard_map/ppermute | solution.py:25
  6.6 1.9 %collective-permute-start.1 = (f32[16,11,512]{2,1,0:T(8,128)S(1)}, f32[16,11,512]{2,1,0:T(8,128)S(1)}, u32[]{:S(2)}, u32[]{:S(2)}) collective-permute-start(f32[16,11,512]{2,1,0:T(8,128)S(1)} %get-tuple-element.66), channel_id=1, source_target_pairs={{2,0},{4,2},{6,4},{3,1},{5,3},{7,5},{10,8},{12,10},{14,12},{11,9},... | collective-permute-start | bytes 1081352 | tf_op jit(solution)/shard_map/ppermute | solution.py:26
  8.6 0.8 slice_bitcast_fusion.25
  9.6 0.2 fusion.33
  9.8 2.9 %collective-permute-done = f32[16,11,512]{2,1,0:T(8,128)S(1)} collective-permute-done((f32[16,11,512]{2,1,0:T(8,128)S(1)}, f32[16,11,512]{2,1,0:T(8,128)S(1)}, u32[]{:S(2)}, u32[]{:S(2)}) %collective-permute-start) | collective-permute-done | bytes 360480 | tf_op jit(solution)/shard_map/ppermute | solution.py:25
  12.7 4.4 %collective-permute-done.1 = f32[16,11,512]{2,1,0:T(8,128)S(1)} collective-permute-done((f32[16,11,512]{2,1,0:T(8,128)S(1)}, f32[16,11,512]{2,1,0:T(8,128)S(1)}, u32[]{:S(2)}, u32[]{:S(2)}) %collective-permute-start.1) | collective-permute-done | bytes 360480 | tf_op jit(solution)/shard_map/ppermute | solution.py:26
  17.1 0.2 fusion.19
  17.3 0.2 copy.16
  17.7 1.3 %collective-permute-start.2 = (f32[11,864]{1,0:T(8,128)S(1)}, f32[11,864]{1,0:T(8,128)S(1)}, u32[]{:S(2)}, u32[]{:S(2)}) collective-permute-start(f32[11,864]{1,0:T(8,128)S(1)} %reshape.84), channel_id=1, source_target_pairs={{0,1},{1,0},{2,3},{3,2},{4,5},{5,4},{6,7},{7,6},{8,9},{9,8},{10,11... | collective-permute-start | bytes 114056 | tf_op jit(solution)/shard_map/ppermute | solution.py:45
  19.0 0.5 add_bitcast_fusion
  19.5 0.6 reshape.82.row_weight
  20.1 0.6 reshape.83.col_weight
  20.9 0.3 copy.17
  21.3 0.3 copy.18
  21.5 2.4 %select_maximum_fusion.padded = f32[16,56,640]{2,1,0:T(8,128)} fusion(f32[16,54,11]{2,1,0:T(8,128)S(1)} %bitcast.73, f32[16,54,11]{2,1,0:T(8,128)S(1)} %bitcast.72, f32[16,11,512]{2,1,0:T(8,128)S(1)} %collective-permute-done.1, f32[16,32,512]{2,1,0:T(8,128)S(1)} %copy-done, f32[16,11,512]{2,1,0:T(8,128)S(1)} %collective-permute-done), kind=kLoop, calls=%fused_computation.6 | loop fusion | flops 9748480 | bytes 4139264 | tf_op jit(solution)/shard_map/concatenate | solution.py:50
  24.0 15.5 %shard_map.68 = (f32[16,32,512]{2,1,0:T(8,128)}, f32[4,16,8,512]{3,2,1,0:T(8,128)}) custom-call(s32[16]{0:T(128)} %get-tuple-element.110.row_shift, s32[16]{0:T(128)} %get-tuple-element.109.col_shift, f32[96]{0:T(128)} %reshape.82.row_weight, f32[96]{0:T(128)} %reshape.83.col_weight, f32[16,56,640]{2,1,0:T(8,128)} %select_maximum_fusion.padded, ...), custom_call_target="tpu_custom_call" | custom-call | tf_op jit(solution)/shard_map/pallas_call | solution.py:188
  39.5 4.6 %all-to-all-start = ((f32[4,16,8,512]{3,2,1,0:T(8,128)}), f32[4,16,8,512]{3,2,1,0:T(8,128)S(1)}, u32[]{:S(2)}, u32[]{:S(2)}) async-start(f32[4,16,8,512]{3,2,1,0:T(8,128)} %get-tuple-element.33), calls=%async_computation | async-start | bytes 2097152 | tf_op jit(solution)/shard_map/all_to_all | solution.py:200
  44.2 21.0 %all-to-all-done = f32[4,16,8,512]{3,2,1,0:T(8,128)S(1)} async-done(((f32[4,16,8,512]{3,2,1,0:T(8,128)}), f32[4,16,8,512]{3,2,1,0:T(8,128)S(1)}, u32[]{:S(2)}, u32[]{:S(2)}) %all-to-all-start) | async-done | bytes 1048608 | tf_op jit(solution)/shard_map/all_to_all | solution.py:200
  65.4 3.6 %while.13 = (s32[]{:T(128)}, f32[8,512]{1,0:T(8,128)S(1)}, f32[8,512]{1,0:T(8,128)S(1)}, f32[64,8,512]{2,1,0:T(8,128)S(1)}, f32[8,512]{1,0:T(8,128)S(1)}, /*index=5*/s32[]{:T(128)}, s32[]{:T(128)}) while((s32[]{:T(128)}, f32[8,512]{1,0:T(8,128)S(1)}, f32[8,512]{1,0:T(8,128)S(1)}, f32[64,8,512]{2,1,0:T(8,128)S(1)}, ...), condition=%wide.region_5.7_spmd.clone, body=%wide.region_3.6_spmd.clone.sunk | while | flops 1110019 | bytes 1302617 | solution.py:109
  69.2 0.6 tile.2
  69.8 3.3 %all-to-all-start.1 = ((f32[4,8,512]{2,1,0:T(8,128)}), f32[4,8,512]{2,1,0:T(8,128)S(1)}, u32[]{:S(2)}, u32[]{:S(2)}) async-start(f32[4,8,512]{2,1,0:T(8,128)} %tile.2), calls=%async_computation.1 | async-start | bytes 131072 | tf_op jit(solution)/shard_map/all_to_all | solution.py:203
  73.1 4.5 %all-to-all-done.1 = f32[4,8,512]{2,1,0:T(8,128)S(1)} async-done(((f32[4,8,512]{2,1,0:T(8,128)}), f32[4,8,512]{2,1,0:T(8,128)S(1)}, u32[]{:S(2)}, u32[]{:S(2)}) %all-to-all-start.1) | async-done | bytes 65568 | tf_op jit(solution)/shard_map/all_to_all | solution.py:203
  77.7 1.9 %collective-permute-start.3 = (f32[4,512]{1,0:T(4,128)S(1)}, f32[4,512]{1,0:T(4,128)S(1)}, u32[]{:S(2)}, u32[]{:S(2)}) collective-permute-start(f32[4,512]{1,0:T(4,128)S(1)} %get-tuple-element.84), channel_id=1, source_target_pairs={{0,2},{2,4},{4,6},{1,3},{3,5},{5,7},{8,10},{10,12},{12,14},{9,11},... | collective-permute-start | bytes 24584 | tf_op jit(solution)/shard_map/ppermute | solution.py:25
  79.6 2.4 %collective-permute-start.4 = (f32[4,512]{1,0:T(4,128)S(1)}, f32[4,512]{1,0:T(4,128)S(1)}, u32[]{:S(2)}, u32[]{:S(2)}) collective-permute-start(f32[4,512]{1,0:T(4,128)S(1)} %get-tuple-element.85), channel_id=1, source_target_pairs={{2,0},{4,2},{6,4},{3,1},{5,3},{7,5},{10,8},{12,10},{14,12},{11,9},... | collective-permute-start | bytes 24584 | tf_op jit(solution)/shard_map/ppermute | solution.py:26
  82.0 2.5 %collective-permute-done.4 = f32[4,512]{1,0:T(4,128)S(1)} collective-permute-done((f32[4,512]{1,0:T(4,128)S(1)}, f32[4,512]{1,0:T(4,128)S(1)}, u32[]{:S(2)}, u32[]{:S(2)}) %collective-permute-start.4) | collective-permute-done | bytes 8224 | tf_op jit(solution)/shard_map/ppermute | solution.py:26
  84.6 1.2 %collective-permute-start.5 = (f32[4,40]{0,1:T(8,128)S(1)}, f32[4,40]{0,1:T(8,128)S(1)}, u32[]{:S(2)}, u32[]{:S(2)}) collective-permute-start(f32[4,40]{0,1:T(8,128)S(1)} %fusion.21), channel_id=1, source_target_pairs={{0,1},{1,0},{2,3},{3,2},{4,5},{5,4},{6,7},{7,6},{8,9},{9,8},{10,11... | collective-permute-start | bytes 1928 | tf_op jit(solution)/shard_map/ppermute | solution.py:45
  85.9 1.4 %collective-permute-done.5 = f32[4,40]{0,1:T(8,128)S(1)} collective-permute-done((f32[4,40]{0,1:T(8,128)S(1)}, f32[4,40]{0,1:T(8,128)S(1)}, u32[]{:S(2)}, u32[]{:S(2)}) %collective-permute-start.5) | collective-permute-done | bytes 672 | tf_op jit(solution)/shard_map/ppermute | solution.py:45
  87.5 0.6 multiply_add_fusion
  88.1 1.3 %fusion.10 = f32[8,32,512]{2,1,0:T(8,128)S(1)} fusion(f32[8,32,520]{2,1,0:T(8,128)S(1)} %multiply_add_fusion, f32[8]{0:T(128)S(1)} %get-tuple-element.91, f32[8]{0:T(128)S(1)} %get-tuple-element.92, f32[8]{0:T(128)S(1)} %get-tuple-element.93, f32[8]{0:T(128)S(1)} %get-tuple-element.94, f32[8]{0:T(128)S(1)} %get-tuple-element.95, f32[8]{0:T(128)S(1)} %get-tuple-element.96, ...), kind=kLoop, calls=%fused_computation.24 | loop fusion | flops 2228224 | bytes 5243168 | tf_op jit(solution)/shard_map/add | solution.py:218
  89.6 1.8 %subtract_select_fusion = f32[16,32,512]{2,1,0:T(8,128)} fusion(f32[16,32,512]{2,1,0:T(8,128)S(1)} %copy-done.2, s32[16,32,512]{2,1,0:T(8,128)S(1)} %copy-done.1, f32[32,512]{1,0:T(8,128)S(1)} %get-tuple-element.68, f32[16]{0:T(128)S(1)} %get-tuple-element.100, f32[32,512]{1,0:T(8,128)S(1)} %get-tuple-element.69, f32[16]{0:T(128)S(1)} %get-tuple-element.101, ...), kind=kLoop, calls=%fused_computation.20 | loop fusion | flops 4718592 | bytes 3670528 | tf_op jit(solution)/shard_map/jit(_where)/select_n | solution.py:226
  91.4 0.6 copy.31
  (117 shorter events, 4.7 us)
Async XLA Ops:
  0.6 16.5 %copy-start = (f32[16,32,512]{2,1,0:T(8,128)S(1)}, f32[16,32,512]{2,1,0:T(8,128)}, u32[]{:S(2)}) copy-start(f32[16,32,512]{2,1,0:T(8,128)} %param.8) | copy-start | bytes 3145732
  2.1 16.9 %copy-start.3 = (s32[16,2]{0,1:T(2,128)S(1)}, s32[16,2]{0,1:T(2,128)}, u32[]{:S(2)}) copy-start(s32[16,2]{0,1:T(2,128)} %param.10) | copy-start | bytes 388
  2.1 10.6 %collective-permute-start = (f32[16,11,512]{2,1,0:T(8,128)S(1)}, f32[16,11,512]{2,1,0:T(8,128)S(1)}, u32[]{:S(2)}, u32[]{:S(2)}) collective-permute-start(f32[16,11,512]{2,1,0:T(8,128)S(1)} %get-tuple-element.65), channel_id=1, source_target_pairs={{0,2},{2,4},{4,6},{1,3},{3,5},{5,7},{8,10},{10,12},{12,14},{9,11},... | collective-permute-start | bytes 1081352 | tf_op jit(solution)/shard_map/ppermute | solution.py:25
  6.6 10.5 %collective-permute-start.1 = (f32[16,11,512]{2,1,0:T(8,128)S(1)}, f32[16,11,512]{2,1,0:T(8,128)S(1)}, u32[]{:S(2)}, u32[]{:S(2)}) collective-permute-start(f32[16,11,512]{2,1,0:T(8,128)S(1)} %get-tuple-element.66), channel_id=1, source_target_pairs={{2,0},{4,2},{6,4},{3,1},{5,3},{7,5},{10,8},{12,10},{14,12},{11,9},... | collective-permute-start | bytes 1081352 | tf_op jit(solution)/shard_map/ppermute | solution.py:26
  17.7 3.1 %collective-permute-start.2 = (f32[11,864]{1,0:T(8,128)S(1)}, f32[11,864]{1,0:T(8,128)S(1)}, u32[]{:S(2)}, u32[]{:S(2)}) collective-permute-start(f32[11,864]{1,0:T(8,128)S(1)} %reshape.84), channel_id=1, source_target_pairs={{0,1},{1,0},{2,3},{3,2},{4,5},{5,4},{6,7},{7,6},{8,9},{9,8},{10,11... | collective-permute-start | bytes 114056 | tf_op jit(solution)/shard_map/ppermute | solution.py:45
  39.5 25.8 %all-to-all-start = ((f32[4,16,8,512]{3,2,1,0:T(8,128)}), f32[4,16,8,512]{3,2,1,0:T(8,128)S(1)}, u32[]{:S(2)}, u32[]{:S(2)}) async-start(f32[4,16,8,512]{3,2,1,0:T(8,128)} %get-tuple-element.33), calls=%async_computation | async-start | bytes 2097152 | tf_op jit(solution)/shard_map/all_to_all | solution.py:200
  65.4 16.6 %copy-start.4 = (s32[16]{0:T(128)S(1)}, s32[16]{0:T(128)}, u32[]{:S(2)}) copy-start(s32[16]{0:T(128)} %param.12) | copy-start | bytes 196
  69.8 7.9 %all-to-all-start.1 = ((f32[4,8,512]{2,1,0:T(8,128)}), f32[4,8,512]{2,1,0:T(8,128)S(1)}, u32[]{:S(2)}, u32[]{:S(2)}) async-start(f32[4,8,512]{2,1,0:T(8,128)} %tile.2), calls=%async_computation.1 | async-start | bytes 131072 | tf_op jit(solution)/shard_map/all_to_all | solution.py:203
  77.7 4.4 %collective-permute-start.3 = (f32[4,512]{1,0:T(4,128)S(1)}, f32[4,512]{1,0:T(4,128)S(1)}, u32[]{:S(2)}, u32[]{:S(2)}) collective-permute-start(f32[4,512]{1,0:T(4,128)S(1)} %get-tuple-element.84), channel_id=1, source_target_pairs={{0,2},{2,4},{4,6},{1,3},{3,5},{5,7},{8,10},{10,12},{12,14},{9,11},... | collective-permute-start | bytes 24584 | tf_op jit(solution)/shard_map/ppermute | solution.py:25
  79.6 5.0 %collective-permute-start.4 = (f32[4,512]{1,0:T(4,128)S(1)}, f32[4,512]{1,0:T(4,128)S(1)}, u32[]{:S(2)}, u32[]{:S(2)}) collective-permute-start(f32[4,512]{1,0:T(4,128)S(1)} %get-tuple-element.85), channel_id=1, source_target_pairs={{2,0},{4,2},{6,4},{3,1},{5,3},{7,5},{10,8},{12,10},{14,12},{11,9},... | collective-permute-start | bytes 24584 | tf_op jit(solution)/shard_map/ppermute | solution.py:26
  84.6 2.6 %collective-permute-start.5 = (f32[4,40]{0,1:T(8,128)S(1)}, f32[4,40]{0,1:T(8,128)S(1)}, u32[]{:S(2)}, u32[]{:S(2)}) collective-permute-start(f32[4,40]{0,1:T(8,128)S(1)} %fusion.21), channel_id=1, source_target_pairs={{0,1},{1,0},{2,3},{3,2},{4,5},{5,4},{6,7},{7,6},{8,9},{9,8},{10,11... | collective-permute-start | bytes 1928 | tf_op jit(solution)/shard_map/ppermute | solution.py:45
  88.1 1.3 %copy-start.1 = (s32[16,32,512]{2,1,0:T(8,128)S(1)}, s32[16,32,512]{2,1,0:T(8,128)}, u32[]{:S(2)}) copy-start(s32[16,32,512]{2,1,0:T(8,128)} %bad.1) | copy-start | bytes 3145732
  88.1 1.5 %copy-start.2 = (f32[16,32,512]{2,1,0:T(8,128)S(1)}, f32[16,32,512]{2,1,0:T(8,128)}, u32[]{:S(2)}) copy-start(f32[16,32,512]{2,1,0:T(8,128)} %get-tuple-element.32) | copy-start | bytes 3145732

commit v5 on v3

--- a/solution.py
+++ b/solution.py
@@ -126,6 +126,7 @@
     row_shift, col_shift, row_weight, col_weight, padded, bad, warped_out, flagged_out
 ):
     group_size, row_count, col_count = warped_out.shape
+    bands, _, band_rows, _ = flagged_out.shape
     width = padded.shape[2]
 
     height = padded.shape[1]
@@ -142,10 +143,12 @@
             term = col_weight[e * TAPS + tap] * across[:, tap : tap + col_count]
             total = term if total is None else total + term
         warped_out[e] = total
-        flagged_out[e] = jnp.where(bad[e] == 1, sentinel, total)
+        flagged = jnp.where(bad[e] == 1, sentinel, total)
+        for band in range(bands):
+            flagged_out[band, e] = flagged[band * band_rows : (band + 1) * band_rows]
         return carry
 
-    lax.fori_loop(0, group_size, one_exposure, 0)
+    lax.fori_loop(0, group_size, one_exposure, 0, unroll=True)
 
 
 def warp_and_flag(padded, bad_pixels, offsets, warp_index):
@@ -163,9 +166,13 @@
     smem = pl.BlockSpec(memory_space=pltpu.SMEM)
     vmem = pl.BlockSpec(memory_space=pltpu.VMEM)
     shape = jax.ShapeDtypeStruct((group_size, row_count, col_count), jnp.float32)
+    bands = lax.axis_size("exp")
+    banded = jax.ShapeDtypeStruct(
+        (bands, group_size, row_count // bands, col_count), jnp.float32
+    )
     return pl.pallas_call(
         _warp_kernel,
-        out_shape=(shape, shape),
+        out_shape=(shape, banded),
         in_specs=[smem, smem, smem, smem, vmem, vmem],
         out_specs=(vmem, vmem),
     )(row_shift, col_shift, row_weight, col_weight, padded, bad_pixels)
@@ -175,7 +182,8 @@
     group_size, row_count, col_count = exposures.shape
     padded = extended(exposures, 1, 2, HALO)
     warped, flagged = warp_and_flag(padded, bad_pixels, offsets, warp_index)
-    band = stack_median(lax.all_to_all(flagged, "exp", split_axis=1, concat_axis=0, tiled=True))
+    gathered = lax.all_to_all(flagged, "exp", split_axis=0, concat_axis=0, tiled=True)
+    band = stack_median(gathered.reshape((-1,) + gathered.shape[2:]))
     groups = lax.axis_size("exp")
     median_sky = lax.all_to_all(
         jnp.tile(band, (groups, 1)), "exp", split_axis=0, concat_axis=0, tiled=True

time: 89.1 us -> 83.8 us (0.941)
  local copies, waits for them, and re-layouts: 9.55 us -> 6.13 us
  Pallas kernels: 8.6 us -> 6.84 us
    pallas_call x1 -> x0, local copies, waits for them, and re-layouts: 2.81 us -> none  [warp_and_flag(): pl.pallas_call(_warp_kernel, out_shape=(shape, shape), in_specs=[smem, sm...]
    pallas_call x1, Pallas kernels: 8.6 us -> 6.84 us  [warp_and_flag(): pl.pallas_call(_warp_kernel, out_shape=(shape, banded), in_specs=[smem, s...]
where the time goes in v5:
time: 83.8 us; the launch traced here: 83.4 us
  waiting for transfers between devices  36.8 us (44%)
  starting transfers between devices  21.1 us (25%)
  other arithmetic  10.5 us (13%)
  Pallas kernels  6.84 us (8%)
  local copies, waits for them, and re-layouts  6.13 us (7%)
  between operations  0.86 us (1%)
    all_to_all x1, waiting for transfers between devices, body(): lax.all_to_all(flagged, 'exp', split_axis=0, concat_axis=0, tiled=True)  21 us
    ppermute x2, waiting for transfers between devices, _row_halo(): lax.ppermute(lax.slice_in_dim(block, 0, width, axis=dim), 'row', backward)  6.92 us
    pallas_call x1, Pallas kernels, warp_and_flag(): pl.pallas_call(_warp_kernel, out_shape=(shape, banded), in_specs=[smem, s...  6.84 us
    ppermute x2, starting transfers between devices, _row_halo(): lax.ppermute(lax.slice_in_dim(block, size - width, None, axis=dim), 'row'...  6.44 us
    all_to_all x1, starting transfers between devices, body(): lax.all_to_all(flagged, 'exp', split_axis=0, concat_axis=0, tiled=True)  4.59 us
    all_to_all x1, waiting for transfers between devices, body(): lax.all_to_all(jnp.tile(band, (groups, 1)), 'exp', split_axis=0, concat_a...  4.55 us
    ppermute x2, starting transfers between devices, _row_halo(): lax.ppermute(lax.slice_in_dim(block, 0, width, axis=dim), 'row', backward)  4.32 us
    all_to_all x1, starting transfers between devices, body(): lax.all_to_all(jnp.tile(band, (groups, 1)), 'exp', split_axis=0, concat_a...  3.28 us
  transfers between devices with their start and end apart: 8, of which 7 were waited for; matrix products, arithmetic and copies ran while one was open for 4% of the time, Pallas kernels for 0%

profile of v5, /device:TPU:1, one launch (start us, length us, event | category | flops | bytes accessed | tf_op | source)
XLA Modules:
  0.0 83.4 jit_solution(3128721942047365540)
XLA Ops:
  0.6 1.4 %fusion.99 = (f32[16,11,512]{2,1,0:T(8,128)S(1)}, f32[16,11,512]{2,1,0:T(8,128)S(1)}) fusion(f32[16,32,512]{2,1,0:T(8,128)} %param.8), kind=kLoop, calls=%fused_computation.182 | loop fusion | bytes 1441792 | tf_op jit(solution)/shard_map/slice | solution.py:25
  2.1 4.5 %collective-permute-start = (f32[16,11,512]{2,1,0:T(8,128)S(1)}, f32[16,11,512]{2,1,0:T(8,128)S(1)}, u32[]{:S(2)}, u32[]{:S(2)}) collective-permute-start(f32[16,11,512]{2,1,0:T(8,128)S(1)} %get-tuple-element.65), channel_id=1, source_target_pairs={{0,2},{2,4},{4,6},{1,3},{3,5},{5,7},{8,10},{10,12},{12,14},{9,11},... | collective-permute-start | bytes 1081352 | tf_op jit(solution)/shard_map/ppermute | solution.py:25
  6.6 1.9 %collective-permute-start.1 = (f32[16,11,512]{2,1,0:T(8,128)S(1)}, f32[16,11,512]{2,1,0:T(8,128)S(1)}, u32[]{:S(2)}, u32[]{:S(2)}) collective-permute-start(f32[16,11,512]{2,1,0:T(8,128)S(1)} %get-tuple-element.66), channel_id=1, source_target_pairs={{2,0},{4,2},{6,4},{3,1},{5,3},{7,5},{10,8},{12,10},{14,12},{11,9},... | collective-permute-start | bytes 1081352 | tf_op jit(solution)/shard_map/ppermute | solution.py:26
  8.6 0.8 slice_bitcast_fusion.25
  9.6 0.2 fusion.33
  9.8 2.9 %collective-permute-done = f32[16,11,512]{2,1,0:T(8,128)S(1)} collective-permute-done((f32[16,11,512]{2,1,0:T(8,128)S(1)}, f32[16,11,512]{2,1,0:T(8,128)S(1)}, u32[]{:S(2)}, u32[]{:S(2)}) %collective-permute-start) | collective-permute-done | bytes 360480 | tf_op jit(solution)/shard_map/ppermute | solution.py:25
  12.7 4.4 %collective-permute-done.1 = f32[16,11,512]{2,1,0:T(8,128)S(1)} collective-permute-done((f32[16,11,512]{2,1,0:T(8,128)S(1)}, f32[16,11,512]{2,1,0:T(8,128)S(1)}, u32[]{:S(2)}, u32[]{:S(2)}) %collective-permute-start.1) | collective-permute-done | bytes 360480 | tf_op jit(solution)/shard_map/ppermute | solution.py:26
  17.1 0.2 fusion.19
  17.3 0.2 copy.16
  17.7 1.3 %collective-permute-start.2 = (f32[11,864]{1,0:T(8,128)S(1)}, f32[11,864]{1,0:T(8,128)S(1)}, u32[]{:S(2)}, u32[]{:S(2)}) collective-permute-start(f32[11,864]{1,0:T(8,128)S(1)} %reshape.84), channel_id=1, source_target_pairs={{0,1},{1,0},{2,3},{3,2},{4,5},{5,4},{6,7},{7,6},{8,9},{9,8},{10,11... | collective-permute-start | bytes 114056 | tf_op jit(solution)/shard_map/ppermute | solution.py:45
  19.0 0.5 add_bitcast_fusion
  19.5 0.6 reshape.82.row_weight
  20.1 0.6 reshape.83.col_weight
  20.9 0.3 copy.17
  21.3 0.3 copy.18
  21.5 2.4 %select_maximum_fusion.padded = f32[16,56,640]{2,1,0:T(8,128)} fusion(f32[16,54,11]{2,1,0:T(8,128)S(1)} %bitcast.73, f32[16,54,11]{2,1,0:T(8,128)S(1)} %bitcast.72, f32[16,11,512]{2,1,0:T(8,128)S(1)} %collective-permute-done.1, f32[16,32,512]{2,1,0:T(8,128)S(1)} %copy-done, f32[16,11,512]{2,1,0:T(8,128)S(1)} %collective-permute-done), kind=kLoop, calls=%fused_computation.6 | loop fusion | flops 9748480 | bytes 4139264 | tf_op jit(solution)/shard_map/concatenate | solution.py:50
  24.0 6.8 %shard_map.68 = (f32[16,32,512]{2,1,0:T(8,128)}, f32[4,16,8,512]{3,2,1,0:T(8,128)}) custom-call(s32[16]{0:T(128)} %get-tuple-element.110.row_shift, s32[16]{0:T(128)} %get-tuple-element.109.col_shift, f32[96]{0:T(128)} %reshape.82.row_weight, f32[96]{0:T(128)} %reshape.83.col_weight, f32[16,56,640]{2,1,0:T(8,128)} %select_maximum_fusion.padded, ...), custom_call_target="tpu_custom_call" | custom-call | tf_op jit(solution)/shard_map/pallas_call | solution.py:173
  30.8 4.6 %all-to-all-start = ((f32[4,16,8,512]{3,2,1,0:T(8,128)}), f32[4,16,8,512]{3,2,1,0:T(8,128)S(1)}, u32[]{:S(2)}, u32[]{:S(2)}) async-start(f32[4,16,8,512]{3,2,1,0:T(8,128)} %get-tuple-element.33), calls=%async_computation | async-start | bytes 2097152 | tf_op jit(solution)/shard_map/all_to_all | solution.py:185
  35.6 21.0 %all-to-all-done = f32[4,16,8,512]{3,2,1,0:T(8,128)S(1)} async-done(((f32[4,16,8,512]{3,2,1,0:T(8,128)}), f32[4,16,8,512]{3,2,1,0:T(8,128)S(1)}, u32[]{:S(2)}, u32[]{:S(2)}) %all-to-all-start) | async-done | bytes 1048608 | tf_op jit(solution)/shard_map/all_to_all | solution.py:185
  56.7 3.6 %while.13 = (s32[]{:T(128)}, f32[8,512]{1,0:T(8,128)S(1)}, f32[8,512]{1,0:T(8,128)S(1)}, f32[64,8,512]{2,1,0:T(8,128)S(1)}, f32[8,512]{1,0:T(8,128)S(1)}, /*index=5*/s32[]{:T(128)}, s32[]{:T(128)}) while((s32[]{:T(128)}, f32[8,512]{1,0:T(8,128)S(1)}, f32[8,512]{1,0:T(8,128)S(1)}, f32[64,8,512]{2,1,0:T(8,128)S(1)}, ...), condition=%wide.region_5.7_spmd.clone, body=%wide.region_3.6_spmd.clone.sunk | while | flops 1110019 | bytes 1302617 | solution.py:109
  60.5 0.6 tile.2
  61.2 3.3 %all-to-all-start.1 = ((f32[4,8,512]{2,1,0:T(8,128)}), f32[4,8,512]{2,1,0:T(8,128)S(1)}, u32[]{:S(2)}, u32[]{:S(2)}) async-start(f32[4,8,512]{2,1,0:T(8,128)} %tile.2), calls=%async_computation.1 | async-start | bytes 131072 | tf_op jit(solution)/shard_map/all_to_all | solution.py:188
  64.5 4.5 %all-to-all-done.1 = f32[4,8,512]{2,1,0:T(8,128)S(1)} async-done(((f32[4,8,512]{2,1,0:T(8,128)}), f32[4,8,512]{2,1,0:T(8,128)S(1)}, u32[]{:S(2)}, u32[]{:S(2)}) %all-to-all-start.1) | async-done | bytes 65568 | tf_op jit(solution)/shard_map/all_to_all | solution.py:188
  69.0 1.9 %collective-permute-start.3 = (f32[4,512]{1,0:T(4,128)S(1)}, f32[4,512]{1,0:T(4,128)S(1)}, u32[]{:S(2)}, u32[]{:S(2)}) collective-permute-start(f32[4,512]{1,0:T(4,128)S(1)} %get-tuple-element.84), channel_id=1, source_target_pairs={{0,2},{2,4},{4,6},{1,3},{3,5},{5,7},{8,10},{10,12},{12,14},{9,11},... | collective-permute-start | bytes 24584 | tf_op jit(solution)/shard_map/ppermute | solution.py:25
  71.0 2.4 %collective-permute-start.4 = (f32[4,512]{1,0:T(4,128)S(1)}, f32[4,512]{1,0:T(4,128)S(1)}, u32[]{:S(2)}, u32[]{:S(2)}) collective-permute-start(f32[4,512]{1,0:T(4,128)S(1)} %get-tuple-element.85), channel_id=1, source_target_pairs={{2,0},{4,2},{6,4},{3,1},{5,3},{7,5},{10,8},{12,10},{14,12},{11,9},... | collective-permute-start | bytes 24584 | tf_op jit(solution)/shard_map/ppermute | solution.py:26
  73.4 2.5 %collective-permute-done.4 = f32[4,512]{1,0:T(4,128)S(1)} collective-permute-done((f32[4,512]{1,0:T(4,128)S(1)}, f32[4,512]{1,0:T(4,128)S(1)}, u32[]{:S(2)}, u32[]{:S(2)}) %collective-permute-start.4) | collective-permute-done | bytes 8224 | tf_op jit(solution)/shard_map/ppermute | solution.py:26
  76.0 1.2 %collective-permute-start.5 = (f32[4,40]{0,1:T(8,128)S(1)}, f32[4,40]{0,1:T(8,128)S(1)}, u32[]{:S(2)}, u32[]{:S(2)}) collective-permute-start(f32[4,40]{0,1:T(8,128)S(1)} %fusion.21), channel_id=1, source_target_pairs={{0,1},{1,0},{2,3},{3,2},{4,5},{5,4},{6,7},{7,6},{8,9},{9,8},{10,11... | collective-permute-start | bytes 1928 | tf_op jit(solution)/shard_map/ppermute | solution.py:45
  77.2 1.4 %collective-permute-done.5 = f32[4,40]{0,1:T(8,128)S(1)} collective-permute-done((f32[4,40]{0,1:T(8,128)S(1)}, f32[4,40]{0,1:T(8,128)S(1)}, u32[]{:S(2)}, u32[]{:S(2)}) %collective-permute-start.5) | collective-permute-done | bytes 672 | tf_op jit(solution)/shard_map/ppermute | solution.py:45
  78.8 0.6 multiply_add_fusion
  79.4 1.3 %fusion.10 = f32[8,32,512]{2,1,0:T(8,128)S(1)} fusion(f32[8,32,520]{2,1,0:T(8,128)S(1)} %multiply_add_fusion, f32[8]{0:T(128)S(1)} %get-tuple-element.91, f32[8]{0:T(128)S(1)} %get-tuple-element.92, f32[8]{0:T(128)S(1)} %get-tuple-element.93, f32[8]{0:T(128)S(1)} %get-tuple-element.94, f32[8]{0:T(128)S(1)} %get-tuple-element.95, f32[8]{0:T(128)S(1)} %get-tuple-element.96, ...), kind=kLoop, calls=%fused_computation.24 | loop fusion | flops 2228224 | bytes 5243168 | tf_op jit(solution)/shard_map/add | solution.py:203
  81.0 1.8 %subtract_select_fusion = f32[16,32,512]{2,1,0:T(8,128)} fusion(f32[16,32,512]{2,1,0:T(8,128)S(1)} %copy-done.2, s32[16,32,512]{2,1,0:T(8,128)S(1)} %copy-done.1, f32[32,512]{1,0:T(8,128)S(1)} %get-tuple-element.68, f32[16]{0:T(128)S(1)} %get-tuple-element.100, f32[32,512]{1,0:T(8,128)S(1)} %get-tuple-element.69, f32[16]{0:T(128)S(1)} %get-tuple-element.101, ...), kind=kLoop, calls=%fused_computation.20 | loop fusion | flops 4718592 | bytes 3670528 | tf_op jit(solution)/shard_map/jit(_where)/select_n | solution.py:211
  82.8 0.6 copy.31
  (117 shorter events, 4.7 us)
Async XLA Ops:
  0.6 16.5 %copy-start = (f32[16,32,512]{2,1,0:T(8,128)S(1)}, f32[16,32,512]{2,1,0:T(8,128)}, u32[]{:S(2)}) copy-start(f32[16,32,512]{2,1,0:T(8,128)} %param.8) | copy-start | bytes 3145732
  2.1 16.9 %copy-start.3 = (s32[16,2]{0,1:T(2,128)S(1)}, s32[16,2]{0,1:T(2,128)}, u32[]{:S(2)}) copy-start(s32[16,2]{0,1:T(2,128)} %param.10) | copy-start | bytes 388
  2.1 10.6 %collective-permute-start = (f32[16,11,512]{2,1,0:T(8,128)S(1)}, f32[16,11,512]{2,1,0:T(8,128)S(1)}, u32[]{:S(2)}, u32[]{:S(2)}) collective-permute-start(f32[16,11,512]{2,1,0:T(8,128)S(1)} %get-tuple-element.65), channel_id=1, source_target_pairs={{0,2},{2,4},{4,6},{1,3},{3,5},{5,7},{8,10},{10,12},{12,14},{9,11},... | collective-permute-start | bytes 1081352 | tf_op jit(solution)/shard_map/ppermute | solution.py:25
  6.6 10.5 %collective-permute-start.1 = (f32[16,11,512]{2,1,0:T(8,128)S(1)}, f32[16,11,512]{2,1,0:T(8,128)S(1)}, u32[]{:S(2)}, u32[]{:S(2)}) collective-permute-start(f32[16,11,512]{2,1,0:T(8,128)S(1)} %get-tuple-element.66), channel_id=1, source_target_pairs={{2,0},{4,2},{6,4},{3,1},{5,3},{7,5},{10,8},{12,10},{14,12},{11,9},... | collective-permute-start | bytes 1081352 | tf_op jit(solution)/shard_map/ppermute | solution.py:26
  17.7 3.1 %collective-permute-start.2 = (f32[11,864]{1,0:T(8,128)S(1)}, f32[11,864]{1,0:T(8,128)S(1)}, u32[]{:S(2)}, u32[]{:S(2)}) collective-permute-start(f32[11,864]{1,0:T(8,128)S(1)} %reshape.84), channel_id=1, source_target_pairs={{0,1},{1,0},{2,3},{3,2},{4,5},{5,4},{6,7},{7,6},{8,9},{9,8},{10,11... | collective-permute-start | bytes 114056 | tf_op jit(solution)/shard_map/ppermute | solution.py:45
  30.8 25.8 %all-to-all-start = ((f32[4,16,8,512]{3,2,1,0:T(8,128)}), f32[4,16,8,512]{3,2,1,0:T(8,128)S(1)}, u32[]{:S(2)}, u32[]{:S(2)}) async-start(f32[4,16,8,512]{3,2,1,0:T(8,128)} %get-tuple-element.33), calls=%async_computation | async-start | bytes 2097152 | tf_op jit(solution)/shard_map/all_to_all | solution.py:185
  56.7 16.6 %copy-start.4 = (s32[16]{0:T(128)S(1)}, s32[16]{0:T(128)}, u32[]{:S(2)}) copy-start(s32[16]{0:T(128)} %param.12) | copy-start | bytes 196
  61.2 7.9 %all-to-all-start.1 = ((f32[4,8,512]{2,1,0:T(8,128)}), f32[4,8,512]{2,1,0:T(8,128)S(1)}, u32[]{:S(2)}, u32[]{:S(2)}) async-start(f32[4,8,512]{2,1,0:T(8,128)} %tile.2), calls=%async_computation.1 | async-start | bytes 131072 | tf_op jit(solution)/shard_map/all_to_all | solution.py:188
  69.0 4.4 %collective-permute-start.3 = (f32[4,512]{1,0:T(4,128)S(1)}, f32[4,512]{1,0:T(4,128)S(1)}, u32[]{:S(2)}, u32[]{:S(2)}) collective-permute-start(f32[4,512]{1,0:T(4,128)S(1)} %get-tuple-element.84), channel_id=1, source_target_pairs={{0,2},{2,4},{4,6},{1,3},{3,5},{5,7},{8,10},{10,12},{12,14},{9,11},... | collective-permute-start | bytes 24584 | tf_op jit(solution)/shard_map/ppermute | solution.py:25
  71.0 5.0 %collective-permute-start.4 = (f32[4,512]{1,0:T(4,128)S(1)}, f32[4,512]{1,0:T(4,128)S(1)}, u32[]{:S(2)}, u32[]{:S(2)}) collective-permute-start(f32[4,512]{1,0:T(4,128)S(1)} %get-tuple-element.85), channel_id=1, source_target_pairs={{2,0},{4,2},{6,4},{3,1},{5,3},{7,5},{10,8},{12,10},{14,12},{11,9},... | collective-permute-start | bytes 24584 | tf_op jit(solution)/shard_map/ppermute | solution.py:26
  76.0 2.6 %collective-permute-start.5 = (f32[4,40]{0,1:T(8,128)S(1)}, f32[4,40]{0,1:T(8,128)S(1)}, u32[]{:S(2)}, u32[]{:S(2)}) collective-permute-start(f32[4,40]{0,1:T(8,128)S(1)} %fusion.21), channel_id=1, source_target_pairs={{0,1},{1,0},{2,3},{3,2},{4,5},{5,4},{6,7},{7,6},{8,9},{9,8},{10,11... | collective-permute-start | bytes 1928 | tf_op jit(solution)/shard_map/ppermute | solution.py:45
  79.4 1.3 %copy-start.1 = (s32[16,32,512]{2,1,0:T(8,128)S(1)}, s32[16,32,512]{2,1,0:T(8,128)}, u32[]{:S(2)}) copy-start(s32[16,32,512]{2,1,0:T(8,128)} %bad.1) | copy-start | bytes 3145732
  79.4 1.5 %copy-start.2 = (f32[16,32,512]{2,1,0:T(8,128)S(1)}, f32[16,32,512]{2,1,0:T(8,128)}, u32[]{:S(2)}) copy-start(f32[16,32,512]{2,1,0:T(8,128)} %get-tuple-element.32) | copy-start | bytes 3145732

commit v6 on v5

--- a/solution.py
+++ b/solution.py
@@ -185,10 +185,18 @@
     gathered = lax.all_to_all(flagged, "exp", split_axis=0, concat_axis=0, tiled=True)
     band = stack_median(gathered.reshape((-1,) + gathered.shape[2:]))
     groups = lax.axis_size("exp")
-    median_sky = lax.all_to_all(
-        jnp.tile(band, (groups, 1)), "exp", split_axis=0, concat_axis=0, tiled=True
-    )
-    bordered = extended(median_sky, 0, 1, PSF_RADIUS)
+    sides = lax.axis_size("col")
+    band_rows = band.shape[0]
+    full = lax.all_to_all(
+        jnp.tile(band, (groups * sides, 1)), ("exp", "col"), split_axis=0, concat_axis=0, tiled=True
+    )
+    full = full.reshape(groups, sides, band_rows, col_count)
+    full = full.transpose(0, 2, 1, 3).reshape(row_count, sides * col_count)
+    start = lax.axis_index("col") * col_count
+    median_sky = lax.dynamic_slice_in_dim(full, start, col_count, axis=1)
+    wide = jnp.pad(full, ((0, 0), (PSF_RADIUS, PSF_RADIUS)))
+    wide = lax.dynamic_slice_in_dim(wide, start, col_count + 2 * PSF_RADIUS, axis=1)
+    bordered = _row_halo(wide, 0, PSF_RADIUS)
     blur = blur_table()
     taps = 2 * PSF_RADIUS + 1
     blurred_rows = jnp.zeros((NPSF, row_count, col_count + 2 * PSF_RADIUS), jnp.float32)
@@ -202,12 +210,7 @@
         smoothed = (
             smoothed + blur[:, tap_no, None, None] * blurred_rows[:, :, tap_no : tap_no + col_count]
         )
-    chooser = (blur_index[:, None] == lax.broadcasted_iota(jnp.int32, (1, NPSF), 1)).astype(
-        jnp.float32
-    )
-    sky_model = jnp.zeros((group_size, row_count, col_count), jnp.float32)
-    for kernel_no in range(NPSF):
-        sky_model = sky_model + chooser[:, kernel_no, None, None] * smoothed[kernel_no][None]
+    sky_model = jnp.take(smoothed, blur_index, axis=0)
     residual = jnp.where(bad_pixels == 1, 0.0, warped - sky_model)
     return (residual, median_sky)
 

time: 83.8 us -> 84 us (level)
  local copies, waits for them, and re-layouts: 6.13 us -> 7.3 us
  starting transfers between devices: 21.1 us -> 20 us
    all_to_all x1, waiting for transfers between devices: 4.55 us -> 6.25 us  [body(): lax.all_to_all(jnp.tile(band, (groups * sides, 1)), ('exp', 'col'), split...]
    ppermute x2 -> x1, waiting for transfers between devices: 1.49 us -> 0.01 us  [_col_halo(): arrived = lax.ppermute(packed, 'col', [(0, 1), (1, 0)])]
    ppermute x2 -> x1, starting transfers between devices: 2.5 us -> 1.28 us  [_col_halo(): arrived = lax.ppermute(packed, 'col', [(0, 1), (1, 0)])]
    concatenate x2 -> x1, other arithmetic: 2.52 us -> 2.42 us  [_col_halo(): return jnp.concatenate([low, block, high], axis=dim)]
  transfers between devices with their start and end apart: 8 -> 7, of which waited for: 7 -> 5; matrix products, arithmetic and copies ran while one was open for 4% -> 5% of each run, Pallas kernels for 0% -> 0%
where the time goes in v6:
time: 84 us; the launch traced here: 83.5 us
  waiting for transfers between devices  36.4 us (43%)
  starting transfers between devices  20 us (24%)
  other arithmetic  11 us (13%)
  local copies, waits for them, and re-layouts  7.3 us (9%)
  Pallas kernels  6.84 us (8%)
    all_to_all x1, waiting for transfers between devices, body(): lax.all_to_all(flagged, 'exp', split_axis=0, concat_axis=0, tiled=True)  20.9 us
    pallas_call x1, Pallas kernels, warp_and_flag(): pl.pallas_call(_warp_kernel, out_shape=(shape, banded), in_specs=[smem, s...  6.84 us
    ppermute x2, starting transfers between devices, _row_halo(): lax.ppermute(lax.slice_in_dim(block, size - width, None, axis=dim), 'row'...  6.49 us
    ppermute x2, waiting for transfers between devices, _row_halo(): lax.ppermute(lax.slice_in_dim(block, 0, width, axis=dim), 'row', backward)  6.39 us
    all_to_all x1, waiting for transfers between devices, body(): lax.all_to_all(jnp.tile(band, (groups * sides, 1)), ('exp', 'col'), split...  6.25 us
    all_to_all x1, starting transfers between devices, body(): lax.all_to_all(flagged, 'exp', split_axis=0, concat_axis=0, tiled=True)  4.59 us
    ppermute x2, starting transfers between devices, _row_halo(): lax.ppermute(lax.slice_in_dim(block, 0, width, axis=dim), 'row', backward)  4.27 us
    all_to_all x1, starting transfers between devices, body(): lax.all_to_all(jnp.tile(band, (groups * sides, 1)), ('exp', 'col'), split...  3.38 us
  transfers between devices with their start and end apart: 7, of which 5 were waited for; matrix products, arithmetic and copies ran while one was open for 5% of the time, Pallas kernels for 0%

profile of v6, /device:TPU:1, one launch (start us, length us, event | category | flops | bytes accessed | tf_op | source)
XLA Modules:
  0.0 83.5 jit_solution(15716398414287585145)
XLA Ops:
  0.6 1.4 %fusion.102 = (f32[16,11,512]{2,1,0:T(8,128)S(1)}, f32[16,11,512]{2,1,0:T(8,128)S(1)}) fusion(f32[16,32,512]{2,1,0:T(8,128)} %param.8), kind=kLoop, calls=%fused_computation.185 | loop fusion | bytes 1441792 | tf_op jit(solution)/shard_map/slice | solution.py:25
  2.1 4.5 %collective-permute-start = (f32[16,11,512]{2,1,0:T(8,128)S(1)}, f32[16,11,512]{2,1,0:T(8,128)S(1)}, u32[]{:S(2)}, u32[]{:S(2)}) collective-permute-start(f32[16,11,512]{2,1,0:T(8,128)S(1)} %get-tuple-element.65), channel_id=1, source_target_pairs={{0,2},{2,4},{4,6},{1,3},{3,5},{5,7},{8,10},{10,12},{12,14},{9,11},... | collective-permute-start | bytes 1081352 | tf_op jit(solution)/shard_map/ppermute | solution.py:25
  6.6 1.9 %collective-permute-start.1 = (f32[16,11,512]{2,1,0:T(8,128)S(1)}, f32[16,11,512]{2,1,0:T(8,128)S(1)}, u32[]{:S(2)}, u32[]{:S(2)}) collective-permute-start(f32[16,11,512]{2,1,0:T(8,128)S(1)} %get-tuple-element.66), channel_id=1, source_target_pairs={{2,0},{4,2},{6,4},{3,1},{5,3},{7,5},{10,8},{12,10},{14,12},{11,9},... | collective-permute-start | bytes 1081352 | tf_op jit(solution)/shard_map/ppermute | solution.py:26
  8.6 0.8 slice_bitcast_fusion.9
  9.6 0.2 fusion.37
  9.8 2.9 %collective-permute-done = f32[16,11,512]{2,1,0:T(8,128)S(1)} collective-permute-done((f32[16,11,512]{2,1,0:T(8,128)S(1)}, f32[16,11,512]{2,1,0:T(8,128)S(1)}, u32[]{:S(2)}, u32[]{:S(2)}) %collective-permute-start) | collective-permute-done | bytes 360480 | tf_op jit(solution)/shard_map/ppermute | solution.py:25
  12.7 4.4 %collective-permute-done.1 = f32[16,11,512]{2,1,0:T(8,128)S(1)} collective-permute-done((f32[16,11,512]{2,1,0:T(8,128)S(1)}, f32[16,11,512]{2,1,0:T(8,128)S(1)}, u32[]{:S(2)}, u32[]{:S(2)}) %collective-permute-start.1) | collective-permute-done | bytes 360480 | tf_op jit(solution)/shard_map/ppermute | solution.py:26
  17.1 0.2 fusion.19
  17.3 0.2 copy.16
  17.7 1.3 %collective-permute-start.2 = (f32[11,864]{1,0:T(8,128)S(1)}, f32[11,864]{1,0:T(8,128)S(1)}, u32[]{:S(2)}, u32[]{:S(2)}) collective-permute-start(f32[11,864]{1,0:T(8,128)S(1)} %reshape.87), channel_id=1, source_target_pairs={{0,1},{1,0},{2,3},{3,2},{4,5},{5,4},{6,7},{7,6},{8,9},{9,8},{10,11... | collective-permute-start | bytes 114056 | tf_op jit(solution)/shard_map/ppermute | solution.py:45
  19.0 0.6 add_bitcast_fusion
  19.5 0.7 reshape.85.row_weight
  20.2 0.6 reshape.86.col_weight
  21.0 0.3 copy.17
  21.3 0.3 copy.18
  21.6 2.4 %select_maximum_fusion.padded = f32[16,56,640]{2,1,0:T(8,128)} fusion(f32[16,54,11]{2,1,0:T(8,128)S(1)} %bitcast.39, f32[16,54,11]{2,1,0:T(8,128)S(1)} %bitcast.38, f32[16,11,512]{2,1,0:T(8,128)S(1)} %collective-permute-done.1, f32[16,32,512]{2,1,0:T(8,128)S(1)} %copy-done, f32[16,11,512]{2,1,0:T(8,128)S(1)} %collective-permute-done), kind=kLoop, calls=%fused_computation.7 | loop fusion | flops 9748480 | bytes 4139264 | tf_op jit(solution)/shard_map/concatenate | solution.py:50
  24.0 6.8 %shard_map.68 = (f32[16,32,512]{2,1,0:T(8,128)}, f32[4,16,8,512]{3,2,1,0:T(8,128)}) custom-call(s32[16]{0:T(128)} %get-tuple-element.95.row_shift, s32[16]{0:T(128)} %get-tuple-element.94.col_shift, f32[96]{0:T(128)} %reshape.85.row_weight, f32[96]{0:T(128)} %reshape.86.col_weight, f32[16,56,640]{2,1,0:T(8,128)} %select_maximum_fusion.padded, s32[16,32,512]{2,1,0:T(8,128)} %bad.1), custom_call_target="tpu_custom_call" | custom-call | tf_op jit(solution)/shard_map/pallas_call | solution.py:173
  30.9 4.6 %all-to-all-start = ((f32[4,16,8,512]{3,2,1,0:T(8,128)}), f32[4,16,8,512]{3,2,1,0:T(8,128)S(1)}, u32[]{:S(2)}, u32[]{:S(2)}) async-start(f32[4,16,8,512]{3,2,1,0:T(8,128)} %get-tuple-element.33), calls=%async_computation | async-start | bytes 2097152 | tf_op jit(solution)/shard_map/all_to_all | solution.py:185
  35.7 20.9 %all-to-all-done = f32[4,16,8,512]{3,2,1,0:T(8,128)S(1)} async-done(((f32[4,16,8,512]{3,2,1,0:T(8,128)}), f32[4,16,8,512]{3,2,1,0:T(8,128)S(1)}, u32[]{:S(2)}, u32[]{:S(2)}) %all-to-all-start) | async-done | bytes 1048608 | tf_op jit(solution)/shard_map/all_to_all | solution.py:185
  56.7 3.6 %while.13 = (s32[]{:T(128)}, f32[8,512]{1,0:T(8,128)S(1)}, f32[8,512]{1,0:T(8,128)S(1)}, f32[64,8,512]{2,1,0:T(8,128)S(1)}, f32[8,512]{1,0:T(8,128)S(1)}, /*index=5*/s32[]{:T(128)}, s32[]{:T(128)}) while((s32[]{:T(128)}, f32[8,512]{1,0:T(8,128)S(1)}, f32[8,512]{1,0:T(8,128)S(1)}, f32[64,8,512]{2,1,0:T(8,128)S(1)}, ...), condition=%wide.region_5.7_spmd.clone, body=%wide.region_3.6_spmd.clone.sunk | while | flops 1110019 | bytes 1302617 | solution.py:109
  60.5 0.7 tile.2
  61.2 3.4 %all-to-all-start.1 = ((f32[8,8,512]{2,1,0:T(8,128)}), f32[8,8,512]{2,1,0:T(8,128)S(1)}, u32[]{:S(2)}, u32[]{:S(2)}) async-start(f32[8,8,512]{2,1,0:T(8,128)} %tile.2), calls=%async_computation.1 | async-start | bytes 262144 | tf_op jit(solution)/shard_map/all_to_all | solution.py:190
  64.6 6.2 %all-to-all-done.1 = f32[8,8,512]{2,1,0:T(8,128)S(1)} async-done(((f32[8,8,512]{2,1,0:T(8,128)}), f32[8,8,512]{2,1,0:T(8,128)S(1)}, u32[]{:S(2)}, u32[]{:S(2)}) %all-to-all-start.1) | async-done | bytes 131104 | tf_op jit(solution)/shard_map/all_to_all | solution.py:190
  71.0 2.0 %collective-permute-start.3 = (f32[4,520]{1,0:T(4,128)S(1)}, f32[4,520]{1,0:T(4,128)S(1)}, u32[]{:S(2)}, u32[]{:S(2)}) collective-permute-start(f32[4,520]{1,0:T(4,128)S(1)} %get-tuple-element.67), channel_id=1, source_target_pairs={{0,2},{2,4},{4,6},{1,3},{3,5},{5,7},{8,10},{10,12},{12,14},{9,11},... | collective-permute-start | bytes 24968 | tf_op jit(solution)/shard_map/ppermute | solution.py:25
  73.0 2.3 %collective-permute-start.4 = (f32[4,520]{1,0:T(4,128)S(1)}, f32[4,520]{1,0:T(4,128)S(1)}, u32[]{:S(2)}, u32[]{:S(2)}) collective-permute-start(f32[4,520]{1,0:T(4,128)S(1)} %get-tuple-element.68), channel_id=1, source_target_pairs={{2,0},{4,2},{6,4},{3,1},{5,3},{7,5},{10,8},{12,10},{14,12},{11,9},... | collective-permute-start | bytes 24968 | tf_op jit(solution)/shard_map/ppermute | solution.py:26
  75.4 0.6 constant_dynamic-slice_fusion
  76.0 2.0 %collective-permute-done.4 = f32[4,520]{1,0:T(4,128)S(1)} collective-permute-done((f32[4,520]{1,0:T(4,128)S(1)}, f32[4,520]{1,0:T(4,128)S(1)}, u32[]{:S(2)}, u32[]{:S(2)}) %collective-permute-start.4) | collective-permute-done | bytes 8352 | tf_op jit(solution)/shard_map/ppermute | solution.py:26
  78.1 0.6 multiply_add_fusion
  78.6 1.3 %fusion.10 = f32[8,32,512]{2,1,0:T(8,128)S(1)} fusion(f32[8,32,520]{2,1,0:T(8,128)S(1)} %multiply_add_fusion, f32[8]{0:T(128)S(1)} %get-tuple-element.84, f32[8]{0:T(128)S(1)} %get-tuple-element.85, f32[8]{0:T(128)S(1)} %get-tuple-element.86, f32[8]{0:T(128)S(1)} %get-tuple-element.87, f32[8]{0:T(128)S(1)} %get-tuple-element.88, f32[8]{0:T(128)S(1)} %get-tuple-element.89, ...), kind=kLoop, calls=%fused_computation.25 | loop fusion | flops 2228224 | bytes 5243168 | tf_op jit(solution)/shard_map/add | solution.py:211
  79.9 0.6 gather_fusion
  80.5 0.6 copy-done.1
  81.1 2.4 %subtract_select_fusion = f32[16,32,512]{2,1,0:T(8,128)} fusion(f32[16,32,512]{2,1,0:T(8,128)} %get-tuple-element.32, f32[16,32,512]{2,1,0:T(8,128)S(1)} %gather_fusion, s32[16,32,512]{2,1,0:T(8,128)S(1)} %copy-done.1, pred[16]{0:T(512)(128)(4,1)S(1)} %compare_and_fusion), kind=kLoop, calls=%fused_computation.21 | loop fusion | flops 1048576 | bytes 4194320 | tf_op jit(solution)/shard_map/jit(_where)/select_n | solution.py:214
  (112 shorter events, 4.4 us)
Async XLA Ops:
  0.6 16.5 %copy-start = (f32[16,32,512]{2,1,0:T(8,128)S(1)}, f32[16,32,512]{2,1,0:T(8,128)}, u32[]{:S(2)}) copy-start(f32[16,32,512]{2,1,0:T(8,128)} %param.8) | copy-start | bytes 3145732
  2.1 16.9 %copy-start.2 = (s32[16,2]{0,1:T(2,128)S(1)}, s32[16,2]{0,1:T(2,128)}, u32[]{:S(2)}) copy-start(s32[16,2]{0,1:T(2,128)} %param.10) | copy-start | bytes 388
  2.1 10.6 %collective-permute-start = (f32[16,11,512]{2,1,0:T(8,128)S(1)}, f32[16,11,512]{2,1,0:T(8,128)S(1)}, u32[]{:S(2)}, u32[]{:S(2)}) collective-permute-start(f32[16,11,512]{2,1,0:T(8,128)S(1)} %get-tuple-element.65), channel_id=1, source_target_pairs={{0,2},{2,4},{4,6},{1,3},{3,5},{5,7},{8,10},{10,12},{12,14},{9,11},... | collective-permute-start | bytes 1081352 | tf_op jit(solution)/shard_map/ppermute | solution.py:25
  6.6 10.5 %collective-permute-start.1 = (f32[16,11,512]{2,1,0:T(8,128)S(1)}, f32[16,11,512]{2,1,0:T(8,128)S(1)}, u32[]{:S(2)}, u32[]{:S(2)}) collective-permute-start(f32[16,11,512]{2,1,0:T(8,128)S(1)} %get-tuple-element.66), channel_id=1, source_target_pairs={{2,0},{4,2},{6,4},{3,1},{5,3},{7,5},{10,8},{12,10},{14,12},{11,9},... | collective-permute-start | bytes 1081352 | tf_op jit(solution)/shard_map/ppermute | solution.py:26
  17.7 3.2 %collective-permute-start.2 = (f32[11,864]{1,0:T(8,128)S(1)}, f32[11,864]{1,0:T(8,128)S(1)}, u32[]{:S(2)}, u32[]{:S(2)}) collective-permute-start(f32[11,864]{1,0:T(8,128)S(1)} %reshape.87), channel_id=1, source_target_pairs={{0,1},{1,0},{2,3},{3,2},{4,5},{5,4},{6,7},{7,6},{8,9},{9,8},{10,11... | collective-permute-start | bytes 114056 | tf_op jit(solution)/shard_map/ppermute | solution.py:45
  24.0 11.6 %copy-start.3 = (s32[16]{0:T(128)S(1)}, s32[16]{0:T(128)}, u32[]{:S(2)}) copy-start(s32[16]{0:T(128)} %param.12) | copy-start | bytes 196
  30.9 25.7 %all-to-all-start = ((f32[4,16,8,512]{3,2,1,0:T(8,128)}), f32[4,16,8,512]{3,2,1,0:T(8,128)S(1)}, u32[]{:S(2)}, u32[]{:S(2)}) async-start(f32[4,16,8,512]{3,2,1,0:T(8,128)} %get-tuple-element.33), calls=%async_computation | async-start | bytes 2097152 | tf_op jit(solution)/shard_map/all_to_all | solution.py:185
  61.2 9.7 %all-to-all-start.1 = ((f32[8,8,512]{2,1,0:T(8,128)}), f32[8,8,512]{2,1,0:T(8,128)S(1)}, u32[]{:S(2)}, u32[]{:S(2)}) async-start(f32[8,8,512]{2,1,0:T(8,128)} %tile.2), calls=%async_computation.1 | async-start | bytes 262144 | tf_op jit(solution)/shard_map/all_to_all | solution.py:190
  71.0 5.0 %collective-permute-start.3 = (f32[4,520]{1,0:T(4,128)S(1)}, f32[4,520]{1,0:T(4,128)S(1)}, u32[]{:S(2)}, u32[]{:S(2)}) collective-permute-start(f32[4,520]{1,0:T(4,128)S(1)} %get-tuple-element.67), channel_id=1, source_target_pairs={{0,2},{2,4},{4,6},{1,3},{3,5},{5,7},{8,10},{10,12},{12,14},{9,11},... | collective-permute-start | bytes 24968 | tf_op jit(solution)/shard_map/ppermute | solution.py:25
  73.0 5.0 %collective-permute-start.4 = (f32[4,520]{1,0:T(4,128)S(1)}, f32[4,520]{1,0:T(4,128)S(1)}, u32[]{:S(2)}, u32[]{:S(2)}) collective-permute-start(f32[4,520]{1,0:T(4,128)S(1)} %get-tuple-element.68), channel_id=1, source_target_pairs={{2,0},{4,2},{6,4},{3,1},{5,3},{7,5},{10,8},{12,10},{14,12},{11,9},... | collective-permute-start | bytes 24968 | tf_op jit(solution)/shard_map/ppermute | solution.py:26
  79.9 1.2 %copy-start.1 = (s32[16,32,512]{2,1,0:T(8,128)S(1)}, s32[16,32,512]{2,1,0:T(8,128)}, u32[]{:S(2)}) copy-start(s32[16,32,512]{2,1,0:T(8,128)} %bad.1) | copy-start | bytes 3145732

commit v7 on v6

--- a/solution.py
+++ b/solution.py
@@ -181,8 +181,16 @@
 def body(exposures, bad_pixels, offsets, warp_index, blur_index):
     group_size, row_count, col_count = exposures.shape
     padded = extended(exposures, 1, 2, HALO)
-    warped, flagged = warp_and_flag(padded, bad_pixels, offsets, warp_index)
-    gathered = lax.all_to_all(flagged, "exp", split_axis=0, concat_axis=0, tiled=True)
+    half = group_size // 2
+    parts = []
+    for lo, hi in ((0, half), (half, group_size)):
+        part_warped, part_flagged = warp_and_flag(
+            padded[lo:hi], bad_pixels[lo:hi], offsets[lo:hi], warp_index[lo:hi]
+        )
+        arrived = lax.all_to_all(part_flagged, "exp", split_axis=0, concat_axis=0, tiled=True)
+        parts.append((part_warped, arrived))
+    warped = jnp.concatenate([w for w, _ in parts], axis=0)
+    gathered = jnp.concatenate([a for _, a in parts], axis=1)
     band = stack_median(gathered.reshape((-1,) + gathered.shape[2:]))
     groups = lax.axis_size("exp")
     sides = lax.axis_size("col")
@@ -210,7 +218,12 @@
         smoothed = (
             smoothed + blur[:, tap_no, None, None] * blurred_rows[:, :, tap_no : tap_no + col_count]
         )
-    sky_model = jnp.take(smoothed, blur_index, axis=0)
+    chooser = (blur_index[:, None] == lax.broadcasted_iota(jnp.int32, (1, NPSF), 1)).astype(
+        jnp.float32
+    )
+    sky_model = jnp.zeros((group_size, row_count, col_count), jnp.float32)
+    for kernel_no in range(NPSF):
+        sky_model = sky_model + chooser[:, kernel_no, None, None] * smoothed[kernel_no][None]
     residual = jnp.where(bad_pixels == 1, 0.0, warped - sky_model)
     return (residual, median_sky)
 

time: 84 us -> 93.9 us (1.12)
  local copies, waits for them, and re-layouts: 7.3 us -> 14.5 us
  starting transfers between devices: 20 us -> 25.9 us
  waiting for transfers between devices: 36.4 us -> 31.2 us
  Pallas kernels: 6.84 us -> 8.42 us
    all_to_all x1 -> x2, waiting for transfers between devices: 20.9 us -> 15.9 us  [body(): lax.all_to_all(part_flagged, 'exp', split_axis=0, concat_axis=0, tiled=True)]
    all_to_all x1 -> x2, starting transfers between devices: 4.59 us -> 8.06 us  [body(): lax.all_to_all(part_flagged, 'exp', split_axis=0, concat_axis=0, tiled=True)]
    ppermute x2, starting transfers between devices: 6.49 us -> 9.37 us  [_row_halo(): lax.ppermute(lax.slice_in_dim(block, size - width, None, axis=dim), 'row'...]
    pad x0 -> x2, local copies, waits for them, and re-layouts: none -> 2.2 us  [warp_and_flag(): jnp.pad(padded, ((0, 0), (0, rows - padded.shape[1]), (0, lanes - padded....]
    pallas_call x1 -> x2, Pallas kernels: 6.84 us -> 8.42 us  [warp_and_flag(): pl.pallas_call(_warp_kernel, out_shape=(shape, banded), in_specs=[smem, s...]
    slice x0 -> x2, local copies, waits for them, and re-layouts: none -> 1.23 us  [the longest x1 1.08 us: body(): bad_pixels[lo:hi]]
    slice x2, local copies, waits for them, and re-layouts: 1.5 us -> 2.52 us  [_row_halo(): lax.slice_in_dim(block, size - width, None, axis=dim)]
    transpose x1, local copies, waits for them, and re-layouts: 0.23 us -> 1.24 us  [_col_halo(): outgoing = jnp.moveaxis(jnp.where(first, right_edge, left_edge), dim, 0)]
  transfers between devices with their start and end apart: 7 -> 8, of which waited for: 5 -> 6; matrix products, arithmetic and copies ran while one was open for 5% -> 8% of each run, Pallas kernels for 0% -> 5%
where the time goes in v7:
time: 93.9 us; the launch traced here: 93.4 us
  waiting for transfers between devices  31.2 us (33%)
  starting transfers between devices  25.9 us (28%)
  local copies, waits for them, and re-layouts  14.5 us (15%)
  other arithmetic  11 us (12%)
  Pallas kernels  8.42 us (9%)
    all_to_all x2, waiting for transfers between devices, body(): lax.all_to_all(part_flagged, 'exp', split_axis=0, concat_axis=0, tiled=True)  15.9 us
    ppermute x2, starting transfers between devices, _row_halo(): lax.ppermute(lax.slice_in_dim(block, size - width, None, axis=dim), 'row'...  9.37 us
    pallas_call x2, Pallas kernels, warp_and_flag(): pl.pallas_call(_warp_kernel, out_shape=(shape, banded), in_specs=[smem, s...  8.42 us
    all_to_all x2, starting transfers between devices, body(): lax.all_to_all(part_flagged, 'exp', split_axis=0, concat_axis=0, tiled=True)  8.06 us
    ppermute x2, waiting for transfers between devices, _row_halo(): lax.ppermute(lax.slice_in_dim(block, 0, width, axis=dim), 'row', backward)  6.71 us
    all_to_all x1, waiting for transfers between devices, body(): lax.all_to_all(jnp.tile(band, (groups * sides, 1)), ('exp', 'col'), split...  6.59 us
    ppermute x2, starting transfers between devices, _row_halo(): lax.ppermute(lax.slice_in_dim(block, 0, width, axis=dim), 'row', backward)  3.84 us
    all_to_all x1, starting transfers between devices, body(): lax.all_to_all(jnp.tile(band, (groups * sides, 1)), ('exp', 'col'), split...  3.38 us
  transfers between devices with their start and end apart: 8, of which 6 were waited for; matrix products, arithmetic and copies ran while one was open for 8% of the time, Pallas kernels for 5%

profile of v7, /device:TPU:1, one launch (start us, length us, event | category | flops | bytes accessed | tf_op | source)
XLA Modules:
  0.0 93.4 jit_solution(15848015602540163614)
XLA Ops:
  0.6 2.4 %fusion.125 = (f32[16,11,512]{2,1,0:T(8,128)}, f32[16,11,512]{2,1,0:T(8,128)}) fusion(f32[16,32,512]{2,1,0:T(8,128)} %param.8), kind=kLoop, calls=%fused_computation.226 | loop fusion | bytes 1441792 | tf_op jit(solution)/shard_map/slice | solution.py:25
  3.1 4.5 %collective-permute-start = (f32[16,11,512]{2,1,0:T(8,128)}, f32[16,11,512]{2,1,0:T(8,128)S(1)}, u32[]{:S(2)}, u32[]{:S(2)}) collective-permute-start(f32[16,11,512]{2,1,0:T(8,128)} %get-tuple-element.73), channel_id=1, source_target_pairs={{0,2},{2,4},{4,6},{1,3},{3,5},{5,7},{8,10},{10,12},{12,14},{9,11},... | collective-permute-start | bytes 1081352 | tf_op jit(solution)/shard_map/ppermute | solution.py:25
  7.6 1.9 %collective-permute-start.1 = (f32[16,11,512]{2,1,0:T(8,128)}, f32[16,11,512]{2,1,0:T(8,128)S(1)}, u32[]{:S(2)}, u32[]{:S(2)}) collective-permute-start(f32[16,11,512]{2,1,0:T(8,128)} %get-tuple-element.74), channel_id=1, source_target_pairs={{2,0},{4,2},{6,4},{3,1},{5,3},{7,5},{10,8},{12,10},{14,12},{11,9},... | collective-permute-start | bytes 1081352 | tf_op jit(solution)/shard_map/ppermute | solution.py:26
  9.6 0.9 slice_bitcast_fusion.27
  11.0 1.1 %fusion.124 = (s32[8,32,512]{2,1,0:T(8,128)}, s32[8,32,512]{2,1,0:T(8,128)}) fusion(s32[16,32,512]{2,1,0:T(8,128)S(1)} %copy-done.1), kind=kLoop, calls=%fused_computation.225 | loop fusion | bytes 2097152 | tf_op jit(solution)/shard_map/slice | solution.py:188
  12.1 1.9 %collective-permute-done = f32[16,11,512]{2,1,0:T(8,128)S(1)} collective-permute-done((f32[16,11,512]{2,1,0:T(8,128)}, f32[16,11,512]{2,1,0:T(8,128)S(1)}, u32[]{:S(2)}, u32[]{:S(2)}) %collective-permute-start) | collective-permute-done | bytes 360480 | tf_op jit(solution)/shard_map/ppermute | solution.py:25
  14.0 4.3 %collective-permute-done.1 = f32[16,11,512]{2,1,0:T(8,128)S(1)} collective-permute-done((f32[16,11,512]{2,1,0:T(8,128)}, f32[16,11,512]{2,1,0:T(8,128)S(1)}, u32[]{:S(2)}, u32[]{:S(2)}) %collective-permute-start.1) | collective-permute-done | bytes 360480 | tf_op jit(solution)/shard_map/ppermute | solution.py:26
  18.3 1.0 %fusion.11 = f32[11,16,54]{0,2,1:T(8,128)} fusion(f32[16,11,512]{2,1,0:T(8,128)S(1)} %collective-permute-done.1, f32[16,32,512]{2,1,0:T(8,128)S(1)} %copy-done, f32[16,11,512]{2,1,0:T(8,128)S(1)} %collective-permute-done, pred[]{:T(512)S(6)} %eq.104), kind=kLoop, calls=%fused_computation.31 | loop fusion | flops 47520 | bytes 1807489 | tf_op jit(solution)/shard_map/transpose | solution.py:42
  19.3 1.2 %copy.10 = f32[11,16,54]{2,1,0:T(8,128)S(1)} copy(f32[11,16,54]{0,2,1:T(8,128)} %fusion.11) | data formatting | bytes 76032 | tf_op jit(solution)/shard_map/transpose | solution.py:42
  20.7 1.3 %collective-permute-start.2 = (f32[11,864]{1,0:T(8,128)S(1)}, f32[11,864]{1,0:T(8,128)S(1)}, u32[]{:S(2)}, u32[]{:S(2)}) collective-permute-start(f32[11,864]{1,0:T(8,128)S(1)} %reshape.101), channel_id=1, source_target_pairs={{0,1},{1,0},{2,3},{3,2},{4,5},{5,4},{6,7},{7,6},{8,9},{9,8},{10,11... | collective-permute-start | bytes 114056 | tf_op jit(solution)/shard_map/ppermute | solution.py:45
  23.9 1.0 %copy.11 = f32[11,16,54]{0,2,1:T(8,128)} copy(f32[11,16,54]{2,1,0:T(8,128)S(1)} %select_n.73) | data formatting | bytes 76032 | tf_op jit(solution)/shard_map/jit(_where)/select_n | solution.py:48
  25.0 1.0 %copy.12 = f32[11,16,54]{0,2,1:T(8,128)} copy(f32[11,16,54]{2,1,0:T(8,128)S(1)} %select_n.76) | data formatting | bytes 76032 | tf_op jit(solution)/shard_map/jit(_where)/select_n | solution.py:49
  26.0 2.2 %pad_maximum_fusion = f32[16,54,534]{2,1,0:T(8,128)S(1)} fusion(f32[16,54,11]{2,1,0:T(8,128)} %bitcast.79, f32[16,11,512]{2,1,0:T(8,128)S(1)} %collective-permute-done.1, f32[16,32,512]{2,1,0:T(8,128)S(1)} %copy-done, f32[16,11,512]{2,1,0:T(8,128)S(1)} %collective-permute-done, f32[16,54,11]{2,1,0:T(8,128)} %bitcast.78), kind=kLoop, calls=%fused_computation.6 | loop fusion | flops 1845504 | bytes 3691008 | tf_op jit(solution)/shard_map/concatenate | solution.py:50
  28.4 1.1 %pad.11.padded = f32[8,56,640]{2,1,0:T(8,128)} pad(f32[8,54,534]{2,1,0:T(8,128)S(1)} %get-tuple-element.69, f32[]{:T(128)} %constant.12.clone.1), padding=0_0x0_2x0_106 | pad | bytes 2069636 | tf_op jit(solution)/shard_map/jit(_pad)/pad | solution.py:163
  29.5 4.2 %shard_map.68 = (f32[8,32,512]{2,1,0:T(8,128)}, f32[4,8,8,512]{3,2,1,0:T(8,128)}) custom-call(s32[8]{0:T(128)} %get-tuple-element.121.row_shift, s32[8]{0:T(128)} %get-tuple-element.120.col_shift, f32[48]{0:T(128)} %reshape.99.row_weight, f32[48]{0:T(128)} %reshape.100.col_weight, f32[8,56,640]{2,1,0:T(8,128)} %pad.11.padded, ...), custom_call_target="tpu_custom_call" | custom-call | tf_op jit(solution)/shard_map/pallas_call | solution.py:173
  33.7 4.6 %all-to-all-start = ((f32[4,8,8,512]{3,2,1,0:T(8,128)}), f32[4,8,8,512]{3,2,1,0:T(8,128)S(1)}, u32[]{:S(2)}, u32[]{:S(2)}) async-start(f32[4,8,8,512]{3,2,1,0:T(8,128)} %get-tuple-element.36), calls=%async_computation | async-start | bytes 1048576 | tf_op jit(solution)/shard_map/all_to_all | solution.py:190
  39.3 0.6 reshape.103.col_weight
  39.9 1.1 %pad.12.padded = f32[8,56,640]{2,1,0:T(8,128)} pad(f32[8,54,534]{2,1,0:T(8,128)S(1)} %get-tuple-element.70, f32[]{:T(128)} %constant.12.clone.1), padding=0_0x0_2x0_106 | pad | bytes 2069636 | tf_op jit(solution)/shard_map/jit(_pad)/pad | solution.py:163
  41.0 4.2 %shard_map.69 = (f32[8,32,512]{2,1,0:T(8,128)}, f32[4,8,8,512]{3,2,1,0:T(8,128)}) custom-call(s32[8]{0:T(128)} %get-tuple-element.123.row_shift, s32[8]{0:T(128)} %get-tuple-element.122.col_shift, f32[48]{0:T(128)} %reshape.102.row_weight, f32[48]{0:T(128)} %reshape.103.col_weight, f32[8,56,640]{2,1,0:T(8,128)} %pad.12.padded, ...), custom_call_target="tpu_custom_call" | custom-call | tf_op jit(solution)/shard_map/pallas_call | solution.py:173
  45.3 3.0 %all-to-all-done = f32[4,8,8,512]{3,2,1,0:T(8,128)S(1)} async-done(((f32[4,8,8,512]{3,2,1,0:T(8,128)}), f32[4,8,8,512]{3,2,1,0:T(8,128)S(1)}, u32[]{:S(2)}, u32[]{:S(2)}) %all-to-all-start) | async-done | bytes 524320 | tf_op jit(solution)/shard_map/all_to_all | solution.py:190
  48.3 3.5 %all-to-all-start.1 = ((f32[4,8,8,512]{3,2,1,0:T(8,128)}), f32[4,8,8,512]{3,2,1,0:T(8,128)S(1)}, u32[]{:S(2)}, u32[]{:S(2)}) async-start(f32[4,8,8,512]{3,2,1,0:T(8,128)} %get-tuple-element.37), calls=%async_computation.1 | async-start | bytes 1048576 | tf_op jit(solution)/shard_map/all_to_all | solution.py:190
  52.0 12.9 %all-to-all-done.1 = f32[4,8,8,512]{3,2,1,0:T(8,128)S(1)} async-done(((f32[4,8,8,512]{3,2,1,0:T(8,128)}), f32[4,8,8,512]{3,2,1,0:T(8,128)S(1)}, u32[]{:S(2)}, u32[]{:S(2)}) %all-to-all-start.1) | async-done | bytes 524320 | tf_op jit(solution)/shard_map/all_to_all | solution.py:190
  65.1 3.6 %while.13 = (s32[]{:T(128)}, f32[8,512]{1,0:T(8,128)S(1)}, f32[8,512]{1,0:T(8,128)S(1)}, f32[64,8,512]{2,1,0:T(8,128)S(1)}, f32[8,512]{1,0:T(8,128)S(1)}, /*index=5*/s32[]{:T(128)}, s32[]{:T(128)}) while((s32[]{:T(128)}, f32[8,512]{1,0:T(8,128)S(1)}, f32[8,512]{1,0:T(8,128)S(1)}, f32[64,8,512]{2,1,0:T(8,128)S(1)}, ...), condition=%wide.region_5.7_spmd.clone, body=%wide.region_3.6_spmd.clone.sunk | while | flops 1110019 | bytes 1302617 | solution.py:109
  68.9 0.7 tile.2
  69.5 3.4 %all-to-all-start.2 = ((f32[8,8,512]{2,1,0:T(8,128)}), f32[8,8,512]{2,1,0:T(8,128)S(1)}, u32[]{:S(2)}, u32[]{:S(2)}) async-start(f32[8,8,512]{2,1,0:T(8,128)} %tile.2), calls=%async_computation.2 | async-start | bytes 262144 | tf_op jit(solution)/shard_map/all_to_all | solution.py:198
  73.0 6.6 %all-to-all-done.2 = f32[8,8,512]{2,1,0:T(8,128)S(1)} async-done(((f32[8,8,512]{2,1,0:T(8,128)}), f32[8,8,512]{2,1,0:T(8,128)S(1)}, u32[]{:S(2)}, u32[]{:S(2)}) %all-to-all-start.2) | async-done | bytes 131104 | tf_op jit(solution)/shard_map/all_to_all | solution.py:198
  79.7 4.9 %collective-permute-start.3 = (f32[4,520]{1,0:T(4,128)S(1)}, f32[4,520]{1,0:T(4,128)S(1)}, u32[]{:S(2)}, u32[]{:S(2)}) collective-permute-start(f32[4,520]{1,0:T(4,128)S(1)} %get-tuple-element.83), channel_id=1, source_target_pairs={{0,2},{2,4},{4,6},{1,3},{3,5},{5,7},{8,10},{10,12},{12,14},{9,11},... | collective-permute-start | bytes 24968 | tf_op jit(solution)/shard_map/ppermute | solution.py:25
  84.6 1.9 %collective-permute-start.4 = (f32[4,520]{1,0:T(4,128)S(1)}, f32[4,520]{1,0:T(4,128)S(1)}, u32[]{:S(2)}, u32[]{:S(2)}) collective-permute-start(f32[4,520]{1,0:T(4,128)S(1)} %get-tuple-element.84), channel_id=1, source_target_pairs={{2,0},{4,2},{6,4},{3,1},{5,3},{7,5},{10,8},{12,10},{14,12},{11,9},... | collective-permute-start | bytes 24968 | tf_op jit(solution)/shard_map/ppermute | solution.py:26
  86.5 0.6 constant_dynamic-slice_fusion
  87.2 2.4 %collective-permute-done.4 = f32[4,520]{1,0:T(4,128)S(1)} collective-permute-done((f32[4,520]{1,0:T(4,128)S(1)}, f32[4,520]{1,0:T(4,128)S(1)}, u32[]{:S(2)}, u32[]{:S(2)}) %collective-permute-start.4) | collective-permute-done | bytes 8352 | tf_op jit(solution)/shard_map/ppermute | solution.py:26
  90.2 1.3 %fusion.2 = f32[8,32,512]{2,1,0:T(8,128)S(1)} fusion(f32[8,32,520]{2,1,0:T(8,128)S(1)} %multiply_add_fusion, f32[8]{0:T(128)S(1)} %get-tuple-element.100, f32[8]{0:T(128)S(1)} %get-tuple-element.101, f32[8]{0:T(128)S(1)} %get-tuple-element.102, f32[8]{0:T(128)S(1)} %get-tuple-element.103, f32[8]{0:T(128)S(1)} %get-tuple-element.104, ...), kind=kLoop, calls=%fused_computation.13 | loop fusion | flops 2228224 | bytes 5243168 | tf_op jit(solution)/shard_map/add | solution.py:219
  91.6 1.8 %fusion.1 = f32[16,32,512]{2,1,0:T(8,128)} fusion(f32[8,32,512]{2,1,0:T(8,128)S(1)} %copy-done.3, f32[8,32,512]{2,1,0:T(8,128)S(1)} %copy-done.2, s32[16,32,512]{2,1,0:T(8,128)S(1)} %copy-done.1, f32[32,512]{1,0:T(8,128)S(1)} %get-tuple-element.76, f32[16]{0:T(128)S(1)} %get-tuple-element.109, f32[32,512]{1,0:T(8,128)S(1)} %get-tuple-element.77, ...), kind=kLoop, calls=%fused_computation.9 | loop fusion | flops 4980736 | bytes 3670528 | tf_op jit(solution)/shard_map/jit(_where)/select_n | solution.py:227
  (128 shorter events, 8.2 us)
Async XLA Ops:
  0.6 17.7 %copy-start = (f32[16,32,512]{2,1,0:T(8,128)S(1)}, f32[16,32,512]{2,1,0:T(8,128)}, u32[]{:S(2)}) copy-start(f32[16,32,512]{2,1,0:T(8,128)} %param.8) | copy-start | bytes 3145732
  0.6 10.3 %copy-start.1 = (s32[16,32,512]{2,1,0:T(8,128)S(1)}, s32[16,32,512]{2,1,0:T(8,128)}, u32[]{:S(2)}) copy-start(s32[16,32,512]{2,1,0:T(8,128)} %param.9) | copy-start | bytes 3145732
  3.1 10.9 %collective-permute-start = (f32[16,11,512]{2,1,0:T(8,128)}, f32[16,11,512]{2,1,0:T(8,128)S(1)}, u32[]{:S(2)}, u32[]{:S(2)}) collective-permute-start(f32[16,11,512]{2,1,0:T(8,128)} %get-tuple-element.73), channel_id=1, source_target_pairs={{0,2},{2,4},{4,6},{1,3},{3,5},{5,7},{8,10},{10,12},{12,14},{9,11},... | collective-permute-start | bytes 1081352 | tf_op jit(solution)/shard_map/ppermute | solution.py:25
  7.6 10.7 %collective-permute-start.1 = (f32[16,11,512]{2,1,0:T(8,128)}, f32[16,11,512]{2,1,0:T(8,128)S(1)}, u32[]{:S(2)}, u32[]{:S(2)}) collective-permute-start(f32[16,11,512]{2,1,0:T(8,128)} %get-tuple-element.74), channel_id=1, source_target_pairs={{2,0},{4,2},{6,4},{3,1},{5,3},{7,5},{10,8},{12,10},{14,12},{11,9},... | collective-permute-start | bytes 1081352 | tf_op jit(solution)/shard_map/ppermute | solution.py:26
  11.0 11.0 %copy-start.4 = (s32[16,2]{0,1:T(2,128)S(1)}, s32[16,2]{0,1:T(2,128)}, u32[]{:S(2)}) copy-start(s32[16,2]{0,1:T(2,128)} %param.10) | copy-start | bytes 388
  20.7 3.1 %collective-permute-start.2 = (f32[11,864]{1,0:T(8,128)S(1)}, f32[11,864]{1,0:T(8,128)S(1)}, u32[]{:S(2)}, u32[]{:S(2)}) collective-permute-start(f32[11,864]{1,0:T(8,128)S(1)} %reshape.101), channel_id=1, source_target_pairs={{0,1},{1,0},{2,3},{3,2},{4,5},{5,4},{6,7},{7,6},{8,9},{9,8},{10,11... | collective-permute-start | bytes 114056 | tf_op jit(solution)/shard_map/ppermute | solution.py:45
  33.7 14.6 %all-to-all-start = ((f32[4,8,8,512]{3,2,1,0:T(8,128)}), f32[4,8,8,512]{3,2,1,0:T(8,128)S(1)}, u32[]{:S(2)}, u32[]{:S(2)}) async-start(f32[4,8,8,512]{3,2,1,0:T(8,128)} %get-tuple-element.36), calls=%async_computation | async-start | bytes 1048576 | tf_op jit(solution)/shard_map/all_to_all | solution.py:190
  39.9 11.9 %copy-start.5 = (s32[16]{0:T(128)S(1)}, s32[16]{0:T(128)}, u32[]{:S(2)}) copy-start(s32[16]{0:T(128)} %param.12) | copy-start | bytes 196
  48.3 16.6 %all-to-all-start.1 = ((f32[4,8,8,512]{3,2,1,0:T(8,128)}), f32[4,8,8,512]{3,2,1,0:T(8,128)S(1)}, u32[]{:S(2)}, u32[]{:S(2)}) async-start(f32[4,8,8,512]{3,2,1,0:T(8,128)} %get-tuple-element.37), calls=%async_computation.1 | async-start | bytes 1048576 | tf_op jit(solution)/shard_map/all_to_all | solution.py:190
  69.5 10.0 %all-to-all-start.2 = ((f32[8,8,512]{2,1,0:T(8,128)}), f32[8,8,512]{2,1,0:T(8,128)S(1)}, u32[]{:S(2)}, u32[]{:S(2)}) async-start(f32[8,8,512]{2,1,0:T(8,128)} %tile.2), calls=%async_computation.2 | async-start | bytes 262144 | tf_op jit(solution)/shard_map/all_to_all | solution.py:198
  79.7 7.4 %collective-permute-start.3 = (f32[4,520]{1,0:T(4,128)S(1)}, f32[4,520]{1,0:T(4,128)S(1)}, u32[]{:S(2)}, u32[]{:S(2)}) collective-permute-start(f32[4,520]{1,0:T(4,128)S(1)} %get-tuple-element.83), channel_id=1, source_target_pairs={{0,2},{2,4},{4,6},{1,3},{3,5},{5,7},{8,10},{10,12},{12,14},{9,11},... | collective-permute-start | bytes 24968 | tf_op jit(solution)/shard_map/ppermute | solution.py:25
  84.6 5.0 %collective-permute-start.4 = (f32[4,520]{1,0:T(4,128)S(1)}, f32[4,520]{1,0:T(4,128)S(1)}, u32[]{:S(2)}, u32[]{:S(2)}) collective-permute-start(f32[4,520]{1,0:T(4,128)S(1)} %get-tuple-element.84), channel_id=1, source_target_pairs={{2,0},{4,2},{6,4},{3,1},{5,3},{7,5},{10,8},{12,10},{14,12},{11,9},... | collective-permute-start | bytes 24968 | tf_op jit(solution)/shard_map/ppermute | solution.py:26
  90.2 1.3 %copy-start.2 = (f32[8,32,512]{2,1,0:T(8,128)S(1)}, f32[8,32,512]{2,1,0:T(8,128)}, u32[]{:S(2)}) copy-start(f32[8,32,512]{2,1,0:T(8,128)} %get-tuple-element.34) | copy-start | bytes 1572868
  90.2 1.3 %copy-start.3 = (f32[8,32,512]{2,1,0:T(8,128)S(1)}, f32[8,32,512]{2,1,0:T(8,128)}, u32[]{:S(2)}) copy-start(f32[8,32,512]{2,1,0:T(8,128)} %get-tuple-element.35) | copy-start | bytes 1572868

commit v8 on v6

--- a/solution.py
+++ b/solution.py
@@ -210,7 +210,12 @@
         smoothed = (
             smoothed + blur[:, tap_no, None, None] * blurred_rows[:, :, tap_no : tap_no + col_count]
         )
-    sky_model = jnp.take(smoothed, blur_index, axis=0)
+    chooser = (blur_index[:, None] == lax.broadcasted_iota(jnp.int32, (1, NPSF), 1)).astype(
+        jnp.float32
+    )
+    sky_model = jnp.zeros((group_size, row_count, col_count), jnp.float32)
+    for kernel_no in range(NPSF):
+        sky_model = sky_model + chooser[:, kernel_no, None, None] * smoothed[kernel_no][None]
     residual = jnp.where(bad_pixels == 1, 0.0, warped - sky_model)
     return (residual, median_sky)
 

time: 84 us -> 82.4 us (0.981)
  local copies, waits for them, and re-layouts: 7.3 us -> 6.18 us
  transfers between devices with their start and end apart: 7 -> 7, of which waited for: 5 -> 6; matrix products, arithmetic and copies ran while one was open for 5% -> 5% of each run, Pallas kernels for 0% -> 0%
where the time goes in v8:
time: 82.4 us; the launch traced here: 82 us
  waiting for transfers between devices  36.6 us (44%)
  starting transfers between devices  20 us (24%)
  other arithmetic  10.3 us (12%)
  Pallas kernels  6.84 us (8%)
  local copies, waits for them, and re-layouts  6.18 us (7%)
  between operations  0.84 us (1%)
    all_to_all x1, waiting for transfers between devices, body(): lax.all_to_all(flagged, 'exp', split_axis=0, concat_axis=0, tiled=True)  21 us
    pallas_call x1, Pallas kernels, warp_and_flag(): pl.pallas_call(_warp_kernel, out_shape=(shape, banded), in_specs=[smem, s...  6.84 us
    ppermute x2, starting transfers between devices, _row_halo(): lax.ppermute(lax.slice_in_dim(block, size - width, None, axis=dim), 'row'...  6.44 us
    ppermute x2, waiting for transfers between devices, _row_halo(): lax.ppermute(lax.slice_in_dim(block, 0, width, axis=dim), 'row', backward)  6.33 us
    all_to_all x1, waiting for transfers between devices, body(): lax.all_to_all(jnp.tile(band, (groups * sides, 1)), ('exp', 'col'), split...  6.31 us
    all_to_all x1, starting transfers between devices, body(): lax.all_to_all(flagged, 'exp', split_axis=0, concat_axis=0, tiled=True)  4.59 us
    ppermute x2, starting transfers between devices, _row_halo(): lax.ppermute(lax.slice_in_dim(block, 0, width, axis=dim), 'row', backward)  4.32 us
    all_to_all x1, starting transfers between devices, body(): lax.all_to_all(jnp.tile(band, (groups * sides, 1)), ('exp', 'col'), split...  3.38 us
  transfers between devices with their start and end apart: 7, of which 6 were waited for; matrix products, arithmetic and copies ran while one was open for 5% of the time, Pallas kernels for 0%

profile of v8, /device:TPU:1, one launch (start us, length us, event | category | flops | bytes accessed | tf_op | source)
XLA Modules:
  0.0 82.0 jit_solution(15641596788251396345)
XLA Ops:
  0.6 1.4 %fusion.103 = (f32[16,11,512]{2,1,0:T(8,128)S(1)}, f32[16,11,512]{2,1,0:T(8,128)S(1)}) fusion(f32[16,32,512]{2,1,0:T(8,128)} %param.8), kind=kLoop, calls=%fused_computation.199 | loop fusion | bytes 1441792 | tf_op jit(solution)/shard_map/slice | solution.py:25
  2.1 4.5 %collective-permute-start = (f32[16,11,512]{2,1,0:T(8,128)S(1)}, f32[16,11,512]{2,1,0:T(8,128)S(1)}, u32[]{:S(2)}, u32[]{:S(2)}) collective-permute-start(f32[16,11,512]{2,1,0:T(8,128)S(1)} %get-tuple-element.65), channel_id=1, source_target_pairs={{0,2},{2,4},{4,6},{1,3},{3,5},{5,7},{8,10},{10,12},{12,14},{9,11},... | collective-permute-start | bytes 1081352 | tf_op jit(solution)/shard_map/ppermute | solution.py:25
  6.6 1.9 %collective-permute-start.1 = (f32[16,11,512]{2,1,0:T(8,128)S(1)}, f32[16,11,512]{2,1,0:T(8,128)S(1)}, u32[]{:S(2)}, u32[]{:S(2)}) collective-permute-start(f32[16,11,512]{2,1,0:T(8,128)S(1)} %get-tuple-element.66), channel_id=1, source_target_pairs={{2,0},{4,2},{6,4},{3,1},{5,3},{7,5},{10,8},{12,10},{14,12},{11,9},... | collective-permute-start | bytes 1081352 | tf_op jit(solution)/shard_map/ppermute | solution.py:26
  8.6 0.8 slice_bitcast_fusion.25
  9.4 0.2 fusion.36
  9.6 0.2 fusion.37
  9.8 2.9 %collective-permute-done = f32[16,11,512]{2,1,0:T(8,128)S(1)} collective-permute-done((f32[16,11,512]{2,1,0:T(8,128)S(1)}, f32[16,11,512]{2,1,0:T(8,128)S(1)}, u32[]{:S(2)}, u32[]{:S(2)}) %collective-permute-start) | collective-permute-done | bytes 360480 | tf_op jit(solution)/shard_map/ppermute | solution.py:25
  12.7 4.4 %collective-permute-done.1 = f32[16,11,512]{2,1,0:T(8,128)S(1)} collective-permute-done((f32[16,11,512]{2,1,0:T(8,128)S(1)}, f32[16,11,512]{2,1,0:T(8,128)S(1)}, u32[]{:S(2)}, u32[]{:S(2)}) %collective-permute-start.1) | collective-permute-done | bytes 360480 | tf_op jit(solution)/shard_map/ppermute | solution.py:26
  17.1 0.2 fusion.19
  17.3 0.2 copy.16
  17.7 1.3 %collective-permute-start.2 = (f32[11,864]{1,0:T(8,128)S(1)}, f32[11,864]{1,0:T(8,128)S(1)}, u32[]{:S(2)}, u32[]{:S(2)}) collective-permute-start(f32[11,864]{1,0:T(8,128)S(1)} %reshape.91), channel_id=1, source_target_pairs={{0,1},{1,0},{2,3},{3,2},{4,5},{5,4},{6,7},{7,6},{8,9},{9,8},{10,11... | collective-permute-start | bytes 114056 | tf_op jit(solution)/shard_map/ppermute | solution.py:45
  19.0 0.5 add_bitcast_fusion
  19.5 0.6 reshape.89.row_weight
  20.0 0.6 reshape.90.col_weight
  20.9 0.3 copy.17
  21.3 0.3 copy.18
  21.5 2.4 %select_maximum_fusion.padded = f32[16,56,640]{2,1,0:T(8,128)} fusion(f32[16,54,11]{2,1,0:T(8,128)S(1)} %bitcast.71, f32[16,54,11]{2,1,0:T(8,128)S(1)} %bitcast.70, f32[16,11,512]{2,1,0:T(8,128)S(1)} %collective-permute-done.1, f32[16,32,512]{2,1,0:T(8,128)S(1)} %copy-done, f32[16,11,512]{2,1,0:T(8,128)S(1)} %collective-permute-done), kind=kLoop, calls=%fused_computation.6 | loop fusion | flops 9748480 | bytes 4139264 | tf_op jit(solution)/shard_map/concatenate | solution.py:50
  24.0 6.8 %shard_map.68 = (f32[16,32,512]{2,1,0:T(8,128)}, f32[4,16,8,512]{3,2,1,0:T(8,128)}) custom-call(s32[16]{0:T(128)} %get-tuple-element.111.row_shift, s32[16]{0:T(128)} %get-tuple-element.110.col_shift, f32[96]{0:T(128)} %reshape.89.row_weight, f32[96]{0:T(128)} %reshape.90.col_weight, f32[16,56,640]{2,1,0:T(8,128)} %select_maximum_fusion.padded, ...), custom_call_target="tpu_custom_call" | custom-call | tf_op jit(solution)/shard_map/pallas_call | solution.py:173
  30.8 4.6 %all-to-all-start = ((f32[4,16,8,512]{3,2,1,0:T(8,128)}), f32[4,16,8,512]{3,2,1,0:T(8,128)S(1)}, u32[]{:S(2)}, u32[]{:S(2)}) async-start(f32[4,16,8,512]{3,2,1,0:T(8,128)} %get-tuple-element.33), calls=%async_computation | async-start | bytes 2097152 | tf_op jit(solution)/shard_map/all_to_all | solution.py:185
  35.6 21.0 %all-to-all-done = f32[4,16,8,512]{3,2,1,0:T(8,128)S(1)} async-done(((f32[4,16,8,512]{3,2,1,0:T(8,128)}), f32[4,16,8,512]{3,2,1,0:T(8,128)S(1)}, u32[]{:S(2)}, u32[]{:S(2)}) %all-to-all-start) | async-done | bytes 1048608 | tf_op jit(solution)/shard_map/all_to_all | solution.py:185
  56.7 3.6 %while.13 = (s32[]{:T(128)}, f32[8,512]{1,0:T(8,128)S(1)}, f32[8,512]{1,0:T(8,128)S(1)}, f32[64,8,512]{2,1,0:T(8,128)S(1)}, f32[8,512]{1,0:T(8,128)S(1)}, /*index=5*/s32[]{:T(128)}, s32[]{:T(128)}) while((s32[]{:T(128)}, f32[8,512]{1,0:T(8,128)S(1)}, f32[8,512]{1,0:T(8,128)S(1)}, f32[64,8,512]{2,1,0:T(8,128)S(1)}, ...), condition=%wide.region_5.7_spmd.clone, body=%wide.region_3.6_spmd.clone.sunk | while | flops 1110019 | bytes 1302617 | solution.py:109
  60.5 0.6 tile.2
  61.2 3.4 %all-to-all-start.1 = ((f32[8,8,512]{2,1,0:T(8,128)}), f32[8,8,512]{2,1,0:T(8,128)S(1)}, u32[]{:S(2)}, u32[]{:S(2)}) async-start(f32[8,8,512]{2,1,0:T(8,128)} %tile.2), calls=%async_computation.1 | async-start | bytes 262144 | tf_op jit(solution)/shard_map/all_to_all | solution.py:190
  64.6 6.3 %all-to-all-done.1 = f32[8,8,512]{2,1,0:T(8,128)S(1)} async-done(((f32[8,8,512]{2,1,0:T(8,128)}), f32[8,8,512]{2,1,0:T(8,128)S(1)}, u32[]{:S(2)}, u32[]{:S(2)}) %all-to-all-start.1) | async-done | bytes 131104 | tf_op jit(solution)/shard_map/all_to_all | solution.py:190
  71.1 1.9 %collective-permute-start.3 = (f32[4,520]{1,0:T(4,128)S(1)}, f32[4,520]{1,0:T(4,128)S(1)}, u32[]{:S(2)}, u32[]{:S(2)}) collective-permute-start(f32[4,520]{1,0:T(4,128)S(1)} %get-tuple-element.75), channel_id=1, source_target_pairs={{0,2},{2,4},{4,6},{1,3},{3,5},{5,7},{8,10},{10,12},{12,14},{9,11},... | collective-permute-start | bytes 24968 | tf_op jit(solution)/shard_map/ppermute | solution.py:25
  73.0 2.4 %collective-permute-start.4 = (f32[4,520]{1,0:T(4,128)S(1)}, f32[4,520]{1,0:T(4,128)S(1)}, u32[]{:S(2)}, u32[]{:S(2)}) collective-permute-start(f32[4,520]{1,0:T(4,128)S(1)} %get-tuple-element.76), channel_id=1, source_target_pairs={{2,0},{4,2},{6,4},{3,1},{5,3},{7,5},{10,8},{12,10},{14,12},{11,9},... | collective-permute-start | bytes 24968 | tf_op jit(solution)/shard_map/ppermute | solution.py:26
  75.4 0.6 constant_dynamic-slice_fusion
  76.0 1.9 %collective-permute-done.4 = f32[4,520]{1,0:T(4,128)S(1)} collective-permute-done((f32[4,520]{1,0:T(4,128)S(1)}, f32[4,520]{1,0:T(4,128)S(1)}, u32[]{:S(2)}, u32[]{:S(2)}) %collective-permute-start.4) | collective-permute-done | bytes 8352 | tf_op jit(solution)/shard_map/ppermute | solution.py:26
  78.0 0.6 multiply_add_fusion
  78.6 1.3 %fusion.10 = f32[8,32,512]{2,1,0:T(8,128)S(1)} fusion(f32[8,32,520]{2,1,0:T(8,128)S(1)} %multiply_add_fusion, f32[8]{0:T(128)S(1)} %get-tuple-element.92, f32[8]{0:T(128)S(1)} %get-tuple-element.93, f32[8]{0:T(128)S(1)} %get-tuple-element.94, f32[8]{0:T(128)S(1)} %get-tuple-element.95, f32[8]{0:T(128)S(1)} %get-tuple-element.96, f32[8]{0:T(128)S(1)} %get-tuple-element.97, ...), kind=kLoop, calls=%fused_computation.24 | loop fusion | flops 2228224 | bytes 5243168 | tf_op jit(solution)/shard_map/add | solution.py:211
  80.0 0.2 copy-done.2
  80.2 1.8 %subtract_select_fusion = f32[16,32,512]{2,1,0:T(8,128)} fusion(f32[16,32,512]{2,1,0:T(8,128)S(1)} %copy-done.2, s32[16,32,512]{2,1,0:T(8,128)S(1)} %copy-done.1, f32[32,512]{1,0:T(8,128)S(1)} %get-tuple-element.68, f32[16]{0:T(128)S(1)} %get-tuple-element.101, f32[32,512]{1,0:T(8,128)S(1)} %get-tuple-element.69, f32[16]{0:T(128)S(1)} %get-tuple-element.102, ...), kind=kLoop, calls=%fused_computation.20 | loop fusion | flops 4718592 | bytes 3670528 | tf_op jit(solution)/shard_map/jit(_where)/select_n | solution.py:219
  (113 shorter events, 4.3 us)
Async XLA Ops:
  0.6 16.5 %copy-start = (f32[16,32,512]{2,1,0:T(8,128)S(1)}, f32[16,32,512]{2,1,0:T(8,128)}, u32[]{:S(2)}) copy-start(f32[16,32,512]{2,1,0:T(8,128)} %param.8) | copy-start | bytes 3145732
  2.1 16.9 %copy-start.3 = (s32[16,2]{0,1:T(2,128)S(1)}, s32[16,2]{0,1:T(2,128)}, u32[]{:S(2)}) copy-start(s32[16,2]{0,1:T(2,128)} %param.10) | copy-start | bytes 388
  2.1 10.6 %collective-permute-start = (f32[16,11,512]{2,1,0:T(8,128)S(1)}, f32[16,11,512]{2,1,0:T(8,128)S(1)}, u32[]{:S(2)}, u32[]{:S(2)}) collective-permute-start(f32[16,11,512]{2,1,0:T(8,128)S(1)} %get-tuple-element.65), channel_id=1, source_target_pairs={{0,2},{2,4},{4,6},{1,3},{3,5},{5,7},{8,10},{10,12},{12,14},{9,11},... | collective-permute-start | bytes 1081352 | tf_op jit(solution)/shard_map/ppermute | solution.py:25
  6.6 10.5 %collective-permute-start.1 = (f32[16,11,512]{2,1,0:T(8,128)S(1)}, f32[16,11,512]{2,1,0:T(8,128)S(1)}, u32[]{:S(2)}, u32[]{:S(2)}) collective-permute-start(f32[16,11,512]{2,1,0:T(8,128)S(1)} %get-tuple-element.66), channel_id=1, source_target_pairs={{2,0},{4,2},{6,4},{3,1},{5,3},{7,5},{10,8},{12,10},{14,12},{11,9},... | collective-permute-start | bytes 1081352 | tf_op jit(solution)/shard_map/ppermute | solution.py:26
  17.7 3.1 %collective-permute-start.2 = (f32[11,864]{1,0:T(8,128)S(1)}, f32[11,864]{1,0:T(8,128)S(1)}, u32[]{:S(2)}, u32[]{:S(2)}) collective-permute-start(f32[11,864]{1,0:T(8,128)S(1)} %reshape.91), channel_id=1, source_target_pairs={{0,1},{1,0},{2,3},{3,2},{4,5},{5,4},{6,7},{7,6},{8,9},{9,8},{10,11... | collective-permute-start | bytes 114056 | tf_op jit(solution)/shard_map/ppermute | solution.py:45
  24.0 11.6 %copy-start.4 = (s32[16]{0:T(128)S(1)}, s32[16]{0:T(128)}, u32[]{:S(2)}) copy-start(s32[16]{0:T(128)} %param.12) | copy-start | bytes 196
  30.8 25.8 %all-to-all-start = ((f32[4,16,8,512]{3,2,1,0:T(8,128)}), f32[4,16,8,512]{3,2,1,0:T(8,128)S(1)}, u32[]{:S(2)}, u32[]{:S(2)}) async-start(f32[4,16,8,512]{3,2,1,0:T(8,128)} %get-tuple-element.33), calls=%async_computation | async-start | bytes 2097152 | tf_op jit(solution)/shard_map/all_to_all | solution.py:185
  61.2 9.7 %all-to-all-start.1 = ((f32[8,8,512]{2,1,0:T(8,128)}), f32[8,8,512]{2,1,0:T(8,128)S(1)}, u32[]{:S(2)}, u32[]{:S(2)}) async-start(f32[8,8,512]{2,1,0:T(8,128)} %tile.2), calls=%async_computation.1 | async-start | bytes 262144 | tf_op jit(solution)/shard_map/all_to_all | solution.py:190
  71.1 5.0 %collective-permute-start.3 = (f32[4,520]{1,0:T(4,128)S(1)}, f32[4,520]{1,0:T(4,128)S(1)}, u32[]{:S(2)}, u32[]{:S(2)}) collective-permute-start(f32[4,520]{1,0:T(4,128)S(1)} %get-tuple-element.75), channel_id=1, source_target_pairs={{0,2},{2,4},{4,6},{1,3},{3,5},{5,7},{8,10},{10,12},{12,14},{9,11},... | collective-permute-start | bytes 24968 | tf_op jit(solution)/shard_map/ppermute | solution.py:25
  73.0 5.0 %collective-permute-start.4 = (f32[4,520]{1,0:T(4,128)S(1)}, f32[4,520]{1,0:T(4,128)S(1)}, u32[]{:S(2)}, u32[]{:S(2)}) collective-permute-start(f32[4,520]{1,0:T(4,128)S(1)} %get-tuple-element.76), channel_id=1, source_target_pairs={{2,0},{4,2},{6,4},{3,1},{5,3},{7,5},{10,8},{12,10},{14,12},{11,9},... | collective-permute-start | bytes 24968 | tf_op jit(solution)/shard_map/ppermute | solution.py:26
  78.6 1.3 %copy-start.1 = (s32[16,32,512]{2,1,0:T(8,128)S(1)}, s32[16,32,512]{2,1,0:T(8,128)}, u32[]{:S(2)}) copy-start(s32[16,32,512]{2,1,0:T(8,128)} %bad.1) | copy-start | bytes 3145732
  78.6 1.5 %copy-start.2 = (f32[16,32,512]{2,1,0:T(8,128)S(1)}, f32[16,32,512]{2,1,0:T(8,128)}, u32[]{:S(2)}) copy-start(f32[16,32,512]{2,1,0:T(8,128)} %get-tuple-element.32) | copy-start | bytes 3145732

commit v9 on v8

--- a/solution.py
+++ b/solution.py
@@ -123,7 +123,7 @@
 
 
 def _warp_kernel(
-    row_shift, col_shift, row_weight, col_weight, padded, bad, warped_out, flagged_out
+    row_shift, col_shift, row_weight, col_weight, me, padded, bad, warped_out, flagged_out
 ):
     group_size, row_count, col_count = warped_out.shape
     bands, _, band_rows, _ = flagged_out.shape
@@ -145,7 +145,8 @@
         warped_out[e] = total
         flagged = jnp.where(bad[e] == 1, sentinel, total)
         for band in range(bands):
-            flagged_out[band, e] = flagged[band * band_rows : (band + 1) * band_rows]
+            slot = lax.rem(band - me[0] + bands, bands)
+            flagged_out[slot, e] = flagged[band * band_rows : (band + 1) * band_rows]
         return carry
 
     lax.fori_loop(0, group_size, one_exposure, 0, unroll=True)
@@ -158,6 +159,7 @@
     col_weight = lookup(warp_index[:, 1], NFRAC, kernel_table).reshape(-1)
     row_shift = offsets[:, 0] + (HALO - 2)
     col_shift = offsets[:, 1] + (HALO - 2)
+    me = lax.axis_index("exp").astype(jnp.int32).reshape(1)
     lanes = -(-padded.shape[2] // 128) * 128
     rows = -(-padded.shape[1] // 8) * 8
     padded = jnp.pad(
@@ -173,17 +175,21 @@
     return pl.pallas_call(
         _warp_kernel,
         out_shape=(shape, banded),
-        in_specs=[smem, smem, smem, smem, vmem, vmem],
+        in_specs=[smem, smem, smem, smem, smem, vmem, vmem],
         out_specs=(vmem, vmem),
-    )(row_shift, col_shift, row_weight, col_weight, padded, bad_pixels)
+    )(row_shift, col_shift, row_weight, col_weight, me, padded, bad_pixels)
 
 
 def body(exposures, bad_pixels, offsets, warp_index, blur_index):
     group_size, row_count, col_count = exposures.shape
     padded = extended(exposures, 1, 2, HALO)
     warped, flagged = warp_and_flag(padded, bad_pixels, offsets, warp_index)
-    gathered = lax.all_to_all(flagged, "exp", split_axis=0, concat_axis=0, tiled=True)
-    band = stack_median(gathered.reshape((-1,) + gathered.shape[2:]))
+    groups = lax.axis_size("exp")
+    arrived = [flagged[0]]
+    for step in range(1, groups):
+        pairs = [(i, (i + step) % groups) for i in range(groups)]
+        arrived.append(lax.ppermute(flagged[step], "exp", pairs))
+    band = stack_median(jnp.concatenate(arrived, axis=0))
     groups = lax.axis_size("exp")
     sides = lax.axis_size("col")
     band_rows = band.shape[0]

time: 82.4 us -> 81.6 us (level)
  waiting for transfers between devices: 36.6 us -> 26.5 us
  starting transfers between devices: 20 us -> 26.6 us
  other arithmetic: 10.3 us -> 11.8 us
  local copies, waits for them, and re-layouts: 6.18 us -> 7.48 us
    all_to_all x1 -> x0, waiting for transfers between devices: 21 us -> none  [body(): lax.all_to_all(flagged, 'exp', split_axis=0, concat_axis=0, tiled=True)]
    ppermute x0 -> x3, waiting for transfers between devices: none -> 11.4 us  [body(): arrived.append(lax.ppermute(flagged[step], 'exp', pairs))]
    all_to_all x1, starting transfers between devices: 3.38 us -> 8.99 us  [body(): lax.all_to_all(jnp.tile(band, (groups * sides, 1)), ('exp', 'col'), split...]
    ppermute x0 -> x3, starting transfers between devices: none -> 4.73 us  [body(): arrived.append(lax.ppermute(flagged[step], 'exp', pairs))]
    all_to_all x1 -> x0, starting transfers between devices: 4.59 us -> none  [body(): lax.all_to_all(flagged, 'exp', split_axis=0, concat_axis=0, tiled=True)]
    ppermute x2, waiting for transfers between devices: 2.86 us -> 0.92 us  [_row_halo(): lax.ppermute(lax.slice_in_dim(block, size - width, None, axis=dim), 'row'...]
    ppermute x2, starting transfers between devices: 6.44 us -> 7.74 us  [_row_halo(): lax.ppermute(lax.slice_in_dim(block, size - width, None, axis=dim), 'row'...]
    squeeze x0 -> x1, local copies, waits for them, and re-layouts: none -> 1.26 us  [body(): arrived = [flagged[0]]]
  transfers between devices with their start and end apart: 7 -> 9, of which waited for: 6 -> 7; matrix products, arithmetic and copies ran while one was open for 5% -> 6% of each run, Pallas kernels for 0% -> 0%
where the time goes in v9:
time: 81.6 us; the launch traced here: 81.2 us
  starting transfers between devices  26.6 us (33%)
  waiting for transfers between devices  26.5 us (32%)
  other arithmetic  11.8 us (14%)
  local copies, waits for them, and re-layouts  7.48 us (9%)
  Pallas kernels  6.84 us (8%)
  between operations  0.83 us (1%)
    ppermute x3, waiting for transfers between devices, body(): arrived.append(lax.ppermute(flagged[step], 'exp', pairs))  11.4 us
    all_to_all x1, starting transfers between devices, body(): lax.all_to_all(jnp.tile(band, (groups * sides, 1)), ('exp', 'col'), split...  8.99 us
    ppermute x2, starting transfers between devices, _row_halo(): lax.ppermute(lax.slice_in_dim(block, size - width, None, axis=dim), 'row'...  7.74 us
    pallas_call x1, Pallas kernels, warp_and_flag(): pl.pallas_call(_warp_kernel, out_shape=(shape, banded), in_specs=[smem, s...  6.84 us
    ppermute x2, waiting for transfers between devices, _row_halo(): lax.ppermute(lax.slice_in_dim(block, 0, width, axis=dim), 'row', backward)  6.81 us
    all_to_all x1, waiting for transfers between devices, body(): lax.all_to_all(jnp.tile(band, (groups * sides, 1)), ('exp', 'col'), split...  6.8 us
    ppermute x3, starting transfers between devices, body(): arrived.append(lax.ppermute(flagged[step], 'exp', pairs))  4.73 us
    ppermute x2, starting transfers between devices, _row_halo(): lax.ppermute(lax.slice_in_dim(block, 0, width, axis=dim), 'row', backward)  3.84 us
  transfers between devices with their start and end apart: 9, of which 7 were waited for; matrix products, arithmetic and copies ran while one was open for 6% of the time, Pallas kernels for 0%

profile of v9, /device:TPU:1, one launch (start us, length us, event | category | flops | bytes accessed | tf_op | source)
XLA Modules:
  0.0 81.2 jit_solution(9614389893448174445)
XLA Ops:
  0.6 1.4 %fusion.103 = (f32[16,11,512]{2,1,0:T(8,128)S(1)}, f32[16,11,512]{2,1,0:T(8,128)S(1)}) fusion(f32[16,32,512]{2,1,0:T(8,128)} %param.8), kind=kLoop, calls=%fused_computation.204 | loop fusion | bytes 1441792 | tf_op jit(solution)/shard_map/slice | solution.py:25
  2.1 4.5 %collective-permute-start = (f32[16,11,512]{2,1,0:T(8,128)S(1)}, f32[16,11,512]{2,1,0:T(8,128)S(1)}, u32[]{:S(2)}, u32[]{:S(2)}) collective-permute-start(f32[16,11,512]{2,1,0:T(8,128)S(1)} %get-tuple-element.71), channel_id=1, source_target_pairs={{0,2},{2,4},{4,6},{1,3},{3,5},{5,7},{8,10},{10,12},{12,14},{9,11},... | collective-permute-start | bytes 1081352 | tf_op jit(solution)/shard_map/ppermute | solution.py:25
  6.6 1.9 %collective-permute-start.1 = (f32[16,11,512]{2,1,0:T(8,128)S(1)}, f32[16,11,512]{2,1,0:T(8,128)S(1)}, u32[]{:S(2)}, u32[]{:S(2)}) collective-permute-start(f32[16,11,512]{2,1,0:T(8,128)S(1)} %get-tuple-element.72), channel_id=1, source_target_pairs={{2,0},{4,2},{6,4},{3,1},{5,3},{7,5},{10,8},{12,10},{14,12},{11,9},... | collective-permute-start | bytes 1081352 | tf_op jit(solution)/shard_map/ppermute | solution.py:26
  8.5 0.8 slice_bitcast_fusion.29
  9.3 0.7 fusion.77
  10.3 1.3 %add_bitcast_fusion = (s32[16]{0:T(128)}, s32[16]{0:T(128)}) fusion(s32[16,2]{0,1:T(2,128)} %param.10), kind=kLoop, calls=%fused_computation.178 | loop fusion | flops 32 | bytes 256 | tf_op jit(solution)/shard_map/add | solution.py:161
  11.8 0.9 %collective-permute-done = f32[16,11,512]{2,1,0:T(8,128)S(1)} collective-permute-done((f32[16,11,512]{2,1,0:T(8,128)S(1)}, f32[16,11,512]{2,1,0:T(8,128)S(1)}, u32[]{:S(2)}, u32[]{:S(2)}) %collective-permute-start) | collective-permute-done | bytes 360480 | tf_op jit(solution)/shard_map/ppermute | solution.py:25
  12.7 4.4 %collective-permute-done.1 = f32[16,11,512]{2,1,0:T(8,128)S(1)} collective-permute-done((f32[16,11,512]{2,1,0:T(8,128)S(1)}, f32[16,11,512]{2,1,0:T(8,128)S(1)}, u32[]{:S(2)}, u32[]{:S(2)}) %collective-permute-start.1) | collective-permute-done | bytes 360480 | tf_op jit(solution)/shard_map/ppermute | solution.py:26
  17.7 1.3 %collective-permute-start.2 = (f32[11,864]{1,0:T(8,128)S(1)}, f32[11,864]{1,0:T(8,128)S(1)}, u32[]{:S(2)}, u32[]{:S(2)}) collective-permute-start(f32[11,864]{1,0:T(8,128)S(1)} %reshape.92), channel_id=1, source_target_pairs={{0,1},{1,0},{2,3},{3,2},{4,5},{5,4},{6,7},{7,6},{8,9},{9,8},{10,11... | collective-permute-start | bytes 114056 | tf_op jit(solution)/shard_map/ppermute | solution.py:45
  18.9 0.6 reshape.89.row_weight
  19.5 0.6 reshape.90.col_weight
  20.1 0.6 collective-permute-done.2
  21.3 0.3 copy.18
  21.5 2.4 %select_maximum_fusion.padded = f32[16,56,640]{2,1,0:T(8,128)} fusion(f32[16,54,11]{2,1,0:T(8,128)S(1)} %bitcast.77, f32[16,54,11]{2,1,0:T(8,128)S(1)} %bitcast.76, f32[16,11,512]{2,1,0:T(8,128)S(1)} %collective-permute-done.1, f32[16,32,512]{2,1,0:T(8,128)S(1)} %copy-done, f32[16,11,512]{2,1,0:T(8,128)S(1)} %collective-permute-done), kind=kLoop, calls=%fused_computation.6 | loop fusion | flops 9748480 | bytes 4139264 | tf_op jit(solution)/shard_map/concatenate | solution.py:50
  24.0 6.8 %shard_map.68 = (f32[16,32,512]{2,1,0:T(8,128)}, f32[4,16,8,512]{3,2,1,0:T(8,128)}) custom-call(s32[16]{0:T(128)} %get-tuple-element.117.row_shift, s32[16]{0:T(128)} %get-tuple-element.116.col_shift, f32[96]{0:T(128)} %reshape.89.row_weight, f32[96]{0:T(128)} %reshape.90.col_weight, s32[1]{0:T(128)} %bitcast.4.me, ...), custom_call_target="tpu_custom_call" | custom-call | tf_op jit(solution)/shard_map/pallas_call | solution.py:175
  30.8 1.3 %slice_bitcast_fusion.3 = (f32[16,8,512]{2,1,0:T(8,128)S(1)}, f32[16,8,512]{2,1,0:T(8,128)S(1)}, f32[16,8,512]{2,1,0:T(8,128)S(1)}, f32[16,8,512]{2,1,0:T(8,128)S(1)}) fusion(f32[4,16,8,512]{3,2,1,0:T(8,128)} %get-tuple-element.33), kind=kLoop, calls=%fused_computation.48 | loop fusion | bytes 2097152 | tf_op jit(solution)/shard_map/squeeze | solution.py:188
  32.1 1.3 %collective-permute-start.3 = (f32[16,8,512]{2,1,0:T(8,128)S(1)}, f32[16,8,512]{2,1,0:T(8,128)S(1)}, u32[]{:S(2)}, u32[]{:S(2)}) collective-permute-start(f32[16,8,512]{2,1,0:T(8,128)S(1)} %get-tuple-element.70), channel_id=1, source_target_pairs={{0,8},{8,16},{16,24},{24,0},{1,9},{9,17},{17,25},{25,1},{2,10},{10... | collective-permute-start | bytes 786440 | tf_op jit(solution)/shard_map/ppermute | solution.py:191
  33.4 2.3 %collective-permute-start.4 = (f32[16,8,512]{2,1,0:T(8,128)S(1)}, f32[16,8,512]{2,1,0:T(8,128)S(1)}, u32[]{:S(2)}, u32[]{:S(2)}) collective-permute-start(f32[16,8,512]{2,1,0:T(8,128)S(1)} %get-tuple-element.69), channel_id=1, source_target_pairs={{0,16},{8,24},{16,0},{24,8},{1,17},{9,25},{17,1},{25,9},{2,18},{10... | collective-permute-start | bytes 786440 | tf_op jit(solution)/shard_map/ppermute | solution.py:191
  35.7 1.1 %collective-permute-start.5 = (f32[16,8,512]{2,1,0:T(8,128)S(1)}, f32[16,8,512]{2,1,0:T(8,128)S(1)}, u32[]{:S(2)}, u32[]{:S(2)}) collective-permute-start(f32[16,8,512]{2,1,0:T(8,128)S(1)} %get-tuple-element.68), channel_id=1, source_target_pairs={{0,24},{8,0},{16,8},{24,16},{1,25},{9,1},{17,9},{25,17},{2,26},{10... | collective-permute-start | bytes 786440 | tf_op jit(solution)/shard_map/ppermute | solution.py:191
  37.0 5.1 %collective-permute-done.3 = f32[16,8,512]{2,1,0:T(8,128)S(1)} collective-permute-done((f32[16,8,512]{2,1,0:T(8,128)S(1)}, f32[16,8,512]{2,1,0:T(8,128)S(1)}, u32[]{:S(2)}, u32[]{:S(2)}) %collective-permute-start.3) | collective-permute-done | bytes 262176 | tf_op jit(solution)/shard_map/ppermute | solution.py:191
  42.1 6.3 %collective-permute-done.4 = f32[16,8,512]{2,1,0:T(8,128)S(1)} collective-permute-done((f32[16,8,512]{2,1,0:T(8,128)S(1)}, f32[16,8,512]{2,1,0:T(8,128)S(1)}, u32[]{:S(2)}, u32[]{:S(2)}) %collective-permute-start.4) | collective-permute-done | bytes 262176 | tf_op jit(solution)/shard_map/ppermute | solution.py:191
  48.5 3.6 %while.13 = (s32[]{:T(128)}, f32[8,512]{1,0:T(8,128)S(1)}, f32[8,512]{1,0:T(8,128)S(1)}, f32[64,8,512]{2,1,0:T(8,128)S(1)}, f32[8,512]{1,0:T(8,128)S(1)}, /*index=5*/s32[]{:T(128)}, s32[]{:T(128)}) while((s32[]{:T(128)}, f32[8,512]{1,0:T(8,128)S(1)}, f32[8,512]{1,0:T(8,128)S(1)}, f32[64,8,512]{2,1,0:T(8,128)S(1)}, ...), condition=%wide.region_5.7_spmd.clone, body=%wide.region_3.6_spmd.clone.sunk | while | flops 1110019 | bytes 1302617 | solution.py:109
  52.3 0.7 tile.2
  53.0 9.0 %all-to-all-start = ((f32[8,8,512]{2,1,0:T(8,128)}), f32[8,8,512]{2,1,0:T(8,128)S(1)}, u32[]{:S(2)}, u32[]{:S(2)}) async-start(f32[8,8,512]{2,1,0:T(8,128)} %tile.2), calls=%async_computation | async-start | bytes 262144 | tf_op jit(solution)/shard_map/all_to_all | solution.py:196
  62.0 6.8 %all-to-all-done = f32[8,8,512]{2,1,0:T(8,128)S(1)} async-done(((f32[8,8,512]{2,1,0:T(8,128)}), f32[8,8,512]{2,1,0:T(8,128)S(1)}, u32[]{:S(2)}, u32[]{:S(2)}) %all-to-all-start) | async-done | bytes 131104 | tf_op jit(solution)/shard_map/all_to_all | solution.py:196
  69.0 3.2 %collective-permute-start.6 = (f32[4,520]{1,0:T(4,128)S(1)}, f32[4,520]{1,0:T(4,128)S(1)}, u32[]{:S(2)}, u32[]{:S(2)}) collective-permute-start(f32[4,520]{1,0:T(4,128)S(1)} %get-tuple-element.81), channel_id=1, source_target_pairs={{0,2},{2,4},{4,6},{1,3},{3,5},{5,7},{8,10},{10,12},{12,14},{9,11},... | collective-permute-start | bytes 24968 | tf_op jit(solution)/shard_map/ppermute | solution.py:25
  72.2 1.9 %collective-permute-start.7 = (f32[4,520]{1,0:T(4,128)S(1)}, f32[4,520]{1,0:T(4,128)S(1)}, u32[]{:S(2)}, u32[]{:S(2)}) collective-permute-start(f32[4,520]{1,0:T(4,128)S(1)} %get-tuple-element.82), channel_id=1, source_target_pairs={{2,0},{4,2},{6,4},{3,1},{5,3},{7,5},{10,8},{12,10},{14,12},{11,9},... | collective-permute-start | bytes 24968 | tf_op jit(solution)/shard_map/ppermute | solution.py:26
  74.1 0.6 constant_dynamic-slice_fusion
  74.8 2.4 %collective-permute-done.7 = f32[4,520]{1,0:T(4,128)S(1)} collective-permute-done((f32[4,520]{1,0:T(4,128)S(1)}, f32[4,520]{1,0:T(4,128)S(1)}, u32[]{:S(2)}, u32[]{:S(2)}) %collective-permute-start.7) | collective-permute-done | bytes 8352 | tf_op jit(solution)/shard_map/ppermute | solution.py:26
  77.3 0.6 multiply_add_fusion
  77.8 1.3 %fusion.10 = f32[8,32,512]{2,1,0:T(8,128)S(1)} fusion(f32[8,32,520]{2,1,0:T(8,128)S(1)} %multiply_add_fusion, f32[8]{0:T(128)S(1)} %get-tuple-element.98, f32[8]{0:T(128)S(1)} %get-tuple-element.99, f32[8]{0:T(128)S(1)} %get-tuple-element.100, f32[8]{0:T(128)S(1)} %get-tuple-element.101, f32[8]{0:T(128)S(1)} %get-tuple-element.102, ...), kind=kLoop, calls=%fused_computation.25 | loop fusion | flops 2228224 | bytes 5243168 | tf_op jit(solution)/shard_map/add | solution.py:217
  79.4 1.8 %subtract_select_fusion = f32[16,32,512]{2,1,0:T(8,128)} fusion(f32[16,32,512]{2,1,0:T(8,128)S(1)} %copy-done.2, s32[16,32,512]{2,1,0:T(8,128)S(1)} %copy-done.1, f32[32,512]{1,0:T(8,128)S(1)} %get-tuple-element.74, f32[16]{0:T(128)S(1)} %get-tuple-element.107, f32[32,512]{1,0:T(8,128)S(1)} %get-tuple-element.75, f32[16]{0:T(128)S(1)} %get-tuple-element.108, ...), kind=kLoop, calls=%fused_computation.21 | loop fusion | flops 4718592 | bytes 3670528 | tf_op jit(solution)/shard_map/jit(_where)/select_n | solution.py:225
  (114 shorter events, 5.6 us)
Async XLA Ops:
  0.6 16.5 %copy-start = (f32[16,32,512]{2,1,0:T(8,128)S(1)}, f32[16,32,512]{2,1,0:T(8,128)}, u32[]{:S(2)}) copy-start(f32[16,32,512]{2,1,0:T(8,128)} %param.8) | copy-start | bytes 3145732
  2.1 10.6 %collective-permute-start = (f32[16,11,512]{2,1,0:T(8,128)S(1)}, f32[16,11,512]{2,1,0:T(8,128)S(1)}, u32[]{:S(2)}, u32[]{:S(2)}) collective-permute-start(f32[16,11,512]{2,1,0:T(8,128)S(1)} %get-tuple-element.71), channel_id=1, source_target_pairs={{0,2},{2,4},{4,6},{1,3},{3,5},{5,7},{8,10},{10,12},{12,14},{9,11},... | collective-permute-start | bytes 1081352 | tf_op jit(solution)/shard_map/ppermute | solution.py:25
  6.6 10.5 %collective-permute-start.1 = (f32[16,11,512]{2,1,0:T(8,128)S(1)}, f32[16,11,512]{2,1,0:T(8,128)S(1)}, u32[]{:S(2)}, u32[]{:S(2)}) collective-permute-start(f32[16,11,512]{2,1,0:T(8,128)S(1)} %get-tuple-element.72), channel_id=1, source_target_pairs={{2,0},{4,2},{6,4},{3,1},{5,3},{7,5},{10,8},{12,10},{14,12},{11,9},... | collective-permute-start | bytes 1081352 | tf_op jit(solution)/shard_map/ppermute | solution.py:26
  17.7 3.1 %collective-permute-start.2 = (f32[11,864]{1,0:T(8,128)S(1)}, f32[11,864]{1,0:T(8,128)S(1)}, u32[]{:S(2)}, u32[]{:S(2)}) collective-permute-start(f32[11,864]{1,0:T(8,128)S(1)} %reshape.92), channel_id=1, source_target_pairs={{0,1},{1,0},{2,3},{3,2},{4,5},{5,4},{6,7},{7,6},{8,9},{9,8},{10,11... | collective-permute-start | bytes 114056 | tf_op jit(solution)/shard_map/ppermute | solution.py:45
  32.1 10.0 %collective-permute-start.3 = (f32[16,8,512]{2,1,0:T(8,128)S(1)}, f32[16,8,512]{2,1,0:T(8,128)S(1)}, u32[]{:S(2)}, u32[]{:S(2)}) collective-permute-start(f32[16,8,512]{2,1,0:T(8,128)S(1)} %get-tuple-element.70), channel_id=1, source_target_pairs={{0,8},{8,16},{16,24},{24,0},{1,9},{9,17},{17,25},{25,1},{2,10},{10... | collective-permute-start | bytes 786440 | tf_op jit(solution)/shard_map/ppermute | solution.py:191
  33.4 14.9 %collective-permute-start.4 = (f32[16,8,512]{2,1,0:T(8,128)S(1)}, f32[16,8,512]{2,1,0:T(8,128)S(1)}, u32[]{:S(2)}, u32[]{:S(2)}) collective-permute-start(f32[16,8,512]{2,1,0:T(8,128)S(1)} %get-tuple-element.69), channel_id=1, source_target_pairs={{0,16},{8,24},{16,0},{24,8},{1,17},{9,25},{17,1},{25,9},{2,18},{10... | collective-permute-start | bytes 786440 | tf_op jit(solution)/shard_map/ppermute | solution.py:191
  35.7 12.6 %collective-permute-start.5 = (f32[16,8,512]{2,1,0:T(8,128)S(1)}, f32[16,8,512]{2,1,0:T(8,128)S(1)}, u32[]{:S(2)}, u32[]{:S(2)}) collective-permute-start(f32[16,8,512]{2,1,0:T(8,128)S(1)} %get-tuple-element.68), channel_id=1, source_target_pairs={{0,24},{8,0},{16,8},{24,16},{1,25},{9,1},{17,9},{25,17},{2,26},{10... | collective-permute-start | bytes 786440 | tf_op jit(solution)/shard_map/ppermute | solution.py:191
  53.0 15.8 %all-to-all-start = ((f32[8,8,512]{2,1,0:T(8,128)}), f32[8,8,512]{2,1,0:T(8,128)S(1)}, u32[]{:S(2)}, u32[]{:S(2)}) async-start(f32[8,8,512]{2,1,0:T(8,128)} %tile.2), calls=%async_computation | async-start | bytes 262144 | tf_op jit(solution)/shard_map/all_to_all | solution.py:196
  69.0 5.8 %collective-permute-start.6 = (f32[4,520]{1,0:T(4,128)S(1)}, f32[4,520]{1,0:T(4,128)S(1)}, u32[]{:S(2)}, u32[]{:S(2)}) collective-permute-start(f32[4,520]{1,0:T(4,128)S(1)} %get-tuple-element.81), channel_id=1, source_target_pairs={{0,2},{2,4},{4,6},{1,3},{3,5},{5,7},{8,10},{10,12},{12,14},{9,11},... | collective-permute-start | bytes 24968 | tf_op jit(solution)/shard_map/ppermute | solution.py:25
  72.2 5.0 %collective-permute-start.7 = (f32[4,520]{1,0:T(4,128)S(1)}, f32[4,520]{1,0:T(4,128)S(1)}, u32[]{:S(2)}, u32[]{:S(2)}) collective-permute-start(f32[4,520]{1,0:T(4,128)S(1)} %get-tuple-element.82), channel_id=1, source_target_pairs={{2,0},{4,2},{6,4},{3,1},{5,3},{7,5},{10,8},{12,10},{14,12},{11,9},... | collective-permute-start | bytes 24968 | tf_op jit(solution)/shard_map/ppermute | solution.py:26
  77.8 1.3 %copy-start.1 = (s32[16,32,512]{2,1,0:T(8,128)S(1)}, s32[16,32,512]{2,1,0:T(8,128)}, u32[]{:S(2)}) copy-start(s32[16,32,512]{2,1,0:T(8,128)} %bad.1) | copy-start | bytes 3145732
  77.8 1.5 %copy-start.2 = (f32[16,32,512]{2,1,0:T(8,128)S(1)}, f32[16,32,512]{2,1,0:T(8,128)}, u32[]{:S(2)}) copy-start(f32[16,32,512]{2,1,0:T(8,128)} %get-tuple-element.32) | copy-start | bytes 3145732

commit v10 on v9

--- a/solution.py
+++ b/solution.py
@@ -1,3 +1,5 @@
+import functools
+
 import jax
 import jax.numpy as jnp
 from jax import lax
@@ -180,16 +182,99 @@
     )(row_shift, col_shift, row_weight, col_weight, me, padded, bad_pixels)
 
 
+def _slot_kernel(
+    step,
+    row_shift,
+    col_shift,
+    row_weight,
+    col_weight,
+    me,
+    padded,
+    bad,
+    warped_in,
+    warped_out,
+    flagged_out,
+):
+    group_size, band_rows, col_count = flagged_out.shape
+    bands = warped_out.shape[1] // band_rows
+    width = padded.shape[2]
+    window = -(-(band_rows + 2 * HALO) // 8) * 8
+    band = lax.rem(me[0] + step, bands)
+    base = pl.multiple_of(band * band_rows, 8)
+
+    def one_exposure(e, carry):
+        block = pltpu.roll(padded[e, pl.ds(base, window), :], window - row_shift[e], 0)
+        across = None
+        for tap in range(TAPS):
+            term = row_weight[e * TAPS + tap] * block[tap : tap + band_rows, :]
+            across = term if across is None else across + term
+        across = pltpu.roll(across, width - col_shift[e], 1)
+        total = None
+        for tap in range(TAPS):
+            term = col_weight[e * TAPS + tap] * across[:, tap : tap + col_count]
+            total = term if total is None else total + term
+        warped_out[e, pl.ds(base, band_rows), :] = total
+        flagged = jnp.where(bad[e, pl.ds(base, band_rows), :] == 1, sentinel, total)
+        flagged_out[e] = flagged
+        return carry
+
+    lax.fori_loop(0, group_size, one_exposure, 0, unroll=True)
+
+
+def warp_by_slot(padded, bad_pixels, offsets, warp_index):
+    group_size, row_count, col_count = bad_pixels.shape
+    bands = lax.axis_size("exp")
+    band_rows = row_count // bands
+    height = -(-padded.shape[1] // 8) * 8
+    window = -(-(band_rows + 2 * HALO) // 8) * 8
+    if band_rows % 8 or row_count - band_rows + window > height:
+        return None
+    kernel_table = lanczos_table()
+    row_weight = lookup(warp_index[:, 0], NFRAC, kernel_table).reshape(-1)
+    col_weight = lookup(warp_index[:, 1], NFRAC, kernel_table).reshape(-1)
+    row_shift = offsets[:, 0] + (HALO - 2)
+    col_shift = offsets[:, 1] + (HALO - 2)
+    me = lax.axis_index("exp").astype(jnp.int32).reshape(1)
+    lanes = -(-padded.shape[2] // 128) * 128
+    padded = jnp.pad(
+        padded, ((0, 0), (0, height - padded.shape[1]), (0, lanes - padded.shape[2]))
+    )
+    smem = pl.BlockSpec(memory_space=pltpu.SMEM)
+    vmem = pl.BlockSpec(memory_space=pltpu.VMEM)
+    shape = jax.ShapeDtypeStruct((group_size, row_count, col_count), jnp.float32)
+    banded = jax.ShapeDtypeStruct((group_size, band_rows, col_count), jnp.float32)
+    warped = jnp.zeros((group_size, row_count, col_count), jnp.float32)
+    order = [bands // 2] + [s for s in range(1, bands) if s != bands // 2] + [0]
+    slots = {}
+    for step in order:
+        warped, slots[step] = pl.pallas_call(
+            functools.partial(_slot_kernel, step),
+            out_shape=(shape, banded),
+            in_specs=[smem, smem, smem, smem, smem, vmem, vmem, vmem],
+            out_specs=(vmem, vmem),
+            input_output_aliases={7: 0},
+        )(row_shift, col_shift, row_weight, col_weight, me, padded, bad_pixels, warped)
+        if step:
+            pairs = [(i, (i + step) % bands) for i in range(bands)]
+            slots[step] = lax.ppermute(slots[step], "exp", pairs)
+    return warped, jnp.concatenate([slots[s] for s in range(bands)], axis=0)
+
+
 def body(exposures, bad_pixels, offsets, warp_index, blur_index):
     group_size, row_count, col_count = exposures.shape
     padded = extended(exposures, 1, 2, HALO)
-    warped, flagged = warp_and_flag(padded, bad_pixels, offsets, warp_index)
+    by_slot = warp_by_slot(padded, bad_pixels, offsets, warp_index)
     groups = lax.axis_size("exp")
-    arrived = [flagged[0]]
-    for step in range(1, groups):
-        pairs = [(i, (i + step) % groups) for i in range(groups)]
-        arrived.append(lax.ppermute(flagged[step], "exp", pairs))
-    band = stack_median(jnp.concatenate(arrived, axis=0))
+    if by_slot is not None:
+        warped, stack = by_slot
+    else:
+        warped, flagged = warp_and_flag(padded, bad_pixels, offsets, warp_index)
+        arrived = [flagged[0]]
+        for step in range(1, groups):
+            pairs = [(i, (i + step) % groups) for i in range(groups)]
+            arrived.append(lax.ppermute(flagged[step], "exp", pairs))
+        stack = jnp.concatenate(arrived, axis=0)
+    band = stack_median(stack)
     groups = lax.axis_size("exp")
     sides = lax.axis_size("col")
     band_rows = band.shape[0]

time: 81.6 us -> 84.6 us (1.037)
  Pallas kernels: 6.84 us -> 19.2 us
  starting transfers between devices: 26.6 us -> 21.7 us
  waiting for transfers between devices: 26.5 us -> 22.4 us
  other arithmetic: 11.8 us -> 10.4 us
  local copies, waits for them, and re-layouts: 7.48 us -> 8.47 us
    pallas_call x1 -> x4, Pallas kernels: 6.84 us -> 19.2 us  [warp_by_slot(): pl.pallas_call(functools.partial(_slot_kernel, step), out_shape=(shape, b...]
    all_to_all x1, starting transfers between devices: 8.99 us -> 3.46 us  [body(): lax.all_to_all(jnp.tile(band, (groups * sides, 1)), ('exp', 'col'), split...]
    ppermute x3, waiting for transfers between devices: 11.4 us -> 6.65 us  [warp_by_slot(): slots[step] = lax.ppermute(slots[step], 'exp', pairs)]
    ppermute x2, waiting for transfers between devices: 0.92 us -> 2.65 us  [_row_halo(): lax.ppermute(lax.slice_in_dim(block, size - width, None, axis=dim), 'row'...]
    squeeze x1 -> x0, local copies, waits for them, and re-layouts: 1.26 us -> none  [body(): arrived = [flagged[0]]]
    broadcast_in_dim x0 -> x1, local copies, waits for them, and re-layouts: none -> 1.1 us  [body(): residual = jnp.where(bad_pixels == 1, 0.0, warped - sky_model)]
    unnamed x6 -> x17, local copies, waits for them, and re-layouts: 0.21 us -> 1.24 us
  transfers between devices with their start and end apart: 9 -> 9, of which waited for: 7 -> 6; matrix products, arithmetic and copies ran while one was open for 6% -> 6% of each run, Pallas kernels for 0% -> 11%
where the time goes in v10:
time: 84.6 us; the launch traced here: 84.2 us
  waiting for transfers between devices  22.4 us (26%)
  starting transfers between devices  21.7 us (26%)
  Pallas kernels  19.2 us (23%)
  other arithmetic  10.4 us (12%)
  local copies, waits for them, and re-layouts  8.47 us (10%)
  between operations  0.87 us (1%)
    pallas_call x4, Pallas kernels, warp_by_slot(): pl.pallas_call(functools.partial(_slot_kernel, step), out_shape=(shape, b...  19.2 us
    ppermute x2, starting transfers between devices, _row_halo(): lax.ppermute(lax.slice_in_dim(block, size - width, None, axis=dim), 'row'...  8.44 us
    ppermute x2, waiting for transfers between devices, _row_halo(): lax.ppermute(lax.slice_in_dim(block, 0, width, axis=dim), 'row', backward)  6.81 us
    ppermute x3, waiting for transfers between devices, warp_by_slot(): slots[step] = lax.ppermute(slots[step], 'exp', pairs)  6.65 us
    all_to_all x1, waiting for transfers between devices, body(): lax.all_to_all(jnp.tile(band, (groups * sides, 1)), ('exp', 'col'), split...  6.34 us
    ppermute x3, starting transfers between devices, warp_by_slot(): slots[step] = lax.ppermute(slots[step], 'exp', pairs)  4.67 us
    ppermute x2, starting transfers between devices, _row_halo(): lax.ppermute(lax.slice_in_dim(block, 0, width, axis=dim), 'row', backward)  3.84 us
    all_to_all x1, starting transfers between devices, body(): lax.all_to_all(jnp.tile(band, (groups * sides, 1)), ('exp', 'col'), split...  3.46 us
  transfers between devices with their start and end apart: 9, of which 6 were waited for; matrix products, arithmetic and copies ran while one was open for 6% of the time, Pallas kernels for 11%

profile of v10, /device:TPU:1, one launch (start us, length us, event | category | flops | bytes accessed | tf_op | source)
XLA Modules:
  0.0 84.2 jit_solution(10208565062943230009)
XLA Ops:
  0.6 1.4 %fusion.103 = (f32[16,11,512]{2,1,0:T(8,128)S(1)}, f32[16,11,512]{2,1,0:T(8,128)S(1)}) fusion(f32[16,32,512]{2,1,0:T(8,128)} %param.8), kind=kLoop, calls=%fused_computation.203 | loop fusion | bytes 1441792 | tf_op jit(solution)/shard_map/slice | solution.py:27
  2.1 4.5 %collective-permute-start = (f32[16,11,512]{2,1,0:T(8,128)S(1)}, f32[16,11,512]{2,1,0:T(8,128)S(1)}, u32[]{:S(2)}, u32[]{:S(2)}) collective-permute-start(f32[16,11,512]{2,1,0:T(8,128)S(1)} %get-tuple-element.77), channel_id=1, source_target_pairs={{0,2},{2,4},{4,6},{1,3},{3,5},{5,7},{8,10},{10,12},{12,14},{9,11},... | collective-permute-start | bytes 1081352 | tf_op jit(solution)/shard_map/ppermute | solution.py:27
  6.6 1.9 %collective-permute-start.1 = (f32[16,11,512]{2,1,0:T(8,128)S(1)}, f32[16,11,512]{2,1,0:T(8,128)S(1)}, u32[]{:S(2)}, u32[]{:S(2)}) collective-permute-start(f32[16,11,512]{2,1,0:T(8,128)S(1)} %get-tuple-element.78), channel_id=1, source_target_pairs={{2,0},{4,2},{6,4},{3,1},{5,3},{7,5},{10,8},{12,10},{14,12},{11,9},... | collective-permute-start | bytes 1081352 | tf_op jit(solution)/shard_map/ppermute | solution.py:28
  8.6 0.8 slice_bitcast_fusion.25
  10.1 2.6 %collective-permute-done = f32[16,11,512]{2,1,0:T(8,128)S(1)} collective-permute-done((f32[16,11,512]{2,1,0:T(8,128)S(1)}, f32[16,11,512]{2,1,0:T(8,128)S(1)}, u32[]{:S(2)}, u32[]{:S(2)}) %collective-permute-start) | collective-permute-done | bytes 360480 | tf_op jit(solution)/shard_map/ppermute | solution.py:27
  12.7 4.4 %collective-permute-done.1 = f32[16,11,512]{2,1,0:T(8,128)S(1)} collective-permute-done((f32[16,11,512]{2,1,0:T(8,128)S(1)}, f32[16,11,512]{2,1,0:T(8,128)S(1)}, u32[]{:S(2)}, u32[]{:S(2)}) %collective-permute-start.1) | collective-permute-done | bytes 360480 | tf_op jit(solution)/shard_map/ppermute | solution.py:28
  17.7 1.3 %collective-permute-start.2 = (f32[11,864]{1,0:T(8,128)S(1)}, f32[11,864]{1,0:T(8,128)S(1)}, u32[]{:S(2)}, u32[]{:S(2)}) collective-permute-start(f32[11,864]{1,0:T(8,128)S(1)} %reshape.92), channel_id=1, source_target_pairs={{0,1},{1,0},{2,3},{3,2},{4,5},{5,4},{6,7},{7,6},{8,9},{9,8},{10,11... | collective-permute-start | bytes 114056 | tf_op jit(solution)/shard_map/ppermute | solution.py:47
  19.0 0.6 add_bitcast_fusion
  19.5 0.6 reshape.89.row_weight
  20.1 0.7 reshape.90.col_weight
  21.6 2.4 %select_maximum_fusion.padded = f32[16,56,640]{2,1,0:T(8,128)} fusion(f32[16,54,11]{2,1,0:T(8,128)S(1)} %bitcast.69, f32[16,54,11]{2,1,0:T(8,128)S(1)} %bitcast.68, f32[16,11,512]{2,1,0:T(8,128)S(1)} %collective-permute-done.1, f32[16,32,512]{2,1,0:T(8,128)S(1)} %copy-done.2, f32[16,11,512]{2,1,0:T(8,128)S(1)} %collective-permute-done), kind=kLoop, calls=%fused_computation.6 | loop fusion | flops 9748480 | bytes 4139264 | tf_op jit(solution)/shard_map/concatenate | solution.py:52
  24.0 1.1 %broadcast_in_dim.17.warped_in = f32[16,32,512]{2,1,0:T(8,128)} broadcast(f32[]{:T(128)} %constant.54.clone.1), dimensions={} | broadcast | bytes 1048580 | tf_op jit(solution)/shard_map/jit(_where)/broadcast_in_dim | solution.py:310
  25.1 4.8 %shard_map.68 = (f32[16,32,512]{2,1,0:T(8,128)}, f32[16,8,512]{2,1,0:T(8,128)}) custom-call(s32[16]{0:T(128)} %get-tuple-element.123.row_shift, s32[16]{0:T(128)} %get-tuple-element.122.col_shift, f32[96]{0:T(128)} %reshape.89.row_weight, f32[96]{0:T(128)} %reshape.90.col_weight, s32[1]{0:T(128)} %bitcast.4.me, ...), custom_call_target="tpu_custom_call", output_to_operand_aliasing={{0}: (7, {})} | custom-call | tf_op jit(solution)/shard_map/pallas_call | solution.py:250
  29.9 4.8 %shard_map.69 = (f32[16,32,512]{2,1,0:T(8,128)}, f32[16,8,512]{2,1,0:T(8,128)}) custom-call(s32[16]{0:T(128)} %get-tuple-element.123.row_shift, s32[16]{0:T(128)} %get-tuple-element.122.col_shift, f32[96]{0:T(128)} %reshape.89.row_weight, f32[96]{0:T(128)} %reshape.90.col_weight, s32[1]{0:T(128)} %bitcast.4.me, ...), custom_call_target="tpu_custom_call", output_to_operand_aliasing={{0}: (7, {})} | custom-call | tf_op jit(solution)/shard_map/pallas_call | solution.py:250
  34.7 1.3 %collective-permute-start.3 = (f32[16,8,512]{2,1,0:T(8,128)}, f32[16,8,512]{2,1,0:T(8,128)S(1)}, u32[]{:S(2)}, u32[]{:S(2)}) collective-permute-start(f32[16,8,512]{2,1,0:T(8,128)} %get-tuple-element.43), channel_id=1, source_target_pairs={{0,8},{8,16},{16,24},{24,0},{1,9},{9,17},{17,25},{25,1},{2,10},{10... | collective-permute-start | bytes 786440 | tf_op jit(solution)/shard_map/ppermute | solution.py:259
  36.0 2.3 %collective-permute-start.4 = (f32[16,8,512]{2,1,0:T(8,128)S(1)}, f32[16,8,512]{2,1,0:T(8,128)S(1)}, u32[]{:S(2)}, u32[]{:S(2)}) collective-permute-start(f32[16,8,512]{2,1,0:T(8,128)S(1)} %copy-done.5), channel_id=1, source_target_pairs={{0,16},{8,24},{16,0},{24,8},{1,17},{9,25},{17,1},{25,9},{2,18},{10... | collective-permute-start | bytes 786440 | tf_op jit(solution)/shard_map/ppermute | solution.py:259
  38.3 4.8 %shard_map.70 = (f32[16,32,512]{2,1,0:T(8,128)}, f32[16,8,512]{2,1,0:T(8,128)}) custom-call(s32[16]{0:T(128)} %get-tuple-element.123.row_shift, s32[16]{0:T(128)} %get-tuple-element.122.col_shift, f32[96]{0:T(128)} %reshape.89.row_weight, f32[96]{0:T(128)} %reshape.90.col_weight, s32[1]{0:T(128)} %bitcast.4.me, ...), custom_call_target="tpu_custom_call", output_to_operand_aliasing={{0}: (7, {})} | custom-call | tf_op jit(solution)/shard_map/pallas_call | solution.py:250
  43.1 4.8 %shard_map.71 = (f32[16,32,512]{2,1,0:T(8,128)}, f32[16,8,512]{2,1,0:T(8,128)}) custom-call(s32[16]{0:T(128)} %get-tuple-element.123.row_shift, s32[16]{0:T(128)} %get-tuple-element.122.col_shift, f32[96]{0:T(128)} %reshape.89.row_weight, f32[96]{0:T(128)} %reshape.90.col_weight, s32[1]{0:T(128)} %bitcast.4.me, ...), custom_call_target="tpu_custom_call", output_to_operand_aliasing={{0}: (7, {})} | custom-call | tf_op jit(solution)/shard_map/pallas_call | solution.py:250
  47.9 1.1 %collective-permute-start.5 = (f32[16,8,512]{2,1,0:T(8,128)S(1)}, f32[16,8,512]{2,1,0:T(8,128)S(1)}, u32[]{:S(2)}, u32[]{:S(2)}) collective-permute-start(f32[16,8,512]{2,1,0:T(8,128)S(1)} %copy-done.6), channel_id=1, source_target_pairs={{0,24},{8,0},{16,8},{24,16},{1,25},{9,1},{17,9},{25,17},{2,26},{10... | collective-permute-start | bytes 786440 | tf_op jit(solution)/shard_map/ppermute | solution.py:259
  49.0 1.0 %constant_dynamic-update-slice_fusion.3 = f32[64,8,512]{2,1,0:T(8,128)S(1)} fusion(f32[16,8,512]{2,1,0:T(8,128)} %get-tuple-element.42), kind=kLoop, calls=%fused_computation.91 | loop fusion | bytes 524288
  50.0 1.1 %collective-permute-done.4 = f32[16,8,512]{2,1,0:T(8,128)S(1)} collective-permute-done((f32[16,8,512]{2,1,0:T(8,128)S(1)}, f32[16,8,512]{2,1,0:T(8,128)S(1)}, u32[]{:S(2)}, u32[]{:S(2)}) %collective-permute-start.4) | collective-permute-done | bytes 262176 | tf_op jit(solution)/shard_map/ppermute | solution.py:259
  51.1 5.6 %collective-permute-done.5 = f32[16,8,512]{2,1,0:T(8,128)S(1)} collective-permute-done((f32[16,8,512]{2,1,0:T(8,128)S(1)}, f32[16,8,512]{2,1,0:T(8,128)S(1)}, u32[]{:S(2)}, u32[]{:S(2)}) %collective-permute-start.5) | collective-permute-done | bytes 262176 | tf_op jit(solution)/shard_map/ppermute | solution.py:259
  56.8 3.6 %while.13 = (s32[]{:T(128)}, f32[8,512]{1,0:T(8,128)S(1)}, f32[8,512]{1,0:T(8,128)S(1)}, f32[64,8,512]{2,1,0:T(8,128)S(1)}, f32[8,512]{1,0:T(8,128)S(1)}, /*index=5*/s32[]{:T(128)}, s32[]{:T(128)}) while((s32[]{:T(128)}, f32[8,512]{1,0:T(8,128)S(1)}, f32[8,512]{1,0:T(8,128)S(1)}, f32[64,8,512]{2,1,0:T(8,128)S(1)}, ...), condition=%wide.region_5.7_spmd.clone, body=%wide.region_3.6_spmd.clone.sunk | while | flops 1110019 | bytes 1302617 | solution.py:111
  60.6 0.7 tile.2
  61.3 3.5 %all-to-all-start = ((f32[8,8,512]{2,1,0:T(8,128)}), f32[8,8,512]{2,1,0:T(8,128)S(1)}, u32[]{:S(2)}, u32[]{:S(2)}) async-start(f32[8,8,512]{2,1,0:T(8,128)} %tile.2), calls=%async_computation | async-start | bytes 262144 | tf_op jit(solution)/shard_map/all_to_all | solution.py:281
  64.8 6.3 %all-to-all-done = f32[8,8,512]{2,1,0:T(8,128)S(1)} async-done(((f32[8,8,512]{2,1,0:T(8,128)}), f32[8,8,512]{2,1,0:T(8,128)S(1)}, u32[]{:S(2)}, u32[]{:S(2)}) %all-to-all-start) | async-done | bytes 131104 | tf_op jit(solution)/shard_map/all_to_all | solution.py:281
  71.3 3.9 %collective-permute-start.6 = (f32[4,520]{1,0:T(4,128)S(1)}, f32[4,520]{1,0:T(4,128)S(1)}, u32[]{:S(2)}, u32[]{:S(2)}) collective-permute-start(f32[4,520]{1,0:T(4,128)S(1)} %get-tuple-element.87), channel_id=1, source_target_pairs={{0,2},{2,4},{4,6},{1,3},{3,5},{5,7},{8,10},{10,12},{12,14},{9,11},... | collective-permute-start | bytes 24968 | tf_op jit(solution)/shard_map/ppermute | solution.py:27
  75.2 1.9 %collective-permute-start.7 = (f32[4,520]{1,0:T(4,128)S(1)}, f32[4,520]{1,0:T(4,128)S(1)}, u32[]{:S(2)}, u32[]{:S(2)}) collective-permute-start(f32[4,520]{1,0:T(4,128)S(1)} %get-tuple-element.88), channel_id=1, source_target_pairs={{2,0},{4,2},{6,4},{3,1},{5,3},{7,5},{10,8},{12,10},{14,12},{11,9},... | collective-permute-start | bytes 24968 | tf_op jit(solution)/shard_map/ppermute | solution.py:28
  77.1 0.6 constant_dynamic-slice_fusion
  77.8 2.4 %collective-permute-done.7 = f32[4,520]{1,0:T(4,128)S(1)} collective-permute-done((f32[4,520]{1,0:T(4,128)S(1)}, f32[4,520]{1,0:T(4,128)S(1)}, u32[]{:S(2)}, u32[]{:S(2)}) %collective-permute-start.7) | collective-permute-done | bytes 8352 | tf_op jit(solution)/shard_map/ppermute | solution.py:28
  80.9 1.3 %fusion.10 = f32[8,32,512]{2,1,0:T(8,128)S(1)} fusion(f32[8,32,520]{2,1,0:T(8,128)S(1)} %multiply_add_fusion, f32[8]{0:T(128)S(1)} %get-tuple-element.104, f32[8]{0:T(128)S(1)} %get-tuple-element.105, f32[8]{0:T(128)S(1)} %get-tuple-element.106, f32[8]{0:T(128)S(1)} %get-tuple-element.107, f32[8]{0:T(128)S(1)} %get-tuple-element.108, ...), kind=kLoop, calls=%fused_computation.24 | loop fusion | flops 2228224 | bytes 5243168 | tf_op jit(solution)/shard_map/add | solution.py:302
  82.4 1.8 %subtract_select_fusion = f32[16,32,512]{2,1,0:T(8,128)} fusion(f32[16,32,512]{2,1,0:T(8,128)S(1)} %copy-done, s32[16,32,512]{2,1,0:T(8,128)S(1)} %copy-done.1, f32[32,512]{1,0:T(8,128)S(1)} %get-tuple-element.80, f32[16]{0:T(128)S(1)} %get-tuple-element.113, f32[32,512]{1,0:T(8,128)S(1)} %get-tuple-element.81, f32[16]{0:T(128)S(1)} %get-tuple-element.114, ...), kind=kLoop, calls=%fused_computation.20 | loop fusion | flops 4718592 | bytes 3670528 | tf_op jit(solution)/shard_map/jit(_where)/select_n | solution.py:310
  (129 shorter events, 6.4 us)
Async XLA Ops:
  0.6 16.5 %copy-start.2 = (f32[16,32,512]{2,1,0:T(8,128)S(1)}, f32[16,32,512]{2,1,0:T(8,128)}, u32[]{:S(2)}) copy-start(f32[16,32,512]{2,1,0:T(8,128)} %param.8) | copy-start | bytes 3145732
  2.1 16.9 %copy-start.3 = (s32[16,2]{0,1:T(2,128)S(1)}, s32[16,2]{0,1:T(2,128)}, u32[]{:S(2)}) copy-start(s32[16,2]{0,1:T(2,128)} %param.10) | copy-start | bytes 388
  2.1 10.6 %collective-permute-start = (f32[16,11,512]{2,1,0:T(8,128)S(1)}, f32[16,11,512]{2,1,0:T(8,128)S(1)}, u32[]{:S(2)}, u32[]{:S(2)}) collective-permute-start(f32[16,11,512]{2,1,0:T(8,128)S(1)} %get-tuple-element.77), channel_id=1, source_target_pairs={{0,2},{2,4},{4,6},{1,3},{3,5},{5,7},{8,10},{10,12},{12,14},{9,11},... | collective-permute-start | bytes 1081352 | tf_op jit(solution)/shard_map/ppermute | solution.py:27
  6.6 10.5 %collective-permute-start.1 = (f32[16,11,512]{2,1,0:T(8,128)S(1)}, f32[16,11,512]{2,1,0:T(8,128)S(1)}, u32[]{:S(2)}, u32[]{:S(2)}) collective-permute-start(f32[16,11,512]{2,1,0:T(8,128)S(1)} %get-tuple-element.78), channel_id=1, source_target_pairs={{2,0},{4,2},{6,4},{3,1},{5,3},{7,5},{10,8},{12,10},{14,12},{11,9},... | collective-permute-start | bytes 1081352 | tf_op jit(solution)/shard_map/ppermute | solution.py:28
  17.7 3.1 %collective-permute-start.2 = (f32[11,864]{1,0:T(8,128)S(1)}, f32[11,864]{1,0:T(8,128)S(1)}, u32[]{:S(2)}, u32[]{:S(2)}) collective-permute-start(f32[11,864]{1,0:T(8,128)S(1)} %reshape.92), channel_id=1, source_target_pairs={{0,1},{1,0},{2,3},{3,2},{4,5},{5,4},{6,7},{7,6},{8,9},{9,8},{10,11... | collective-permute-start | bytes 114056 | tf_op jit(solution)/shard_map/ppermute | solution.py:47
  29.9 6.1 %copy-start.5 = (f32[16,8,512]{2,1,0:T(8,128)S(1)}, f32[16,8,512]{2,1,0:T(8,128)}, u32[]{:S(2)}) copy-start(f32[16,8,512]{2,1,0:T(8,128)} %get-tuple-element.44) | copy-start | bytes 786436
  29.9 8.4 %copy-start.4 = (s32[16]{0:T(128)S(1)}, s32[16]{0:T(128)}, u32[]{:S(2)}) copy-start(s32[16]{0:T(128)} %param.12) | copy-start | bytes 196
  34.7 15.3 %collective-permute-start.3 = (f32[16,8,512]{2,1,0:T(8,128)}, f32[16,8,512]{2,1,0:T(8,128)S(1)}, u32[]{:S(2)}, u32[]{:S(2)}) collective-permute-start(f32[16,8,512]{2,1,0:T(8,128)} %get-tuple-element.43), channel_id=1, source_target_pairs={{0,8},{8,16},{16,24},{24,0},{1,9},{9,17},{17,25},{25,1},{2,10},{10... | collective-permute-start | bytes 786440 | tf_op jit(solution)/shard_map/ppermute | solution.py:259
  36.0 15.1 %collective-permute-start.4 = (f32[16,8,512]{2,1,0:T(8,128)S(1)}, f32[16,8,512]{2,1,0:T(8,128)S(1)}, u32[]{:S(2)}, u32[]{:S(2)}) collective-permute-start(f32[16,8,512]{2,1,0:T(8,128)S(1)} %copy-done.5), channel_id=1, source_target_pairs={{0,16},{8,24},{16,0},{24,8},{1,17},{9,25},{17,1},{25,9},{2,18},{10... | collective-permute-start | bytes 786440 | tf_op jit(solution)/shard_map/ppermute | solution.py:259
  43.1 4.8 %copy-start.6 = (f32[16,8,512]{2,1,0:T(8,128)S(1)}, f32[16,8,512]{2,1,0:T(8,128)}, u32[]{:S(2)}) copy-start(f32[16,8,512]{2,1,0:T(8,128)} %get-tuple-element.45) | copy-start | bytes 786436
  47.9 8.7 %collective-permute-start.5 = (f32[16,8,512]{2,1,0:T(8,128)S(1)}, f32[16,8,512]{2,1,0:T(8,128)S(1)}, u32[]{:S(2)}, u32[]{:S(2)}) collective-permute-start(f32[16,8,512]{2,1,0:T(8,128)S(1)} %copy-done.6), channel_id=1, source_target_pairs={{0,24},{8,0},{16,8},{24,16},{1,25},{9,1},{17,9},{25,17},{2,26},{10... | collective-permute-start | bytes 786440 | tf_op jit(solution)/shard_map/ppermute | solution.py:259
  61.3 9.8 %all-to-all-start = ((f32[8,8,512]{2,1,0:T(8,128)}), f32[8,8,512]{2,1,0:T(8,128)S(1)}, u32[]{:S(2)}, u32[]{:S(2)}) async-start(f32[8,8,512]{2,1,0:T(8,128)} %tile.2), calls=%async_computation | async-start | bytes 262144 | tf_op jit(solution)/shard_map/all_to_all | solution.py:281
  71.3 6.5 %collective-permute-start.6 = (f32[4,520]{1,0:T(4,128)S(1)}, f32[4,520]{1,0:T(4,128)S(1)}, u32[]{:S(2)}, u32[]{:S(2)}) collective-permute-start(f32[4,520]{1,0:T(4,128)S(1)} %get-tuple-element.87), channel_id=1, source_target_pairs={{0,2},{2,4},{4,6},{1,3},{3,5},{5,7},{8,10},{10,12},{12,14},{9,11},... | collective-permute-start | bytes 24968 | tf_op jit(solution)/shard_map/ppermute | solution.py:27
  75.2 5.0 %collective-permute-start.7 = (f32[4,520]{1,0:T(4,128)S(1)}, f32[4,520]{1,0:T(4,128)S(1)}, u32[]{:S(2)}, u32[]{:S(2)}) collective-permute-start(f32[4,520]{1,0:T(4,128)S(1)} %get-tuple-element.88), channel_id=1, source_target_pairs={{2,0},{4,2},{6,4},{3,1},{5,3},{7,5},{10,8},{12,10},{14,12},{11,9},... | collective-permute-start | bytes 24968 | tf_op jit(solution)/shard_map/ppermute | solution.py:28
  80.8 1.3 %copy-start = (f32[16,32,512]{2,1,0:T(8,128)S(1)}, f32[16,32,512]{2,1,0:T(8,128)}, u32[]{:S(2)}) copy-start(f32[16,32,512]{2,1,0:T(8,128)} %get-tuple-element.41) | copy-start | bytes 3145732
  80.8 1.5 %copy-start.1 = (s32[16,32,512]{2,1,0:T(8,128)S(1)}, s32[16,32,512]{2,1,0:T(8,128)}, u32[]{:S(2)}) copy-start(s32[16,32,512]{2,1,0:T(8,128)} %bad.7) | copy-start | bytes 3145732

commit v11 on v10

--- a/solution.py
+++ b/solution.py
@@ -6,6 +6,7 @@
 from jax.sharding import PartitionSpec as P
 from jax.experimental import pallas as pl
 from jax.experimental.pallas import tpu as pltpu
+
 
 NFRAC = 16
 NPSF = 8
@@ -78,24 +79,6 @@
     return jnp.dot(chooser, kernel_table, precision=lax.Precision.HIGHEST)
 
 
-def placed_taps(weights, shifts):
-    reach = 2 * HALO + 1
-    positions = lax.broadcasted_iota(jnp.int32, (1, 1, reach), 2)
-    tap_slot = HALO + shifts[:, None, None] + lax.broadcasted_iota(jnp.int32, (1, 6, 1), 1) - 2
-    spread = (tap_slot == positions).astype(jnp.float32)
-    return jnp.sum(weights[:, :, None] * spread, axis=1)
-
-
-def resample_axis(stack, coefficients, out_len, which_axis):
-    out_shape = list(stack.shape)
-    out_shape[which_axis] = out_len
-    total = jnp.zeros(tuple(out_shape), jnp.float32)
-    for position in range(2 * HALO + 1):
-        window = lax.slice_in_dim(stack, position, position + out_len, 1, which_axis)
-        total = total + coefficients[:, position, None, None] * window
-    return total
-
-
 def bisect_lower(valid_count, count_below):
 
     def one_pass(sweep_no, bounds):
@@ -191,19 +174,27 @@
     me,
     padded,
     bad,
-    warped_in,
     warped_out,
     flagged_out,
+    window_buf,
+    bad_buf,
+    sems,
 ):
     group_size, band_rows, col_count = flagged_out.shape
-    bands = warped_out.shape[1] // band_rows
+    bands = bad.shape[1] // band_rows
     width = padded.shape[2]
-    window = -(-(band_rows + 2 * HALO) // 8) * 8
+    window = window_buf.shape[1]
     band = lax.rem(me[0] + step, bands)
     base = pl.multiple_of(band * band_rows, 8)
+    fetch_rows = pltpu.make_async_copy(padded.at[:, pl.ds(base, window), :], window_buf, sems.at[0])
+    fetch_bad = pltpu.make_async_copy(bad.at[:, pl.ds(base, band_rows), :], bad_buf, sems.at[1])
+    fetch_rows.start()
+    fetch_bad.start()
+    fetch_rows.wait()
+    fetch_bad.wait()
 
     def one_exposure(e, carry):
-        block = pltpu.roll(padded[e, pl.ds(base, window), :], window - row_shift[e], 0)
+        block = pltpu.roll(window_buf[e], window - row_shift[e], 0)
         across = None
         for tap in range(TAPS):
             term = row_weight[e * TAPS + tap] * block[tap : tap + band_rows, :]
@@ -213,9 +204,8 @@
         for tap in range(TAPS):
             term = col_weight[e * TAPS + tap] * across[:, tap : tap + col_count]
             total = term if total is None else total + term
-        warped_out[e, pl.ds(base, band_rows), :] = total
-        flagged = jnp.where(bad[e, pl.ds(base, band_rows), :] == 1, sentinel, total)
-        flagged_out[e] = flagged
+        warped_out[e] = total
+        flagged_out[e] = jnp.where(bad_buf[e] == 1, sentinel, total)
         return carry
 
     lax.fori_loop(0, group_size, one_exposure, 0, unroll=True)
@@ -241,22 +231,31 @@
     )
     smem = pl.BlockSpec(memory_space=pltpu.SMEM)
     vmem = pl.BlockSpec(memory_space=pltpu.VMEM)
-    shape = jax.ShapeDtypeStruct((group_size, row_count, col_count), jnp.float32)
+    anywhere = pl.BlockSpec(memory_space=pl.ANY)
     banded = jax.ShapeDtypeStruct((group_size, band_rows, col_count), jnp.float32)
-    warped = jnp.zeros((group_size, row_count, col_count), jnp.float32)
     order = [bands // 2] + [s for s in range(1, bands) if s != bands // 2] + [0]
     slots = {}
+    warped_slots = {}
     for step in order:
-        warped, slots[step] = pl.pallas_call(
+        warped_slots[step], flagged = pl.pallas_call(
             functools.partial(_slot_kernel, step),
-            out_shape=(shape, banded),
-            in_specs=[smem, smem, smem, smem, smem, vmem, vmem, vmem],
+            out_shape=(banded, banded),
+            in_specs=[smem, smem, smem, smem, smem, anywhere, anywhere],
             out_specs=(vmem, vmem),
-            input_output_aliases={7: 0},
-        )(row_shift, col_shift, row_weight, col_weight, me, padded, bad_pixels, warped)
+            scratch_shapes=[
+                pltpu.VMEM((group_size, window, lanes), jnp.float32),
+                pltpu.VMEM((group_size, band_rows, col_count), jnp.int32),
+                pltpu.SemaphoreType.DMA((2,)),
+            ],
+        )(row_shift, col_shift, row_weight, col_weight, me, padded, bad_pixels)
         if step:
             pairs = [(i, (i + step) % bands) for i in range(bands)]
-            slots[step] = lax.ppermute(slots[step], "exp", pairs)
+            slots[step] = lax.ppermute(flagged, "exp", pairs)
+        else:
+            slots[step] = flagged
+    stacked = jnp.stack([warped_slots[s] for s in range(bands)])
+    natural = jnp.take(stacked, lax.rem(jnp.arange(bands) - me[0] + bands, bands), axis=0)
+    warped = natural.transpose(1, 0, 2, 3).reshape(group_size, row_count, col_count)
     return warped, jnp.concatenate([slots[s] for s in range(bands)], axis=0)
 
 

time: 84.6 us -> 82.1 us (0.970)
  waiting for transfers between devices: 22.4 us -> 20.4 us
  Pallas kernels: 19.2 us -> 17.5 us
  other arithmetic: 10.4 us -> 11.3 us
    pallas_call x4, Pallas kernels: 19.2 us -> 17.5 us  [warp_by_slot(): pl.pallas_call(functools.partial(_slot_kernel, step), out_shape=(banded,...]
    ppermute x3, waiting for transfers between devices: 6.65 us -> 5.05 us  [warp_by_slot(): slots[step] = lax.ppermute(flagged, 'exp', pairs)]
    broadcast_in_dim x1 -> x0, local copies, waits for them, and re-layouts: 1.1 us -> none  [body(): residual = jnp.where(bad_pixels == 1, 0.0, warped - sky_model)]
  transfers between devices with their start and end apart: 9 -> 9, of which waited for: 6 -> 5; matrix products, arithmetic and copies ran while one was open for 6% -> 8% of each run, Pallas kernels for 11% -> 16%
where the time goes in v11:
time: 82.1 us; the launch traced here: 81.6 us
  starting transfers between devices  22.5 us (27%)
  waiting for transfers between devices  20.4 us (25%)
  Pallas kernels  17.5 us (21%)
  other arithmetic  11.3 us (14%)
  local copies, waits for them, and re-layouts  7.79 us (9%)
  between operations  0.99 us (1%)
    pallas_call x4, Pallas kernels, warp_by_slot(): pl.pallas_call(functools.partial(_slot_kernel, step), out_shape=(banded,...  17.5 us
    ppermute x2, starting transfers between devices, _row_halo(): lax.ppermute(lax.slice_in_dim(block, size - width, None, axis=dim), 'row'...  8.91 us
    ppermute x2, waiting for transfers between devices, _row_halo(): lax.ppermute(lax.slice_in_dim(block, 0, width, axis=dim), 'row', backward)  6.81 us
    all_to_all x1, waiting for transfers between devices, body(): lax.all_to_all(jnp.tile(band, (groups * sides, 1)), ('exp', 'col'), split...  6.55 us
    ppermute x3, waiting for transfers between devices, warp_by_slot(): slots[step] = lax.ppermute(flagged, 'exp', pairs)  5.05 us
    ppermute x3, starting transfers between devices, warp_by_slot(): slots[step] = lax.ppermute(flagged, 'exp', pairs)  4.84 us
    ppermute x2, starting transfers between devices, _row_halo(): lax.ppermute(lax.slice_in_dim(block, 0, width, axis=dim), 'row', backward)  3.84 us
    all_to_all x1, starting transfers between devices, body(): lax.all_to_all(jnp.tile(band, (groups * sides, 1)), ('exp', 'col'), split...  3.62 us
  transfers between devices with their start and end apart: 9, of which 5 were waited for; matrix products, arithmetic and copies ran while one was open for 8% of the time, Pallas kernels for 16%

profile of v11, /device:TPU:1, one launch (start us, length us, event | category | flops | bytes accessed | tf_op | source)
XLA Modules:
  0.0 81.6 jit_solution(17503228050127440701)
XLA Ops:
  0.6 1.4 %fusion.107 = (f32[16,11,512]{2,1,0:T(8,128)S(1)}, f32[16,11,512]{2,1,0:T(8,128)S(1)}) fusion(f32[16,32,512]{2,1,0:T(8,128)} %param.8), kind=kLoop, calls=%fused_computation.218 | loop fusion | bytes 1441792 | tf_op jit(solution)/shard_map/slice | solution.py:28
  2.1 4.5 %collective-permute-start = (f32[16,11,512]{2,1,0:T(8,128)S(1)}, f32[16,11,512]{2,1,0:T(8,128)S(1)}, u32[]{:S(2)}, u32[]{:S(2)}) collective-permute-start(f32[16,11,512]{2,1,0:T(8,128)S(1)} %get-tuple-element.77), channel_id=1, source_target_pairs={{0,2},{2,4},{4,6},{1,3},{3,5},{5,7},{8,10},{10,12},{12,14},{9,11},... | collective-permute-start | bytes 1081352 | tf_op jit(solution)/shard_map/ppermute | solution.py:28
  6.6 1.9 %collective-permute-start.1 = (f32[16,11,512]{2,1,0:T(8,128)S(1)}, f32[16,11,512]{2,1,0:T(8,128)S(1)}, u32[]{:S(2)}, u32[]{:S(2)}) collective-permute-start(f32[16,11,512]{2,1,0:T(8,128)S(1)} %get-tuple-element.78), channel_id=1, source_target_pairs={{2,0},{4,2},{6,4},{3,1},{5,3},{7,5},{10,8},{12,10},{14,12},{11,9},... | collective-permute-start | bytes 1081352 | tf_op jit(solution)/shard_map/ppermute | solution.py:29
  8.6 0.8 slice_bitcast_fusion.25
  9.5 0.7 fusion.78
  10.7 2.0 %collective-permute-done = f32[16,11,512]{2,1,0:T(8,128)S(1)} collective-permute-done((f32[16,11,512]{2,1,0:T(8,128)S(1)}, f32[16,11,512]{2,1,0:T(8,128)S(1)}, u32[]{:S(2)}, u32[]{:S(2)}) %collective-permute-start) | collective-permute-done | bytes 360480 | tf_op jit(solution)/shard_map/ppermute | solution.py:28
  12.7 4.4 %collective-permute-done.1 = f32[16,11,512]{2,1,0:T(8,128)S(1)} collective-permute-done((f32[16,11,512]{2,1,0:T(8,128)S(1)}, f32[16,11,512]{2,1,0:T(8,128)S(1)}, u32[]{:S(2)}, u32[]{:S(2)}) %collective-permute-start.1) | collective-permute-done | bytes 360480 | tf_op jit(solution)/shard_map/ppermute | solution.py:29
  17.7 1.3 %collective-permute-start.2 = (f32[11,864]{1,0:T(8,128)S(1)}, f32[11,864]{1,0:T(8,128)S(1)}, u32[]{:S(2)}, u32[]{:S(2)}) collective-permute-start(f32[11,864]{1,0:T(8,128)S(1)} %reshape.137), channel_id=1, source_target_pairs={{0,1},{1,0},{2,3},{3,2},{4,5},{5,4},{6,7},{7,6},{8,9},{9,8},{10,11... | collective-permute-start | bytes 114056 | tf_op jit(solution)/shard_map/ppermute | solution.py:48
  19.0 0.6 add_bitcast_fusion
  19.6 0.6 reshape.134.row_weight
  20.2 0.6 reshape.135.col_weight
  21.6 2.4 %select_maximum_fusion.padded = f32[16,56,640]{2,1,0:T(8,128)} fusion(f32[16,54,11]{2,1,0:T(8,128)S(1)} %bitcast.82, f32[16,54,11]{2,1,0:T(8,128)S(1)} %bitcast.81, f32[16,11,512]{2,1,0:T(8,128)S(1)} %collective-permute-done.1, f32[16,32,512]{2,1,0:T(8,128)S(1)} %copy-done.1, f32[16,11,512]{2,1,0:T(8,128)S(1)} %collective-permute-done), kind=kLoop, calls=%fused_computation.7 | loop fusion | flops 9748480 | bytes 4139264 | tf_op jit(solution)/shard_map/concatenate | solution.py:53
  24.0 4.3 %shard_map.69 = (f32[16,8,512]{2,1,0:T(8,128)}, f32[16,8,512]{2,1,0:T(8,128)}) custom-call(s32[16]{0:T(128)} %get-tuple-element.123.row_shift, s32[16]{0:T(128)} %get-tuple-element.122.col_shift, f32[96]{0:T(128)} %reshape.134.row_weight, f32[96]{0:T(128)} %reshape.135.col_weight, s32[1]{0:T(128)} %bitcast.4.me, f32[16,56,640]{2,1,0:T(8,128)} %select_maximum_fusion.padded, ...), custom_call_target="tpu_custom_call" | custom-call | tf_op jit(solution)/shard_map/pallas_call | solution.py:240
  28.4 1.3 %collective-permute-start.3 = (f32[16,8,512]{2,1,0:T(8,128)}, f32[16,8,512]{2,1,0:T(8,128)S(1)}, u32[]{:S(2)}, u32[]{:S(2)}) collective-permute-start(f32[16,8,512]{2,1,0:T(8,128)} %get-tuple-element.43), channel_id=1, source_target_pairs={{0,8},{8,16},{16,24},{24,0},{1,9},{9,17},{17,25},{25,1},{2,10},{10... | collective-permute-start | bytes 786440 | tf_op jit(solution)/shard_map/ppermute | solution.py:253
  29.7 4.3 %shard_map.70 = (f32[16,8,512]{2,1,0:T(8,128)}, f32[16,8,512]{2,1,0:T(8,128)}) custom-call(s32[16]{0:T(128)} %get-tuple-element.123.row_shift, s32[16]{0:T(128)} %get-tuple-element.122.col_shift, f32[96]{0:T(128)} %reshape.134.row_weight, f32[96]{0:T(128)} %reshape.135.col_weight, s32[1]{0:T(128)} %bitcast.4.me, f32[16,56,640]{2,1,0:T(8,128)} %select_maximum_fusion.padded, ...), custom_call_target="tpu_custom_call" | custom-call | tf_op jit(solution)/shard_map/pallas_call | solution.py:240
  34.1 2.4 %collective-permute-start.4 = (f32[16,8,512]{2,1,0:T(8,128)}, f32[16,8,512]{2,1,0:T(8,128)S(1)}, u32[]{:S(2)}, u32[]{:S(2)}) collective-permute-start(f32[16,8,512]{2,1,0:T(8,128)} %get-tuple-element.44), channel_id=1, source_target_pairs={{0,16},{8,24},{16,0},{24,8},{1,17},{9,25},{17,1},{25,9},{2,18},{10... | collective-permute-start | bytes 786440 | tf_op jit(solution)/shard_map/ppermute | solution.py:253
  36.4 4.3 %shard_map.71 = (f32[16,8,512]{2,1,0:T(8,128)}, f32[16,8,512]{2,1,0:T(8,128)}) custom-call(s32[16]{0:T(128)} %get-tuple-element.123.row_shift, s32[16]{0:T(128)} %get-tuple-element.122.col_shift, f32[96]{0:T(128)} %reshape.134.row_weight, f32[96]{0:T(128)} %reshape.135.col_weight, s32[1]{0:T(128)} %bitcast.4.me, f32[16,56,640]{2,1,0:T(8,128)} %select_maximum_fusion.padded, ...), custom_call_target="tpu_custom_call" | custom-call | tf_op jit(solution)/shard_map/pallas_call | solution.py:240
  40.8 4.4 %shard_map.68 = (f32[16,8,512]{2,1,0:T(8,128)}, f32[16,8,512]{2,1,0:T(8,128)}) custom-call(s32[16]{0:T(128)} %get-tuple-element.123.row_shift, s32[16]{0:T(128)} %get-tuple-element.122.col_shift, f32[96]{0:T(128)} %reshape.134.row_weight, f32[96]{0:T(128)} %reshape.135.col_weight, s32[1]{0:T(128)} %bitcast.4.me, f32[16,56,640]{2,1,0:T(8,128)} %select_maximum_fusion.padded, ...), custom_call_target="tpu_custom_call" | custom-call | tf_op jit(solution)/shard_map/pallas_call | solution.py:240
  45.3 1.1 %collective-permute-start.5 = (f32[16,8,512]{2,1,0:T(8,128)S(1)}, f32[16,8,512]{2,1,0:T(8,128)S(1)}, u32[]{:S(2)}, u32[]{:S(2)}) collective-permute-start(f32[16,8,512]{2,1,0:T(8,128)S(1)} %copy-done.7), channel_id=1, source_target_pairs={{0,24},{8,0},{16,8},{24,16},{1,25},{9,1},{17,9},{25,17},{2,26},{10... | collective-permute-start | bytes 786440 | tf_op jit(solution)/shard_map/ppermute | solution.py:253
  46.4 1.0 %constant_dynamic-update-slice_fusion.3 = f32[64,8,512]{2,1,0:T(8,128)S(1)} fusion(f32[16,8,512]{2,1,0:T(8,128)} %get-tuple-element.42), kind=kLoop, calls=%fused_computation.101 | loop fusion | bytes 524288
  47.4 5.0 %collective-permute-done.5 = f32[16,8,512]{2,1,0:T(8,128)S(1)} collective-permute-done((f32[16,8,512]{2,1,0:T(8,128)S(1)}, f32[16,8,512]{2,1,0:T(8,128)S(1)}, u32[]{:S(2)}, u32[]{:S(2)}) %collective-permute-start.5) | collective-permute-done | bytes 262176 | tf_op jit(solution)/shard_map/ppermute | solution.py:253
  52.7 3.6 %while.13 = (s32[]{:T(128)}, f32[8,512]{1,0:T(8,128)S(1)}, f32[8,512]{1,0:T(8,128)S(1)}, f32[64,8,512]{2,1,0:T(8,128)S(1)}, f32[8,512]{1,0:T(8,128)S(1)}, /*index=5*/s32[]{:T(128)}, s32[]{:T(128)}) while((s32[]{:T(128)}, f32[8,512]{1,0:T(8,128)S(1)}, f32[8,512]{1,0:T(8,128)S(1)}, f32[64,8,512]{2,1,0:T(8,128)S(1)}, ...), condition=%wide.region_5.7_spmd.clone, body=%wide.region_3.6_spmd.clone.sunk | while | flops 1110019 | bytes 1302617 | solution.py:94
  56.5 0.7 tile.2
  57.2 3.6 %all-to-all-start = ((f32[8,8,512]{2,1,0:T(8,128)}), f32[8,8,512]{2,1,0:T(8,128)S(1)}, u32[]{:S(2)}, u32[]{:S(2)}) async-start(f32[8,8,512]{2,1,0:T(8,128)} %tile.2), calls=%async_computation | async-start | bytes 262144 | tf_op jit(solution)/shard_map/all_to_all | solution.py:280
  60.9 0.6 gather_fusion
  61.6 6.6 %all-to-all-done = f32[8,8,512]{2,1,0:T(8,128)S(1)} async-done(((f32[8,8,512]{2,1,0:T(8,128)}), f32[8,8,512]{2,1,0:T(8,128)S(1)}, u32[]{:S(2)}, u32[]{:S(2)}) %all-to-all-start) | async-done | bytes 131104 | tf_op jit(solution)/shard_map/all_to_all | solution.py:280
  68.3 4.4 %collective-permute-start.6 = (f32[4,520]{1,0:T(4,128)S(1)}, f32[4,520]{1,0:T(4,128)S(1)}, u32[]{:S(2)}, u32[]{:S(2)}) collective-permute-start(f32[4,520]{1,0:T(4,128)S(1)} %get-tuple-element.87), channel_id=1, source_target_pairs={{0,2},{2,4},{4,6},{1,3},{3,5},{5,7},{8,10},{10,12},{12,14},{9,11},... | collective-permute-start | bytes 24968 | tf_op jit(solution)/shard_map/ppermute | solution.py:28
  72.7 1.9 %collective-permute-start.7 = (f32[4,520]{1,0:T(4,128)S(1)}, f32[4,520]{1,0:T(4,128)S(1)}, u32[]{:S(2)}, u32[]{:S(2)}) collective-permute-start(f32[4,520]{1,0:T(4,128)S(1)} %get-tuple-element.88), channel_id=1, source_target_pairs={{2,0},{4,2},{6,4},{3,1},{5,3},{7,5},{10,8},{12,10},{14,12},{11,9},... | collective-permute-start | bytes 24968 | tf_op jit(solution)/shard_map/ppermute | solution.py:29
  74.6 0.6 constant_dynamic-slice_fusion
  75.3 2.4 %collective-permute-done.7 = f32[4,520]{1,0:T(4,128)S(1)} collective-permute-done((f32[4,520]{1,0:T(4,128)S(1)}, f32[4,520]{1,0:T(4,128)S(1)}, u32[]{:S(2)}, u32[]{:S(2)}) %collective-permute-start.7) | collective-permute-done | bytes 8352 | tf_op jit(solution)/shard_map/ppermute | solution.py:29
  78.3 1.3 %fusion.11 = f32[8,32,512]{2,1,0:T(8,128)S(1)} fusion(f32[8,32,520]{2,1,0:T(8,128)S(1)} %multiply_add_fusion, f32[8]{0:T(128)S(1)} %get-tuple-element.104, f32[8]{0:T(128)S(1)} %get-tuple-element.105, f32[8]{0:T(128)S(1)} %get-tuple-element.106, f32[8]{0:T(128)S(1)} %get-tuple-element.107, f32[8]{0:T(128)S(1)} %get-tuple-element.108, ...), kind=kLoop, calls=%fused_computation.28 | loop fusion | flops 2228224 | bytes 5243168 | tf_op jit(solution)/shard_map/add | solution.py:301
  79.6 2.0 %fusion.10 = f32[16,32,512]{2,1,0:T(8,128)} fusion(s32[16,32,512]{2,1,0:T(8,128)S(1)} %copy-done, f32[32,512]{1,0:T(8,128)S(1)} %get-tuple-element.80, f32[16]{0:T(128)S(1)} %get-tuple-element.113, f32[32,512]{1,0:T(8,128)S(1)} %get-tuple-element.81, f32[16]{0:T(128)S(1)} %get-tuple-element.114, f32[32,512]{1,0:T(8,128)S(1)} %get-tuple-element.82, ...), kind=kLoop, calls=%fused_computation.23 | loop fusion | flops 4980736 | bytes 3670532 | tf_op jit(solution)/shard_map/jit(_where)/select_n | solution.py:309
  (135 shorter events, 6.3 us)
Async XLA Ops:
  0.6 16.5 %copy-start.1 = (f32[16,32,512]{2,1,0:T(8,128)S(1)}, f32[16,32,512]{2,1,0:T(8,128)}, u32[]{:S(2)}) copy-start(f32[16,32,512]{2,1,0:T(8,128)} %param.8) | copy-start | bytes 3145732
  2.1 16.9 %copy-start.6 = (s32[16,2]{0,1:T(2,128)S(1)}, s32[16,2]{0,1:T(2,128)}, u32[]{:S(2)}) copy-start(s32[16,2]{0,1:T(2,128)} %param.10) | copy-start | bytes 388
  2.1 10.6 %collective-permute-start = (f32[16,11,512]{2,1,0:T(8,128)S(1)}, f32[16,11,512]{2,1,0:T(8,128)S(1)}, u32[]{:S(2)}, u32[]{:S(2)}) collective-permute-start(f32[16,11,512]{2,1,0:T(8,128)S(1)} %get-tuple-element.77), channel_id=1, source_target_pairs={{0,2},{2,4},{4,6},{1,3},{3,5},{5,7},{8,10},{10,12},{12,14},{9,11},... | collective-permute-start | bytes 1081352 | tf_op jit(solution)/shard_map/ppermute | solution.py:28
  6.6 10.5 %collective-permute-start.1 = (f32[16,11,512]{2,1,0:T(8,128)S(1)}, f32[16,11,512]{2,1,0:T(8,128)S(1)}, u32[]{:S(2)}, u32[]{:S(2)}) collective-permute-start(f32[16,11,512]{2,1,0:T(8,128)S(1)} %get-tuple-element.78), channel_id=1, source_target_pairs={{2,0},{4,2},{6,4},{3,1},{5,3},{7,5},{10,8},{12,10},{14,12},{11,9},... | collective-permute-start | bytes 1081352 | tf_op jit(solution)/shard_map/ppermute | solution.py:29
  17.7 3.1 %collective-permute-start.2 = (f32[11,864]{1,0:T(8,128)S(1)}, f32[11,864]{1,0:T(8,128)S(1)}, u32[]{:S(2)}, u32[]{:S(2)}) collective-permute-start(f32[11,864]{1,0:T(8,128)S(1)} %reshape.137), channel_id=1, source_target_pairs={{0,1},{1,0},{2,3},{3,2},{4,5},{5,4},{6,7},{7,6},{8,9},{9,8},{10,11... | collective-permute-start | bytes 114056 | tf_op jit(solution)/shard_map/ppermute | solution.py:48
  28.4 19.0 %collective-permute-start.3 = (f32[16,8,512]{2,1,0:T(8,128)}, f32[16,8,512]{2,1,0:T(8,128)S(1)}, u32[]{:S(2)}, u32[]{:S(2)}) collective-permute-start(f32[16,8,512]{2,1,0:T(8,128)} %get-tuple-element.43), channel_id=1, source_target_pairs={{0,8},{8,16},{16,24},{24,0},{1,9},{9,17},{17,25},{25,1},{2,10},{10... | collective-permute-start | bytes 786440 | tf_op jit(solution)/shard_map/ppermute | solution.py:253
  34.1 13.3 %collective-permute-start.4 = (f32[16,8,512]{2,1,0:T(8,128)}, f32[16,8,512]{2,1,0:T(8,128)S(1)}, u32[]{:S(2)}, u32[]{:S(2)}) collective-permute-start(f32[16,8,512]{2,1,0:T(8,128)} %get-tuple-element.44), channel_id=1, source_target_pairs={{0,16},{8,24},{16,0},{24,8},{1,17},{9,25},{17,1},{25,9},{2,18},{10... | collective-permute-start | bytes 786440 | tf_op jit(solution)/shard_map/ppermute | solution.py:253
  40.8 4.5 %copy-start.7 = (f32[16,8,512]{2,1,0:T(8,128)S(1)}, f32[16,8,512]{2,1,0:T(8,128)}, u32[]{:S(2)}) copy-start(f32[16,8,512]{2,1,0:T(8,128)} %get-tuple-element.45) | copy-start | bytes 786436
  45.3 7.2 %collective-permute-start.5 = (f32[16,8,512]{2,1,0:T(8,128)S(1)}, f32[16,8,512]{2,1,0:T(8,128)S(1)}, u32[]{:S(2)}, u32[]{:S(2)}) collective-permute-start(f32[16,8,512]{2,1,0:T(8,128)S(1)} %copy-done.7), channel_id=1, source_target_pairs={{0,24},{8,0},{16,8},{24,16},{1,25},{9,1},{17,9},{25,17},{2,26},{10... | collective-permute-start | bytes 786440 | tf_op jit(solution)/shard_map/ppermute | solution.py:253
  52.7 8.2 %copy-start.2 = (f32[16,8,512]{2,1,0:T(8,128)S(1)}, f32[16,8,512]{2,1,0:T(8,128)}, u32[]{:S(2)}) copy-start(f32[16,8,512]{2,1,0:T(8,128)} %get-tuple-element.39) | copy-start | bytes 786436
  52.7 8.2 %copy-start.3 = (f32[16,8,512]{2,1,0:T(8,128)S(1)}, f32[16,8,512]{2,1,0:T(8,128)}, u32[]{:S(2)}) copy-start(f32[16,8,512]{2,1,0:T(8,128)} %get-tuple-element.40) | copy-start | bytes 786436
  52.7 8.2 %copy-start.4 = (f32[16,8,512]{2,1,0:T(8,128)S(1)}, f32[16,8,512]{2,1,0:T(8,128)}, u32[]{:S(2)}) copy-start(f32[16,8,512]{2,1,0:T(8,128)} %get-tuple-element.41) | copy-start | bytes 786436
  52.7 8.2 %copy-start.5 = (f32[16,8,512]{2,1,0:T(8,128)S(1)}, f32[16,8,512]{2,1,0:T(8,128)}, u32[]{:S(2)}) copy-start(f32[16,8,512]{2,1,0:T(8,128)} %get-tuple-element.38) | copy-start | bytes 786436
  57.2 10.9 %all-to-all-start = ((f32[8,8,512]{2,1,0:T(8,128)}), f32[8,8,512]{2,1,0:T(8,128)S(1)}, u32[]{:S(2)}, u32[]{:S(2)}) async-start(f32[8,8,512]{2,1,0:T(8,128)} %tile.2), calls=%async_computation | async-start | bytes 262144 | tf_op jit(solution)/shard_map/all_to_all | solution.py:280
  68.3 7.0 %collective-permute-start.6 = (f32[4,520]{1,0:T(4,128)S(1)}, f32[4,520]{1,0:T(4,128)S(1)}, u32[]{:S(2)}, u32[]{:S(2)}) collective-permute-start(f32[4,520]{1,0:T(4,128)S(1)} %get-tuple-element.87), channel_id=1, source_target_pairs={{0,2},{2,4},{4,6},{1,3},{3,5},{5,7},{8,10},{10,12},{12,14},{9,11},... | collective-permute-start | bytes 24968 | tf_op jit(solution)/shard_map/ppermute | solution.py:28
  72.7 5.0 %collective-permute-start.7 = (f32[4,520]{1,0:T(4,128)S(1)}, f32[4,520]{1,0:T(4,128)S(1)}, u32[]{:S(2)}, u32[]{:S(2)}) collective-permute-start(f32[4,520]{1,0:T(4,128)S(1)} %get-tuple-element.88), channel_id=1, source_target_pairs={{2,0},{4,2},{6,4},{3,1},{5,3},{7,5},{10,8},{12,10},{14,12},{11,9},... | collective-permute-start | bytes 24968 | tf_op jit(solution)/shard_map/ppermute | solution.py:29
  78.3 1.3 %copy-start = (s32[16,32,512]{2,1,0:T(8,128)S(1)}, s32[16,32,512]{2,1,0:T(8,128)}, u32[]{:S(2)}) copy-start(s32[16,32,512]{2,1,0:T(8,128)} %bad.7) | copy-start | bytes 3145732

commit v12 on v11

--- a/solution.py
+++ b/solution.py
@@ -186,15 +186,21 @@
     window = window_buf.shape[1]
     band = lax.rem(me[0] + step, bands)
     base = pl.multiple_of(band * band_rows, 8)
-    fetch_rows = pltpu.make_async_copy(padded.at[:, pl.ds(base, window), :], window_buf, sems.at[0])
-    fetch_bad = pltpu.make_async_copy(bad.at[:, pl.ds(base, band_rows), :], bad_buf, sems.at[1])
-    fetch_rows.start()
+    fetch_bad = pltpu.make_async_copy(bad.at[:, pl.ds(base, band_rows), :], bad_buf, sems.at[2])
+
+    def fetch(e):
+        return pltpu.make_async_copy(
+            padded.at[e, pl.ds(base, window), :], window_buf.at[e % 2], sems.at[e % 2]
+        )
+
+    fetch(0).start()
     fetch_bad.start()
-    fetch_rows.wait()
     fetch_bad.wait()
-
-    def one_exposure(e, carry):
-        block = pltpu.roll(window_buf[e], window - row_shift[e], 0)
+    for e in range(group_size):
+        if e + 1 < group_size:
+            fetch(e + 1).start()
+        fetch(e).wait()
+        block = pltpu.roll(window_buf[e % 2], window - row_shift[e], 0)
         across = None
         for tap in range(TAPS):
             term = row_weight[e * TAPS + tap] * block[tap : tap + band_rows, :]
@@ -206,9 +212,6 @@
             total = term if total is None else total + term
         warped_out[e] = total
         flagged_out[e] = jnp.where(bad_buf[e] == 1, sentinel, total)
-        return carry
-
-    lax.fori_loop(0, group_size, one_exposure, 0, unroll=True)
 
 
 def warp_by_slot(padded, bad_pixels, offsets, warp_index):
@@ -243,9 +246,9 @@
             in_specs=[smem, smem, smem, smem, smem, anywhere, anywhere],
             out_specs=(vmem, vmem),
             scratch_shapes=[
-                pltpu.VMEM((group_size, window, lanes), jnp.float32),
+                pltpu.VMEM((2, window, lanes), jnp.float32),
                 pltpu.VMEM((group_size, band_rows, col_count), jnp.int32),
-                pltpu.SemaphoreType.DMA((2,)),
+                pltpu.SemaphoreType.DMA((3,)),
             ],
         )(row_shift, col_shift, row_weight, col_weight, me, padded, bad_pixels)
         if step:

time: 82.1 us -> 106 us (1.29); the launches traced: 81.6 us -> 104 us
  Pallas kernels: 17.5 us -> 40.1 us
  starting transfers between devices: 22.5 us -> 25.7 us
  waiting for transfers between devices: 20.4 us -> 17.2 us
    pallas_call x4, Pallas kernels: 17.5 us -> 40.1 us  [warp_by_slot(): pl.pallas_call(functools.partial(_slot_kernel, step), out_shape=(banded,...]
    ppermute x3, waiting for transfers between devices: 5.05 us -> 3.11 us  [warp_by_slot(): slots[step] = lax.ppermute(flagged, 'exp', pairs)]
    ppermute x2, starting transfers between devices: 8.91 us -> 10.6 us  [_row_halo(): lax.ppermute(lax.slice_in_dim(block, size - width, None, axis=dim), 'row'...]
    all_to_all x1, starting transfers between devices: 3.62 us -> 5.04 us  [body(): lax.all_to_all(jnp.tile(band, (groups * sides, 1)), ('exp', 'col'), split...]
    all_to_all x1, waiting for transfers between devices: 6.55 us -> 5.44 us  [body(): lax.all_to_all(jnp.tile(band, (groups * sides, 1)), ('exp', 'col'), split...]
  transfers between devices with their start and end apart: 9 -> 9, of which waited for: 5 -> 5; matrix products, arithmetic and copies ran while one was open for 8% -> 6% of each run, Pallas kernels for 16% -> 29%
where the time goes in v12:
time: 106 us; the launch traced here: 104 us
  Pallas kernels  40.1 us (38%)
  starting transfers between devices  25.7 us (24%)
  waiting for transfers between devices  17.2 us (16%)
  other arithmetic  11.3 us (11%)
  local copies, waits for them, and re-layouts  7.79 us (7%)
    pallas_call x4, Pallas kernels, warp_by_slot(): pl.pallas_call(functools.partial(_slot_kernel, step), out_shape=(banded,...  40.1 us
    ppermute x2, starting transfers between devices, _row_halo(): lax.ppermute(lax.slice_in_dim(block, size - width, None, axis=dim), 'row'...  10.6 us
    ppermute x2, waiting for transfers between devices, _row_halo(): lax.ppermute(lax.slice_in_dim(block, 0, width, axis=dim), 'row', backward)  6.63 us
    all_to_all x1, waiting for transfers between devices, body(): lax.all_to_all(jnp.tile(band, (groups * sides, 1)), ('exp', 'col'), split...  5.44 us
    all_to_all x1, starting transfers between devices, body(): lax.all_to_all(jnp.tile(band, (groups * sides, 1)), ('exp', 'col'), split...  5.04 us
    ppermute x3, starting transfers between devices, warp_by_slot(): slots[step] = lax.ppermute(flagged, 'exp', pairs)  4.84 us
    ppermute x2, starting transfers between devices, _row_halo(): lax.ppermute(lax.slice_in_dim(block, 0, width, axis=dim), 'row', backward)  4.02 us
    ppermute x3, waiting for transfers between devices, warp_by_slot(): slots[step] = lax.ppermute(flagged, 'exp', pairs)  3.11 us
  transfers between devices with their start and end apart: 9, of which 5 were waited for; matrix products, arithmetic and copies ran while one was open for 6% of the time, Pallas kernels for 29%

profile of v12, /device:TPU:1, one launch (start us, length us, event | category | flops | bytes accessed | tf_op | source)
XLA Modules:
  0.0 104.2 jit_solution(7102857420785936269)
XLA Ops:
  0.6 1.4 %fusion.107 = (f32[16,11,512]{2,1,0:T(8,128)S(1)}, f32[16,11,512]{2,1,0:T(8,128)S(1)}) fusion(f32[16,32,512]{2,1,0:T(8,128)} %param.8), kind=kLoop, calls=%fused_computation.218 | loop fusion | bytes 1441792 | tf_op jit(solution)/shard_map/slice | solution.py:28
  2.1 4.5 %collective-permute-start = (f32[16,11,512]{2,1,0:T(8,128)S(1)}, f32[16,11,512]{2,1,0:T(8,128)S(1)}, u32[]{:S(2)}, u32[]{:S(2)}) collective-permute-start(f32[16,11,512]{2,1,0:T(8,128)S(1)} %get-tuple-element.77), channel_id=1, source_target_pairs={{0,2},{2,4},{4,6},{1,3},{3,5},{5,7},{8,10},{10,12},{12,14},{9,11},... | collective-permute-start | bytes 1081352 | tf_op jit(solution)/shard_map/ppermute | solution.py:28
  6.6 1.9 %collective-permute-start.1 = (f32[16,11,512]{2,1,0:T(8,128)S(1)}, f32[16,11,512]{2,1,0:T(8,128)S(1)}, u32[]{:S(2)}, u32[]{:S(2)}) collective-permute-start(f32[16,11,512]{2,1,0:T(8,128)S(1)} %get-tuple-element.78), channel_id=1, source_target_pairs={{2,0},{4,2},{6,4},{3,1},{5,3},{7,5},{10,8},{12,10},{14,12},{11,9},... | collective-permute-start | bytes 1081352 | tf_op jit(solution)/shard_map/ppermute | solution.py:29
  8.6 0.8 slice_bitcast_fusion.25
  9.5 0.7 fusion.78
  10.7 2.0 %collective-permute-done = f32[16,11,512]{2,1,0:T(8,128)S(1)} collective-permute-done((f32[16,11,512]{2,1,0:T(8,128)S(1)}, f32[16,11,512]{2,1,0:T(8,128)S(1)}, u32[]{:S(2)}, u32[]{:S(2)}) %collective-permute-start) | collective-permute-done | bytes 360480 | tf_op jit(solution)/shard_map/ppermute | solution.py:28
  12.7 4.4 %collective-permute-done.1 = f32[16,11,512]{2,1,0:T(8,128)S(1)} collective-permute-done((f32[16,11,512]{2,1,0:T(8,128)S(1)}, f32[16,11,512]{2,1,0:T(8,128)S(1)}, u32[]{:S(2)}, u32[]{:S(2)}) %collective-permute-start.1) | collective-permute-done | bytes 360480 | tf_op jit(solution)/shard_map/ppermute | solution.py:29
  17.7 1.3 %collective-permute-start.2 = (f32[11,864]{1,0:T(8,128)S(1)}, f32[11,864]{1,0:T(8,128)S(1)}, u32[]{:S(2)}, u32[]{:S(2)}) collective-permute-start(f32[11,864]{1,0:T(8,128)S(1)} %reshape.137), channel_id=1, source_target_pairs={{0,1},{1,0},{2,3},{3,2},{4,5},{5,4},{6,7},{7,6},{8,9},{9,8},{10,11... | collective-permute-start | bytes 114056 | tf_op jit(solution)/shard_map/ppermute | solution.py:48
  19.0 0.6 add_bitcast_fusion
  19.6 0.6 reshape.134.row_weight
  20.2 0.6 reshape.135.col_weight
  21.6 2.4 %select_maximum_fusion.padded = f32[16,56,640]{2,1,0:T(8,128)} fusion(f32[16,54,11]{2,1,0:T(8,128)S(1)} %bitcast.82, f32[16,54,11]{2,1,0:T(8,128)S(1)} %bitcast.81, f32[16,11,512]{2,1,0:T(8,128)S(1)} %collective-permute-done.1, f32[16,32,512]{2,1,0:T(8,128)S(1)} %copy-done.1, f32[16,11,512]{2,1,0:T(8,128)S(1)} %collective-permute-done), kind=kLoop, calls=%fused_computation.7 | loop fusion | flops 9748480 | bytes 4139264 | tf_op jit(solution)/shard_map/concatenate | solution.py:53
  24.0 10.0 %shard_map.69 = (f32[16,8,512]{2,1,0:T(8,128)}, f32[16,8,512]{2,1,0:T(8,128)}) custom-call(s32[16]{0:T(128)} %get-tuple-element.123.row_shift, s32[16]{0:T(128)} %get-tuple-element.122.col_shift, f32[96]{0:T(128)} %reshape.134.row_weight, f32[96]{0:T(128)} %reshape.135.col_weight, s32[1]{0:T(128)} %bitcast.4.me, f32[16,56,640]{2,1,0:T(8,128)} %select_maximum_fusion.padded, ...), custom_call_target="tpu_custom_call" | custom-call | tf_op jit(solution)/shard_map/pallas_call | solution.py:243
  34.0 1.3 %collective-permute-start.3 = (f32[16,8,512]{2,1,0:T(8,128)}, f32[16,8,512]{2,1,0:T(8,128)S(1)}, u32[]{:S(2)}, u32[]{:S(2)}) collective-permute-start(f32[16,8,512]{2,1,0:T(8,128)} %get-tuple-element.43), channel_id=1, source_target_pairs={{0,8},{8,16},{16,24},{24,0},{1,9},{9,17},{17,25},{25,1},{2,10},{10... | collective-permute-start | bytes 786440 | tf_op jit(solution)/shard_map/ppermute | solution.py:256
  35.4 10.0 %shard_map.70 = (f32[16,8,512]{2,1,0:T(8,128)}, f32[16,8,512]{2,1,0:T(8,128)}) custom-call(s32[16]{0:T(128)} %get-tuple-element.123.row_shift, s32[16]{0:T(128)} %get-tuple-element.122.col_shift, f32[96]{0:T(128)} %reshape.134.row_weight, f32[96]{0:T(128)} %reshape.135.col_weight, s32[1]{0:T(128)} %bitcast.4.me, f32[16,56,640]{2,1,0:T(8,128)} %select_maximum_fusion.padded, ...), custom_call_target="tpu_custom_call" | custom-call | tf_op jit(solution)/shard_map/pallas_call | solution.py:243
  45.4 2.4 %collective-permute-start.4 = (f32[16,8,512]{2,1,0:T(8,128)}, f32[16,8,512]{2,1,0:T(8,128)S(1)}, u32[]{:S(2)}, u32[]{:S(2)}) collective-permute-start(f32[16,8,512]{2,1,0:T(8,128)} %get-tuple-element.44), channel_id=1, source_target_pairs={{0,16},{8,24},{16,0},{24,8},{1,17},{9,25},{17,1},{25,9},{2,18},{10... | collective-permute-start | bytes 786440 | tf_op jit(solution)/shard_map/ppermute | solution.py:256
  47.8 10.0 %shard_map.71 = (f32[16,8,512]{2,1,0:T(8,128)}, f32[16,8,512]{2,1,0:T(8,128)}) custom-call(s32[16]{0:T(128)} %get-tuple-element.123.row_shift, s32[16]{0:T(128)} %get-tuple-element.122.col_shift, f32[96]{0:T(128)} %reshape.134.row_weight, f32[96]{0:T(128)} %reshape.135.col_weight, s32[1]{0:T(128)} %bitcast.4.me, f32[16,56,640]{2,1,0:T(8,128)} %select_maximum_fusion.padded, ...), custom_call_target="tpu_custom_call" | custom-call | tf_op jit(solution)/shard_map/pallas_call | solution.py:243
  57.8 10.1 %shard_map.68 = (f32[16,8,512]{2,1,0:T(8,128)}, f32[16,8,512]{2,1,0:T(8,128)}) custom-call(s32[16]{0:T(128)} %get-tuple-element.123.row_shift, s32[16]{0:T(128)} %get-tuple-element.122.col_shift, f32[96]{0:T(128)} %reshape.134.row_weight, f32[96]{0:T(128)} %reshape.135.col_weight, s32[1]{0:T(128)} %bitcast.4.me, f32[16,56,640]{2,1,0:T(8,128)} %select_maximum_fusion.padded, ...), custom_call_target="tpu_custom_call" | custom-call | tf_op jit(solution)/shard_map/pallas_call | solution.py:243
  67.9 1.1 %collective-permute-start.5 = (f32[16,8,512]{2,1,0:T(8,128)S(1)}, f32[16,8,512]{2,1,0:T(8,128)S(1)}, u32[]{:S(2)}, u32[]{:S(2)}) collective-permute-start(f32[16,8,512]{2,1,0:T(8,128)S(1)} %copy-done.7), channel_id=1, source_target_pairs={{0,24},{8,0},{16,8},{24,16},{1,25},{9,1},{17,9},{25,17},{2,26},{10... | collective-permute-start | bytes 786440 | tf_op jit(solution)/shard_map/ppermute | solution.py:256
  69.0 1.0 constant_dynamic-update-slice_fusion.3
  70.1 3.1 %collective-permute-done.5 = f32[16,8,512]{2,1,0:T(8,128)S(1)} collective-permute-done((f32[16,8,512]{2,1,0:T(8,128)S(1)}, f32[16,8,512]{2,1,0:T(8,128)S(1)}, u32[]{:S(2)}, u32[]{:S(2)}) %collective-permute-start.5) | collective-permute-done | bytes 262176 | tf_op jit(solution)/shard_map/ppermute | solution.py:256
  73.4 3.6 %while.13 = (s32[]{:T(128)}, f32[8,512]{1,0:T(8,128)S(1)}, f32[8,512]{1,0:T(8,128)S(1)}, f32[64,8,512]{2,1,0:T(8,128)S(1)}, f32[8,512]{1,0:T(8,128)S(1)}, /*index=5*/s32[]{:T(128)}, s32[]{:T(128)}) while((s32[]{:T(128)}, f32[8,512]{1,0:T(8,128)S(1)}, f32[8,512]{1,0:T(8,128)S(1)}, f32[64,8,512]{2,1,0:T(8,128)S(1)}, ...), condition=%wide.region_5.7_spmd.clone, body=%wide.region_3.6_spmd.clone.sunk | while | flops 1110019 | bytes 1302617 | solution.py:94
  77.2 0.7 tile.2
  77.9 5.0 %all-to-all-start = ((f32[8,8,512]{2,1,0:T(8,128)}), f32[8,8,512]{2,1,0:T(8,128)S(1)}, u32[]{:S(2)}, u32[]{:S(2)}) async-start(f32[8,8,512]{2,1,0:T(8,128)} %tile.2), calls=%async_computation | async-start | bytes 262144 | tf_op jit(solution)/shard_map/all_to_all | solution.py:283
  83.0 0.6 gather_fusion
  83.7 5.4 %all-to-all-done = f32[8,8,512]{2,1,0:T(8,128)S(1)} async-done(((f32[8,8,512]{2,1,0:T(8,128)}), f32[8,8,512]{2,1,0:T(8,128)S(1)}, u32[]{:S(2)}, u32[]{:S(2)}) %all-to-all-start) | async-done | bytes 131104 | tf_op jit(solution)/shard_map/all_to_all | solution.py:283
  89.3 6.0 %collective-permute-start.6 = (f32[4,520]{1,0:T(4,128)S(1)}, f32[4,520]{1,0:T(4,128)S(1)}, u32[]{:S(2)}, u32[]{:S(2)}) collective-permute-start(f32[4,520]{1,0:T(4,128)S(1)} %get-tuple-element.87), channel_id=1, source_target_pairs={{0,2},{2,4},{4,6},{1,3},{3,5},{5,7},{8,10},{10,12},{12,14},{9,11},... | collective-permute-start | bytes 24968 | tf_op jit(solution)/shard_map/ppermute | solution.py:28
  95.3 2.1 %collective-permute-start.7 = (f32[4,520]{1,0:T(4,128)S(1)}, f32[4,520]{1,0:T(4,128)S(1)}, u32[]{:S(2)}, u32[]{:S(2)}) collective-permute-start(f32[4,520]{1,0:T(4,128)S(1)} %get-tuple-element.88), channel_id=1, source_target_pairs={{2,0},{4,2},{6,4},{3,1},{5,3},{7,5},{10,8},{12,10},{14,12},{11,9},... | collective-permute-start | bytes 24968 | tf_op jit(solution)/shard_map/ppermute | solution.py:29
  97.4 0.6 constant_dynamic-slice_fusion
  98.1 2.2 %collective-permute-done.7 = f32[4,520]{1,0:T(4,128)S(1)} collective-permute-done((f32[4,520]{1,0:T(4,128)S(1)}, f32[4,520]{1,0:T(4,128)S(1)}, u32[]{:S(2)}, u32[]{:S(2)}) %collective-permute-start.7) | collective-permute-done | bytes 8352 | tf_op jit(solution)/shard_map/ppermute | solution.py:29
  100.9 1.3 %fusion.11 = f32[8,32,512]{2,1,0:T(8,128)S(1)} fusion(f32[8,32,520]{2,1,0:T(8,128)S(1)} %multiply_add_fusion, f32[8]{0:T(128)S(1)} %get-tuple-element.104, f32[8]{0:T(128)S(1)} %get-tuple-element.105, f32[8]{0:T(128)S(1)} %get-tuple-element.106, f32[8]{0:T(128)S(1)} %get-tuple-element.107, f32[8]{0:T(128)S(1)} %get-tuple-element.108, ...), kind=kLoop, calls=%fused_computation.28 | loop fusion | flops 2228224 | bytes 5243168 | tf_op jit(solution)/shard_map/add | solution.py:304
  102.3 2.0 %fusion.10 = f32[16,32,512]{2,1,0:T(8,128)} fusion(s32[16,32,512]{2,1,0:T(8,128)S(1)} %copy-done, f32[32,512]{1,0:T(8,128)S(1)} %get-tuple-element.80, f32[16]{0:T(128)S(1)} %get-tuple-element.113, f32[32,512]{1,0:T(8,128)S(1)} %get-tuple-element.81, f32[16]{0:T(128)S(1)} %get-tuple-element.114, f32[32,512]{1,0:T(8,128)S(1)} %get-tuple-element.82, ...), kind=kLoop, calls=%fused_computation.23 | loop fusion | flops 4980736 | bytes 3670532 | tf_op jit(solution)/shard_map/jit(_where)/select_n | solution.py:312
  (135 shorter events, 6.3 us)
Async XLA Ops:
  0.6 16.5 %copy-start.1 = (f32[16,32,512]{2,1,0:T(8,128)S(1)}, f32[16,32,512]{2,1,0:T(8,128)}, u32[]{:S(2)}) copy-start(f32[16,32,512]{2,1,0:T(8,128)} %param.8) | copy-start | bytes 3145732
  2.1 16.9 %copy-start.6 = (s32[16,2]{0,1:T(2,128)S(1)}, s32[16,2]{0,1:T(2,128)}, u32[]{:S(2)}) copy-start(s32[16,2]{0,1:T(2,128)} %param.10) | copy-start | bytes 388
  2.1 10.6 %collective-permute-start = (f32[16,11,512]{2,1,0:T(8,128)S(1)}, f32[16,11,512]{2,1,0:T(8,128)S(1)}, u32[]{:S(2)}, u32[]{:S(2)}) collective-permute-start(f32[16,11,512]{2,1,0:T(8,128)S(1)} %get-tuple-element.77), channel_id=1, source_target_pairs={{0,2},{2,4},{4,6},{1,3},{3,5},{5,7},{8,10},{10,12},{12,14},{9,11},... | collective-permute-start | bytes 1081352 | tf_op jit(solution)/shard_map/ppermute | solution.py:28
  6.6 10.5 %collective-permute-start.1 = (f32[16,11,512]{2,1,0:T(8,128)S(1)}, f32[16,11,512]{2,1,0:T(8,128)S(1)}, u32[]{:S(2)}, u32[]{:S(2)}) collective-permute-start(f32[16,11,512]{2,1,0:T(8,128)S(1)} %get-tuple-element.78), channel_id=1, source_target_pairs={{2,0},{4,2},{6,4},{3,1},{5,3},{7,5},{10,8},{12,10},{14,12},{11,9},... | collective-permute-start | bytes 1081352 | tf_op jit(solution)/shard_map/ppermute | solution.py:29
  17.7 3.1 %collective-permute-start.2 = (f32[11,864]{1,0:T(8,128)S(1)}, f32[11,864]{1,0:T(8,128)S(1)}, u32[]{:S(2)}, u32[]{:S(2)}) collective-permute-start(f32[11,864]{1,0:T(8,128)S(1)} %reshape.137), channel_id=1, source_target_pairs={{0,1},{1,0},{2,3},{3,2},{4,5},{5,4},{6,7},{7,6},{8,9},{9,8},{10,11... | collective-permute-start | bytes 114056 | tf_op jit(solution)/shard_map/ppermute | solution.py:48
  34.0 36.0 %collective-permute-start.3 = (f32[16,8,512]{2,1,0:T(8,128)}, f32[16,8,512]{2,1,0:T(8,128)S(1)}, u32[]{:S(2)}, u32[]{:S(2)}) collective-permute-start(f32[16,8,512]{2,1,0:T(8,128)} %get-tuple-element.43), channel_id=1, source_target_pairs={{0,8},{8,16},{16,24},{24,0},{1,9},{9,17},{17,25},{25,1},{2,10},{10... | collective-permute-start | bytes 786440 | tf_op jit(solution)/shard_map/ppermute | solution.py:256
  45.4 24.7 %collective-permute-start.4 = (f32[16,8,512]{2,1,0:T(8,128)}, f32[16,8,512]{2,1,0:T(8,128)S(1)}, u32[]{:S(2)}, u32[]{:S(2)}) collective-permute-start(f32[16,8,512]{2,1,0:T(8,128)} %get-tuple-element.44), channel_id=1, source_target_pairs={{0,16},{8,24},{16,0},{24,8},{1,17},{9,25},{17,1},{25,9},{2,18},{10... | collective-permute-start | bytes 786440 | tf_op jit(solution)/shard_map/ppermute | solution.py:256
  57.8 10.1 %copy-start.7 = (f32[16,8,512]{2,1,0:T(8,128)S(1)}, f32[16,8,512]{2,1,0:T(8,128)}, u32[]{:S(2)}) copy-start(f32[16,8,512]{2,1,0:T(8,128)} %get-tuple-element.45) | copy-start | bytes 786436
  67.9 5.3 %collective-permute-start.5 = (f32[16,8,512]{2,1,0:T(8,128)S(1)}, f32[16,8,512]{2,1,0:T(8,128)S(1)}, u32[]{:S(2)}, u32[]{:S(2)}) collective-permute-start(f32[16,8,512]{2,1,0:T(8,128)S(1)} %copy-done.7), channel_id=1, source_target_pairs={{0,24},{8,0},{16,8},{24,16},{1,25},{9,1},{17,9},{25,17},{2,26},{10... | collective-permute-start | bytes 786440 | tf_op jit(solution)/shard_map/ppermute | solution.py:256
  73.3 9.6 %copy-start.2 = (f32[16,8,512]{2,1,0:T(8,128)S(1)}, f32[16,8,512]{2,1,0:T(8,128)}, u32[]{:S(2)}) copy-start(f32[16,8,512]{2,1,0:T(8,128)} %get-tuple-element.39) | copy-start | bytes 786436
  73.3 9.6 %copy-start.3 = (f32[16,8,512]{2,1,0:T(8,128)S(1)}, f32[16,8,512]{2,1,0:T(8,128)}, u32[]{:S(2)}) copy-start(f32[16,8,512]{2,1,0:T(8,128)} %get-tuple-element.40) | copy-start | bytes 786436
  73.4 9.6 %copy-start.4 = (f32[16,8,512]{2,1,0:T(8,128)S(1)}, f32[16,8,512]{2,1,0:T(8,128)}, u32[]{:S(2)}) copy-start(f32[16,8,512]{2,1,0:T(8,128)} %get-tuple-element.41) | copy-start | bytes 786436
  73.4 9.6 %copy-start.5 = (f32[16,8,512]{2,1,0:T(8,128)S(1)}, f32[16,8,512]{2,1,0:T(8,128)}, u32[]{:S(2)}) copy-start(f32[16,8,512]{2,1,0:T(8,128)} %get-tuple-element.38) | copy-start | bytes 786436
  77.9 11.2 %all-to-all-start = ((f32[8,8,512]{2,1,0:T(8,128)}), f32[8,8,512]{2,1,0:T(8,128)S(1)}, u32[]{:S(2)}, u32[]{:S(2)}) async-start(f32[8,8,512]{2,1,0:T(8,128)} %tile.2), calls=%async_computation | async-start | bytes 262144 | tf_op jit(solution)/shard_map/all_to_all | solution.py:283
  89.3 8.8 %collective-permute-start.6 = (f32[4,520]{1,0:T(4,128)S(1)}, f32[4,520]{1,0:T(4,128)S(1)}, u32[]{:S(2)}, u32[]{:S(2)}) collective-permute-start(f32[4,520]{1,0:T(4,128)S(1)} %get-tuple-element.87), channel_id=1, source_target_pairs={{0,2},{2,4},{4,6},{1,3},{3,5},{5,7},{8,10},{10,12},{12,14},{9,11},... | collective-permute-start | bytes 24968 | tf_op jit(solution)/shard_map/ppermute | solution.py:28
  95.3 5.0 %collective-permute-start.7 = (f32[4,520]{1,0:T(4,128)S(1)}, f32[4,520]{1,0:T(4,128)S(1)}, u32[]{:S(2)}, u32[]{:S(2)}) collective-permute-start(f32[4,520]{1,0:T(4,128)S(1)} %get-tuple-element.88), channel_id=1, source_target_pairs={{2,0},{4,2},{6,4},{3,1},{5,3},{7,5},{10,8},{12,10},{14,12},{11,9},... | collective-permute-start | bytes 24968 | tf_op jit(solution)/shard_map/ppermute | solution.py:29
  100.9 1.3 %copy-start = (s32[16,32,512]{2,1,0:T(8,128)S(1)}, s32[16,32,512]{2,1,0:T(8,128)}, u32[]{:S(2)}) copy-start(s32[16,32,512]{2,1,0:T(8,128)} %bad.7) | copy-start | bytes 3145732

commit v13 on v11

--- a/solution.py
+++ b/solution.py
@@ -186,14 +186,21 @@
     window = window_buf.shape[1]
     band = lax.rem(me[0] + step, bands)
     base = pl.multiple_of(band * band_rows, 8)
-    fetch_rows = pltpu.make_async_copy(padded.at[:, pl.ds(base, window), :], window_buf, sems.at[0])
-    fetch_bad = pltpu.make_async_copy(bad.at[:, pl.ds(base, band_rows), :], bad_buf, sems.at[1])
-    fetch_rows.start()
+    fetch_bad = pltpu.make_async_copy(
+        bad.at[:, pl.ds(base, band_rows), :], bad_buf, sems.at[group_size]
+    )
+    fetches = [
+        pltpu.make_async_copy(
+            padded.at[e, pl.ds(base, window), :], window_buf.at[e], sems.at[e]
+        )
+        for e in range(group_size)
+    ]
+    for fetch in fetches:
+        fetch.start()
     fetch_bad.start()
-    fetch_rows.wait()
     fetch_bad.wait()
-
-    def one_exposure(e, carry):
+    for e in range(group_size):
+        fetches[e].wait()
         block = pltpu.roll(window_buf[e], window - row_shift[e], 0)
         across = None
         for tap in range(TAPS):
@@ -206,9 +213,6 @@
             total = term if total is None else total + term
         warped_out[e] = total
         flagged_out[e] = jnp.where(bad_buf[e] == 1, sentinel, total)
-        return carry
-
-    lax.fori_loop(0, group_size, one_exposure, 0, unroll=True)
 
 
 def warp_by_slot(padded, bad_pixels, offsets, warp_index):
@@ -245,7 +249,7 @@
             scratch_shapes=[
                 pltpu.VMEM((group_size, window, lanes), jnp.float32),
                 pltpu.VMEM((group_size, band_rows, col_count), jnp.int32),
-                pltpu.SemaphoreType.DMA((2,)),
+                pltpu.SemaphoreType.DMA((group_size + 1,)),
             ],
         )(row_shift, col_shift, row_weight, col_weight, me, padded, bad_pixels)
         if step:

time: 82.1 us -> 90.3 us (1.100)
  Pallas kernels: 17.5 us -> 25.7 us
  starting transfers between devices: 22.5 us -> 25.7 us
  waiting for transfers between devices: 20.4 us -> 17.2 us
    pallas_call x4, Pallas kernels: 17.5 us -> 25.7 us  [warp_by_slot(): pl.pallas_call(functools.partial(_slot_kernel, step), out_shape=(banded,...]
    ppermute x3, waiting for transfers between devices: 5.05 us -> 3.11 us  [warp_by_slot(): slots[step] = lax.ppermute(flagged, 'exp', pairs)]
    ppermute x2, starting transfers between devices: 8.91 us -> 10.6 us  [_row_halo(): lax.ppermute(lax.slice_in_dim(block, size - width, None, axis=dim), 'row'...]
    all_to_all x1, starting transfers between devices: 3.62 us -> 5.04 us  [body(): lax.all_to_all(jnp.tile(band, (groups * sides, 1)), ('exp', 'col'), split...]
    all_to_all x1, waiting for transfers between devices: 6.55 us -> 5.44 us  [body(): lax.all_to_all(jnp.tile(band, (groups * sides, 1)), ('exp', 'col'), split...]
  transfers between devices with their start and end apart: 9 -> 9, of which waited for: 5 -> 5; matrix products, arithmetic and copies ran while one was open for 8% -> 7% of each run, Pallas kernels for 16% -> 21%
where the time goes in v13:
time: 90.3 us; the launch traced here: 89.8 us
  starting transfers between devices  25.7 us (28%)
  Pallas kernels  25.7 us (28%)
  waiting for transfers between devices  17.2 us (19%)
  other arithmetic  11.3 us (13%)
  local copies, waits for them, and re-layouts  7.79 us (9%)
  between operations  0.99 us (1%)
    pallas_call x4, Pallas kernels, warp_by_slot(): pl.pallas_call(functools.partial(_slot_kernel, step), out_shape=(banded,...  25.7 us
    ppermute x2, starting transfers between devices, _row_halo(): lax.ppermute(lax.slice_in_dim(block, size - width, None, axis=dim), 'row'...  10.6 us
    ppermute x2, waiting for transfers between devices, _row_halo(): lax.ppermute(lax.slice_in_dim(block, 0, width, axis=dim), 'row', backward)  6.63 us
    all_to_all x1, waiting for transfers between devices, body(): lax.all_to_all(jnp.tile(band, (groups * sides, 1)), ('exp', 'col'), split...  5.44 us
    all_to_all x1, starting transfers between devices, body(): lax.all_to_all(jnp.tile(band, (groups * sides, 1)), ('exp', 'col'), split...  5.04 us
    ppermute x3, starting transfers between devices, warp_by_slot(): slots[step] = lax.ppermute(flagged, 'exp', pairs)  4.84 us
    ppermute x2, starting transfers between devices, _row_halo(): lax.ppermute(lax.slice_in_dim(block, 0, width, axis=dim), 'row', backward)  4.02 us
    ppermute x3, waiting for transfers between devices, warp_by_slot(): slots[step] = lax.ppermute(flagged, 'exp', pairs)  3.11 us
  transfers between devices with their start and end apart: 9, of which 5 were waited for; matrix products, arithmetic and copies ran while one was open for 7% of the time, Pallas kernels for 21%

profile of v13, /device:TPU:1, one launch (start us, length us, event | category | flops | bytes accessed | tf_op | source)
XLA Modules:
  0.0 89.8 jit_solution(11915888514512395529)
XLA Ops:
  0.6 1.4 %fusion.107 = (f32[16,11,512]{2,1,0:T(8,128)S(1)}, f32[16,11,512]{2,1,0:T(8,128)S(1)}) fusion(f32[16,32,512]{2,1,0:T(8,128)} %param.8), kind=kLoop, calls=%fused_computation.218 | loop fusion | bytes 1441792 | tf_op jit(solution)/shard_map/slice | solution.py:28
  2.1 4.5 %collective-permute-start = (f32[16,11,512]{2,1,0:T(8,128)S(1)}, f32[16,11,512]{2,1,0:T(8,128)S(1)}, u32[]{:S(2)}, u32[]{:S(2)}) collective-permute-start(f32[16,11,512]{2,1,0:T(8,128)S(1)} %get-tuple-element.77), channel_id=1, source_target_pairs={{0,2},{2,4},{4,6},{1,3},{3,5},{5,7},{8,10},{10,12},{12,14},{9,11},... | collective-permute-start | bytes 1081352 | tf_op jit(solution)/shard_map/ppermute | solution.py:28
  6.6 1.9 %collective-permute-start.1 = (f32[16,11,512]{2,1,0:T(8,128)S(1)}, f32[16,11,512]{2,1,0:T(8,128)S(1)}, u32[]{:S(2)}, u32[]{:S(2)}) collective-permute-start(f32[16,11,512]{2,1,0:T(8,128)S(1)} %get-tuple-element.78), channel_id=1, source_target_pairs={{2,0},{4,2},{6,4},{3,1},{5,3},{7,5},{10,8},{12,10},{14,12},{11,9},... | collective-permute-start | bytes 1081352 | tf_op jit(solution)/shard_map/ppermute | solution.py:29
  8.6 0.8 slice_bitcast_fusion.25
  9.5 0.7 fusion.78
  10.7 2.0 %collective-permute-done = f32[16,11,512]{2,1,0:T(8,128)S(1)} collective-permute-done((f32[16,11,512]{2,1,0:T(8,128)S(1)}, f32[16,11,512]{2,1,0:T(8,128)S(1)}, u32[]{:S(2)}, u32[]{:S(2)}) %collective-permute-start) | collective-permute-done | bytes 360480 | tf_op jit(solution)/shard_map/ppermute | solution.py:28
  12.7 4.4 %collective-permute-done.1 = f32[16,11,512]{2,1,0:T(8,128)S(1)} collective-permute-done((f32[16,11,512]{2,1,0:T(8,128)S(1)}, f32[16,11,512]{2,1,0:T(8,128)S(1)}, u32[]{:S(2)}, u32[]{:S(2)}) %collective-permute-start.1) | collective-permute-done | bytes 360480 | tf_op jit(solution)/shard_map/ppermute | solution.py:29
  17.7 1.3 %collective-permute-start.2 = (f32[11,864]{1,0:T(8,128)S(1)}, f32[11,864]{1,0:T(8,128)S(1)}, u32[]{:S(2)}, u32[]{:S(2)}) collective-permute-start(f32[11,864]{1,0:T(8,128)S(1)} %reshape.137), channel_id=1, source_target_pairs={{0,1},{1,0},{2,3},{3,2},{4,5},{5,4},{6,7},{7,6},{8,9},{9,8},{10,11... | collective-permute-start | bytes 114056 | tf_op jit(solution)/shard_map/ppermute | solution.py:48
  19.0 0.6 add_bitcast_fusion
  19.6 0.6 reshape.134.row_weight
  20.2 0.6 reshape.135.col_weight
  21.6 2.4 %select_maximum_fusion.padded = f32[16,56,640]{2,1,0:T(8,128)} fusion(f32[16,54,11]{2,1,0:T(8,128)S(1)} %bitcast.82, f32[16,54,11]{2,1,0:T(8,128)S(1)} %bitcast.81, f32[16,11,512]{2,1,0:T(8,128)S(1)} %collective-permute-done.1, f32[16,32,512]{2,1,0:T(8,128)S(1)} %copy-done.1, f32[16,11,512]{2,1,0:T(8,128)S(1)} %collective-permute-done), kind=kLoop, calls=%fused_computation.7 | loop fusion | flops 9748480 | bytes 4139264 | tf_op jit(solution)/shard_map/concatenate | solution.py:53
  24.0 6.4 %shard_map.69 = (f32[16,8,512]{2,1,0:T(8,128)}, f32[16,8,512]{2,1,0:T(8,128)}) custom-call(s32[16]{0:T(128)} %get-tuple-element.123.row_shift, s32[16]{0:T(128)} %get-tuple-element.122.col_shift, f32[96]{0:T(128)} %reshape.134.row_weight, f32[96]{0:T(128)} %reshape.135.col_weight, s32[1]{0:T(128)} %bitcast.4.me, f32[16,56,640]{2,1,0:T(8,128)} %select_maximum_fusion.padded, ...), custom_call_target="tpu_custom_call" | custom-call | tf_op jit(solution)/shard_map/pallas_call | solution.py:244
  30.4 1.3 %collective-permute-start.3 = (f32[16,8,512]{2,1,0:T(8,128)}, f32[16,8,512]{2,1,0:T(8,128)S(1)}, u32[]{:S(2)}, u32[]{:S(2)}) collective-permute-start(f32[16,8,512]{2,1,0:T(8,128)} %get-tuple-element.43), channel_id=1, source_target_pairs={{0,8},{8,16},{16,24},{24,0},{1,9},{9,17},{17,25},{25,1},{2,10},{10... | collective-permute-start | bytes 786440 | tf_op jit(solution)/shard_map/ppermute | solution.py:257
  31.8 6.4 %shard_map.70 = (f32[16,8,512]{2,1,0:T(8,128)}, f32[16,8,512]{2,1,0:T(8,128)}) custom-call(s32[16]{0:T(128)} %get-tuple-element.123.row_shift, s32[16]{0:T(128)} %get-tuple-element.122.col_shift, f32[96]{0:T(128)} %reshape.134.row_weight, f32[96]{0:T(128)} %reshape.135.col_weight, s32[1]{0:T(128)} %bitcast.4.me, f32[16,56,640]{2,1,0:T(8,128)} %select_maximum_fusion.padded, ...), custom_call_target="tpu_custom_call" | custom-call | tf_op jit(solution)/shard_map/pallas_call | solution.py:244
  38.2 2.4 %collective-permute-start.4 = (f32[16,8,512]{2,1,0:T(8,128)}, f32[16,8,512]{2,1,0:T(8,128)S(1)}, u32[]{:S(2)}, u32[]{:S(2)}) collective-permute-start(f32[16,8,512]{2,1,0:T(8,128)} %get-tuple-element.44), channel_id=1, source_target_pairs={{0,16},{8,24},{16,0},{24,8},{1,17},{9,25},{17,1},{25,9},{2,18},{10... | collective-permute-start | bytes 786440 | tf_op jit(solution)/shard_map/ppermute | solution.py:257
  40.5 6.4 %shard_map.71 = (f32[16,8,512]{2,1,0:T(8,128)}, f32[16,8,512]{2,1,0:T(8,128)}) custom-call(s32[16]{0:T(128)} %get-tuple-element.123.row_shift, s32[16]{0:T(128)} %get-tuple-element.122.col_shift, f32[96]{0:T(128)} %reshape.134.row_weight, f32[96]{0:T(128)} %reshape.135.col_weight, s32[1]{0:T(128)} %bitcast.4.me, f32[16,56,640]{2,1,0:T(8,128)} %select_maximum_fusion.padded, ...), custom_call_target="tpu_custom_call" | custom-call | tf_op jit(solution)/shard_map/pallas_call | solution.py:244
  47.0 6.5 %shard_map.68 = (f32[16,8,512]{2,1,0:T(8,128)}, f32[16,8,512]{2,1,0:T(8,128)}) custom-call(s32[16]{0:T(128)} %get-tuple-element.123.row_shift, s32[16]{0:T(128)} %get-tuple-element.122.col_shift, f32[96]{0:T(128)} %reshape.134.row_weight, f32[96]{0:T(128)} %reshape.135.col_weight, s32[1]{0:T(128)} %bitcast.4.me, f32[16,56,640]{2,1,0:T(8,128)} %select_maximum_fusion.padded, ...), custom_call_target="tpu_custom_call" | custom-call | tf_op jit(solution)/shard_map/pallas_call | solution.py:244
  53.5 1.1 %collective-permute-start.5 = (f32[16,8,512]{2,1,0:T(8,128)S(1)}, f32[16,8,512]{2,1,0:T(8,128)S(1)}, u32[]{:S(2)}, u32[]{:S(2)}) collective-permute-start(f32[16,8,512]{2,1,0:T(8,128)S(1)} %copy-done.7), channel_id=1, source_target_pairs={{0,24},{8,0},{16,8},{24,16},{1,25},{9,1},{17,9},{25,17},{2,26},{10... | collective-permute-start | bytes 786440 | tf_op jit(solution)/shard_map/ppermute | solution.py:257
  54.6 1.0 %constant_dynamic-update-slice_fusion.3 = f32[64,8,512]{2,1,0:T(8,128)S(1)} fusion(f32[16,8,512]{2,1,0:T(8,128)} %get-tuple-element.42), kind=kLoop, calls=%fused_computation.101 | loop fusion | bytes 524288
  55.6 3.1 %collective-permute-done.5 = f32[16,8,512]{2,1,0:T(8,128)S(1)} collective-permute-done((f32[16,8,512]{2,1,0:T(8,128)S(1)}, f32[16,8,512]{2,1,0:T(8,128)S(1)}, u32[]{:S(2)}, u32[]{:S(2)}) %collective-permute-start.5) | collective-permute-done | bytes 262176 | tf_op jit(solution)/shard_map/ppermute | solution.py:257
  58.9 3.6 %while.13 = (s32[]{:T(128)}, f32[8,512]{1,0:T(8,128)S(1)}, f32[8,512]{1,0:T(8,128)S(1)}, f32[64,8,512]{2,1,0:T(8,128)S(1)}, f32[8,512]{1,0:T(8,128)S(1)}, /*index=5*/s32[]{:T(128)}, s32[]{:T(128)}) while((s32[]{:T(128)}, f32[8,512]{1,0:T(8,128)S(1)}, f32[8,512]{1,0:T(8,128)S(1)}, f32[64,8,512]{2,1,0:T(8,128)S(1)}, ...), condition=%wide.region_5.7_spmd.clone, body=%wide.region_3.6_spmd.clone.sunk | while | flops 1110019 | bytes 1302617 | solution.py:94
  62.7 0.7 tile.2
  63.4 5.0 %all-to-all-start = ((f32[8,8,512]{2,1,0:T(8,128)}), f32[8,8,512]{2,1,0:T(8,128)S(1)}, u32[]{:S(2)}, u32[]{:S(2)}) async-start(f32[8,8,512]{2,1,0:T(8,128)} %tile.2), calls=%async_computation | async-start | bytes 262144 | tf_op jit(solution)/shard_map/all_to_all | solution.py:284
  68.6 0.6 gather_fusion
  69.2 5.4 %all-to-all-done = f32[8,8,512]{2,1,0:T(8,128)S(1)} async-done(((f32[8,8,512]{2,1,0:T(8,128)}), f32[8,8,512]{2,1,0:T(8,128)S(1)}, u32[]{:S(2)}, u32[]{:S(2)}) %all-to-all-start) | async-done | bytes 131104 | tf_op jit(solution)/shard_map/all_to_all | solution.py:284
  74.8 6.0 %collective-permute-start.6 = (f32[4,520]{1,0:T(4,128)S(1)}, f32[4,520]{1,0:T(4,128)S(1)}, u32[]{:S(2)}, u32[]{:S(2)}) collective-permute-start(f32[4,520]{1,0:T(4,128)S(1)} %get-tuple-element.87), channel_id=1, source_target_pairs={{0,2},{2,4},{4,6},{1,3},{3,5},{5,7},{8,10},{10,12},{12,14},{9,11},... | collective-permute-start | bytes 24968 | tf_op jit(solution)/shard_map/ppermute | solution.py:28
  80.9 2.1 %collective-permute-start.7 = (f32[4,520]{1,0:T(4,128)S(1)}, f32[4,520]{1,0:T(4,128)S(1)}, u32[]{:S(2)}, u32[]{:S(2)}) collective-permute-start(f32[4,520]{1,0:T(4,128)S(1)} %get-tuple-element.88), channel_id=1, source_target_pairs={{2,0},{4,2},{6,4},{3,1},{5,3},{7,5},{10,8},{12,10},{14,12},{11,9},... | collective-permute-start | bytes 24968 | tf_op jit(solution)/shard_map/ppermute | solution.py:29
  83.0 0.6 constant_dynamic-slice_fusion
  83.6 2.2 %collective-permute-done.7 = f32[4,520]{1,0:T(4,128)S(1)} collective-permute-done((f32[4,520]{1,0:T(4,128)S(1)}, f32[4,520]{1,0:T(4,128)S(1)}, u32[]{:S(2)}, u32[]{:S(2)}) %collective-permute-start.7) | collective-permute-done | bytes 8352 | tf_op jit(solution)/shard_map/ppermute | solution.py:29
  86.5 1.3 %fusion.11 = f32[8,32,512]{2,1,0:T(8,128)S(1)} fusion(f32[8,32,520]{2,1,0:T(8,128)S(1)} %multiply_add_fusion, f32[8]{0:T(128)S(1)} %get-tuple-element.104, f32[8]{0:T(128)S(1)} %get-tuple-element.105, f32[8]{0:T(128)S(1)} %get-tuple-element.106, f32[8]{0:T(128)S(1)} %get-tuple-element.107, f32[8]{0:T(128)S(1)} %get-tuple-element.108, ...), kind=kLoop, calls=%fused_computation.28 | loop fusion | flops 2228224 | bytes 5243168 | tf_op jit(solution)/shard_map/add | solution.py:305
  87.8 2.0 %fusion.10 = f32[16,32,512]{2,1,0:T(8,128)} fusion(s32[16,32,512]{2,1,0:T(8,128)S(1)} %copy-done, f32[32,512]{1,0:T(8,128)S(1)} %get-tuple-element.80, f32[16]{0:T(128)S(1)} %get-tuple-element.113, f32[32,512]{1,0:T(8,128)S(1)} %get-tuple-element.81, f32[16]{0:T(128)S(1)} %get-tuple-element.114, f32[32,512]{1,0:T(8,128)S(1)} %get-tuple-element.82, ...), kind=kLoop, calls=%fused_computation.23 | loop fusion | flops 4980736 | bytes 3670532 | tf_op jit(solution)/shard_map/jit(_where)/select_n | solution.py:313
  (135 shorter events, 6.3 us)
Async XLA Ops:
  0.6 16.5 %copy-start.1 = (f32[16,32,512]{2,1,0:T(8,128)S(1)}, f32[16,32,512]{2,1,0:T(8,128)}, u32[]{:S(2)}) copy-start(f32[16,32,512]{2,1,0:T(8,128)} %param.8) | copy-start | bytes 3145732
  2.1 16.9 %copy-start.6 = (s32[16,2]{0,1:T(2,128)S(1)}, s32[16,2]{0,1:T(2,128)}, u32[]{:S(2)}) copy-start(s32[16,2]{0,1:T(2,128)} %param.10) | copy-start | bytes 388
  2.1 10.6 %collective-permute-start = (f32[16,11,512]{2,1,0:T(8,128)S(1)}, f32[16,11,512]{2,1,0:T(8,128)S(1)}, u32[]{:S(2)}, u32[]{:S(2)}) collective-permute-start(f32[16,11,512]{2,1,0:T(8,128)S(1)} %get-tuple-element.77), channel_id=1, source_target_pairs={{0,2},{2,4},{4,6},{1,3},{3,5},{5,7},{8,10},{10,12},{12,14},{9,11},... | collective-permute-start | bytes 1081352 | tf_op jit(solution)/shard_map/ppermute | solution.py:28
  6.6 10.5 %collective-permute-start.1 = (f32[16,11,512]{2,1,0:T(8,128)S(1)}, f32[16,11,512]{2,1,0:T(8,128)S(1)}, u32[]{:S(2)}, u32[]{:S(2)}) collective-permute-start(f32[16,11,512]{2,1,0:T(8,128)S(1)} %get-tuple-element.78), channel_id=1, source_target_pairs={{2,0},{4,2},{6,4},{3,1},{5,3},{7,5},{10,8},{12,10},{14,12},{11,9},... | collective-permute-start | bytes 1081352 | tf_op jit(solution)/shard_map/ppermute | solution.py:29
  17.7 3.1 %collective-permute-start.2 = (f32[11,864]{1,0:T(8,128)S(1)}, f32[11,864]{1,0:T(8,128)S(1)}, u32[]{:S(2)}, u32[]{:S(2)}) collective-permute-start(f32[11,864]{1,0:T(8,128)S(1)} %reshape.137), channel_id=1, source_target_pairs={{0,1},{1,0},{2,3},{3,2},{4,5},{5,4},{6,7},{7,6},{8,9},{9,8},{10,11... | collective-permute-start | bytes 114056 | tf_op jit(solution)/shard_map/ppermute | solution.py:48
  30.4 25.2 %collective-permute-start.3 = (f32[16,8,512]{2,1,0:T(8,128)}, f32[16,8,512]{2,1,0:T(8,128)S(1)}, u32[]{:S(2)}, u32[]{:S(2)}) collective-permute-start(f32[16,8,512]{2,1,0:T(8,128)} %get-tuple-element.43), channel_id=1, source_target_pairs={{0,8},{8,16},{16,24},{24,0},{1,9},{9,17},{17,25},{25,1},{2,10},{10... | collective-permute-start | bytes 786440 | tf_op jit(solution)/shard_map/ppermute | solution.py:257
  38.2 17.4 %collective-permute-start.4 = (f32[16,8,512]{2,1,0:T(8,128)}, f32[16,8,512]{2,1,0:T(8,128)S(1)}, u32[]{:S(2)}, u32[]{:S(2)}) collective-permute-start(f32[16,8,512]{2,1,0:T(8,128)} %get-tuple-element.44), channel_id=1, source_target_pairs={{0,16},{8,24},{16,0},{24,8},{1,17},{9,25},{17,1},{25,9},{2,18},{10... | collective-permute-start | bytes 786440 | tf_op jit(solution)/shard_map/ppermute | solution.py:257
  46.9 6.5 %copy-start.7 = (f32[16,8,512]{2,1,0:T(8,128)S(1)}, f32[16,8,512]{2,1,0:T(8,128)}, u32[]{:S(2)}) copy-start(f32[16,8,512]{2,1,0:T(8,128)} %get-tuple-element.45) | copy-start | bytes 786436
  53.5 5.3 %collective-permute-start.5 = (f32[16,8,512]{2,1,0:T(8,128)S(1)}, f32[16,8,512]{2,1,0:T(8,128)S(1)}, u32[]{:S(2)}, u32[]{:S(2)}) collective-permute-start(f32[16,8,512]{2,1,0:T(8,128)S(1)} %copy-done.7), channel_id=1, source_target_pairs={{0,24},{8,0},{16,8},{24,16},{1,25},{9,1},{17,9},{25,17},{2,26},{10... | collective-permute-start | bytes 786440 | tf_op jit(solution)/shard_map/ppermute | solution.py:257
  58.9 9.6 %copy-start.2 = (f32[16,8,512]{2,1,0:T(8,128)S(1)}, f32[16,8,512]{2,1,0:T(8,128)}, u32[]{:S(2)}) copy-start(f32[16,8,512]{2,1,0:T(8,128)} %get-tuple-element.39) | copy-start | bytes 786436
  58.9 9.6 %copy-start.3 = (f32[16,8,512]{2,1,0:T(8,128)S(1)}, f32[16,8,512]{2,1,0:T(8,128)}, u32[]{:S(2)}) copy-start(f32[16,8,512]{2,1,0:T(8,128)} %get-tuple-element.40) | copy-start | bytes 786436
  58.9 9.6 %copy-start.4 = (f32[16,8,512]{2,1,0:T(8,128)S(1)}, f32[16,8,512]{2,1,0:T(8,128)}, u32[]{:S(2)}) copy-start(f32[16,8,512]{2,1,0:T(8,128)} %get-tuple-element.41) | copy-start | bytes 786436
  58.9 9.6 %copy-start.5 = (f32[16,8,512]{2,1,0:T(8,128)S(1)}, f32[16,8,512]{2,1,0:T(8,128)}, u32[]{:S(2)}) copy-start(f32[16,8,512]{2,1,0:T(8,128)} %get-tuple-element.38) | copy-start | bytes 786436
  63.4 11.2 %all-to-all-start = ((f32[8,8,512]{2,1,0:T(8,128)}), f32[8,8,512]{2,1,0:T(8,128)S(1)}, u32[]{:S(2)}, u32[]{:S(2)}) async-start(f32[8,8,512]{2,1,0:T(8,128)} %tile.2), calls=%async_computation | async-start | bytes 262144 | tf_op jit(solution)/shard_map/all_to_all | solution.py:284
  74.8 8.8 %collective-permute-start.6 = (f32[4,520]{1,0:T(4,128)S(1)}, f32[4,520]{1,0:T(4,128)S(1)}, u32[]{:S(2)}, u32[]{:S(2)}) collective-permute-start(f32[4,520]{1,0:T(4,128)S(1)} %get-tuple-element.87), channel_id=1, source_target_pairs={{0,2},{2,4},{4,6},{1,3},{3,5},{5,7},{8,10},{10,12},{12,14},{9,11},... | collective-permute-start | bytes 24968 | tf_op jit(solution)/shard_map/ppermute | solution.py:28
  80.9 5.0 %collective-permute-start.7 = (f32[4,520]{1,0:T(4,128)S(1)}, f32[4,520]{1,0:T(4,128)S(1)}, u32[]{:S(2)}, u32[]{:S(2)}) collective-permute-start(f32[4,520]{1,0:T(4,128)S(1)} %get-tuple-element.88), channel_id=1, source_target_pairs={{2,0},{4,2},{6,4},{3,1},{5,3},{7,5},{10,8},{12,10},{14,12},{11,9},... | collective-permute-start | bytes 24968 | tf_op jit(solution)/shard_map/ppermute | solution.py:29
  86.5 1.3 %copy-start = (s32[16,32,512]{2,1,0:T(8,128)S(1)}, s32[16,32,512]{2,1,0:T(8,128)}, u32[]{:S(2)}) copy-start(s32[16,32,512]{2,1,0:T(8,128)} %bad.7) | copy-start | bytes 3145732

commit v14 on v11

--- a/solution.py
+++ b/solution.py
@@ -186,11 +186,21 @@
     window = window_buf.shape[1]
     band = lax.rem(me[0] + step, bands)
     base = pl.multiple_of(band * band_rows, 8)
-    fetch_rows = pltpu.make_async_copy(padded.at[:, pl.ds(base, window), :], window_buf, sems.at[0])
-    fetch_bad = pltpu.make_async_copy(bad.at[:, pl.ds(base, band_rows), :], bad_buf, sems.at[1])
-    fetch_rows.start()
+    half = group_size // 2
+    spans = [(0, half), (half, group_size - half)]
+    fetches = [
+        pltpu.make_async_copy(
+            padded.at[pl.ds(lo, count), pl.ds(base, window), :],
+            window_buf.at[pl.ds(lo, count)],
+            sems.at[part],
+        )
+        for part, (lo, count) in enumerate(spans)
+    ]
+    fetch_bad = pltpu.make_async_copy(bad.at[:, pl.ds(base, band_rows), :], bad_buf, sems.at[2])
+    fetches[0].start()
     fetch_bad.start()
-    fetch_rows.wait()
+    fetches[1].start()
+    fetches[0].wait()
     fetch_bad.wait()
 
     def one_exposure(e, carry):
@@ -208,7 +218,9 @@
         flagged_out[e] = jnp.where(bad_buf[e] == 1, sentinel, total)
         return carry
 
-    lax.fori_loop(0, group_size, one_exposure, 0, unroll=True)
+    lax.fori_loop(0, half, one_exposure, 0, unroll=True)
+    fetches[1].wait()
+    lax.fori_loop(half, group_size, one_exposure, 0, unroll=True)
 
 
 def warp_by_slot(padded, bad_pixels, offsets, warp_index):
@@ -245,7 +257,7 @@
             scratch_shapes=[
                 pltpu.VMEM((group_size, window, lanes), jnp.float32),
                 pltpu.VMEM((group_size, band_rows, col_count), jnp.int32),
-                pltpu.SemaphoreType.DMA((2,)),
+                pltpu.SemaphoreType.DMA((3,)),
             ],
         )(row_shift, col_shift, row_weight, col_weight, me, padded, bad_pixels)
         if step:

time: 82.1 us -> 80.9 us (0.985)
  Pallas kernels: 17.5 us -> 16.2 us
    pallas_call x4, Pallas kernels: 17.5 us -> 16.2 us  [warp_by_slot(): pl.pallas_call(functools.partial(_slot_kernel, step), out_shape=(banded,...]
    ppermute x2, starting transfers between devices: 8.91 us -> 8.08 us  [_row_halo(): lax.ppermute(lax.slice_in_dim(block, size - width, None, axis=dim), 'row'...]
  transfers between devices with their start and end apart: 9 -> 9, of which waited for: 5 -> 6; matrix products, arithmetic and copies ran while one was open for 8% -> 8% of each run, Pallas kernels for 16% -> 15%
where the time goes in v14:
time: 80.9 us; the launch traced here: 80.4 us
  starting transfers between devices  22 us (27%)
  waiting for transfers between devices  20.9 us (26%)
  Pallas kernels  16.2 us (20%)
  other arithmetic  11.3 us (14%)
  local copies, waits for them, and re-layouts  7.78 us (10%)
  between operations  0.97 us (1%)
    pallas_call x4, Pallas kernels, warp_by_slot(): pl.pallas_call(functools.partial(_slot_kernel, step), out_shape=(banded,...  16.2 us
    ppermute x2, starting transfers between devices, _row_halo(): lax.ppermute(lax.slice_in_dim(block, size - width, None, axis=dim), 'row'...  8.08 us
    ppermute x2, waiting for transfers between devices, _row_halo(): lax.ppermute(lax.slice_in_dim(block, 0, width, axis=dim), 'row', backward)  6.81 us
    all_to_all x1, waiting for transfers between devices, body(): lax.all_to_all(jnp.tile(band, (groups * sides, 1)), ('exp', 'col'), split...  6.46 us
    ppermute x3, waiting for transfers between devices, warp_by_slot(): slots[step] = lax.ppermute(flagged, 'exp', pairs)  5.68 us
    ppermute x3, starting transfers between devices, warp_by_slot(): slots[step] = lax.ppermute(flagged, 'exp', pairs)  4.84 us
    all_to_all x1, starting transfers between devices, body(): lax.all_to_all(jnp.tile(band, (groups * sides, 1)), ('exp', 'col'), split...  3.93 us
    ppermute x2, starting transfers between devices, _row_halo(): lax.ppermute(lax.slice_in_dim(block, 0, width, axis=dim), 'row', backward)  3.84 us
  transfers between devices with their start and end apart: 9, of which 6 were waited for; matrix products, arithmetic and copies ran while one was open for 8% of the time, Pallas kernels for 15%

profile of v14, /device:TPU:1, one launch (start us, length us, event | category | flops | bytes accessed | tf_op | source)
XLA Modules:
  0.0 80.4 jit_solution(4538336796079979222)
XLA Ops:
  0.6 1.4 %fusion.107 = (f32[16,11,512]{2,1,0:T(8,128)S(1)}, f32[16,11,512]{2,1,0:T(8,128)S(1)}) fusion(f32[16,32,512]{2,1,0:T(8,128)} %param.8), kind=kLoop, calls=%fused_computation.218 | loop fusion | bytes 1441792 | tf_op jit(solution)/shard_map/slice | solution.py:28
  2.1 4.5 %collective-permute-start = (f32[16,11,512]{2,1,0:T(8,128)S(1)}, f32[16,11,512]{2,1,0:T(8,128)S(1)}, u32[]{:S(2)}, u32[]{:S(2)}) collective-permute-start(f32[16,11,512]{2,1,0:T(8,128)S(1)} %get-tuple-element.77), channel_id=1, source_target_pairs={{0,2},{2,4},{4,6},{1,3},{3,5},{5,7},{8,10},{10,12},{12,14},{9,11},... | collective-permute-start | bytes 1081352 | tf_op jit(solution)/shard_map/ppermute | solution.py:28
  6.6 1.9 %collective-permute-start.1 = (f32[16,11,512]{2,1,0:T(8,128)S(1)}, f32[16,11,512]{2,1,0:T(8,128)S(1)}, u32[]{:S(2)}, u32[]{:S(2)}) collective-permute-start(f32[16,11,512]{2,1,0:T(8,128)S(1)} %get-tuple-element.78), channel_id=1, source_target_pairs={{2,0},{4,2},{6,4},{3,1},{5,3},{7,5},{10,8},{12,10},{14,12},{11,9},... | collective-permute-start | bytes 1081352 | tf_op jit(solution)/shard_map/ppermute | solution.py:29
  8.6 0.8 slice_bitcast_fusion.25
  9.5 0.7 fusion.78
  10.7 2.0 %collective-permute-done = f32[16,11,512]{2,1,0:T(8,128)S(1)} collective-permute-done((f32[16,11,512]{2,1,0:T(8,128)S(1)}, f32[16,11,512]{2,1,0:T(8,128)S(1)}, u32[]{:S(2)}, u32[]{:S(2)}) %collective-permute-start) | collective-permute-done | bytes 360480 | tf_op jit(solution)/shard_map/ppermute | solution.py:28
  12.7 4.4 %collective-permute-done.1 = f32[16,11,512]{2,1,0:T(8,128)S(1)} collective-permute-done((f32[16,11,512]{2,1,0:T(8,128)S(1)}, f32[16,11,512]{2,1,0:T(8,128)S(1)}, u32[]{:S(2)}, u32[]{:S(2)}) %collective-permute-start.1) | collective-permute-done | bytes 360480 | tf_op jit(solution)/shard_map/ppermute | solution.py:29
  17.7 1.3 %collective-permute-start.2 = (f32[11,864]{1,0:T(8,128)S(1)}, f32[11,864]{1,0:T(8,128)S(1)}, u32[]{:S(2)}, u32[]{:S(2)}) collective-permute-start(f32[11,864]{1,0:T(8,128)S(1)} %reshape.137), channel_id=1, source_target_pairs={{0,1},{1,0},{2,3},{3,2},{4,5},{5,4},{6,7},{7,6},{8,9},{9,8},{10,11... | collective-permute-start | bytes 114056 | tf_op jit(solution)/shard_map/ppermute | solution.py:48
  19.6 0.6 reshape.134.row_weight
  20.2 0.6 reshape.135.col_weight
  21.6 2.4 %select_maximum_fusion.padded = f32[16,56,640]{2,1,0:T(8,128)} fusion(f32[16,54,11]{2,1,0:T(8,128)S(1)} %bitcast.82, f32[16,54,11]{2,1,0:T(8,128)S(1)} %bitcast.81, f32[16,11,512]{2,1,0:T(8,128)S(1)} %collective-permute-done.1, f32[16,32,512]{2,1,0:T(8,128)S(1)} %copy-done.1, f32[16,11,512]{2,1,0:T(8,128)S(1)} %collective-permute-done), kind=kLoop, calls=%fused_computation.7 | loop fusion | flops 9748480 | bytes 4139264 | tf_op jit(solution)/shard_map/concatenate | solution.py:53
  24.0 4.0 %shard_map.69 = (f32[16,8,512]{2,1,0:T(8,128)}, f32[16,8,512]{2,1,0:T(8,128)}) custom-call(s32[16]{0:T(128)} %get-tuple-element.123.row_shift, s32[16]{0:T(128)} %get-tuple-element.122.col_shift, f32[96]{0:T(128)} %reshape.134.row_weight, f32[96]{0:T(128)} %reshape.135.col_weight, s32[1]{0:T(128)} %bitcast.4.me, f32[16,56,640]{2,1,0:T(8,128)} %select_maximum_fusion.padded, ...), custom_call_target="tpu_custom_call" | custom-call | tf_op jit(solution)/shard_map/pallas_call | solution.py:252
  28.0 1.3 %collective-permute-start.3 = (f32[16,8,512]{2,1,0:T(8,128)}, f32[16,8,512]{2,1,0:T(8,128)S(1)}, u32[]{:S(2)}, u32[]{:S(2)}) collective-permute-start(f32[16,8,512]{2,1,0:T(8,128)} %get-tuple-element.43), channel_id=1, source_target_pairs={{0,8},{8,16},{16,24},{24,0},{1,9},{9,17},{17,25},{25,1},{2,10},{10... | collective-permute-start | bytes 786440 | tf_op jit(solution)/shard_map/ppermute | solution.py:265
  29.4 4.0 %shard_map.70 = (f32[16,8,512]{2,1,0:T(8,128)}, f32[16,8,512]{2,1,0:T(8,128)}) custom-call(s32[16]{0:T(128)} %get-tuple-element.123.row_shift, s32[16]{0:T(128)} %get-tuple-element.122.col_shift, f32[96]{0:T(128)} %reshape.134.row_weight, f32[96]{0:T(128)} %reshape.135.col_weight, s32[1]{0:T(128)} %bitcast.4.me, f32[16,56,640]{2,1,0:T(8,128)} %select_maximum_fusion.padded, ...), custom_call_target="tpu_custom_call" | custom-call | tf_op jit(solution)/shard_map/pallas_call | solution.py:252
  33.4 2.4 %collective-permute-start.4 = (f32[16,8,512]{2,1,0:T(8,128)}, f32[16,8,512]{2,1,0:T(8,128)S(1)}, u32[]{:S(2)}, u32[]{:S(2)}) collective-permute-start(f32[16,8,512]{2,1,0:T(8,128)} %get-tuple-element.44), channel_id=1, source_target_pairs={{0,16},{8,24},{16,0},{24,8},{1,17},{9,25},{17,1},{25,9},{2,18},{10... | collective-permute-start | bytes 786440 | tf_op jit(solution)/shard_map/ppermute | solution.py:265
  35.8 4.0 %shard_map.71 = (f32[16,8,512]{2,1,0:T(8,128)}, f32[16,8,512]{2,1,0:T(8,128)}) custom-call(s32[16]{0:T(128)} %get-tuple-element.123.row_shift, s32[16]{0:T(128)} %get-tuple-element.122.col_shift, f32[96]{0:T(128)} %reshape.134.row_weight, f32[96]{0:T(128)} %reshape.135.col_weight, s32[1]{0:T(128)} %bitcast.4.me, f32[16,56,640]{2,1,0:T(8,128)} %select_maximum_fusion.padded, ...), custom_call_target="tpu_custom_call" | custom-call | tf_op jit(solution)/shard_map/pallas_call | solution.py:252
  39.9 4.1 %shard_map.68 = (f32[16,8,512]{2,1,0:T(8,128)}, f32[16,8,512]{2,1,0:T(8,128)}) custom-call(s32[16]{0:T(128)} %get-tuple-element.123.row_shift, s32[16]{0:T(128)} %get-tuple-element.122.col_shift, f32[96]{0:T(128)} %reshape.134.row_weight, f32[96]{0:T(128)} %reshape.135.col_weight, s32[1]{0:T(128)} %bitcast.4.me, f32[16,56,640]{2,1,0:T(8,128)} %select_maximum_fusion.padded, ...), custom_call_target="tpu_custom_call" | custom-call | tf_op jit(solution)/shard_map/pallas_call | solution.py:252
  44.0 1.1 %collective-permute-start.5 = (f32[16,8,512]{2,1,0:T(8,128)S(1)}, f32[16,8,512]{2,1,0:T(8,128)S(1)}, u32[]{:S(2)}, u32[]{:S(2)}) collective-permute-start(f32[16,8,512]{2,1,0:T(8,128)S(1)} %copy-done.7), channel_id=1, source_target_pairs={{0,24},{8,0},{16,8},{24,16},{1,25},{9,1},{17,9},{25,17},{2,26},{10... | collective-permute-start | bytes 786440 | tf_op jit(solution)/shard_map/ppermute | solution.py:265
  45.2 1.0 %constant_dynamic-update-slice_fusion.3 = f32[64,8,512]{2,1,0:T(8,128)S(1)} fusion(f32[16,8,512]{2,1,0:T(8,128)} %get-tuple-element.42), kind=kLoop, calls=%fused_computation.101 | loop fusion | bytes 524288
  46.2 0.6 collective-permute-done.4
  46.8 5.1 %collective-permute-done.5 = f32[16,8,512]{2,1,0:T(8,128)S(1)} collective-permute-done((f32[16,8,512]{2,1,0:T(8,128)S(1)}, f32[16,8,512]{2,1,0:T(8,128)S(1)}, u32[]{:S(2)}, u32[]{:S(2)}) %collective-permute-start.5) | collective-permute-done | bytes 262176 | tf_op jit(solution)/shard_map/ppermute | solution.py:265
  52.1 3.6 %while.13 = (s32[]{:T(128)}, f32[8,512]{1,0:T(8,128)S(1)}, f32[8,512]{1,0:T(8,128)S(1)}, f32[64,8,512]{2,1,0:T(8,128)S(1)}, f32[8,512]{1,0:T(8,128)S(1)}, /*index=5*/s32[]{:T(128)}, s32[]{:T(128)}) while((s32[]{:T(128)}, f32[8,512]{1,0:T(8,128)S(1)}, f32[8,512]{1,0:T(8,128)S(1)}, f32[64,8,512]{2,1,0:T(8,128)S(1)}, ...), condition=%wide.region_5.7_spmd.clone, body=%wide.region_3.6_spmd.clone.sunk | while | flops 1110019 | bytes 1302617 | solution.py:94
  55.9 0.7 tile.2
  56.6 3.9 %all-to-all-start = ((f32[8,8,512]{2,1,0:T(8,128)}), f32[8,8,512]{2,1,0:T(8,128)S(1)}, u32[]{:S(2)}, u32[]{:S(2)}) async-start(f32[8,8,512]{2,1,0:T(8,128)} %tile.2), calls=%async_computation | async-start | bytes 262144 | tf_op jit(solution)/shard_map/all_to_all | solution.py:292
  60.6 0.6 gather_fusion
  61.2 6.5 %all-to-all-done = f32[8,8,512]{2,1,0:T(8,128)S(1)} async-done(((f32[8,8,512]{2,1,0:T(8,128)}), f32[8,8,512]{2,1,0:T(8,128)S(1)}, u32[]{:S(2)}, u32[]{:S(2)}) %all-to-all-start) | async-done | bytes 131104 | tf_op jit(solution)/shard_map/all_to_all | solution.py:292
  67.9 3.5 %collective-permute-start.6 = (f32[4,520]{1,0:T(4,128)S(1)}, f32[4,520]{1,0:T(4,128)S(1)}, u32[]{:S(2)}, u32[]{:S(2)}) collective-permute-start(f32[4,520]{1,0:T(4,128)S(1)} %get-tuple-element.87), channel_id=1, source_target_pairs={{0,2},{2,4},{4,6},{1,3},{3,5},{5,7},{8,10},{10,12},{12,14},{9,11},... | collective-permute-start | bytes 24968 | tf_op jit(solution)/shard_map/ppermute | solution.py:28
  71.4 1.9 %collective-permute-start.7 = (f32[4,520]{1,0:T(4,128)S(1)}, f32[4,520]{1,0:T(4,128)S(1)}, u32[]{:S(2)}, u32[]{:S(2)}) collective-permute-start(f32[4,520]{1,0:T(4,128)S(1)} %get-tuple-element.88), channel_id=1, source_target_pairs={{2,0},{4,2},{6,4},{3,1},{5,3},{7,5},{10,8},{12,10},{14,12},{11,9},... | collective-permute-start | bytes 24968 | tf_op jit(solution)/shard_map/ppermute | solution.py:29
  73.4 0.6 constant_dynamic-slice_fusion
  74.0 2.4 %collective-permute-done.7 = f32[4,520]{1,0:T(4,128)S(1)} collective-permute-done((f32[4,520]{1,0:T(4,128)S(1)}, f32[4,520]{1,0:T(4,128)S(1)}, u32[]{:S(2)}, u32[]{:S(2)}) %collective-permute-start.7) | collective-permute-done | bytes 8352 | tf_op jit(solution)/shard_map/ppermute | solution.py:29
  77.1 1.3 %fusion.11 = f32[8,32,512]{2,1,0:T(8,128)S(1)} fusion(f32[8,32,520]{2,1,0:T(8,128)S(1)} %multiply_add_fusion, f32[8]{0:T(128)S(1)} %get-tuple-element.104, f32[8]{0:T(128)S(1)} %get-tuple-element.105, f32[8]{0:T(128)S(1)} %get-tuple-element.106, f32[8]{0:T(128)S(1)} %get-tuple-element.107, f32[8]{0:T(128)S(1)} %get-tuple-element.108, ...), kind=kLoop, calls=%fused_computation.28 | loop fusion | flops 2228224 | bytes 5243168 | tf_op jit(solution)/shard_map/add | solution.py:313
  78.4 2.0 %fusion.10 = f32[16,32,512]{2,1,0:T(8,128)} fusion(s32[16,32,512]{2,1,0:T(8,128)S(1)} %copy-done, f32[32,512]{1,0:T(8,128)S(1)} %get-tuple-element.80, f32[16]{0:T(128)S(1)} %get-tuple-element.113, f32[32,512]{1,0:T(8,128)S(1)} %get-tuple-element.81, f32[16]{0:T(128)S(1)} %get-tuple-element.114, f32[32,512]{1,0:T(8,128)S(1)} %get-tuple-element.82, ...), kind=kLoop, calls=%fused_computation.23 | loop fusion | flops 4980736 | bytes 3670532 | tf_op jit(solution)/shard_map/jit(_where)/select_n | solution.py:321
  (135 shorter events, 6.9 us)
Async XLA Ops:
  0.6 16.5 %copy-start.1 = (f32[16,32,512]{2,1,0:T(8,128)S(1)}, f32[16,32,512]{2,1,0:T(8,128)}, u32[]{:S(2)}) copy-start(f32[16,32,512]{2,1,0:T(8,128)} %param.8) | copy-start | bytes 3145732
  2.1 16.9 %copy-start.6 = (s32[16,2]{0,1:T(2,128)S(1)}, s32[16,2]{0,1:T(2,128)}, u32[]{:S(2)}) copy-start(s32[16,2]{0,1:T(2,128)} %param.10) | copy-start | bytes 388
  2.1 10.6 %collective-permute-start = (f32[16,11,512]{2,1,0:T(8,128)S(1)}, f32[16,11,512]{2,1,0:T(8,128)S(1)}, u32[]{:S(2)}, u32[]{:S(2)}) collective-permute-start(f32[16,11,512]{2,1,0:T(8,128)S(1)} %get-tuple-element.77), channel_id=1, source_target_pairs={{0,2},{2,4},{4,6},{1,3},{3,5},{5,7},{8,10},{10,12},{12,14},{9,11},... | collective-permute-start | bytes 1081352 | tf_op jit(solution)/shard_map/ppermute | solution.py:28
  6.6 10.5 %collective-permute-start.1 = (f32[16,11,512]{2,1,0:T(8,128)S(1)}, f32[16,11,512]{2,1,0:T(8,128)S(1)}, u32[]{:S(2)}, u32[]{:S(2)}) collective-permute-start(f32[16,11,512]{2,1,0:T(8,128)S(1)} %get-tuple-element.78), channel_id=1, source_target_pairs={{2,0},{4,2},{6,4},{3,1},{5,3},{7,5},{10,8},{12,10},{14,12},{11,9},... | collective-permute-start | bytes 1081352 | tf_op jit(solution)/shard_map/ppermute | solution.py:29
  17.7 3.1 %collective-permute-start.2 = (f32[11,864]{1,0:T(8,128)S(1)}, f32[11,864]{1,0:T(8,128)S(1)}, u32[]{:S(2)}, u32[]{:S(2)}) collective-permute-start(f32[11,864]{1,0:T(8,128)S(1)} %reshape.137), channel_id=1, source_target_pairs={{0,1},{1,0},{2,3},{3,2},{4,5},{5,4},{6,7},{7,6},{8,9},{9,8},{10,11... | collective-permute-start | bytes 114056 | tf_op jit(solution)/shard_map/ppermute | solution.py:48
  28.0 18.1 %collective-permute-start.3 = (f32[16,8,512]{2,1,0:T(8,128)}, f32[16,8,512]{2,1,0:T(8,128)S(1)}, u32[]{:S(2)}, u32[]{:S(2)}) collective-permute-start(f32[16,8,512]{2,1,0:T(8,128)} %get-tuple-element.43), channel_id=1, source_target_pairs={{0,8},{8,16},{16,24},{24,0},{1,9},{9,17},{17,25},{25,1},{2,10},{10... | collective-permute-start | bytes 786440 | tf_op jit(solution)/shard_map/ppermute | solution.py:265
  33.4 13.3 %collective-permute-start.4 = (f32[16,8,512]{2,1,0:T(8,128)}, f32[16,8,512]{2,1,0:T(8,128)S(1)}, u32[]{:S(2)}, u32[]{:S(2)}) collective-permute-start(f32[16,8,512]{2,1,0:T(8,128)} %get-tuple-element.44), channel_id=1, source_target_pairs={{0,16},{8,24},{16,0},{24,8},{1,17},{9,25},{17,1},{25,9},{2,18},{10... | collective-permute-start | bytes 786440 | tf_op jit(solution)/shard_map/ppermute | solution.py:265
  39.9 4.2 %copy-start.7 = (f32[16,8,512]{2,1,0:T(8,128)S(1)}, f32[16,8,512]{2,1,0:T(8,128)}, u32[]{:S(2)}) copy-start(f32[16,8,512]{2,1,0:T(8,128)} %get-tuple-element.45) | copy-start | bytes 786436
  44.0 7.8 %collective-permute-start.5 = (f32[16,8,512]{2,1,0:T(8,128)S(1)}, f32[16,8,512]{2,1,0:T(8,128)S(1)}, u32[]{:S(2)}, u32[]{:S(2)}) collective-permute-start(f32[16,8,512]{2,1,0:T(8,128)S(1)} %copy-done.7), channel_id=1, source_target_pairs={{0,24},{8,0},{16,8},{24,16},{1,25},{9,1},{17,9},{25,17},{2,26},{10... | collective-permute-start | bytes 786440 | tf_op jit(solution)/shard_map/ppermute | solution.py:265
  52.0 8.5 %copy-start.2 = (f32[16,8,512]{2,1,0:T(8,128)S(1)}, f32[16,8,512]{2,1,0:T(8,128)}, u32[]{:S(2)}) copy-start(f32[16,8,512]{2,1,0:T(8,128)} %get-tuple-element.39) | copy-start | bytes 786436
  52.0 8.5 %copy-start.3 = (f32[16,8,512]{2,1,0:T(8,128)S(1)}, f32[16,8,512]{2,1,0:T(8,128)}, u32[]{:S(2)}) copy-start(f32[16,8,512]{2,1,0:T(8,128)} %get-tuple-element.40) | copy-start | bytes 786436
  52.1 8.5 %copy-start.4 = (f32[16,8,512]{2,1,0:T(8,128)S(1)}, f32[16,8,512]{2,1,0:T(8,128)}, u32[]{:S(2)}) copy-start(f32[16,8,512]{2,1,0:T(8,128)} %get-tuple-element.41) | copy-start | bytes 786436
  52.1 8.5 %copy-start.5 = (f32[16,8,512]{2,1,0:T(8,128)S(1)}, f32[16,8,512]{2,1,0:T(8,128)}, u32[]{:S(2)}) copy-start(f32[16,8,512]{2,1,0:T(8,128)} %get-tuple-element.38) | copy-start | bytes 786436
  56.6 11.2 %all-to-all-start = ((f32[8,8,512]{2,1,0:T(8,128)}), f32[8,8,512]{2,1,0:T(8,128)S(1)}, u32[]{:S(2)}, u32[]{:S(2)}) async-start(f32[8,8,512]{2,1,0:T(8,128)} %tile.2), calls=%async_computation | async-start | bytes 262144 | tf_op jit(solution)/shard_map/all_to_all | solution.py:292
  67.9 6.1 %collective-permute-start.6 = (f32[4,520]{1,0:T(4,128)S(1)}, f32[4,520]{1,0:T(4,128)S(1)}, u32[]{:S(2)}, u32[]{:S(2)}) collective-permute-start(f32[4,520]{1,0:T(4,128)S(1)} %get-tuple-element.87), channel_id=1, source_target_pairs={{0,2},{2,4},{4,6},{1,3},{3,5},{5,7},{8,10},{10,12},{12,14},{9,11},... | collective-permute-start | bytes 24968 | tf_op jit(solution)/shard_map/ppermute | solution.py:28
  71.4 5.0 %collective-permute-start.7 = (f32[4,520]{1,0:T(4,128)S(1)}, f32[4,520]{1,0:T(4,128)S(1)}, u32[]{:S(2)}, u32[]{:S(2)}) collective-permute-start(f32[4,520]{1,0:T(4,128)S(1)} %get-tuple-element.88), channel_id=1, source_target_pairs={{2,0},{4,2},{6,4},{3,1},{5,3},{7,5},{10,8},{12,10},{14,12},{11,9},... | collective-permute-start | bytes 24968 | tf_op jit(solution)/shard_map/ppermute | solution.py:29
  77.1 1.3 %copy-start = (s32[16,32,512]{2,1,0:T(8,128)S(1)}, s32[16,32,512]{2,1,0:T(8,128)}, u32[]{:S(2)}) copy-start(s32[16,32,512]{2,1,0:T(8,128)} %bad.7) | copy-start | bytes 3145732

commit v15 on v14

--- a/solution.py
+++ b/solution.py
@@ -77,31 +77,6 @@
         jnp.float32
     )
     return jnp.dot(chooser, kernel_table, precision=lax.Precision.HIGHEST)
-
-
-def bisect_lower(valid_count, count_below):
-
-    def one_pass(sweep_no, bounds):
-        lower_edge, upper_edge = bounds
-        middle = 0.5 * (lower_edge + upper_edge)
-        enough = 2.0 * count_below(middle) >= valid_count
-        return (jnp.where(enough, lower_edge, middle), jnp.where(enough, middle, upper_edge))
-
-    initial = (
-        jnp.full(valid_count.shape, -pivot_span, jnp.float32),
-        jnp.full(valid_count.shape, pivot_span, jnp.float32),
-    )
-    return lax.fori_loop(0, PASSES, one_pass, initial)[0]
-
-
-def stack_median(pixel_stack):
-    valid_count = jnp.sum(pixel_stack < half_sentinel, axis=0, dtype=jnp.float32)
-
-    def count_below(middle):
-        return jnp.sum(pixel_stack <= middle[None], axis=0, dtype=jnp.float32)
-
-    lower_edge = bisect_lower(valid_count, count_below)
-    return jnp.min(jnp.where(pixel_stack > lower_edge[None], pixel_stack, sentinel), axis=0)
 
 
 TAPS = 6
@@ -271,6 +246,56 @@
     return warped, jnp.concatenate([slots[s] for s in range(bands)], axis=0)
 
 
+def _median_kernel(stack, out):
+    depth = stack.shape[0]
+    band_rows = stack.shape[1]
+    copies = out.shape[0] // band_rows
+
+    def count_valid(e, total):
+        return total + (stack[e] < half_sentinel).astype(jnp.float32)
+
+    valid_count = lax.fori_loop(
+        0, depth, count_valid, jnp.zeros(stack.shape[1:], jnp.float32), unroll=8
+    )
+
+    def one_pass(sweep_no, bounds):
+        lower_edge, upper_edge = bounds
+        middle = 0.5 * (lower_edge + upper_edge)
+
+        def count_below(e, total):
+            return total + (stack[e] <= middle).astype(jnp.float32)
+
+        counted = lax.fori_loop(
+            0, depth, count_below, jnp.zeros(stack.shape[1:], jnp.float32), unroll=8
+        )
+        enough = 2.0 * counted >= valid_count
+        return (jnp.where(enough, lower_edge, middle), jnp.where(enough, middle, upper_edge))
+
+    initial = (
+        jnp.full(stack.shape[1:], -pivot_span, jnp.float32),
+        jnp.full(stack.shape[1:], pivot_span, jnp.float32),
+    )
+    lower_edge = lax.fori_loop(0, PASSES, one_pass, initial)[0]
+
+    def smallest_above(e, best):
+        value = stack[e]
+        return jnp.minimum(best, jnp.where(value > lower_edge, value, sentinel))
+
+    median = lax.fori_loop(
+        0, depth, smallest_above, jnp.full(stack.shape[1:], sentinel, jnp.float32), unroll=8
+    )
+    for copy_no in range(copies):
+        out[copy_no * band_rows : (copy_no + 1) * band_rows] = median
+
+
+def median_copies(stack, copies):
+    vmem = pl.BlockSpec(memory_space=pltpu.VMEM)
+    shape = jax.ShapeDtypeStruct((copies * stack.shape[1], stack.shape[2]), jnp.float32)
+    return pl.pallas_call(
+        _median_kernel, out_shape=shape, in_specs=[vmem], out_specs=vmem
+    )(stack)
+
+
 def body(exposures, bad_pixels, offsets, warp_index, blur_index):
     group_size, row_count, col_count = exposures.shape
     padded = extended(exposures, 1, 2, HALO)
@@ -285,12 +310,11 @@
             pairs = [(i, (i + step) % groups) for i in range(groups)]
             arrived.append(lax.ppermute(flagged[step], "exp", pairs))
         stack = jnp.concatenate(arrived, axis=0)
-    band = stack_median(stack)
     groups = lax.axis_size("exp")
     sides = lax.axis_size("col")
-    band_rows = band.shape[0]
+    band_rows = stack.shape[1]
     full = lax.all_to_all(
-        jnp.tile(band, (groups * sides, 1)), ("exp", "col"), split_axis=0, concat_axis=0, tiled=True
+        median_copies(stack, groups * sides), ("exp", "col"), split_axis=0, concat_axis=0, tiled=True
     )
     full = full.reshape(groups, sides, band_rows, col_count)
     full = full.transpose(0, 2, 1, 3).reshape(row_count, sides * col_count)

time: 80.9 us -> 87 us (1.075)
  Pallas kernels: 16.2 us -> 20.5 us
  starting transfers between devices: 22 us -> 26.1 us
  local copies, waits for them, and re-layouts: 7.78 us -> 5.98 us
  waiting for transfers between devices: 20.9 us -> 22.4 us
  other arithmetic: 11.3 us -> 10.2 us
    all_to_all x1, starting transfers between devices: 3.93 us -> 8.99 us  [body(): lax.all_to_all(median_copies(stack, groups * sides), ('exp', 'col'), spli...]
    pallas_call x0 -> x1, Pallas kernels: none -> 4.32 us  [median_copies(): pl.pallas_call(_median_kernel, out_shape=shape, in_specs=[vmem], out_spec...]
    reduce_sum x17 -> x0, other arithmetic: 2.53 us -> none  [the longest x16 2.39 us: count_below(): return jnp.sum(pixel_stack <= middle[None], axis=0, dtype=jnp.float32)]
    concatenate x0 -> x1, other arithmetic: none -> 1.99 us  [warp_by_slot(): return (warped, jnp.concatenate([slots[s] for s in range(bands)], axis=0))]
    ppermute x3, waiting for transfers between devices: 5.68 us -> 7.47 us  [warp_by_slot(): slots[step] = lax.ppermute(flagged, 'exp', pairs)]
    unnamed x19 -> x18, local copies, waits for them, and re-layouts: 1.05 us -> 0.04 us
  transfers between devices with their start and end apart: 9 -> 9, of which waited for: 6 -> 7; matrix products, arithmetic and copies ran while one was open for 8% -> 6% of each run, Pallas kernels for 15% -> 5%
where the time goes in v15:
time: 87 us; the launch traced here: 86.5 us
  starting transfers between devices  26.1 us (30%)
  waiting for transfers between devices  22.4 us (26%)
  Pallas kernels  20.5 us (24%)
  other arithmetic  10.2 us (12%)
  local copies, waits for them, and re-layouts  5.98 us (7%)
  between operations  0.94 us (1%)
    pallas_call x4, Pallas kernels, warp_by_slot(): pl.pallas_call(functools.partial(_slot_kernel, step), out_shape=(banded,...  16.2 us
    all_to_all x1, starting transfers between devices, body(): lax.all_to_all(median_copies(stack, groups * sides), ('exp', 'col'), spli...  8.99 us
    ppermute x3, waiting for transfers between devices, warp_by_slot(): slots[step] = lax.ppermute(flagged, 'exp', pairs)  7.47 us
    ppermute x2, starting transfers between devices, _row_halo(): lax.ppermute(lax.slice_in_dim(block, size - width, None, axis=dim), 'row'...  7.26 us
    ppermute x2, waiting for transfers between devices, _row_halo(): lax.ppermute(lax.slice_in_dim(block, 0, width, axis=dim), 'row', backward)  6.81 us
    all_to_all x1, waiting for transfers between devices, body(): lax.all_to_all(median_copies(stack, groups * sides), ('exp', 'col'), spli...  6.07 us
    ppermute x3, starting transfers between devices, warp_by_slot(): slots[step] = lax.ppermute(flagged, 'exp', pairs)  4.73 us
    pallas_call x1, Pallas kernels, median_copies(): pl.pallas_call(_median_kernel, out_shape=shape, in_specs=[vmem], out_spec...  4.32 us
  transfers between devices with their start and end apart: 9, of which 7 were waited for; matrix products, arithmetic and copies ran while one was open for 6% of the time, Pallas kernels for 5%

profile of v15, /device:TPU:1, one launch (start us, length us, event | category | flops | bytes accessed | tf_op | source)
XLA Modules:
  0.0 86.5 jit_solution(14442705871815356582)
XLA Ops:
  0.6 1.4 %fusion.106 = (f32[16,11,512]{2,1,0:T(8,128)S(1)}, f32[16,11,512]{2,1,0:T(8,128)S(1)}) fusion(f32[16,32,512]{2,1,0:T(8,128)} %param.6), kind=kLoop, calls=%fused_computation.207 | loop fusion | bytes 1441792 | tf_op jit(solution)/shard_map/slice | solution.py:28
  2.1 4.5 %collective-permute-start = (f32[16,11,512]{2,1,0:T(8,128)S(1)}, f32[16,11,512]{2,1,0:T(8,128)S(1)}, u32[]{:S(2)}, u32[]{:S(2)}) collective-permute-start(f32[16,11,512]{2,1,0:T(8,128)S(1)} %get-tuple-element.19), channel_id=1, source_target_pairs={{0,2},{2,4},{4,6},{1,3},{3,5},{5,7},{8,10},{10,12},{12,14},{9,11},... | collective-permute-start | bytes 1081352 | tf_op jit(solution)/shard_map/ppermute | solution.py:28
  6.6 1.9 %collective-permute-start.1 = (f32[16,11,512]{2,1,0:T(8,128)S(1)}, f32[16,11,512]{2,1,0:T(8,128)S(1)}, u32[]{:S(2)}, u32[]{:S(2)}) collective-permute-start(f32[16,11,512]{2,1,0:T(8,128)S(1)} %get-tuple-element.20), channel_id=1, source_target_pairs={{2,0},{4,2},{6,4},{3,1},{5,3},{7,5},{10,8},{12,10},{14,12},{11,9},... | collective-permute-start | bytes 1081352 | tf_op jit(solution)/shard_map/ppermute | solution.py:29
  8.6 0.8 slice_bitcast_fusion.25
  9.5 0.7 fusion.77
  10.5 0.6 add_bitcast_fusion
  11.3 1.4 %collective-permute-done = f32[16,11,512]{2,1,0:T(8,128)S(1)} collective-permute-done((f32[16,11,512]{2,1,0:T(8,128)S(1)}, f32[16,11,512]{2,1,0:T(8,128)S(1)}, u32[]{:S(2)}, u32[]{:S(2)}) %collective-permute-start) | collective-permute-done | bytes 360480 | tf_op jit(solution)/shard_map/ppermute | solution.py:28
  12.7 4.4 %collective-permute-done.1 = f32[16,11,512]{2,1,0:T(8,128)S(1)} collective-permute-done((f32[16,11,512]{2,1,0:T(8,128)S(1)}, f32[16,11,512]{2,1,0:T(8,128)S(1)}, u32[]{:S(2)}, u32[]{:S(2)}) %collective-permute-start.1) | collective-permute-done | bytes 360480 | tf_op jit(solution)/shard_map/ppermute | solution.py:29
  17.7 1.3 %collective-permute-start.2 = (f32[11,864]{1,0:T(8,128)S(1)}, f32[11,864]{1,0:T(8,128)S(1)}, u32[]{:S(2)}, u32[]{:S(2)}) collective-permute-start(f32[11,864]{1,0:T(8,128)S(1)} %reshape.130), channel_id=1, source_target_pairs={{0,1},{1,0},{2,3},{3,2},{4,5},{5,4},{6,7},{7,6},{8,9},{9,8},{10,11... | collective-permute-start | bytes 114056 | tf_op jit(solution)/shard_map/ppermute | solution.py:48
  19.0 0.6 reshape.127.row_weight
  20.2 0.6 collective-permute-done.2
  21.5 2.5 %select_maximum_fusion.padded = f32[16,56,640]{2,1,0:T(8,128)} fusion(f32[16,54,11]{2,1,0:T(8,128)S(1)} %bitcast.83, f32[16,54,11]{2,1,0:T(8,128)S(1)} %bitcast.82, f32[16,11,512]{2,1,0:T(8,128)S(1)} %collective-permute-done.1, f32[16,32,512]{2,1,0:T(8,128)S(1)} %copy-done.1, f32[16,11,512]{2,1,0:T(8,128)S(1)} %collective-permute-done), kind=kLoop, calls=%fused_computation.1 | loop fusion | flops 9748480 | bytes 4139264 | tf_op jit(solution)/shard_map/concatenate | solution.py:53
  24.0 4.0 %shard_map.70 = (f32[16,8,512]{2,1,0:T(8,128)}, f32[16,8,512]{2,1,0:T(8,128)}) custom-call(s32[16]{0:T(128)} %get-tuple-element.65.row_shift, s32[16]{0:T(128)} %get-tuple-element.64.col_shift, f32[96]{0:T(128)} %reshape.127.row_weight, f32[96]{0:T(128)} %reshape.128.col_weight, s32[1]{0:T(128)} %bitcast.4.me, f32[16,56,640]{2,1,0:T(8,128)} %select_maximum_fusion.padded, ...), custom_call_target="tpu_custom_call" | custom-call | tf_op jit(solution)/shard_map/pallas_call | solution.py:227
  28.0 4.0 %shard_map.69 = (f32[16,8,512]{2,1,0:T(8,128)}, f32[16,8,512]{2,1,0:T(8,128)}) custom-call(s32[16]{0:T(128)} %get-tuple-element.65.row_shift, s32[16]{0:T(128)} %get-tuple-element.64.col_shift, f32[96]{0:T(128)} %reshape.127.row_weight, f32[96]{0:T(128)} %reshape.128.col_weight, s32[1]{0:T(128)} %bitcast.4.me, f32[16,56,640]{2,1,0:T(8,128)} %select_maximum_fusion.padded, ...), custom_call_target="tpu_custom_call" | custom-call | tf_op jit(solution)/shard_map/pallas_call | solution.py:227
  32.1 4.1 %shard_map.71 = (f32[16,8,512]{2,1,0:T(8,128)}, f32[16,8,512]{2,1,0:T(8,128)}) custom-call(s32[16]{0:T(128)} %get-tuple-element.65.row_shift, s32[16]{0:T(128)} %get-tuple-element.64.col_shift, f32[96]{0:T(128)} %reshape.127.row_weight, f32[96]{0:T(128)} %reshape.128.col_weight, s32[1]{0:T(128)} %bitcast.4.me, f32[16,56,640]{2,1,0:T(8,128)} %select_maximum_fusion.padded, ...), custom_call_target="tpu_custom_call" | custom-call | tf_op jit(solution)/shard_map/pallas_call | solution.py:227
  36.2 1.3 %collective-permute-start.3 = (f32[16,8,512]{2,1,0:T(8,128)S(1)}, f32[16,8,512]{2,1,0:T(8,128)S(1)}, u32[]{:S(2)}, u32[]{:S(2)}) collective-permute-start(f32[16,8,512]{2,1,0:T(8,128)S(1)} %copy-done.8), channel_id=1, source_target_pairs={{0,8},{8,16},{16,24},{24,0},{1,9},{9,17},{17,25},{25,1},{2,10},{10... | collective-permute-start | bytes 786440 | tf_op jit(solution)/shard_map/ppermute | solution.py:240
  37.6 2.3 %collective-permute-start.4 = (f32[16,8,512]{2,1,0:T(8,128)S(1)}, f32[16,8,512]{2,1,0:T(8,128)S(1)}, u32[]{:S(2)}, u32[]{:S(2)}) collective-permute-start(f32[16,8,512]{2,1,0:T(8,128)S(1)} %copy-done.7), channel_id=1, source_target_pairs={{0,16},{8,24},{16,0},{24,8},{1,17},{9,25},{17,1},{25,9},{2,18},{10... | collective-permute-start | bytes 786440 | tf_op jit(solution)/shard_map/ppermute | solution.py:240
  39.9 1.1 %collective-permute-start.5 = (f32[16,8,512]{2,1,0:T(8,128)}, f32[16,8,512]{2,1,0:T(8,128)S(1)}, u32[]{:S(2)}, u32[]{:S(2)}) collective-permute-start(f32[16,8,512]{2,1,0:T(8,128)} %get-tuple-element.18), channel_id=1, source_target_pairs={{0,24},{8,0},{16,8},{24,16},{1,25},{9,1},{17,9},{25,17},{2,26},{10... | collective-permute-start | bytes 786440 | tf_op jit(solution)/shard_map/ppermute | solution.py:240
  41.0 4.0 %shard_map.68 = (f32[16,8,512]{2,1,0:T(8,128)}, f32[16,8,512]{2,1,0:T(8,128)}) custom-call(s32[16]{0:T(128)} %get-tuple-element.65.row_shift, s32[16]{0:T(128)} %get-tuple-element.64.col_shift, f32[96]{0:T(128)} %reshape.127.row_weight, f32[96]{0:T(128)} %reshape.128.col_weight, s32[1]{0:T(128)} %bitcast.4.me, f32[16,56,640]{2,1,0:T(8,128)} %select_maximum_fusion.padded, ...), custom_call_target="tpu_custom_call" | custom-call | tf_op jit(solution)/shard_map/pallas_call | solution.py:227
  45.0 1.2 %collective-permute-done.3 = f32[16,8,512]{2,1,0:T(8,128)S(1)} collective-permute-done((f32[16,8,512]{2,1,0:T(8,128)S(1)}, f32[16,8,512]{2,1,0:T(8,128)S(1)}, u32[]{:S(2)}, u32[]{:S(2)}) %collective-permute-start.3) | collective-permute-done | bytes 262176 | tf_op jit(solution)/shard_map/ppermute | solution.py:240
  46.2 6.3 %collective-permute-done.4 = f32[16,8,512]{2,1,0:T(8,128)S(1)} collective-permute-done((f32[16,8,512]{2,1,0:T(8,128)S(1)}, f32[16,8,512]{2,1,0:T(8,128)S(1)}, u32[]{:S(2)}, u32[]{:S(2)}) %collective-permute-start.4) | collective-permute-done | bytes 262176 | tf_op jit(solution)/shard_map/ppermute | solution.py:240
  52.5 2.0 %pad_maximum_fusion.1.stack = f32[64,8,512]{2,1,0:T(8,128)} fusion(f32[16,8,512]{2,1,0:T(8,128)S(1)} %collective-permute-done.5, f32[16,8,512]{2,1,0:T(8,128)S(1)} %collective-permute-done.4, f32[16,8,512]{2,1,0:T(8,128)S(1)} %collective-permute-done.3, f32[16,8,512]{2,1,0:T(8,128)} %get-tuple-element.15), kind=kLoop, calls=%fused_computation.15 | loop fusion | flops 786432 | bytes 2097152 | tf_op jit(solution)/shard_map/concatenate | solution.py:246
  54.5 4.3 %shard_map.72 = f32[64,512]{1,0:T(8,128)} custom-call(f32[64,8,512]{2,1,0:T(8,128)} %pad_maximum_fusion.1.stack), custom_call_target="tpu_custom_call" | custom-call | tf_op jit(solution)/shard_map/pallas_call | solution.py:294
  58.8 9.0 %all-to-all-start = ((f32[8,8,512]{2,1,0:T(8,128)}), f32[8,8,512]{2,1,0:T(8,128)S(1)}, u32[]{:S(2)}, u32[]{:S(2)}) async-start(f32[8,8,512]{2,1,0:T(8,128)} %bitcast.87), calls=%async_computation | async-start | bytes 262144 | tf_op jit(solution)/shard_map/all_to_all | solution.py:316
  68.0 0.6 gather_fusion
  68.6 6.1 %all-to-all-done = f32[8,8,512]{2,1,0:T(8,128)S(1)} async-done(((f32[8,8,512]{2,1,0:T(8,128)}), f32[8,8,512]{2,1,0:T(8,128)S(1)}, u32[]{:S(2)}, u32[]{:S(2)}) %all-to-all-start) | async-done | bytes 131104 | tf_op jit(solution)/shard_map/all_to_all | solution.py:316
  74.8 2.7 %collective-permute-start.6 = (f32[4,520]{1,0:T(4,128)S(1)}, f32[4,520]{1,0:T(4,128)S(1)}, u32[]{:S(2)}, u32[]{:S(2)}) collective-permute-start(f32[4,520]{1,0:T(4,128)S(1)} %get-tuple-element.29), channel_id=1, source_target_pairs={{0,2},{2,4},{4,6},{1,3},{3,5},{5,7},{8,10},{10,12},{12,14},{9,11},... | collective-permute-start | bytes 24968 | tf_op jit(solution)/shard_map/ppermute | solution.py:28
  77.6 1.9 %collective-permute-start.7 = (f32[4,520]{1,0:T(4,128)S(1)}, f32[4,520]{1,0:T(4,128)S(1)}, u32[]{:S(2)}, u32[]{:S(2)}) collective-permute-start(f32[4,520]{1,0:T(4,128)S(1)} %get-tuple-element.30), channel_id=1, source_target_pairs={{2,0},{4,2},{6,4},{3,1},{5,3},{7,5},{10,8},{12,10},{14,12},{11,9},... | collective-permute-start | bytes 24968 | tf_op jit(solution)/shard_map/ppermute | solution.py:29
  79.5 0.6 constant_dynamic-slice_fusion
  80.1 2.4 %collective-permute-done.7 = f32[4,520]{1,0:T(4,128)S(1)} collective-permute-done((f32[4,520]{1,0:T(4,128)S(1)}, f32[4,520]{1,0:T(4,128)S(1)}, u32[]{:S(2)}, u32[]{:S(2)}) %collective-permute-start.7) | collective-permute-done | bytes 8352 | tf_op jit(solution)/shard_map/ppermute | solution.py:29
  83.2 1.3 %fusion.10 = f32[8,32,512]{2,1,0:T(8,128)S(1)} fusion(f32[8,32,520]{2,1,0:T(8,128)S(1)} %multiply_add_fusion, f32[8]{0:T(128)S(1)} %get-tuple-element.46, f32[8]{0:T(128)S(1)} %get-tuple-element.47, f32[8]{0:T(128)S(1)} %get-tuple-element.48, f32[8]{0:T(128)S(1)} %get-tuple-element.49, f32[8]{0:T(128)S(1)} %get-tuple-element.50, f32[8]{0:T(128)S(1)} %get-tuple-element.51, ...), kind=kLoop, calls=%fused_computation.21 | loop fusion | flops 2228224 | bytes 5243168 | tf_op jit(solution)/shard_map/add | solution.py:337
  84.5 2.0 %fusion.9 = f32[16,32,512]{2,1,0:T(8,128)} fusion(s32[16,32,512]{2,1,0:T(8,128)S(1)} %copy-done, f32[32,512]{1,0:T(8,128)S(1)} %get-tuple-element.22, f32[16]{0:T(128)S(1)} %get-tuple-element.55, f32[32,512]{1,0:T(8,128)S(1)} %get-tuple-element.23, f32[16]{0:T(128)S(1)} %get-tuple-element.56, f32[32,512]{1,0:T(8,128)S(1)} %get-tuple-element.24, ...), kind=kLoop, calls=%fused_computation.17 | loop fusion | flops 4980736 | bytes 3670532 | tf_op jit(solution)/shard_map/jit(_where)/select_n | solution.py:345
  (49 shorter events, 3.6 us)
Async XLA Ops:
  0.6 16.5 %copy-start.1 = (f32[16,32,512]{2,1,0:T(8,128)S(1)}, f32[16,32,512]{2,1,0:T(8,128)}, u32[]{:S(2)}) copy-start(f32[16,32,512]{2,1,0:T(8,128)} %param.6) | copy-start | bytes 3145732
  0.6 9.9 %copy-start.6 = (s32[16,2]{0,1:T(2,128)S(1)}, s32[16,2]{0,1:T(2,128)}, u32[]{:S(2)}) copy-start(s32[16,2]{0,1:T(2,128)} %param.8) | copy-start | bytes 388
  2.1 10.6 %collective-permute-start = (f32[16,11,512]{2,1,0:T(8,128)S(1)}, f32[16,11,512]{2,1,0:T(8,128)S(1)}, u32[]{:S(2)}, u32[]{:S(2)}) collective-permute-start(f32[16,11,512]{2,1,0:T(8,128)S(1)} %get-tuple-element.19), channel_id=1, source_target_pairs={{0,2},{2,4},{4,6},{1,3},{3,5},{5,7},{8,10},{10,12},{12,14},{9,11},... | collective-permute-start | bytes 1081352 | tf_op jit(solution)/shard_map/ppermute | solution.py:28
  6.6 10.5 %collective-permute-start.1 = (f32[16,11,512]{2,1,0:T(8,128)S(1)}, f32[16,11,512]{2,1,0:T(8,128)S(1)}, u32[]{:S(2)}, u32[]{:S(2)}) collective-permute-start(f32[16,11,512]{2,1,0:T(8,128)S(1)} %get-tuple-element.20), channel_id=1, source_target_pairs={{2,0},{4,2},{6,4},{3,1},{5,3},{7,5},{10,8},{12,10},{14,12},{11,9},... | collective-permute-start | bytes 1081352 | tf_op jit(solution)/shard_map/ppermute | solution.py:29
  17.7 3.1 %collective-permute-start.2 = (f32[11,864]{1,0:T(8,128)S(1)}, f32[11,864]{1,0:T(8,128)S(1)}, u32[]{:S(2)}, u32[]{:S(2)}) collective-permute-start(f32[11,864]{1,0:T(8,128)S(1)} %reshape.130), channel_id=1, source_target_pairs={{0,1},{1,0},{2,3},{3,2},{4,5},{5,4},{6,7},{7,6},{8,9},{9,8},{10,11... | collective-permute-start | bytes 114056 | tf_op jit(solution)/shard_map/ppermute | solution.py:48
  32.1 4.2 %copy-start.8 = (f32[16,8,512]{2,1,0:T(8,128)S(1)}, f32[16,8,512]{2,1,0:T(8,128)}, u32[]{:S(2)}) copy-start(f32[16,8,512]{2,1,0:T(8,128)} %get-tuple-element.16) | copy-start | bytes 786436
  32.1 5.5 %copy-start.7 = (f32[16,8,512]{2,1,0:T(8,128)S(1)}, f32[16,8,512]{2,1,0:T(8,128)}, u32[]{:S(2)}) copy-start(f32[16,8,512]{2,1,0:T(8,128)} %get-tuple-element.17) | copy-start | bytes 786436
  36.2 10.0 %collective-permute-start.3 = (f32[16,8,512]{2,1,0:T(8,128)S(1)}, f32[16,8,512]{2,1,0:T(8,128)S(1)}, u32[]{:S(2)}, u32[]{:S(2)}) collective-permute-start(f32[16,8,512]{2,1,0:T(8,128)S(1)} %copy-done.8), channel_id=1, source_target_pairs={{0,8},{8,16},{16,24},{24,0},{1,9},{9,17},{17,25},{25,1},{2,10},{10... | collective-permute-start | bytes 786440 | tf_op jit(solution)/shard_map/ppermute | solution.py:240
  37.6 14.9 %collective-permute-start.4 = (f32[16,8,512]{2,1,0:T(8,128)S(1)}, f32[16,8,512]{2,1,0:T(8,128)S(1)}, u32[]{:S(2)}, u32[]{:S(2)}) collective-permute-start(f32[16,8,512]{2,1,0:T(8,128)S(1)} %copy-done.7), channel_id=1, source_target_pairs={{0,16},{8,24},{16,0},{24,8},{1,17},{9,25},{17,1},{25,9},{2,18},{10... | collective-permute-start | bytes 786440 | tf_op jit(solution)/shard_map/ppermute | solution.py:240
  39.9 12.6 %collective-permute-start.5 = (f32[16,8,512]{2,1,0:T(8,128)}, f32[16,8,512]{2,1,0:T(8,128)S(1)}, u32[]{:S(2)}, u32[]{:S(2)}) collective-permute-start(f32[16,8,512]{2,1,0:T(8,128)} %get-tuple-element.18), channel_id=1, source_target_pairs={{0,24},{8,0},{16,8},{24,16},{1,25},{9,1},{17,9},{25,17},{2,26},{10... | collective-permute-start | bytes 786440 | tf_op jit(solution)/shard_map/ppermute | solution.py:240
  45.0 22.8 %copy-start.2 = (f32[16,8,512]{2,1,0:T(8,128)S(1)}, f32[16,8,512]{2,1,0:T(8,128)}, u32[]{:S(2)}) copy-start(f32[16,8,512]{2,1,0:T(8,128)} %get-tuple-element.13) | copy-start | bytes 786436
  45.0 22.8 %copy-start.3 = (f32[16,8,512]{2,1,0:T(8,128)S(1)}, f32[16,8,512]{2,1,0:T(8,128)}, u32[]{:S(2)}) copy-start(f32[16,8,512]{2,1,0:T(8,128)} %get-tuple-element.12) | copy-start | bytes 786436
  45.0 22.8 %copy-start.4 = (f32[16,8,512]{2,1,0:T(8,128)S(1)}, f32[16,8,512]{2,1,0:T(8,128)}, u32[]{:S(2)}) copy-start(f32[16,8,512]{2,1,0:T(8,128)} %get-tuple-element.14) | copy-start | bytes 786436
  45.0 22.8 %copy-start.5 = (f32[16,8,512]{2,1,0:T(8,128)S(1)}, f32[16,8,512]{2,1,0:T(8,128)}, u32[]{:S(2)}) copy-start(f32[16,8,512]{2,1,0:T(8,128)} %get-tuple-element.11) | copy-start | bytes 786436
  58.8 15.8 %all-to-all-start = ((f32[8,8,512]{2,1,0:T(8,128)}), f32[8,8,512]{2,1,0:T(8,128)S(1)}, u32[]{:S(2)}, u32[]{:S(2)}) async-start(f32[8,8,512]{2,1,0:T(8,128)} %bitcast.87), calls=%async_computation | async-start | bytes 262144 | tf_op jit(solution)/shard_map/all_to_all | solution.py:316
  74.8 5.3 %collective-permute-start.6 = (f32[4,520]{1,0:T(4,128)S(1)}, f32[4,520]{1,0:T(4,128)S(1)}, u32[]{:S(2)}, u32[]{:S(2)}) collective-permute-start(f32[4,520]{1,0:T(4,128)S(1)} %get-tuple-element.29), channel_id=1, source_target_pairs={{0,2},{2,4},{4,6},{1,3},{3,5},{5,7},{8,10},{10,12},{12,14},{9,11},... | collective-permute-start | bytes 24968 | tf_op jit(solution)/shard_map/ppermute | solution.py:28
  77.6 5.0 %collective-permute-start.7 = (f32[4,520]{1,0:T(4,128)S(1)}, f32[4,520]{1,0:T(4,128)S(1)}, u32[]{:S(2)}, u32[]{:S(2)}) collective-permute-start(f32[4,520]{1,0:T(4,128)S(1)} %get-tuple-element.30), channel_id=1, source_target_pairs={{2,0},{4,2},{6,4},{3,1},{5,3},{7,5},{10,8},{12,10},{14,12},{11,9},... | collective-permute-start | bytes 24968 | tf_op jit(solution)/shard_map/ppermute | solution.py:29
  83.2 1.3 %copy-start = (s32[16,32,512]{2,1,0:T(8,128)S(1)}, s32[16,32,512]{2,1,0:T(8,128)}, u32[]{:S(2)}) copy-start(s32[16,32,512]{2,1,0:T(8,128)} %bad.7) | copy-start | bytes 3145732

commit v16 on v14

--- a/solution.py
+++ b/solution.py
@@ -186,8 +186,10 @@
     window = window_buf.shape[1]
     band = lax.rem(me[0] + step, bands)
     base = pl.multiple_of(band * band_rows, 8)
-    half = group_size // 2
-    spans = [(0, half), (half, group_size - half)]
+    parts = 8 if group_size % 8 == 0 else 2
+    share = group_size // parts
+    spans = [(part * share, share) for part in range(parts - 1)]
+    spans.append(((parts - 1) * share, group_size - (parts - 1) * share))
     fetches = [
         pltpu.make_async_copy(
             padded.at[pl.ds(lo, count), pl.ds(base, window), :],
@@ -196,11 +198,13 @@
         )
         for part, (lo, count) in enumerate(spans)
     ]
-    fetch_bad = pltpu.make_async_copy(bad.at[:, pl.ds(base, band_rows), :], bad_buf, sems.at[2])
+    fetch_bad = pltpu.make_async_copy(
+        bad.at[:, pl.ds(base, band_rows), :], bad_buf, sems.at[len(spans)]
+    )
     fetches[0].start()
     fetch_bad.start()
-    fetches[1].start()
-    fetches[0].wait()
+    for fetch in fetches[1:]:
+        fetch.start()
     fetch_bad.wait()
 
     def one_exposure(e, carry):
@@ -218,9 +222,9 @@
         flagged_out[e] = jnp.where(bad_buf[e] == 1, sentinel, total)
         return carry
 
-    lax.fori_loop(0, half, one_exposure, 0, unroll=True)
-    fetches[1].wait()
-    lax.fori_loop(half, group_size, one_exposure, 0, unroll=True)
+    for fetch, (lo, count) in zip(fetches, spans):
+        fetch.wait()
+        lax.fori_loop(lo, lo + count, one_exposure, 0, unroll=True)
 
 
 def warp_by_slot(padded, bad_pixels, offsets, warp_index):
@@ -257,7 +261,7 @@
             scratch_shapes=[
                 pltpu.VMEM((group_size, window, lanes), jnp.float32),
                 pltpu.VMEM((group_size, band_rows, col_count), jnp.int32),
-                pltpu.SemaphoreType.DMA((3,)),
+                pltpu.SemaphoreType.DMA((9,)),
             ],
         )(row_shift, col_shift, row_weight, col_weight, me, padded, bad_pixels)
         if step:

time: 80.9 us -> 83.2 us (1.028)
  Pallas kernels: 16.2 us -> 18.6 us
  starting transfers between devices: 22 us -> 24.4 us
  waiting for transfers between devices: 20.9 us -> 18.5 us
    ppermute x2, starting transfers between devices: 8.08 us -> 10.5 us  [_row_halo(): lax.ppermute(lax.slice_in_dim(block, size - width, None, axis=dim), 'row'...]
    pallas_call x4, Pallas kernels: 16.2 us -> 18.6 us  [warp_by_slot(): pl.pallas_call(functools.partial(_slot_kernel, step), out_shape=(banded,...]
    ppermute x3, waiting for transfers between devices: 5.68 us -> 4.29 us  [warp_by_slot(): slots[step] = lax.ppermute(flagged, 'exp', pairs)]
    all_to_all x1, waiting for transfers between devices: 6.46 us -> 5.46 us  [body(): lax.all_to_all(jnp.tile(band, (groups * sides, 1)), ('exp', 'col'), split...]
  transfers between devices with their start and end apart: 9 -> 9, of which waited for: 6 -> 5; matrix products, arithmetic and copies ran while one was open for 8% -> 8% of each run, Pallas kernels for 15% -> 17%
where the time goes in v16:
time: 83.2 us; the launch traced here: 82.7 us
  starting transfers between devices  24.4 us (29%)
  Pallas kernels  18.6 us (22%)
  waiting for transfers between devices  18.5 us (22%)
  other arithmetic  11.3 us (14%)
  local copies, waits for them, and re-layouts  7.79 us (9%)
  between operations  0.99 us (1%)
    pallas_call x4, Pallas kernels, warp_by_slot(): pl.pallas_call(functools.partial(_slot_kernel, step), out_shape=(banded,...  18.6 us
    ppermute x2, starting transfers between devices, _row_halo(): lax.ppermute(lax.slice_in_dim(block, size - width, None, axis=dim), 'row'...  10.5 us
    ppermute x2, waiting for transfers between devices, _row_halo(): lax.ppermute(lax.slice_in_dim(block, 0, width, axis=dim), 'row', backward)  6.81 us
    all_to_all x1, waiting for transfers between devices, body(): lax.all_to_all(jnp.tile(band, (groups * sides, 1)), ('exp', 'col'), split...  5.46 us
    ppermute x3, starting transfers between devices, warp_by_slot(): slots[step] = lax.ppermute(flagged, 'exp', pairs)  4.84 us
    ppermute x3, waiting for transfers between devices, warp_by_slot(): slots[step] = lax.ppermute(flagged, 'exp', pairs)  4.29 us
    all_to_all x1, starting transfers between devices, body(): lax.all_to_all(jnp.tile(band, (groups * sides, 1)), ('exp', 'col'), split...  3.86 us
    ppermute x2, starting transfers between devices, _row_halo(): lax.ppermute(lax.slice_in_dim(block, 0, width, axis=dim), 'row', backward)  3.84 us
  transfers between devices with their start and end apart: 9, of which 5 were waited for; matrix products, arithmetic and copies ran while one was open for 8% of the time, Pallas kernels for 17%

profile of v16, /device:TPU:1, one launch (start us, length us, event | category | flops | bytes accessed | tf_op | source)
XLA Modules:
  0.0 82.7 jit_solution(11933845924376522950)
XLA Ops:
  0.6 1.4 %fusion.107 = (f32[16,11,512]{2,1,0:T(8,128)S(1)}, f32[16,11,512]{2,1,0:T(8,128)S(1)}) fusion(f32[16,32,512]{2,1,0:T(8,128)} %param.8), kind=kLoop, calls=%fused_computation.218 | loop fusion | bytes 1441792 | tf_op jit(solution)/shard_map/slice | solution.py:28
  2.1 4.5 %collective-permute-start = (f32[16,11,512]{2,1,0:T(8,128)S(1)}, f32[16,11,512]{2,1,0:T(8,128)S(1)}, u32[]{:S(2)}, u32[]{:S(2)}) collective-permute-start(f32[16,11,512]{2,1,0:T(8,128)S(1)} %get-tuple-element.77), channel_id=1, source_target_pairs={{0,2},{2,4},{4,6},{1,3},{3,5},{5,7},{8,10},{10,12},{12,14},{9,11},... | collective-permute-start | bytes 1081352 | tf_op jit(solution)/shard_map/ppermute | solution.py:28
  6.6 1.9 %collective-permute-start.1 = (f32[16,11,512]{2,1,0:T(8,128)S(1)}, f32[16,11,512]{2,1,0:T(8,128)S(1)}, u32[]{:S(2)}, u32[]{:S(2)}) collective-permute-start(f32[16,11,512]{2,1,0:T(8,128)S(1)} %get-tuple-element.78), channel_id=1, source_target_pairs={{2,0},{4,2},{6,4},{3,1},{5,3},{7,5},{10,8},{12,10},{14,12},{11,9},... | collective-permute-start | bytes 1081352 | tf_op jit(solution)/shard_map/ppermute | solution.py:29
  8.6 0.8 slice_bitcast_fusion.25
  9.5 0.7 fusion.78
  10.7 2.0 %collective-permute-done = f32[16,11,512]{2,1,0:T(8,128)S(1)} collective-permute-done((f32[16,11,512]{2,1,0:T(8,128)S(1)}, f32[16,11,512]{2,1,0:T(8,128)S(1)}, u32[]{:S(2)}, u32[]{:S(2)}) %collective-permute-start) | collective-permute-done | bytes 360480 | tf_op jit(solution)/shard_map/ppermute | solution.py:28
  12.7 4.4 %collective-permute-done.1 = f32[16,11,512]{2,1,0:T(8,128)S(1)} collective-permute-done((f32[16,11,512]{2,1,0:T(8,128)S(1)}, f32[16,11,512]{2,1,0:T(8,128)S(1)}, u32[]{:S(2)}, u32[]{:S(2)}) %collective-permute-start.1) | collective-permute-done | bytes 360480 | tf_op jit(solution)/shard_map/ppermute | solution.py:29
  17.7 1.3 %collective-permute-start.2 = (f32[11,864]{1,0:T(8,128)S(1)}, f32[11,864]{1,0:T(8,128)S(1)}, u32[]{:S(2)}, u32[]{:S(2)}) collective-permute-start(f32[11,864]{1,0:T(8,128)S(1)} %reshape.137), channel_id=1, source_target_pairs={{0,1},{1,0},{2,3},{3,2},{4,5},{5,4},{6,7},{7,6},{8,9},{9,8},{10,11... | collective-permute-start | bytes 114056 | tf_op jit(solution)/shard_map/ppermute | solution.py:48
  19.0 0.6 add_bitcast_fusion
  19.6 0.6 reshape.134.row_weight
  20.2 0.6 reshape.135.col_weight
  21.6 2.4 %select_maximum_fusion.padded = f32[16,56,640]{2,1,0:T(8,128)} fusion(f32[16,54,11]{2,1,0:T(8,128)S(1)} %bitcast.82, f32[16,54,11]{2,1,0:T(8,128)S(1)} %bitcast.81, f32[16,11,512]{2,1,0:T(8,128)S(1)} %collective-permute-done.1, f32[16,32,512]{2,1,0:T(8,128)S(1)} %copy-done.1, f32[16,11,512]{2,1,0:T(8,128)S(1)} %collective-permute-done), kind=kLoop, calls=%fused_computation.7 | loop fusion | flops 9748480 | bytes 4139264 | tf_op jit(solution)/shard_map/concatenate | solution.py:53
  24.0 4.6 %shard_map.69 = (f32[16,8,512]{2,1,0:T(8,128)}, f32[16,8,512]{2,1,0:T(8,128)}) custom-call(s32[16]{0:T(128)} %get-tuple-element.123.row_shift, s32[16]{0:T(128)} %get-tuple-element.122.col_shift, f32[96]{0:T(128)} %reshape.134.row_weight, f32[96]{0:T(128)} %reshape.135.col_weight, s32[1]{0:T(128)} %bitcast.4.me, f32[16,56,640]{2,1,0:T(8,128)} %select_maximum_fusion.padded, ...), custom_call_target="tpu_custom_call" | custom-call | tf_op jit(solution)/shard_map/pallas_call | solution.py:256
  28.6 1.3 %collective-permute-start.3 = (f32[16,8,512]{2,1,0:T(8,128)}, f32[16,8,512]{2,1,0:T(8,128)S(1)}, u32[]{:S(2)}, u32[]{:S(2)}) collective-permute-start(f32[16,8,512]{2,1,0:T(8,128)} %get-tuple-element.43), channel_id=1, source_target_pairs={{0,8},{8,16},{16,24},{24,0},{1,9},{9,17},{17,25},{25,1},{2,10},{10... | collective-permute-start | bytes 786440 | tf_op jit(solution)/shard_map/ppermute | solution.py:269
  30.0 4.6 %shard_map.70 = (f32[16,8,512]{2,1,0:T(8,128)}, f32[16,8,512]{2,1,0:T(8,128)}) custom-call(s32[16]{0:T(128)} %get-tuple-element.123.row_shift, s32[16]{0:T(128)} %get-tuple-element.122.col_shift, f32[96]{0:T(128)} %reshape.134.row_weight, f32[96]{0:T(128)} %reshape.135.col_weight, s32[1]{0:T(128)} %bitcast.4.me, f32[16,56,640]{2,1,0:T(8,128)} %select_maximum_fusion.padded, ...), custom_call_target="tpu_custom_call" | custom-call | tf_op jit(solution)/shard_map/pallas_call | solution.py:256
  34.6 2.4 %collective-permute-start.4 = (f32[16,8,512]{2,1,0:T(8,128)}, f32[16,8,512]{2,1,0:T(8,128)S(1)}, u32[]{:S(2)}, u32[]{:S(2)}) collective-permute-start(f32[16,8,512]{2,1,0:T(8,128)} %get-tuple-element.44), channel_id=1, source_target_pairs={{0,16},{8,24},{16,0},{24,8},{1,17},{9,25},{17,1},{25,9},{2,18},{10... | collective-permute-start | bytes 786440 | tf_op jit(solution)/shard_map/ppermute | solution.py:269
  37.0 4.6 %shard_map.71 = (f32[16,8,512]{2,1,0:T(8,128)}, f32[16,8,512]{2,1,0:T(8,128)}) custom-call(s32[16]{0:T(128)} %get-tuple-element.123.row_shift, s32[16]{0:T(128)} %get-tuple-element.122.col_shift, f32[96]{0:T(128)} %reshape.134.row_weight, f32[96]{0:T(128)} %reshape.135.col_weight, s32[1]{0:T(128)} %bitcast.4.me, f32[16,56,640]{2,1,0:T(8,128)} %select_maximum_fusion.padded, ...), custom_call_target="tpu_custom_call" | custom-call | tf_op jit(solution)/shard_map/pallas_call | solution.py:256
  41.6 4.7 %shard_map.68 = (f32[16,8,512]{2,1,0:T(8,128)}, f32[16,8,512]{2,1,0:T(8,128)}) custom-call(s32[16]{0:T(128)} %get-tuple-element.123.row_shift, s32[16]{0:T(128)} %get-tuple-element.122.col_shift, f32[96]{0:T(128)} %reshape.134.row_weight, f32[96]{0:T(128)} %reshape.135.col_weight, s32[1]{0:T(128)} %bitcast.4.me, f32[16,56,640]{2,1,0:T(8,128)} %select_maximum_fusion.padded, ...), custom_call_target="tpu_custom_call" | custom-call | tf_op jit(solution)/shard_map/pallas_call | solution.py:256
  46.4 1.1 %collective-permute-start.5 = (f32[16,8,512]{2,1,0:T(8,128)S(1)}, f32[16,8,512]{2,1,0:T(8,128)S(1)}, u32[]{:S(2)}, u32[]{:S(2)}) collective-permute-start(f32[16,8,512]{2,1,0:T(8,128)S(1)} %copy-done.7), channel_id=1, source_target_pairs={{0,24},{8,0},{16,8},{24,16},{1,25},{9,1},{17,9},{25,17},{2,26},{10... | collective-permute-start | bytes 786440 | tf_op jit(solution)/shard_map/ppermute | solution.py:269
  47.5 1.0 %constant_dynamic-update-slice_fusion.3 = f32[64,8,512]{2,1,0:T(8,128)S(1)} fusion(f32[16,8,512]{2,1,0:T(8,128)} %get-tuple-element.42), kind=kLoop, calls=%fused_computation.101 | loop fusion | bytes 524288
  48.5 4.3 %collective-permute-done.5 = f32[16,8,512]{2,1,0:T(8,128)S(1)} collective-permute-done((f32[16,8,512]{2,1,0:T(8,128)S(1)}, f32[16,8,512]{2,1,0:T(8,128)S(1)}, u32[]{:S(2)}, u32[]{:S(2)}) %collective-permute-start.5) | collective-permute-done | bytes 262176 | tf_op jit(solution)/shard_map/ppermute | solution.py:269
  53.0 3.6 %while.13 = (s32[]{:T(128)}, f32[8,512]{1,0:T(8,128)S(1)}, f32[8,512]{1,0:T(8,128)S(1)}, f32[64,8,512]{2,1,0:T(8,128)S(1)}, f32[8,512]{1,0:T(8,128)S(1)}, /*index=5*/s32[]{:T(128)}, s32[]{:T(128)}) while((s32[]{:T(128)}, f32[8,512]{1,0:T(8,128)S(1)}, f32[8,512]{1,0:T(8,128)S(1)}, f32[64,8,512]{2,1,0:T(8,128)S(1)}, ...), condition=%wide.region_5.7_spmd.clone, body=%wide.region_3.6_spmd.clone.sunk | while | flops 1110019 | bytes 1302617 | solution.py:94
  56.8 0.7 tile.2
  57.5 3.9 %all-to-all-start = ((f32[8,8,512]{2,1,0:T(8,128)}), f32[8,8,512]{2,1,0:T(8,128)S(1)}, u32[]{:S(2)}, u32[]{:S(2)}) async-start(f32[8,8,512]{2,1,0:T(8,128)} %tile.2), calls=%async_computation | async-start | bytes 262144 | tf_op jit(solution)/shard_map/all_to_all | solution.py:296
  61.5 0.6 gather_fusion
  62.1 5.5 %all-to-all-done = f32[8,8,512]{2,1,0:T(8,128)S(1)} async-done(((f32[8,8,512]{2,1,0:T(8,128)}), f32[8,8,512]{2,1,0:T(8,128)S(1)}, u32[]{:S(2)}, u32[]{:S(2)}) %all-to-all-start) | async-done | bytes 131104 | tf_op jit(solution)/shard_map/all_to_all | solution.py:296
  67.8 6.0 %collective-permute-start.6 = (f32[4,520]{1,0:T(4,128)S(1)}, f32[4,520]{1,0:T(4,128)S(1)}, u32[]{:S(2)}, u32[]{:S(2)}) collective-permute-start(f32[4,520]{1,0:T(4,128)S(1)} %get-tuple-element.87), channel_id=1, source_target_pairs={{0,2},{2,4},{4,6},{1,3},{3,5},{5,7},{8,10},{10,12},{12,14},{9,11},... | collective-permute-start | bytes 24968 | tf_op jit(solution)/shard_map/ppermute | solution.py:28
  73.8 1.9 %collective-permute-start.7 = (f32[4,520]{1,0:T(4,128)S(1)}, f32[4,520]{1,0:T(4,128)S(1)}, u32[]{:S(2)}, u32[]{:S(2)}) collective-permute-start(f32[4,520]{1,0:T(4,128)S(1)} %get-tuple-element.88), channel_id=1, source_target_pairs={{2,0},{4,2},{6,4},{3,1},{5,3},{7,5},{10,8},{12,10},{14,12},{11,9},... | collective-permute-start | bytes 24968 | tf_op jit(solution)/shard_map/ppermute | solution.py:29
  75.7 0.6 constant_dynamic-slice_fusion
  76.4 2.4 %collective-permute-done.7 = f32[4,520]{1,0:T(4,128)S(1)} collective-permute-done((f32[4,520]{1,0:T(4,128)S(1)}, f32[4,520]{1,0:T(4,128)S(1)}, u32[]{:S(2)}, u32[]{:S(2)}) %collective-permute-start.7) | collective-permute-done | bytes 8352 | tf_op jit(solution)/shard_map/ppermute | solution.py:29
  79.4 1.3 %fusion.11 = f32[8,32,512]{2,1,0:T(8,128)S(1)} fusion(f32[8,32,520]{2,1,0:T(8,128)S(1)} %multiply_add_fusion, f32[8]{0:T(128)S(1)} %get-tuple-element.104, f32[8]{0:T(128)S(1)} %get-tuple-element.105, f32[8]{0:T(128)S(1)} %get-tuple-element.106, f32[8]{0:T(128)S(1)} %get-tuple-element.107, f32[8]{0:T(128)S(1)} %get-tuple-element.108, ...), kind=kLoop, calls=%fused_computation.28 | loop fusion | flops 2228224 | bytes 5243168 | tf_op jit(solution)/shard_map/add | solution.py:317
  80.7 2.0 %fusion.10 = f32[16,32,512]{2,1,0:T(8,128)} fusion(s32[16,32,512]{2,1,0:T(8,128)S(1)} %copy-done, f32[32,512]{1,0:T(8,128)S(1)} %get-tuple-element.80, f32[16]{0:T(128)S(1)} %get-tuple-element.113, f32[32,512]{1,0:T(8,128)S(1)} %get-tuple-element.81, f32[16]{0:T(128)S(1)} %get-tuple-element.114, f32[32,512]{1,0:T(8,128)S(1)} %get-tuple-element.82, ...), kind=kLoop, calls=%fused_computation.23 | loop fusion | flops 4980736 | bytes 3670532 | tf_op jit(solution)/shard_map/jit(_where)/select_n | solution.py:325
  (135 shorter events, 6.3 us)
Async XLA Ops:
  0.6 16.5 %copy-start.1 = (f32[16,32,512]{2,1,0:T(8,128)S(1)}, f32[16,32,512]{2,1,0:T(8,128)}, u32[]{:S(2)}) copy-start(f32[16,32,512]{2,1,0:T(8,128)} %param.8) | copy-start | bytes 3145732
  2.1 16.9 %copy-start.6 = (s32[16,2]{0,1:T(2,128)S(1)}, s32[16,2]{0,1:T(2,128)}, u32[]{:S(2)}) copy-start(s32[16,2]{0,1:T(2,128)} %param.10) | copy-start | bytes 388
  2.1 10.6 %collective-permute-start = (f32[16,11,512]{2,1,0:T(8,128)S(1)}, f32[16,11,512]{2,1,0:T(8,128)S(1)}, u32[]{:S(2)}, u32[]{:S(2)}) collective-permute-start(f32[16,11,512]{2,1,0:T(8,128)S(1)} %get-tuple-element.77), channel_id=1, source_target_pairs={{0,2},{2,4},{4,6},{1,3},{3,5},{5,7},{8,10},{10,12},{12,14},{9,11},... | collective-permute-start | bytes 1081352 | tf_op jit(solution)/shard_map/ppermute | solution.py:28
  6.6 10.5 %collective-permute-start.1 = (f32[16,11,512]{2,1,0:T(8,128)S(1)}, f32[16,11,512]{2,1,0:T(8,128)S(1)}, u32[]{:S(2)}, u32[]{:S(2)}) collective-permute-start(f32[16,11,512]{2,1,0:T(8,128)S(1)} %get-tuple-element.78), channel_id=1, source_target_pairs={{2,0},{4,2},{6,4},{3,1},{5,3},{7,5},{10,8},{12,10},{14,12},{11,9},... | collective-permute-start | bytes 1081352 | tf_op jit(solution)/shard_map/ppermute | solution.py:29
  17.7 3.1 %collective-permute-start.2 = (f32[11,864]{1,0:T(8,128)S(1)}, f32[11,864]{1,0:T(8,128)S(1)}, u32[]{:S(2)}, u32[]{:S(2)}) collective-permute-start(f32[11,864]{1,0:T(8,128)S(1)} %reshape.137), channel_id=1, source_target_pairs={{0,1},{1,0},{2,3},{3,2},{4,5},{5,4},{6,7},{7,6},{8,9},{9,8},{10,11... | collective-permute-start | bytes 114056 | tf_op jit(solution)/shard_map/ppermute | solution.py:48
  28.6 19.8 %collective-permute-start.3 = (f32[16,8,512]{2,1,0:T(8,128)}, f32[16,8,512]{2,1,0:T(8,128)S(1)}, u32[]{:S(2)}, u32[]{:S(2)}) collective-permute-start(f32[16,8,512]{2,1,0:T(8,128)} %get-tuple-element.43), channel_id=1, source_target_pairs={{0,8},{8,16},{16,24},{24,0},{1,9},{9,17},{17,25},{25,1},{2,10},{10... | collective-permute-start | bytes 786440 | tf_op jit(solution)/shard_map/ppermute | solution.py:269
  34.6 13.9 %collective-permute-start.4 = (f32[16,8,512]{2,1,0:T(8,128)}, f32[16,8,512]{2,1,0:T(8,128)S(1)}, u32[]{:S(2)}, u32[]{:S(2)}) collective-permute-start(f32[16,8,512]{2,1,0:T(8,128)} %get-tuple-element.44), channel_id=1, source_target_pairs={{0,16},{8,24},{16,0},{24,8},{1,17},{9,25},{17,1},{25,9},{2,18},{10... | collective-permute-start | bytes 786440 | tf_op jit(solution)/shard_map/ppermute | solution.py:269
  41.6 4.7 %copy-start.7 = (f32[16,8,512]{2,1,0:T(8,128)S(1)}, f32[16,8,512]{2,1,0:T(8,128)}, u32[]{:S(2)}) copy-start(f32[16,8,512]{2,1,0:T(8,128)} %get-tuple-element.45) | copy-start | bytes 786436
  46.4 6.5 %collective-permute-start.5 = (f32[16,8,512]{2,1,0:T(8,128)S(1)}, f32[16,8,512]{2,1,0:T(8,128)S(1)}, u32[]{:S(2)}, u32[]{:S(2)}) collective-permute-start(f32[16,8,512]{2,1,0:T(8,128)S(1)} %copy-done.7), channel_id=1, source_target_pairs={{0,24},{8,0},{16,8},{24,16},{1,25},{9,1},{17,9},{25,17},{2,26},{10... | collective-permute-start | bytes 786440 | tf_op jit(solution)/shard_map/ppermute | solution.py:269
  53.0 8.4 %copy-start.2 = (f32[16,8,512]{2,1,0:T(8,128)S(1)}, f32[16,8,512]{2,1,0:T(8,128)}, u32[]{:S(2)}) copy-start(f32[16,8,512]{2,1,0:T(8,128)} %get-tuple-element.39) | copy-start | bytes 786436
  53.0 8.4 %copy-start.3 = (f32[16,8,512]{2,1,0:T(8,128)S(1)}, f32[16,8,512]{2,1,0:T(8,128)}, u32[]{:S(2)}) copy-start(f32[16,8,512]{2,1,0:T(8,128)} %get-tuple-element.40) | copy-start | bytes 786436
  53.0 8.4 %copy-start.4 = (f32[16,8,512]{2,1,0:T(8,128)S(1)}, f32[16,8,512]{2,1,0:T(8,128)}, u32[]{:S(2)}) copy-start(f32[16,8,512]{2,1,0:T(8,128)} %get-tuple-element.41) | copy-start | bytes 786436
  53.0 8.4 %copy-start.5 = (f32[16,8,512]{2,1,0:T(8,128)S(1)}, f32[16,8,512]{2,1,0:T(8,128)}, u32[]{:S(2)}) copy-start(f32[16,8,512]{2,1,0:T(8,128)} %get-tuple-element.38) | copy-start | bytes 786436
  57.5 10.1 %all-to-all-start = ((f32[8,8,512]{2,1,0:T(8,128)}), f32[8,8,512]{2,1,0:T(8,128)S(1)}, u32[]{:S(2)}, u32[]{:S(2)}) async-start(f32[8,8,512]{2,1,0:T(8,128)} %tile.2), calls=%async_computation | async-start | bytes 262144 | tf_op jit(solution)/shard_map/all_to_all | solution.py:296
  67.8 8.6 %collective-permute-start.6 = (f32[4,520]{1,0:T(4,128)S(1)}, f32[4,520]{1,0:T(4,128)S(1)}, u32[]{:S(2)}, u32[]{:S(2)}) collective-permute-start(f32[4,520]{1,0:T(4,128)S(1)} %get-tuple-element.87), channel_id=1, source_target_pairs={{0,2},{2,4},{4,6},{1,3},{3,5},{5,7},{8,10},{10,12},{12,14},{9,11},... | collective-permute-start | bytes 24968 | tf_op jit(solution)/shard_map/ppermute | solution.py:28
  73.8 5.0 %collective-permute-start.7 = (f32[4,520]{1,0:T(4,128)S(1)}, f32[4,520]{1,0:T(4,128)S(1)}, u32[]{:S(2)}, u32[]{:S(2)}) collective-permute-start(f32[4,520]{1,0:T(4,128)S(1)} %get-tuple-element.88), channel_id=1, source_target_pairs={{2,0},{4,2},{6,4},{3,1},{5,3},{7,5},{10,8},{12,10},{14,12},{11,9},... | collective-permute-start | bytes 24968 | tf_op jit(solution)/shard_map/ppermute | solution.py:29
  79.4 1.3 %copy-start = (s32[16,32,512]{2,1,0:T(8,128)S(1)}, s32[16,32,512]{2,1,0:T(8,128)}, u32[]{:S(2)}) copy-start(s32[16,32,512]{2,1,0:T(8,128)} %bad.7) | copy-start | bytes 3145732

commit v17 on v16

--- a/solution.py
+++ b/solution.py
@@ -81,7 +81,7 @@
 
 def bisect_lower(valid_count, count_below):
 
-    def one_pass(sweep_no, bounds):
+    def one_pass(bounds):
         lower_edge, upper_edge = bounds
         middle = 0.5 * (lower_edge + upper_edge)
         enough = 2.0 * count_below(middle) >= valid_count
@@ -91,7 +91,10 @@
         jnp.full(valid_count.shape, -pivot_span, jnp.float32),
         jnp.full(valid_count.shape, pivot_span, jnp.float32),
     )
-    return lax.fori_loop(0, PASSES, one_pass, initial)[0]
+    bounds = initial
+    for _ in range(PASSES):
+        bounds = one_pass(bounds)
+    return bounds[0]
 
 
 def stack_median(pixel_stack):
@@ -186,7 +189,7 @@
     window = window_buf.shape[1]
     band = lax.rem(me[0] + step, bands)
     base = pl.multiple_of(band * band_rows, 8)
-    parts = 8 if group_size % 8 == 0 else 2
+    parts = 4 if group_size % 4 == 0 else 2
     share = group_size // parts
     spans = [(part * share, share) for part in range(parts - 1)]
     spans.append(((parts - 1) * share, group_size - (parts - 1) * share))
@@ -261,7 +264,7 @@
             scratch_shapes=[
                 pltpu.VMEM((group_size, window, lanes), jnp.float32),
                 pltpu.VMEM((group_size, band_rows, col_count), jnp.int32),
-                pltpu.SemaphoreType.DMA((9,)),
+                pltpu.SemaphoreType.DMA((5,)),
             ],
         )(row_shift, col_shift, row_weight, col_weight, me, padded, bad_pixels)
         if step:

time: 83.2 us -> 79.1 us (0.951)
  Pallas kernels: 18.6 us -> 15.5 us
  starting transfers between devices: 24.4 us -> 21.7 us
  waiting for transfers between devices: 18.5 us -> 21.2 us
    ppermute x2, starting transfers between devices: 10.5 us -> 7.43 us  [_row_halo(): lax.ppermute(lax.slice_in_dim(block, size - width, None, axis=dim), 'row'...]
    pallas_call x4, Pallas kernels: 18.6 us -> 15.5 us  [warp_by_slot(): pl.pallas_call(functools.partial(_slot_kernel, step), out_shape=(banded,...]
    ppermute x3, waiting for transfers between devices: 4.29 us -> 6.07 us  [warp_by_slot(): slots[step] = lax.ppermute(flagged, 'exp', pairs)]
    all_to_all x1, waiting for transfers between devices: 5.46 us -> 6.56 us  [body(): lax.all_to_all(jnp.tile(band, (groups * sides, 1)), ('exp', 'col'), split...]
  transfers between devices with their start and end apart: 9 -> 9, of which waited for: 5 -> 6; matrix products, arithmetic and copies ran while one was open for 8% -> 8% of each run, Pallas kernels for 17% -> 15%
where the time goes in v17:
time: 79.1 us; the launch traced here: 78.6 us
  starting transfers between devices  21.7 us (27%)
  waiting for transfers between devices  21.2 us (27%)
  Pallas kernels  15.5 us (20%)
  other arithmetic  11 us (14%)
  local copies, waits for them, and re-layouts  7.68 us (10%)
  between operations  1.03 us (1%)
    pallas_call x4, Pallas kernels, warp_by_slot(): pl.pallas_call(functools.partial(_slot_kernel, step), out_shape=(banded,...  15.5 us
    ppermute x2, starting transfers between devices, _row_halo(): lax.ppermute(lax.slice_in_dim(block, size - width, None, axis=dim), 'row'...  7.43 us
    ppermute x2, waiting for transfers between devices, _row_halo(): lax.ppermute(lax.slice_in_dim(block, 0, width, axis=dim), 'row', backward)  6.63 us
    all_to_all x1, waiting for transfers between devices, body(): lax.all_to_all(jnp.tile(band, (groups * sides, 1)), ('exp', 'col'), split...  6.56 us
    ppermute x3, waiting for transfers between devices, warp_by_slot(): slots[step] = lax.ppermute(flagged, 'exp', pairs)  6.07 us
    ppermute x3, starting transfers between devices, warp_by_slot(): slots[step] = lax.ppermute(flagged, 'exp', pairs)  4.84 us
    all_to_all x1, starting transfers between devices, body(): lax.all_to_all(jnp.tile(band, (groups * sides, 1)), ('exp', 'col'), split...  4.12 us
    ppermute x2, starting transfers between devices, _row_halo(): lax.ppermute(lax.slice_in_dim(block, 0, width, axis=dim), 'row', backward)  4.02 us
  transfers between devices with their start and end apart: 9, of which 6 were waited for; matrix products, arithmetic and copies ran while one was open for 8% of the time, Pallas kernels for 15%

profile of v17, /device:TPU:1, one launch (start us, length us, event | category | flops | bytes accessed | tf_op | source)
XLA Modules:
  0.0 78.6 jit_solution(12068459513255389747)
XLA Ops:
  0.6 1.4 %fusion.146 = (f32[16,11,512]{2,1,0:T(8,128)S(1)}, f32[16,11,512]{2,1,0:T(8,128)S(1)}) fusion(f32[16,32,512]{2,1,0:T(8,128)} %param.6), kind=kLoop, calls=%fused_computation.289 | loop fusion | bytes 1441792 | tf_op jit(solution)/shard_map/slice | solution.py:28
  2.1 4.5 %collective-permute-start = (f32[16,11,512]{2,1,0:T(8,128)S(1)}, f32[16,11,512]{2,1,0:T(8,128)S(1)}, u32[]{:S(2)}, u32[]{:S(2)}) collective-permute-start(f32[16,11,512]{2,1,0:T(8,128)S(1)} %get-tuple-element.57), channel_id=1, source_target_pairs={{0,2},{2,4},{4,6},{1,3},{3,5},{5,7},{8,10},{10,12},{12,14},{9,11},... | collective-permute-start | bytes 1081352 | tf_op jit(solution)/shard_map/ppermute | solution.py:28
  6.6 1.9 %collective-permute-start.1 = (f32[16,11,512]{2,1,0:T(8,128)S(1)}, f32[16,11,512]{2,1,0:T(8,128)S(1)}, u32[]{:S(2)}, u32[]{:S(2)}) collective-permute-start(f32[16,11,512]{2,1,0:T(8,128)S(1)} %get-tuple-element.58), channel_id=1, source_target_pairs={{2,0},{4,2},{6,4},{3,1},{5,3},{7,5},{10,8},{12,10},{14,12},{11,9},... | collective-permute-start | bytes 1081352 | tf_op jit(solution)/shard_map/ppermute | solution.py:29
  8.6 0.8 slice_bitcast_fusion.25
  9.5 0.7 fusion.82
  10.7 2.0 %collective-permute-done = f32[16,11,512]{2,1,0:T(8,128)S(1)} collective-permute-done((f32[16,11,512]{2,1,0:T(8,128)S(1)}, f32[16,11,512]{2,1,0:T(8,128)S(1)}, u32[]{:S(2)}, u32[]{:S(2)}) %collective-permute-start) | collective-permute-done | bytes 360480 | tf_op jit(solution)/shard_map/ppermute | solution.py:28
  12.7 4.4 %collective-permute-done.1 = f32[16,11,512]{2,1,0:T(8,128)S(1)} collective-permute-done((f32[16,11,512]{2,1,0:T(8,128)S(1)}, f32[16,11,512]{2,1,0:T(8,128)S(1)}, u32[]{:S(2)}, u32[]{:S(2)}) %collective-permute-start.1) | collective-permute-done | bytes 360480 | tf_op jit(solution)/shard_map/ppermute | solution.py:29
  17.7 1.3 %collective-permute-start.2 = (f32[11,864]{1,0:T(8,128)S(1)}, f32[11,864]{1,0:T(8,128)S(1)}, u32[]{:S(2)}, u32[]{:S(2)}) collective-permute-start(f32[11,864]{1,0:T(8,128)S(1)} %reshape.532), channel_id=1, source_target_pairs={{0,1},{1,0},{2,3},{3,2},{4,5},{5,4},{6,7},{7,6},{8,9},{9,8},{10,11... | collective-permute-start | bytes 114056 | tf_op jit(solution)/shard_map/ppermute | solution.py:48
  19.0 0.6 add_bitcast_fusion
  19.5 0.6 reshape.529.row_weight
  20.2 0.6 reshape.530.col_weight
  21.6 2.4 %select_maximum_fusion.padded = f32[16,56,640]{2,1,0:T(8,128)} fusion(f32[16,54,11]{2,1,0:T(8,128)S(1)} %bitcast.82, f32[16,54,11]{2,1,0:T(8,128)S(1)} %bitcast.81, f32[16,11,512]{2,1,0:T(8,128)S(1)} %collective-permute-done.1, f32[16,32,512]{2,1,0:T(8,128)S(1)} %copy-done.1, f32[16,11,512]{2,1,0:T(8,128)S(1)} %collective-permute-done), kind=kLoop, calls=%fused_computation.2 | loop fusion | flops 9748480 | bytes 4139264 | tf_op jit(solution)/shard_map/concatenate | solution.py:53
  24.0 3.9 %shard_map.69 = (f32[16,8,512]{2,1,0:T(8,128)}, f32[16,8,512]{2,1,0:T(8,128)}) custom-call(s32[16]{0:T(128)} %get-tuple-element.103.row_shift, s32[16]{0:T(128)} %get-tuple-element.102.col_shift, f32[96]{0:T(128)} %reshape.529.row_weight, f32[96]{0:T(128)} %reshape.530.col_weight, s32[1]{0:T(128)} %bitcast.4.me, f32[16,56,640]{2,1,0:T(8,128)} %select_maximum_fusion.padded, ...), custom_call_target="tpu_custom_call" | custom-call | tf_op jit(solution)/shard_map/pallas_call | solution.py:259
  27.8 1.3 %collective-permute-start.3 = (f32[16,8,512]{2,1,0:T(8,128)}, f32[16,8,512]{2,1,0:T(8,128)S(1)}, u32[]{:S(2)}, u32[]{:S(2)}) collective-permute-start(f32[16,8,512]{2,1,0:T(8,128)} %get-tuple-element.16), channel_id=1, source_target_pairs={{0,8},{8,16},{16,24},{24,0},{1,9},{9,17},{17,25},{25,1},{2,10},{10... | collective-permute-start | bytes 786440 | tf_op jit(solution)/shard_map/ppermute | solution.py:272
  29.2 3.8 %shard_map.70 = (f32[16,8,512]{2,1,0:T(8,128)}, f32[16,8,512]{2,1,0:T(8,128)}) custom-call(s32[16]{0:T(128)} %get-tuple-element.103.row_shift, s32[16]{0:T(128)} %get-tuple-element.102.col_shift, f32[96]{0:T(128)} %reshape.529.row_weight, f32[96]{0:T(128)} %reshape.530.col_weight, s32[1]{0:T(128)} %bitcast.4.me, f32[16,56,640]{2,1,0:T(8,128)} %select_maximum_fusion.padded, ...), custom_call_target="tpu_custom_call" | custom-call | tf_op jit(solution)/shard_map/pallas_call | solution.py:259
  33.0 2.4 %collective-permute-start.4 = (f32[16,8,512]{2,1,0:T(8,128)}, f32[16,8,512]{2,1,0:T(8,128)S(1)}, u32[]{:S(2)}, u32[]{:S(2)}) collective-permute-start(f32[16,8,512]{2,1,0:T(8,128)} %get-tuple-element.17), channel_id=1, source_target_pairs={{0,16},{8,24},{16,0},{24,8},{1,17},{9,25},{17,1},{25,9},{2,18},{10... | collective-permute-start | bytes 786440 | tf_op jit(solution)/shard_map/ppermute | solution.py:272
  35.4 3.9 %shard_map.71 = (f32[16,8,512]{2,1,0:T(8,128)}, f32[16,8,512]{2,1,0:T(8,128)}) custom-call(s32[16]{0:T(128)} %get-tuple-element.103.row_shift, s32[16]{0:T(128)} %get-tuple-element.102.col_shift, f32[96]{0:T(128)} %reshape.529.row_weight, f32[96]{0:T(128)} %reshape.530.col_weight, s32[1]{0:T(128)} %bitcast.4.me, f32[16,56,640]{2,1,0:T(8,128)} %select_maximum_fusion.padded, ...), custom_call_target="tpu_custom_call" | custom-call | tf_op jit(solution)/shard_map/pallas_call | solution.py:259
  39.3 4.0 %shard_map.68 = (f32[16,8,512]{2,1,0:T(8,128)}, f32[16,8,512]{2,1,0:T(8,128)}) custom-call(s32[16]{0:T(128)} %get-tuple-element.103.row_shift, s32[16]{0:T(128)} %get-tuple-element.102.col_shift, f32[96]{0:T(128)} %reshape.529.row_weight, f32[96]{0:T(128)} %reshape.530.col_weight, s32[1]{0:T(128)} %bitcast.4.me, f32[16,56,640]{2,1,0:T(8,128)} %select_maximum_fusion.padded, ...), custom_call_target="tpu_custom_call" | custom-call | tf_op jit(solution)/shard_map/pallas_call | solution.py:259
  43.3 1.1 %collective-permute-start.5 = (f32[16,8,512]{2,1,0:T(8,128)S(1)}, f32[16,8,512]{2,1,0:T(8,128)S(1)}, u32[]{:S(2)}, u32[]{:S(2)}) collective-permute-start(f32[16,8,512]{2,1,0:T(8,128)S(1)} %copy-done.7), channel_id=1, source_target_pairs={{0,24},{8,0},{16,8},{24,16},{1,25},{9,1},{17,9},{25,17},{2,26},{10... | collective-permute-start | bytes 786440 | tf_op jit(solution)/shard_map/ppermute | solution.py:272
  44.4 1.0 %constant_dynamic-update-slice_fusion.3 = f32[64,8,512]{2,1,0:T(8,128)S(1)} fusion(f32[16,8,512]{2,1,0:T(8,128)} %get-tuple-element.15), kind=kLoop, calls=%fused_computation.149 | loop fusion | bytes 524288
  45.4 1.1 %collective-permute-done.4 = f32[16,8,512]{2,1,0:T(8,128)S(1)} collective-permute-done((f32[16,8,512]{2,1,0:T(8,128)}, f32[16,8,512]{2,1,0:T(8,128)S(1)}, u32[]{:S(2)}, u32[]{:S(2)}) %collective-permute-start.4) | collective-permute-done | bytes 262176 | tf_op jit(solution)/shard_map/ppermute | solution.py:272
  46.6 4.9 %collective-permute-done.5 = f32[16,8,512]{2,1,0:T(8,128)S(1)} collective-permute-done((f32[16,8,512]{2,1,0:T(8,128)S(1)}, f32[16,8,512]{2,1,0:T(8,128)S(1)}, u32[]{:S(2)}, u32[]{:S(2)}) %collective-permute-start.5) | collective-permute-done | bytes 262176 | tf_op jit(solution)/shard_map/ppermute | solution.py:272
  54.5 0.6 tile.2
  55.1 4.1 %all-to-all-start = ((f32[8,8,512]{2,1,0:T(8,128)}), f32[8,8,512]{2,1,0:T(8,128)S(1)}, u32[]{:S(2)}, u32[]{:S(2)}) async-start(f32[8,8,512]{2,1,0:T(8,128)} %tile.2), calls=%async_computation | async-start | bytes 262144 | tf_op jit(solution)/shard_map/all_to_all | solution.py:299
  59.4 0.6 gather_fusion
  60.0 6.6 %all-to-all-done = f32[8,8,512]{2,1,0:T(8,128)S(1)} async-done(((f32[8,8,512]{2,1,0:T(8,128)}), f32[8,8,512]{2,1,0:T(8,128)S(1)}, u32[]{:S(2)}, u32[]{:S(2)}) %all-to-all-start) | async-done | bytes 131104 | tf_op jit(solution)/shard_map/all_to_all | solution.py:299
  66.7 2.9 %collective-permute-start.6 = (f32[4,520]{1,0:T(4,128)S(1)}, f32[4,520]{1,0:T(4,128)S(1)}, u32[]{:S(2)}, u32[]{:S(2)}) collective-permute-start(f32[4,520]{1,0:T(4,128)S(1)} %get-tuple-element.67), channel_id=1, source_target_pairs={{0,2},{2,4},{4,6},{1,3},{3,5},{5,7},{8,10},{10,12},{12,14},{9,11},... | collective-permute-start | bytes 24968 | tf_op jit(solution)/shard_map/ppermute | solution.py:28
  69.7 2.1 %collective-permute-start.7 = (f32[4,520]{1,0:T(4,128)S(1)}, f32[4,520]{1,0:T(4,128)S(1)}, u32[]{:S(2)}, u32[]{:S(2)}) collective-permute-start(f32[4,520]{1,0:T(4,128)S(1)} %get-tuple-element.68), channel_id=1, source_target_pairs={{2,0},{4,2},{6,4},{3,1},{5,3},{7,5},{10,8},{12,10},{14,12},{11,9},... | collective-permute-start | bytes 24968 | tf_op jit(solution)/shard_map/ppermute | solution.py:29
  71.8 0.6 constant_dynamic-slice_fusion
  72.4 2.2 %collective-permute-done.7 = f32[4,520]{1,0:T(4,128)S(1)} collective-permute-done((f32[4,520]{1,0:T(4,128)S(1)}, f32[4,520]{1,0:T(4,128)S(1)}, u32[]{:S(2)}, u32[]{:S(2)}) %collective-permute-start.7) | collective-permute-done | bytes 8352 | tf_op jit(solution)/shard_map/ppermute | solution.py:29
  75.3 1.3 %fusion.11 = f32[8,32,512]{2,1,0:T(8,128)S(1)} fusion(f32[8,32,520]{2,1,0:T(8,128)S(1)} %multiply_add_fusion, f32[8]{0:T(128)S(1)} %get-tuple-element.84, f32[8]{0:T(128)S(1)} %get-tuple-element.85, f32[8]{0:T(128)S(1)} %get-tuple-element.86, f32[8]{0:T(128)S(1)} %get-tuple-element.87, f32[8]{0:T(128)S(1)} %get-tuple-element.88, f32[8]{0:T(128)S(1)} %get-tuple-element.89, ...), kind=kLoop, calls=%fused_computation.39 | loop fusion | flops 2228224 | bytes 5243168 | tf_op jit(solution)/shard_map/add | solution.py:320
  76.6 2.0 %fusion.10 = f32[16,32,512]{2,1,0:T(8,128)} fusion(s32[16,32,512]{2,1,0:T(8,128)S(1)} %copy-done, f32[32,512]{1,0:T(8,128)S(1)} %get-tuple-element.60, f32[16]{0:T(128)S(1)} %get-tuple-element.93, f32[32,512]{1,0:T(8,128)S(1)} %get-tuple-element.61, f32[16]{0:T(128)S(1)} %get-tuple-element.94, f32[32,512]{1,0:T(8,128)S(1)} %get-tuple-element.62, ...), kind=kLoop, calls=%fused_computation.18 | loop fusion | flops 4980736 | bytes 3670532 | tf_op jit(solution)/shard_map/jit(_where)/select_n | solution.py:328
  (83 shorter events, 5.9 us)
Async XLA Ops:
  0.6 16.5 %copy-start.1 = (f32[16,32,512]{2,1,0:T(8,128)S(1)}, f32[16,32,512]{2,1,0:T(8,128)}, u32[]{:S(2)}) copy-start(f32[16,32,512]{2,1,0:T(8,128)} %param.6) | copy-start | bytes 3145732
  2.1 16.9 %copy-start.6 = (s32[16,2]{0,1:T(2,128)S(1)}, s32[16,2]{0,1:T(2,128)}, u32[]{:S(2)}) copy-start(s32[16,2]{0,1:T(2,128)} %param.8) | copy-start | bytes 388
  2.1 10.6 %collective-permute-start = (f32[16,11,512]{2,1,0:T(8,128)S(1)}, f32[16,11,512]{2,1,0:T(8,128)S(1)}, u32[]{:S(2)}, u32[]{:S(2)}) collective-permute-start(f32[16,11,512]{2,1,0:T(8,128)S(1)} %get-tuple-element.57), channel_id=1, source_target_pairs={{0,2},{2,4},{4,6},{1,3},{3,5},{5,7},{8,10},{10,12},{12,14},{9,11},... | collective-permute-start | bytes 1081352 | tf_op jit(solution)/shard_map/ppermute | solution.py:28
  6.6 10.5 %collective-permute-start.1 = (f32[16,11,512]{2,1,0:T(8,128)S(1)}, f32[16,11,512]{2,1,0:T(8,128)S(1)}, u32[]{:S(2)}, u32[]{:S(2)}) collective-permute-start(f32[16,11,512]{2,1,0:T(8,128)S(1)} %get-tuple-element.58), channel_id=1, source_target_pairs={{2,0},{4,2},{6,4},{3,1},{5,3},{7,5},{10,8},{12,10},{14,12},{11,9},... | collective-permute-start | bytes 1081352 | tf_op jit(solution)/shard_map/ppermute | solution.py:29
  17.7 3.1 %collective-permute-start.2 = (f32[11,864]{1,0:T(8,128)S(1)}, f32[11,864]{1,0:T(8,128)S(1)}, u32[]{:S(2)}, u32[]{:S(2)}) collective-permute-start(f32[11,864]{1,0:T(8,128)S(1)} %reshape.532), channel_id=1, source_target_pairs={{0,1},{1,0},{2,3},{3,2},{4,5},{5,4},{6,7},{7,6},{8,9},{9,8},{10,11... | collective-permute-start | bytes 114056 | tf_op jit(solution)/shard_map/ppermute | solution.py:48
  27.8 17.5 %collective-permute-start.3 = (f32[16,8,512]{2,1,0:T(8,128)}, f32[16,8,512]{2,1,0:T(8,128)S(1)}, u32[]{:S(2)}, u32[]{:S(2)}) collective-permute-start(f32[16,8,512]{2,1,0:T(8,128)} %get-tuple-element.16), channel_id=1, source_target_pairs={{0,8},{8,16},{16,24},{24,0},{1,9},{9,17},{17,25},{25,1},{2,10},{10... | collective-permute-start | bytes 786440 | tf_op jit(solution)/shard_map/ppermute | solution.py:272
  33.0 13.5 %collective-permute-start.4 = (f32[16,8,512]{2,1,0:T(8,128)}, f32[16,8,512]{2,1,0:T(8,128)S(1)}, u32[]{:S(2)}, u32[]{:S(2)}) collective-permute-start(f32[16,8,512]{2,1,0:T(8,128)} %get-tuple-element.17), channel_id=1, source_target_pairs={{0,16},{8,24},{16,0},{24,8},{1,17},{9,25},{17,1},{25,9},{2,18},{10... | collective-permute-start | bytes 786440 | tf_op jit(solution)/shard_map/ppermute | solution.py:272
  39.3 4.0 %copy-start.7 = (f32[16,8,512]{2,1,0:T(8,128)S(1)}, f32[16,8,512]{2,1,0:T(8,128)}, u32[]{:S(2)}) copy-start(f32[16,8,512]{2,1,0:T(8,128)} %get-tuple-element.18) | copy-start | bytes 786436
  43.3 8.2 %collective-permute-start.5 = (f32[16,8,512]{2,1,0:T(8,128)S(1)}, f32[16,8,512]{2,1,0:T(8,128)S(1)}, u32[]{:S(2)}, u32[]{:S(2)}) collective-permute-start(f32[16,8,512]{2,1,0:T(8,128)S(1)} %copy-done.7), channel_id=1, source_target_pairs={{0,24},{8,0},{16,8},{24,16},{1,25},{9,1},{17,9},{25,17},{2,26},{10... | collective-permute-start | bytes 786440 | tf_op jit(solution)/shard_map/ppermute | solution.py:272
  53.8 5.5 %copy-start.2 = (f32[16,8,512]{2,1,0:T(8,128)S(1)}, f32[16,8,512]{2,1,0:T(8,128)}, u32[]{:S(2)}) copy-start(f32[16,8,512]{2,1,0:T(8,128)} %get-tuple-element.12) | copy-start | bytes 786436
  53.8 5.5 %copy-start.3 = (f32[16,8,512]{2,1,0:T(8,128)S(1)}, f32[16,8,512]{2,1,0:T(8,128)}, u32[]{:S(2)}) copy-start(f32[16,8,512]{2,1,0:T(8,128)} %get-tuple-element.13) | copy-start | bytes 786436
  53.8 5.5 %copy-start.4 = (f32[16,8,512]{2,1,0:T(8,128)S(1)}, f32[16,8,512]{2,1,0:T(8,128)}, u32[]{:S(2)}) copy-start(f32[16,8,512]{2,1,0:T(8,128)} %get-tuple-element.14) | copy-start | bytes 786436
  53.8 5.5 %copy-start.5 = (f32[16,8,512]{2,1,0:T(8,128)S(1)}, f32[16,8,512]{2,1,0:T(8,128)}, u32[]{:S(2)}) copy-start(f32[16,8,512]{2,1,0:T(8,128)} %get-tuple-element.11) | copy-start | bytes 786436
  55.1 11.4 %all-to-all-start = ((f32[8,8,512]{2,1,0:T(8,128)}), f32[8,8,512]{2,1,0:T(8,128)S(1)}, u32[]{:S(2)}, u32[]{:S(2)}) async-start(f32[8,8,512]{2,1,0:T(8,128)} %tile.2), calls=%async_computation | async-start | bytes 262144 | tf_op jit(solution)/shard_map/all_to_all | solution.py:299
  66.7 5.7 %collective-permute-start.6 = (f32[4,520]{1,0:T(4,128)S(1)}, f32[4,520]{1,0:T(4,128)S(1)}, u32[]{:S(2)}, u32[]{:S(2)}) collective-permute-start(f32[4,520]{1,0:T(4,128)S(1)} %get-tuple-element.67), channel_id=1, source_target_pairs={{0,2},{2,4},{4,6},{1,3},{3,5},{5,7},{8,10},{10,12},{12,14},{9,11},... | collective-permute-start | bytes 24968 | tf_op jit(solution)/shard_map/ppermute | solution.py:28
  69.7 5.0 %collective-permute-start.7 = (f32[4,520]{1,0:T(4,128)S(1)}, f32[4,520]{1,0:T(4,128)S(1)}, u32[]{:S(2)}, u32[]{:S(2)}) collective-permute-start(f32[4,520]{1,0:T(4,128)S(1)} %get-tuple-element.68), channel_id=1, source_target_pairs={{2,0},{4,2},{6,4},{3,1},{5,3},{7,5},{10,8},{12,10},{14,12},{11,9},... | collective-permute-start | bytes 24968 | tf_op jit(solution)/shard_map/ppermute | solution.py:29
  75.3 1.3 %copy-start = (s32[16,32,512]{2,1,0:T(8,128)S(1)}, s32[16,32,512]{2,1,0:T(8,128)}, u32[]{:S(2)}) copy-start(s32[16,32,512]{2,1,0:T(8,128)} %bad.7) | copy-start | bytes 3145732
